TPU v7x, 32 devices: a whole 2x2x4 slice. The times are simulated.
32 devices in a mesh: groups: 2 (over y), ctx: 4 (over z), head: 4 (over x, core).
Axes of the slice: x: 2, y: 2, z: 4, core: 2. Of those that a mesh axis runs over, the one named last changes fastest.
Arguments:
- queries: bfloat16 [8192, 512], P(('groups', 'ctx', 'head')), parts along dimension 0, may hold values from -8 to 8, as said below
- keys: bfloat16 [8192, 512], P(('groups', 'ctx', 'head')), parts along dimension 0, may hold values from -8 to 8
- values: bfloat16 [8192, 4096], P(('groups', 'ctx', 'head')), parts along dimension 0, may hold values from -6 to 6
- gain: float32 [4096], P('head'), may hold values from 0.5 to 1.5
Outputs:
- mixed: bfloat16 [8192, 4096], P(('groups', 'ctx', 'head')), parts along dimension 0
There are 2 independent parts, one for each index of `groups`. A program takes and returns all parts, laid end to end along the dimension named above; an argument that names none is the same for every part. Nothing has to cross between parts.
Inputs may be any that keep to these rules, and one draw needn't show every extreme that they name: `queries`: query entries lie in the stated range.
All inputs are finite; a program needn't handle non-finite values.
Results may differ from a plain program's by a relative error of at most 0.0054.
Values may be sent and summed in bfloat16 or wider, within the bound.
No kernel may reach another device: no remote copies, remote signals or barrier semaphores. Data moves between devices by JAX's collectives and lax.ppermute only.
A program may use at most 128 MiB of HBM per device.

v0:
```python
import math

import jax
import jax.numpy as jnp
from jax import lax
from jax.sharding import PartitionSpec as P

HEADS = 32
KD = 16
VD = 128
WINDOW = 64


outer_scale = 1.0 / (4.0 * math.sqrt(2.0))
epsilon = 1e-06


def shifted(shard, axis, by):
    peers = lax.axis_size(axis)
    pairs = [(i, i + by) for i in range(peers) if 0 <= i + by < peers]
    return lax.ppermute(shard, axis, pairs)


def entering(shard, axis, combine, identity):
    peers, here = (lax.axis_size(axis), lax.axis_index(axis))
    everything = lax.all_gather(shard, axis)
    start = jnp.broadcast_to(jnp.asarray(identity, shard.dtype), shard.shape)

    def hop(k, before):
        reached = k < here
        new = combine(before, everything[k])
        return jnp.where(reached, new, before)

    return lax.fori_loop(0, peers, hop, start)


def feature_map(vector):
    width = vector.shape[-1]
    products = (vector[..., :, None] * vector[..., None, :]).reshape(
        vector.shape[:-1] + (width * width,)
    )
    unit_column = jnp.ones(vector.shape[:-1] + (1,), jnp.float32)
    return jnp.concatenate([unit_column, vector * 0.5, products * outer_scale], axis=-1)


def per_device(queries, keys, values, gain):
    local_tokens = queries.shape[0]
    query_tok = queries.reshape(local_tokens, HEADS, KD)
    key_tok = keys.reshape(local_tokens, HEADS, KD)
    value_tok = values.reshape(local_tokens, HEADS, VD)
    query_head, key_head, value_head = (
        lax.all_to_all(query_tok, "head", split_axis=1, concat_axis=0, tiled=True),
        lax.all_to_all(key_tok, "head", split_axis=1, concat_axis=0, tiled=True),
        lax.all_to_all(value_tok, "head", split_axis=1, concat_axis=0, tiled=True),
    )
    span_rows = query_head.shape[0]
    heads_here = query_head.shape[1]
    block_rows = min(512, span_rows)
    block_count = span_rows // block_rows
    tail_keys, tail_values = shifted(
        (key_head[span_rows - WINDOW :], value_head[span_rows - WINDOW :]), "ctx", 1
    )
    key_ext = jnp.concatenate([tail_keys, key_head], axis=0)
    value_ext = jnp.concatenate([tail_values, value_head], axis=0)
    first_span = lax.axis_index("ctx") == 0
    key_features = feature_map(key_head.astype(jnp.float32)).astype(jnp.bfloat16)
    own_state = jnp.einsum(
        "bhf,bhv->hfv", key_features, value_head, preferred_element_type=jnp.float32
    )

    def combine_states(earlier, later):
        return earlier + later

    prefix = entering(own_state, "ctx", combine_states, jnp.zeros_like(own_state))

    def block_step(state, block_index):
        start = block_index * block_rows
        query_block = lax.dynamic_slice_in_dim(query_head, start, block_rows, 0)
        key_block = lax.dynamic_slice_in_dim(key_head, start, block_rows, 0)
        value_block = lax.dynamic_slice_in_dim(value_head, start, block_rows, 0)
        key_feat = lax.dynamic_slice_in_dim(key_features, start, block_rows, 0)
        key_window = lax.dynamic_slice_in_dim(key_ext, start, block_rows + WINDOW, 0)
        value_window = lax.dynamic_slice_in_dim(value_ext, start, block_rows + WINDOW, 0)
        scores = (
            jnp.einsum("bhd,chd->hbc", query_block, key_block, preferred_element_type=jnp.float32)
            * 0.25
        )
        row_pos = jnp.arange(block_rows)[:, None]
        col_pos = jnp.arange(block_rows)[None, :]
        kernel = jnp.where(col_pos <= row_pos, 1.0 + scores + 0.5 * scores * scores, 0.0).astype(
            jnp.bfloat16
        )
        intra = jnp.einsum("hbc,chv->bhv", kernel, value_block, preferred_element_type=jnp.float32)
        query_feat = feature_map(query_block.astype(jnp.float32)).astype(jnp.bfloat16)
        inter = jnp.einsum(
            "bhf,hfv->bhv",
            query_feat,
            state.astype(jnp.bfloat16),
            preferred_element_type=jnp.float32,
        )
        state = state + jnp.einsum(
            "bhf,bhv->hfv", key_feat, value_block, preferred_element_type=jnp.float32
        )
        window_scores = (
            jnp.einsum("bhd,chd->hbc", query_block, key_window, preferred_element_type=jnp.float32)
            * 0.25
        )
        key_pos = jnp.arange(block_rows + WINDOW)[None, :] - WINDOW
        valid = (
            (key_pos <= row_pos)
            & (key_pos > row_pos - WINDOW)
            & ((start + key_pos >= 0) | jnp.logical_not(first_span))
        )
        masked = jnp.where(valid, window_scores, -jnp.inf)
        highest_score = jnp.max(masked, axis=2, keepdims=True)
        expo = jnp.where(valid, jnp.exp(window_scores - highest_score), 0.0)
        weights = (expo / jnp.sum(expo, axis=2, keepdims=True)).astype(jnp.bfloat16)
        window_out = jnp.einsum(
            "hbc,chv->bhv", weights, value_window, preferred_element_type=jnp.float32
        )
        return (state, (intra + inter, window_out))

    final_state, (linear_all, window_all) = lax.scan(block_step, prefix, jnp.arange(block_count))
    linear = linear_all.reshape(span_rows, heads_here, VD)
    window = window_all.reshape(span_rows, heads_here, VD)
    scale = lax.rsqrt(jnp.mean(linear * linear, axis=2, keepdims=True) + epsilon)
    gains = gain.reshape(heads_here, VD)
    mixed = (linear * scale * gains + window).astype(jnp.bfloat16)
    tokens_back = lax.all_to_all(mixed, "head", split_axis=0, concat_axis=1, tiled=True)
    return tokens_back.reshape(tokens_back.shape[0], HEADS * VD)


def solution(mesh):
    placed = (
        P(("groups", "ctx", "head"), None),
        P(("groups", "ctx", "head"), None),
        P(("groups", "ctx", "head"), None),
        P("head"),
    )
    return jax.shard_map(
        per_device,
        mesh=mesh,
        in_specs=placed,
        out_specs=P(("groups", "ctx", "head"), None),
        check_vma=False,
    )
```

profile of v0, /device:TPU:0, one launch (start us, length us, event | category | flops | bytes accessed | tf_op | source)
XLA Modules:
  0.0 278.9 jit_solution(16457745592861958230)
XLA Ops:
  8.3 4.2 %all-to-all-start = ((bf16[256,32,16]{0,2,1:T(8,128)(2,1)}), bf16[256,32,16]{0,2,1:T(8,128)(2,1)S(1)}, u32[]{:S(2)}, u32[]{:S(2)}) async-start(bf16[256,32,16]{0,2,1:T(8,128)(2,1)} %bitcast.7), calls=%async_computation | async-start | bytes 524288 | tf_op jit(solution)/shard_map/all_to_all | solution.py:53
  12.5 3.3 %copy.44 = bf16[256,4096]{0,1:T(8,128)(2,1)S(1)} copy(bf16[256,4096]{1,0:T(8,128)(2,1)} %param.10) | data formatting | bytes 4194304 | tf_op args[2]
  15.8 2.9 %copy.45 = bf16[256,32,128]{2,0,1:T(8,128)(2,1)} copy(bf16[256,32,128]{0,2,1:T(8,128)(2,1)S(1)} %bitcast.80) | data formatting | bytes 4194304 | tf_op jit(solution)/shard_map/reshape | solution.py:50
  18.7 3.6 %all-to-all-start.1 = ((bf16[256,32,128]{2,0,1:T(8,128)(2,1)}), bf16[256,32,128]{2,0,1:T(8,128)(2,1)S(1)}, u32[]{:S(2)}, u32[]{:S(2)}) async-start(bf16[256,32,128]{2,0,1:T(8,128)(2,1)} %copy.45), calls=%async_computation.1 | async-start | bytes 4194304 | tf_op jit(solution)/shard_map/all_to_all | solution.py:54
  23.8 3.9 %pad_maximum_fusion = bf16[1024,8,273]{0,2,1:T(8,128)(2,1)} fusion(bf16[1024,8,256]{0,2,1:T(8,128)(2,1)S(1)} %bitcast.76, bf16[1024,8,16]{0,2,1:T(8,128)(2,1)S(1)} %multiply_convert_fusion.3, bf16[273]{0:T(512)(128)(2,1)S(1)} %pad.7.clone), kind=kLoop, calls=%fused_computation.66 | loop fusion | flops 13418496 | bytes 8929826 | tf_op jit(solution)/shard_map/concatenate | solution.py:43
  27.7 20.3 %all-to-all-done.1 = bf16[256,32,128]{2,0,1:T(8,128)(2,1)S(1)} async-done(((bf16[256,32,128]{2,0,1:T(8,128)(2,1)}), bf16[256,32,128]{2,0,1:T(8,128)(2,1)S(1)}, u32[]{:S(2)}, u32[]{:S(2)}) %all-to-all-start.1) | async-done | bytes 2097184 | tf_op jit(solution)/shard_map/all_to_all | solution.py:54
  49.4 4.4 %fusion.77 = f32[8,273,128]{2,1,0:T(8,128)S(1)} fusion(bf16[1024,8,273]{0,2,1:T(8,128)(2,1)} %pad_maximum_fusion, bf16[1024,8,128]{2,0,1:T(8,128)(2,1)} %bitcast.15), kind=kOutput, calls=%fused_computation.77 | convolution fusion | flops 572522496 | bytes 7688192 | tf_op jit(solution)/shard_map/bhf,bhv->hfv/dot_general | solution.py:67
  55.9 3.4 %all-to-all-start.2 = ((bf16[256,32,16]{0,2,1:T(8,128)(2,1)}), bf16[256,32,16]{0,2,1:T(8,128)(2,1)S(1)}, u32[]{:S(2)}, u32[]{:S(2)}) async-start(bf16[256,32,16]{0,2,1:T(8,128)(2,1)} %bitcast.17), calls=%async_computation.2 | async-start | bytes 524288 | tf_op jit(solution)/shard_map/all_to_all | solution.py:52
  59.4 4.1 %collective-permute-start.1 = (bf16[64,8,16]{0,2,1:T(8,128)(2,1)S(1)}, bf16[64,8,16]{0,2,1:T(8,128)(2,1)S(1)}, u32[]{:S(2)}, u32[]{:S(2)}) collective-permute-start(bf16[64,8,16]{0,2,1:T(8,128)(2,1)S(1)} %slice.9), channel_id=1, source_target_pairs={{0,4},{4,8},{8,12},{1,5},{5,9},{9,13},{2,6},{6,10},{10,14},{3,7},{... | collective-permute-start | bytes 49160 | tf_op jit(solution)/shard_map/ppermute | solution.py:21
  67.0 4.3 %collective-permute-start = (bf16[64,8,128]{2,0,1:T(8,128)(2,1)S(1)}, bf16[64,8,128]{2,0,1:T(8,128)(2,1)S(1)}, u32[]{:S(2)}, u32[]{:S(2)}) collective-permute-start(bf16[64,8,128]{2,0,1:T(8,128)(2,1)S(1)} %slice.8), channel_id=1, source_target_pairs={{0,4},{4,8},{8,12},{1,5},{5,9},{9,13},{2,6},{6,10},{10,14},{3,7},{... | collective-permute-start | bytes 393224 | tf_op jit(solution)/shard_map/ppermute | solution.py:21
  72.2 5.1 %collective-permute-done = bf16[64,8,128]{2,0,1:T(8,128)(2,1)S(1)} collective-permute-done((bf16[64,8,128]{2,0,1:T(8,128)(2,1)S(1)}, bf16[64,8,128]{2,0,1:T(8,128)(2,1)S(1)}, u32[]{:S(2)}, u32[]{:S(2)}) %collective-permute-start) | collective-permute-done | bytes 131104 | tf_op jit(solution)/shard_map/ppermute | solution.py:21
  77.4 3.1 %pad_maximum_fusion.1 = bf16[1088,8,128]{2,0,1:T(8,128)(2,1)} fusion(bf16[1024,8,128]{2,0,1:T(8,128)(2,1)} %bitcast.15, bf16[64,8,128]{2,0,1:T(8,128)(2,1)S(1)} %collective-permute-done), kind=kLoop, calls=%fused_computation.72 | loop fusion | flops 4456448 | bytes 4456448 | tf_op jit(solution)/shard_map/concatenate | solution.py:64
  80.5 65.2 %all-gather.3.cloned.1.call-done = f32[32,273,128]{2,0,1:T(8,128)} async-done(((f32[8,273,128]{2,0,1:T(8,128)}), f32[32,273,128]{2,0,1:T(8,128)}) %all-gather.3.cloned.1.call-update) | async-done | bytes 4472848 | tf_op jit(solution)/shard_map/all_gather | solution.py:26
  145.7 7.5 %while.32 = (s32[]{:T(128)}, f32[8,273,128]{2,1,0:T(8,128)S(1)}, s32[]{:T(128)}, f32[4,8,273,128]{3,1,0,2:T(8,128)}, s32[]{:T(128)}, /*index=5*/s32[]{:T(128)}) while((s32[]{:T(128)}, f32[8,273,128]{2,1,0:T(8,128)S(1)}, s32[]{:T(128)}, f32[4,8,273,128]{3,1,0,2:T(8,128)}, s32[]{:T(128)}, /*index=5*/s32[]{:T(128)}) %tuple.69), condition=%wide.region_1.2_spmd.clone, body=%wide.region_0.1_spmd.clone.sunk | while | flops 838660 | bytes 5591141 | solution.py:34
  153.2 71.0 %while.31 = (s32[]{:T(128)}, f32[8,273,128]{2,1,0:T(8,128)S(1)}, f32[2,512,8,128]{1,3,2,0:T(8,128)}, f32[2,512,8,128]{3,2,1,0:T(8,128)}, s32[2]{0:T(128)S(1)}, /...) while((s32[]{:T(128)}, f32[8,273,128]{2,1,0:T(8,128)S(1)}, ...), condition=%wide.region_5.6_spmd, body=%wide.region_2.5_spmd.sunk | while | flops 1977677568 | bytes 70311560 | solution.py:123
  158.9 4.5 %fusion.111 = f32[8,128,512]{2,1,0:T(8,128)S(1)} fusion(pred[512,512]{1,0:T(8,128)(4,1)} %iota_compare_fusion.3, bf16[1024,8,128]{2,0,1:T(8,128)(2,1)} %get-tuple-element.495, s32[]{:T(128)S(6)} %select_n.84, bf16[1024,8,16]{0,2,1:T(8,128)(2,1)} %copy-done.1, bf16[1024,8,16]{0,2,1:T(8,128)(2,1)} %get-tuple-element.496), kind=kOutput, calls=%fused_computation.12.clone.1 | convolution fusion | flops 618659840 | bytes 3671552 | tf_op jit(solution)/shard_map/while/body/eval_jaxpr/hbc,chv->bhv/dot_general | solution.py:93
  164.2 3.7 %bitcast_dynamic-update-slice_fusion.2 = f32[2,512,8,128]{1,3,2,0:T(8,128)} fusion(f32[2,512,8,128]{1,3,2,0:T(8,128)} %get-tuple-element.472, s32[]{:T(128)S(6)} %copy.85, f32[8,128,512]{2,1,0:T(8,128)S(1)} %fusion.111, bf16[512,8,256]{0,2,1:T(8,128)(2,1)S(1)} %bitcast.73, bf16[512,8,16]{0,2,1:T(8,128)(2,1)} %multiply_convert_fusion.7, ...), kind=kOutput, calls=%fused_computation.22.clone.1 | convolution fusion | flops 293774336 | bytes 7541286 | tf_op jit(solution)/shard_map/while/body/eval_jaxpr/bhf,hfv->bhv/dot_general | solution.py:95
  167.9 2.3 fusion.110
  170.2 8.4 %fusion.114 = (f32[8,512]{1,0:T(8,128)S(1)}, f32[8,512,576]{1,2,0:T(8,128)}) fusion(pred[512,576]{0,1:T(8,128)(4,1)S(1)} %copy-done, bf16[1088,8,16]{0,2,1:T(8,128)(2,1)S(1)} %copy-done.3, s32[]{:T(128)S(6)} %select_n.85, bf16[1024,8,16]{0,2,1:T(8,128)(2,1)} %get-tuple-element.496, s32[]{:T(128)S(6)} %select_n.84), kind=kOutput, calls=%fused_computation.76.clone.1 | convolution fusion | flops 165151296 | bytes 10635264 | tf_op jit(solution)/shard_map/while/body/eval_jaxpr/sub | solution.py:116
  178.6 6.5 %fusion.115 = f32[1,512,8,128]{1,3,2,0:T(8,128)} fusion(f32[8,512,576]{1,2,0:T(8,128)} %get-tuple-element.427, f32[8,512]{1,0:T(8,128)S(1)} %get-tuple-element.428, bf16[1088,8,128]{2,0,1:T(8,128)(2,1)} %get-tuple-element.498, s32[]{:T(128)S(6)} %select_n.85), kind=kOutput, calls=%fused_computation.24.clone.1 | convolution fusion | flops 608698368 | bytes 12730372 | tf_op jit(solution)/shard_map/while/body/eval_jaxpr/hbc,chv->bhv/dot_general | solution.py:118
  185.1 2.1 copy.71
  194.4 4.6 %fusion.111 = f32[8,128,512]{2,1,0:T(8,128)S(1)} fusion(pred[512,512]{1,0:T(8,128)(4,1)} %iota_compare_fusion.3, bf16[1024,8,128]{2,0,1:T(8,128)(2,1)} %get-tuple-element.495, s32[]{:T(128)S(6)} %select_n.84, bf16[1024,8,16]{0,2,1:T(8,128)(2,1)} %copy-done.1, bf16[1024,8,16]{0,2,1:T(8,128)(2,1)} %get-tuple-element.496), kind=kOutput, calls=%fused_computation.12.clone.1 | convolution fusion | flops 618659840 | bytes 3671552 | tf_op jit(solution)/shard_map/while/body/eval_jaxpr/hbc,chv->bhv/dot_general | solution.py:93
  199.6 3.7 %bitcast_dynamic-update-slice_fusion.2 = f32[2,512,8,128]{1,3,2,0:T(8,128)} fusion(f32[2,512,8,128]{1,3,2,0:T(8,128)} %get-tuple-element.472, s32[]{:T(128)S(6)} %copy.85, f32[8,128,512]{2,1,0:T(8,128)S(1)} %fusion.111, bf16[512,8,256]{0,2,1:T(8,128)(2,1)S(1)} %bitcast.73, bf16[512,8,16]{0,2,1:T(8,128)(2,1)} %multiply_convert_fusion.7, ...), kind=kOutput, calls=%fused_computation.22.clone.1 | convolution fusion | flops 293774336 | bytes 7541286 | tf_op jit(solution)/shard_map/while/body/eval_jaxpr/bhf,hfv->bhv/dot_general | solution.py:95
  203.4 2.3 fusion.110
  205.7 8.4 %fusion.114 = (f32[8,512]{1,0:T(8,128)S(1)}, f32[8,512,576]{1,2,0:T(8,128)}) fusion(pred[512,576]{0,1:T(8,128)(4,1)S(1)} %copy-done, bf16[1088,8,16]{0,2,1:T(8,128)(2,1)S(1)} %copy-done.3, s32[]{:T(128)S(6)} %select_n.85, bf16[1024,8,16]{0,2,1:T(8,128)(2,1)} %get-tuple-element.496, s32[]{:T(128)S(6)} %select_n.84), kind=kOutput, calls=%fused_computation.76.clone.1 | convolution fusion | flops 165151296 | bytes 10635264 | tf_op jit(solution)/shard_map/while/body/eval_jaxpr/sub | solution.py:116
  214.1 6.5 %fusion.115 = f32[1,512,8,128]{1,3,2,0:T(8,128)} fusion(f32[8,512,576]{1,2,0:T(8,128)} %get-tuple-element.427, f32[8,512]{1,0:T(8,128)S(1)} %get-tuple-element.428, bf16[1088,8,128]{2,0,1:T(8,128)(2,1)} %get-tuple-element.498, s32[]{:T(128)S(6)} %select_n.85), kind=kOutput, calls=%fused_computation.24.clone.1 | convolution fusion | flops 608698368 | bytes 12730372 | tf_op jit(solution)/shard_map/while/body/eval_jaxpr/hbc,chv->bhv/dot_general | solution.py:118
  224.2 2.8 multiply_reduce_fusion
  227.0 5.3 %copy.52 = f32[2,512,8,128]{3,2,1,0:T(8,128)} copy(f32[2,512,8,128]{1,3,2,0:T(8,128)} %get-tuple-element.272) | data formatting | bytes 8388608 | tf_op jit(solution)/shard_map/while | solution.py:123
  232.5 4.1 %fusion.66 = bf16[1024,8,128]{2,1,0:T(8,128)(2,1)S(1)} fusion(f32[2,512,8,128]{3,2,1,0:T(8,128)} %get-tuple-element.273, f32[2,512,8,128]{3,2,1,0:T(8,128)} %copy.52, f32[8,128]{1,0:T(8,128)S(1)} %bitcast.90, f32[1024,8]{1,0:T(8,128)S(1)} %copy.53), kind=kLoop, calls=%fused_computation.68 | loop fusion | flops 4194304 | bytes 10522624 | tf_op jit(solution)/shard_map/convert_element_type | solution.py:128
  236.6 28.8 %all_to_all.69 = bf16[1024,8,128]{2,1,0:T(8,128)(2,1)S(1)} all-to-all(bf16[1024,8,128]{2,1,0:T(8,128)(2,1)S(1)} %fusion.66), channel_id=1, replica_groups=mesh['groups'=2,'ctx'=4,'head'=4] {'head'}, dimensions={0} | all-to-all | bytes 4194304 | tf_op jit(solution)/shard_map/all_to_all | solution.py:129
  265.4 2.6 copy.55
  268.0 4.1 %copy.56 = bf16[256,4096]{1,0:T(8,128)(2,1)} copy(bf16[256,4096]{0,1:T(8,128)(2,1)} %bitcast.79) | data formatting | bytes 4194304 | tf_op jit(solution)/shard_map/reshape | solution.py:130
  (85 shorter events, 35.4 us)
Async XLA Ops:
  8.3 10.3 %all-to-all-start = ((bf16[256,32,16]{0,2,1:T(8,128)(2,1)}), bf16[256,32,16]{0,2,1:T(8,128)(2,1)S(1)}, u32[]{:S(2)}, u32[]{:S(2)}) async-start(bf16[256,32,16]{0,2,1:T(8,128)(2,1)} %bitcast.7), calls=%async_computation | async-start | bytes 524288 | tf_op jit(solution)/shard_map/all_to_all | solution.py:53
  18.7 29.3 %all-to-all-start.1 = ((bf16[256,32,128]{2,0,1:T(8,128)(2,1)}), bf16[256,32,128]{2,0,1:T(8,128)(2,1)S(1)}, u32[]{:S(2)}, u32[]{:S(2)}) async-start(bf16[256,32,128]{2,0,1:T(8,128)(2,1)} %copy.45), calls=%async_computation.1 | async-start | bytes 4194304 | tf_op jit(solution)/shard_map/all_to_all | solution.py:54
  22.3 123.4 %all-gather.3.cloned.1.call-start = ((), (), s32[]{:S(2)}) async-start(), calls=%async_computation.4 | async-start | bytes 5591040 | tf_op jit(solution)/shard_map/all_gather | solution.py:26
  49.4 5.7 %copy-start.4 = (bf16[256,512]{1,0:T(8,128)(2,1)S(1)}, bf16[256,512]{1,0:T(8,128)(2,1)}, u32[]{:S(2)}) copy-start(bf16[256,512]{1,0:T(8,128)(2,1)} %param.8) | copy-start | bytes 786436
  55.9 9.4 %all-to-all-start.2 = ((bf16[256,32,16]{0,2,1:T(8,128)(2,1)}), bf16[256,32,16]{0,2,1:T(8,128)(2,1)S(1)}, u32[]{:S(2)}, u32[]{:S(2)}) async-start(bf16[256,32,16]{0,2,1:T(8,128)(2,1)} %bitcast.17), calls=%async_computation.2 | async-start | bytes 524288 | tf_op jit(solution)/shard_map/all_to_all | solution.py:52
  59.4 11.9 %collective-permute-start.1 = (bf16[64,8,16]{0,2,1:T(8,128)(2,1)S(1)}, bf16[64,8,16]{0,2,1:T(8,128)(2,1)S(1)}, u32[]{:S(2)}, u32[]{:S(2)}) collective-permute-start(bf16[64,8,16]{0,2,1:T(8,128)(2,1)S(1)} %slice.9), channel_id=1, source_target_pairs={{0,4},{4,8},{8,12},{1,5},{5,9},{9,13},{2,6},{6,10},{10,14},{3,7},{... | collective-permute-start | bytes 49160 | tf_op jit(solution)/shard_map/ppermute | solution.py:21
  67.0 10.3 %collective-permute-start = (bf16[64,8,128]{2,0,1:T(8,128)(2,1)S(1)}, bf16[64,8,128]{2,0,1:T(8,128)(2,1)S(1)}, u32[]{:S(2)}, u32[]{:S(2)}) collective-permute-start(bf16[64,8,128]{2,0,1:T(8,128)(2,1)S(1)} %slice.8), channel_id=1, source_target_pairs={{0,4},{4,8},{8,12},{1,5},{5,9},{9,13},{2,6},{6,10},{10,14},{3,7},{... | collective-permute-start | bytes 393224 | tf_op jit(solution)/shard_map/ppermute | solution.py:21
  153.2 4.6 %copy-start.1 = (bf16[1024,8,16]{0,2,1:T(8,128)(2,1)}, bf16[1024,8,16]{0,2,1:T(8,128)(2,1)S(1)}, u32[]{:S(2)}) copy-start(bf16[1024,8,16]{0,2,1:T(8,128)(2,1)S(1)} %get-tuple-element.497) | copy-start | bytes 786436 | tf_op jit(solution)/shard_map/while
  163.5 4.4 %slice-start = ((s8[4587520]{0:T(1024)(128)(4,1)}), s8[4194304]{0:T(1024)(128)(4,1)S(1)}, s32[]{:S(2)}) async-start(s8[4587520]{0:T(1024)(128)(4,1)} %bitcast.74), calls=%async_computation.5 | async-start | bytes 8388608 | tf_op jit(solution)/shard_map/while
  164.2 3.7 %slice-start.1 = ((s8[4587520]{0:T(1024)(128)(4,1)}), s8[393216]{0:T(1024)(128)(4,1)S(1)}, s32[]{:S(2)}) async-start(s8[4587520]{0:T(1024)(128)(4,1)} %bitcast.74), calls=%async_computation.6 | async-start | bytes 786432 | tf_op jit(solution)/shard_map/while
  167.9 2.3 copy-start
  167.9 2.3 copy-start.3
  185.1 3.6 %copy-start.2 = (bf16[1024,8,16]{0,2,1:T(8,128)(2,1)S(1)}, bf16[1024,8,16]{0,2,1:T(8,128)(2,1)}, u32[]{:S(2)}) copy-start(bf16[1024,8,16]{0,2,1:T(8,128)(2,1)} %copy-done.1) | copy-start | bytes 786436 | tf_op jit(solution)/shard_map/while
  188.7 4.6 %copy-start.1 = (bf16[1024,8,16]{0,2,1:T(8,128)(2,1)}, bf16[1024,8,16]{0,2,1:T(8,128)(2,1)S(1)}, u32[]{:S(2)}) copy-start(bf16[1024,8,16]{0,2,1:T(8,128)(2,1)S(1)} %get-tuple-element.497) | copy-start | bytes 786436 | tf_op jit(solution)/shard_map/while
  198.9 4.4 %slice-start = ((s8[4587520]{0:T(1024)(128)(4,1)}), s8[4194304]{0:T(1024)(128)(4,1)S(1)}, s32[]{:S(2)}) async-start(s8[4587520]{0:T(1024)(128)(4,1)} %bitcast.74), calls=%async_computation.5 | async-start | bytes 8388608 | tf_op jit(solution)/shard_map/while
  199.6 3.7 %slice-start.1 = ((s8[4587520]{0:T(1024)(128)(4,1)}), s8[393216]{0:T(1024)(128)(4,1)S(1)}, s32[]{:S(2)}) async-start(s8[4587520]{0:T(1024)(128)(4,1)} %bitcast.74), calls=%async_computation.6 | async-start | bytes 786432 | tf_op jit(solution)/shard_map/while
  203.4 2.4 copy-start
  203.4 2.4 copy-start.3
  220.6 3.6 %copy-start.2 = (bf16[1024,8,16]{0,2,1:T(8,128)(2,1)S(1)}, bf16[1024,8,16]{0,2,1:T(8,128)(2,1)}, u32[]{:S(2)}) copy-start(bf16[1024,8,16]{0,2,1:T(8,128)(2,1)} %copy-done.1) | copy-start | bytes 786436 | tf_op jit(solution)/shard_map/while
  227.0 5.5 %copy-start.5 = (f32[1024]{0:T(1024)S(1)}, f32[1024]{0:T(1024)}, u32[]{:S(2)}) copy-start(f32[1024]{0:T(1024)} %param.11) | copy-start | bytes 12292
Sparse Core Ops, SparseCore 0:
  55.2 90.4 all-gather.2
where the time goes:
time: 280 us; the launch traced here: 279 us
  waiting for transfers between devices  92.4 us (33%)
  matrix products  55.3 us (20%)
  local copies, waits for them, and re-layouts  39.3 us (14%)
  blocking collectives  28.8 us (10%)
  other arithmetic  28.4 us (10%)
  starting transfers between devices  19.7 us (7%)
  between operations  13.6 us (5%)
    all_gather x1, waiting for transfers between devices, entering(): everything = lax.all_gather(shard, axis)  65.2 us
    all_to_all x1, blocking collectives, per_device(): lax.all_to_all(mixed, 'head', split_axis=0, concat_axis=1, tiled=True)  28.8 us
    all_to_all x1, waiting for transfers between devices, per_device(): lax.all_to_all(value_tok, 'head', split_axis=1, concat_axis=0, tiled=True)  20.3 us
    sub x2, matrix products, block_step(): expo = jnp.where(valid, jnp.exp(window_scores - highest_score), 0.0)  16.7 us
    dot_general x2, matrix products, block_step(): jnp.einsum('hbc,chv->bhv', weights, value_window, preferred_element_type=...  13 us
    dot_general x2, matrix products, block_step(): jnp.einsum('hbc,chv->bhv', kernel, value_block, preferred_element_type=jn...  9.1 us
    ppermute x2, starting transfers between devices, shifted(): return lax.ppermute(shard, axis, pairs)  8.46 us
    dot_general x2, matrix products, block_step(): jnp.einsum('bhf,hfv->bhv', query_feat, state.astype(jnp.bfloat16), prefer...  7.45 us
  transfers between devices with their start and end apart: 6, of which 4 were waited for; matrix products, arithmetic and copies ran while one was open for 6% of the time, Pallas kernels for 0%

commit v1 on v0

v1 whole, which is shorter than its diff:
```python
import math

import jax
import jax.numpy as jnp
from jax import lax
from jax.sharding import PartitionSpec as P

HEADS = 32
KD = 16
VD = 128
WINDOW = 64


outer_scale = 1.0 / (4.0 * math.sqrt(2.0))
epsilon = 1e-06


def shifted(shard, axis, by):
    peers = lax.axis_size(axis)
    pairs = [(i, i + by) for i in range(peers) if 0 <= i + by < peers]
    return lax.ppermute(shard, axis, pairs)


def unique_features(vector, doubled):
    lead = vector.shape[:-1]
    pieces = [jnp.ones(lead + (1,), jnp.bfloat16), (vector * 0.5).astype(jnp.bfloat16)]
    for i in range(KD):
        prod = ((vector[..., i : i + 1] * vector[..., i:]) * outer_scale).astype(jnp.bfloat16)
        if doubled and i + 1 < KD:
            prod = jnp.concatenate([prod[..., :1], prod[..., 1:] * 2], axis=-1)
        pieces.append(prod)
    return jnp.concatenate(pieces, axis=-1)


def per_device(queries, keys, values, gain):
    local_tokens = queries.shape[0]
    query_tok = queries.reshape(local_tokens, HEADS, KD)
    key_tok = keys.reshape(local_tokens, HEADS, KD)
    value_tok = values.reshape(local_tokens, HEADS, VD)
    query_head, key_head, value_head = (
        lax.all_to_all(query_tok, "head", split_axis=1, concat_axis=0, tiled=True),
        lax.all_to_all(key_tok, "head", split_axis=1, concat_axis=0, tiled=True),
        lax.all_to_all(value_tok, "head", split_axis=1, concat_axis=0, tiled=True),
    )
    span_rows = query_head.shape[0]
    heads_here = query_head.shape[1]
    block_rows = min(512, span_rows)
    block_count = span_rows // block_rows
    first_span = lax.axis_index("ctx") == 0

    key_feat = unique_features(key_head.astype(jnp.float32), False)
    feat = key_feat.shape[-1]
    block_states = jnp.einsum(
        "nrhf,nrhv->nhfv",
        key_feat.reshape(block_count, block_rows, heads_here, feat),
        value_head.reshape(block_count, block_rows, heads_here, VD),
        preferred_element_type=jnp.float32,
    )
    span_state = jnp.sum(block_states, axis=0)
    everything = lax.all_gather(span_state, "ctx")
    peers = everything.shape[0]
    here = lax.axis_index("ctx")
    entering = jnp.sum(
        jnp.where(
            (jnp.arange(peers) < here)[:, None, None, None], everything, jnp.zeros_like(everything)
        ),
        axis=0,
    )
    before = jnp.concatenate(
        [jnp.zeros_like(block_states[:1]), jnp.cumsum(block_states[:-1], axis=0)], axis=0
    )
    states = (before + entering[None]).astype(jnp.bfloat16)

    query_blocks = query_head.reshape(block_count, block_rows, heads_here, KD)
    key_blocks = key_head.reshape(block_count, block_rows, heads_here, KD)
    value_blocks = value_head.reshape(block_count, block_rows, heads_here, VD)
    scores = (
        jnp.einsum("nrhd,nshd->nhrs", query_blocks, key_blocks, preferred_element_type=jnp.float32)
        * 0.25
    )
    row_pos = jnp.arange(block_rows)[:, None]
    col_pos = jnp.arange(block_rows)[None, :]
    kernel = jnp.where(col_pos <= row_pos, 1.0 + scores + 0.5 * scores * scores, 0.0).astype(
        jnp.bfloat16
    )
    intra = jnp.einsum("nhrs,nshv->nrhv", kernel, value_blocks, preferred_element_type=jnp.float32)
    query_feat = unique_features(query_blocks.astype(jnp.float32), True)
    inter = jnp.einsum("nrhf,nhfv->nrhv", query_feat, states, preferred_element_type=jnp.float32)
    linear = (intra + inter).reshape(span_rows, heads_here, VD)

    tail_keys, tail_values = shifted(
        (key_head[span_rows - WINDOW :], value_head[span_rows - WINDOW :]), "ctx", 1
    )
    chunks = span_rows // WINDOW
    key_prev = jnp.concatenate([tail_keys, key_head[: span_rows - WINDOW]], axis=0)
    value_prev = jnp.concatenate([tail_values, value_head[: span_rows - WINDOW]], axis=0)
    key_win = jnp.concatenate(
        [
            key_prev.reshape(chunks, WINDOW, heads_here, KD),
            key_head.reshape(chunks, WINDOW, heads_here, KD),
        ],
        axis=1,
    )
    value_win = jnp.concatenate(
        [
            value_prev.reshape(chunks, WINDOW, heads_here, VD),
            value_head.reshape(chunks, WINDOW, heads_here, VD),
        ],
        axis=1,
    )
    query_chunks = query_head.reshape(chunks, WINDOW, heads_here, KD)
    window_scores = (
        jnp.einsum("crhd,cphd->chrp", query_chunks, key_win, preferred_element_type=jnp.float32)
        * 0.25
    )
    r_pos = jnp.arange(WINDOW)[:, None]
    p_pos = jnp.arange(2 * WINDOW)[None, :]
    chunk_pos = jnp.arange(chunks)[:, None, None, None]
    valid = (p_pos > r_pos) & (p_pos <= r_pos + WINDOW)
    valid = valid[None, None] & ((chunk_pos > 0) | (p_pos >= WINDOW) | jnp.logical_not(first_span))
    masked = jnp.where(valid, window_scores, -jnp.inf)
    highest_score = jnp.max(masked, axis=3, keepdims=True)
    expo = jnp.where(valid, jnp.exp(window_scores - highest_score), 0.0)
    weights = (expo / jnp.sum(expo, axis=3, keepdims=True)).astype(jnp.bfloat16)
    window = jnp.einsum(
        "chrp,cphv->crhv", weights, value_win, preferred_element_type=jnp.float32
    ).reshape(span_rows, heads_here, VD)

    scale = lax.rsqrt(jnp.mean(linear * linear, axis=2, keepdims=True) + epsilon)
    gains = gain.reshape(heads_here, VD)
    mixed = (linear * scale * gains + window).astype(jnp.bfloat16)
    tokens_back = lax.all_to_all(mixed, "head", split_axis=0, concat_axis=1, tiled=True)
    return tokens_back.reshape(tokens_back.shape[0], HEADS * VD)


def solution(mesh):
    placed = (
        P(("groups", "ctx", "head"), None),
        P(("groups", "ctx", "head"), None),
        P(("groups", "ctx", "head"), None),
        P("head"),
    )
    return jax.shard_map(
        per_device,
        mesh=mesh,
        in_specs=placed,
        out_specs=P(("groups", "ctx", "head"), None),
        check_vma=False,
    )
```

time: 280 us -> 206 us (0.74)
  waiting for transfers between devices: 92.4 us -> 21.1 us
  matrix products: 55.3 us -> 27 us
  local copies, waits for them, and re-layouts: 39.3 us -> 58.9 us
  other arithmetic: 28.4 us -> 36.7 us
    all_gather x1, waiting for transfers between devices: 65.2 us -> 16 us  [per_device(): everything = lax.all_gather(span_state, 'ctx')]
    unnamed x1 -> x30, other arithmetic: 0.01 us -> 20.6 us
    all_to_all x1, waiting for transfers between devices: 20.3 us -> 0.01 us  [per_device(): lax.all_to_all(value_tok, 'head', split_axis=1, concat_axis=0, tiled=True)]
    dot_general x9 -> x4, matrix products: 38.5 us -> 19 us  [the longest x1 7.3 us: per_device(): jnp.einsum('nhrs,nshv->nrhv', kernel, value_blocks, preferred_element_typ...]
    unnamed x7 -> x44, local copies, waits for them, and re-layouts: 5.9 us -> 20.3 us
    reshape x0 -> x10, local copies, waits for them, and re-layouts: none -> 12 us  [the longest x1 7.01 us: per_device(): key_feat.reshape(block_count, block_rows, heads_here, feat)]
    sub x2 -> x1, matrix products: 16.7 us -> 8.02 us  [per_device(): expo = jnp.where(valid, jnp.exp(window_scores - highest_score), 0.0)]
    dynamic_update_slice x4 -> x0, local copies, waits for them, and re-layouts: 7.22 us -> none  [per_device(): lax.scan(block_step, prefix, jnp.arange(block_count))]
  transfers between devices with their start and end apart: 6 -> 6, of which waited for: 4 -> 2; matrix products, arithmetic and copies ran while one was open for 6% -> 46% of each run, Pallas kernels for 0% -> 0%
where the time goes in v1:
time: 206 us; the launch traced here: 205 us
  local copies, waits for them, and re-layouts  58.9 us (29%)
  other arithmetic  36.7 us (18%)
  blocking collectives  28.2 us (14%)
  matrix products  27 us (13%)
  waiting for transfers between devices  21.1 us (10%)
  starting transfers between devices  19 us (9%)
  between operations  13.8 us (7%)
    all_to_all x1, blocking collectives, per_device(): lax.all_to_all(mixed, 'head', split_axis=0, concat_axis=1, tiled=True)  28.2 us
    unnamed x30, other arithmetic  20.6 us
    unnamed x44, local copies, waits for them, and re-layouts  20.3 us
    all_gather x1, waiting for transfers between devices, per_device(): everything = lax.all_gather(span_state, 'ctx')  16 us
    sub x1, matrix products, per_device(): expo = jnp.where(valid, jnp.exp(window_scores - highest_score), 0.0)  8.02 us
    ppermute x2, starting transfers between devices, shifted(): return lax.ppermute(shard, axis, pairs)  7.77 us
    dot_general x1, matrix products, per_device(): jnp.einsum('nhrs,nshv->nrhv', kernel, value_blocks, preferred_element_typ...  7.3 us
    reshape x1, local copies, waits for them, and re-layouts, per_device(): key_feat.reshape(block_count, block_rows, heads_here, feat)  7.01 us
  transfers between devices with their start and end apart: 6, of which 2 were waited for; matrix products, arithmetic and copies ran while one was open for 46% of the time, Pallas kernels for 0%

profile of v1, /device:TPU:0, one launch (start us, length us, event | category | flops | bytes accessed | tf_op | source)
XLA Modules:
  0.0 204.7 jit_solution(14537195635476565313)
XLA Ops:
  6.5 1.8 copy.132
  8.3 4.2 %all-to-all-start = ((bf16[256,32,16]{0,2,1:T(8,128)(2,1)}), bf16[256,32,16]{0,2,1:T(8,128)(2,1)S(1)}, u32[]{:S(2)}, u32[]{:S(2)}) async-start(bf16[256,32,16]{0,2,1:T(8,128)(2,1)} %bitcast), calls=%async_computation | async-start | bytes 524288 | tf_op jit(solution)/shard_map/all_to_all | solution.py:41
  14.6 3.3 %copy.138 = bf16[256,4096]{0,1:T(8,128)(2,1)S(1)} copy(bf16[256,4096]{1,0:T(8,128)(2,1)} %param.6) | data formatting | bytes 4194304 | tf_op args[2]
  17.8 2.9 %copy.139 = bf16[256,32,128]{2,0,1:T(8,128)(2,1)} copy(bf16[256,32,128]{0,2,1:T(8,128)(2,1)S(1)} %bitcast.145) | data formatting | bytes 4194304 | tf_op jit(solution)/shard_map/reshape | solution.py:39
  22.3 3.4 %all-to-all-start.1 = ((bf16[256,32,16]{0,2,1:T(8,128)(2,1)}), bf16[256,32,16]{0,2,1:T(8,128)(2,1)S(1)}, u32[]{:S(2)}, u32[]{:S(2)}) async-start(bf16[256,32,16]{0,2,1:T(8,128)(2,1)} %bitcast.3), calls=%async_computation.1 | async-start | bytes 524288 | tf_op jit(solution)/shard_map/all_to_all | solution.py:42
  26.7 5.1 %all-to-all-done.1 = bf16[256,32,16]{0,2,1:T(8,128)(2,1)S(1)} async-done(((bf16[256,32,16]{0,2,1:T(8,128)(2,1)}), bf16[256,32,16]{0,2,1:T(8,128)(2,1)S(1)}, u32[]{:S(2)}, u32[]{:S(2)}) %all-to-all-start.1) | async-done | bytes 262176 | tf_op jit(solution)/shard_map/all_to_all | solution.py:42
  31.8 3.6 %all-to-all-start.2 = ((bf16[256,32,128]{2,0,1:T(8,128)(2,1)}), bf16[256,32,128]{2,0,1:T(8,128)(2,1)S(1)}, u32[]{:S(2)}, u32[]{:S(2)}) async-start(bf16[256,32,128]{2,0,1:T(8,128)(2,1)} %copy.139), calls=%async_computation.2 | async-start | bytes 4194304 | tf_op jit(solution)/shard_map/all_to_all | solution.py:43
  36.5 4.7 %collective-permute-start.1 = (bf16[64,8,16]{0,2,1:T(8,128)(2,1)}, bf16[64,8,16]{0,2,1:T(8,128)(2,1)}, u32[]{:S(2)}, u32[]{:S(2)}) collective-permute-start(bf16[64,8,16]{0,2,1:T(8,128)(2,1)} %slice.473), channel_id=1, source_target_pairs={{0,4},{4,8},{8,12},{1,5},{5,9},{9,13},{2,6},{6,10},{10,14},{3,7},{... | collective-permute-start | bytes 49160 | tf_op jit(solution)/shard_map/ppermute | solution.py:21
  42.1 1.8 copy_convert_fusion
  44.6 1.1 multiply_convert_fusion
  72.5 7.0 %reshape.170 = bf16[2,512,8,153]{1,0,2,3:T(2,128)(2,1)} reshape(bf16[1024,8,153]{0,1,2:T(8,128)(2,1)} %constant_dynamic-update-slice_fusion) | data formatting | bytes 5013504 | tf_op jit(solution)/shard_map/reshape | solution.py:55
  83.4 1.3 copy-done
  84.7 3.1 %copy.141 = bf16[4,256,8,128]{3,2,1,0:T(8,128)(2,1)S(1)} copy(bf16[4,256,8,128]{3,1,2,0:T(8,128)(2,1)} %bitcast.141) | data formatting | bytes 4194304 | tf_op jit(solution)/shard_map/all_to_all | solution.py:43
  87.8 4.2 %fusion.144 = (f32[8,153,128]{2,1,0:T(8,128)S(1)}, f32[2,8,153,128]{3,2,1,0:T(8,128)}) fusion(bf16[2,512,8,128]{3,2,1,0:T(8,128)(2,1)S(1)} %bitcast.136, bf16[2,512,8,153]{1,0,2,3:T(2,128)(2,1)S(1)} %copy-done.2), kind=kOutput, calls=%fused_computation.262 | convolution fusion | flops 321020928 | bytes 6483968 | tf_op jit(solution)/shard_map/nrhf,nrhv->nhfv/dot_general | solution.py:53
  92.0 1.2 copy.146
  95.7 1.1 reshape.176
  97.2 0.9 copy.158
  98.2 0.9 pad_maximum_fusion.2
  99.6 8.0 %fusion.139 = (f32[16,8,64]{2,1,0:T(8,128)}, f32[16,8,64,128]{3,2,1,0:T(8,128)}) fusion(pred[16,64,128]{2,1,0:T(8,128)(4,1)S(1)} %copy-done.7, bf16[16,64,8,16]{1,0,3,2:T(8,128)(2,1)} %reshape.176, bf16[16,64,8,16]{1,3,2,0:T(8,128)(2,1)} %copy.158, bf16[16,64,8,16]{1,3,2,0:T(8,128)(2,1)S(1)} %copy.157), kind=kOutput, calls=%fused_computation.261 | convolution fusion | flops 75497600 | bytes 5144576 | tf_op jit(solution)/shard_map/sub | solution.py:123
  108.3 3.1 %collective-permute-start = (bf16[64,8,128]{2,1,0:T(8,128)(2,1)}, bf16[64,8,128]{2,1,0:T(8,128)(2,1)S(1)}, u32[]{:S(2)}, u32[]{:S(2)}) collective-permute-start(bf16[64,8,128]{2,1,0:T(8,128)(2,1)} %slice.475), channel_id=1, source_target_pairs={{0,4},{4,8},{8,12},{1,5},{5,9},{9,13},{2,6},{6,10},{10,14},{3,7},{... | collective-permute-start | bytes 393224 | tf_op jit(solution)/shard_map/ppermute | solution.py:21
  111.4 7.3 %fusion.1 = f32[2,8,512,128]{3,2,1,0:T(8,128)} fusion(pred[512,512]{1,0:T(8,128)(4,1)S(1)} %copy-done.6, bf16[2,512,8,128]{3,2,1,0:T(8,128)(2,1)S(1)} %bitcast.138, bf16[2,512,8,16]{1,0,3,2:T(2,128)(2,1)S(1)} %reshape.167, bf16[2,512,8,16]{1,0,3,2:T(2,128)(2,1)S(1)} %copy-done.3), kind=kOutput, calls=%fused_computation.2 | convolution fusion | flops 1237319680 | bytes 7077888 | tf_op jit(solution)/shard_map/nhrs,nshv->nrhv/dot_general | solution.py:86
  121.0 1.6 copy-done.10
  122.6 2.7 %fusion.22 = f32[16,64,8,128]{3,1,2,0:T(8,128)S(1)} fusion(bf16[16,64,8,128]{3,1,2,0:T(8,128)(2,1)S(1)} %copy.156, bf16[16,64,8,128]{3,1,2,0:T(8,128)(2,1)S(1)} %copy.155, f32[16,8,64,128]{3,2,1,0:T(8,128)S(1)} %copy-done.10, f32[16,8,64]{2,1,0:T(8,128)S(1)} %copy-done.11), kind=kOutput, calls=%fused_computation.28 | convolution fusion | flops 278921216 | bytes 12615680 | tf_op jit(solution)/shard_map/chrp,cphv->crhv/dot_general | solution.py:125
  125.3 5.2 %copy.160 = f32[16,64,8,128]{3,2,1,0:T(8,128)} copy(f32[16,64,8,128]{3,1,2,0:T(8,128)S(1)} %fusion.22) | data formatting | bytes 8388608 | tf_op jit(solution)/shard_map/chrp,cphv->crhv/transpose | solution.py:125
  130.5 16.0 %all-gather.3.cloned.1.call-done = f32[32,153,128]{2,0,1:T(8,128)} async-done(((f32[8,153,128]{2,0,1:T(8,128)}), f32[32,153,128]{2,0,1:T(8,128)}) %all-gather.3.cloned.1.call-update) | async-done | bytes 2506768 | tf_op jit(solution)/shard_map/all_gather | solution.py:60
  146.5 2.4 %fusion.19 = f32[8,153,128]{2,0,1:T(8,128)S(1)} fusion(f32[32,153,128]{2,0,1:T(8,128)} %all-gather.3.cloned.1.call-done, pred[4]{0:T(512)(128)(4,1)S(1)} %copy-done.9), kind=kLoop, calls=%fused_computation.27 | loop fusion | flops 1096704 | bytes 3133444 | tf_op jit(solution)/shard_map/reduce_sum | solution.py:63
  149.4 4.8 %multiply_reduce_fusion = (f32[2,512,8]{1,2,0:T(8,128)S(1)}, f32[2,512,8,128]{3,1,2,0:T(8,128)S(1)}) fusion(bf16[2,512,8,153]{1,2,3,0:T(8,128)(2,1)} %constant_dynamic-update-slice_fusion.7, f32[1,8,153,128]{3,2,1,0:T(8,128)S(1)} %slice.412, f32[8,153,128]{2,1,0:T(8,128)S(1)} %copy.147, f32[2,8,512,128]{3,2,1,0:T(8,128)S(1)} %copy-done.1), kind=kOutput, calls=%fused_computation.19 | convolution fusion | flops 324628480 | bytes 12181504 | tf_op jit(solution)/shard_map/nrhf,nhfv->nrhv/dot_general | solution.py:88
  154.3 4.4 %copy.151 = f32[2,512,8,128]{3,2,1,0:T(8,128)} copy(f32[2,512,8,128]{3,1,2,0:T(8,128)S(1)} %get-tuple-element.44) | data formatting | bytes 8388608 | tf_op jit(solution)/shard_map/add | solution.py:89
  158.9 4.1 %fusion.9 = bf16[1024,8,128]{2,1,0:T(8,128)(2,1)S(1)} fusion(f32[16,64,8,128]{3,2,1,0:T(8,128)} %copy.160, f32[2,512,8,128]{3,2,1,0:T(8,128)} %copy.151, f32[8,128]{1,0:T(8,128)S(1)} %bitcast.155, f32[1024,8]{1,0:T(8,128)S(1)} %copy.152), kind=kLoop, calls=%fused_computation.10 | loop fusion | flops 4194304 | bytes 10522624 | tf_op jit(solution)/shard_map/convert_element_type | solution.py:131
  163.0 28.2 %all_to_all.66 = bf16[1024,8,128]{2,1,0:T(8,128)(2,1)S(1)} all-to-all(bf16[1024,8,128]{2,1,0:T(8,128)(2,1)S(1)} %fusion.9), channel_id=1, replica_groups=mesh['groups'=2,'ctx'=4,'head'=4] {'head'}, dimensions={0} | all-to-all | bytes 4194304 | tf_op jit(solution)/shard_map/all_to_all | solution.py:132
  191.2 2.6 %copy.161 = bf16[256,4,8,128]{0,3,2,1:T(8,128)(2,1)} copy(bf16[256,4,8,128]{3,2,0,1:T(8,128)(2,1)S(1)} %bitcast.143) | data formatting | bytes 4194304 | tf_op jit(solution)/shard_map/all_to_all | solution.py:132
  193.8 4.1 %copy.162 = bf16[256,4096]{1,0:T(8,128)(2,1)} copy(bf16[256,4096]{0,1:T(8,128)(2,1)} %bitcast.144) | data formatting | bytes 4194304 | tf_op jit(solution)/shard_map/reshape | solution.py:133
  (121 shorter events, 44.9 us)
Async XLA Ops:
  8.3 14.0 %all-to-all-start = ((bf16[256,32,16]{0,2,1:T(8,128)(2,1)}), bf16[256,32,16]{0,2,1:T(8,128)(2,1)S(1)}, u32[]{:S(2)}, u32[]{:S(2)}) async-start(bf16[256,32,16]{0,2,1:T(8,128)(2,1)} %bitcast), calls=%async_computation | async-start | bytes 524288 | tf_op jit(solution)/shard_map/all_to_all | solution.py:41
  17.8 3.6 %copy-start.5 = (bf16[256,512]{1,0:T(8,128)(2,1)S(1)}, bf16[256,512]{1,0:T(8,128)(2,1)}, u32[]{:S(2)}) copy-start(bf16[256,512]{1,0:T(8,128)(2,1)} %param.5) | copy-start | bytes 786436
  22.3 9.5 %all-to-all-start.1 = ((bf16[256,32,16]{0,2,1:T(8,128)(2,1)}), bf16[256,32,16]{0,2,1:T(8,128)(2,1)S(1)}, u32[]{:S(2)}, u32[]{:S(2)}) async-start(bf16[256,32,16]{0,2,1:T(8,128)(2,1)} %bitcast.3), calls=%async_computation.1 | async-start | bytes 524288 | tf_op jit(solution)/shard_map/all_to_all | solution.py:42
  31.8 51.6 %all-to-all-start.2 = ((bf16[256,32,128]{2,0,1:T(8,128)(2,1)}), bf16[256,32,128]{2,0,1:T(8,128)(2,1)S(1)}, u32[]{:S(2)}, u32[]{:S(2)}) async-start(bf16[256,32,128]{2,0,1:T(8,128)(2,1)} %copy.139), calls=%async_computation.2 | async-start | bytes 4194304 | tf_op jit(solution)/shard_map/all_to_all | solution.py:43
  35.4 111.1 %all-gather.3.cloned.1.call-start = ((), (), s32[]{:S(2)}) async-start(), calls=%async_computation.4 | async-start | bytes 3133440 | tf_op jit(solution)/shard_map/all_gather | solution.py:60
  36.5 61.6 %collective-permute-start.1 = (bf16[64,8,16]{0,2,1:T(8,128)(2,1)}, bf16[64,8,16]{0,2,1:T(8,128)(2,1)}, u32[]{:S(2)}, u32[]{:S(2)}) collective-permute-start(bf16[64,8,16]{0,2,1:T(8,128)(2,1)} %slice.473), channel_id=1, source_target_pairs={{0,4},{4,8},{8,12},{1,5},{5,9},{9,13},{2,6},{6,10},{10,14},{3,7},{... | collective-permute-start | bytes 49160 | tf_op jit(solution)/shard_map/ppermute | solution.py:21
  83.4 1.3 copy-start
  84.7 3.1 %copy-start.2 = (bf16[2,512,8,153]{1,0,2,3:T(2,128)(2,1)S(1)}, bf16[2,512,8,153]{1,0,2,3:T(2,128)(2,1)}, u32[]{:S(2)}) copy-start(bf16[2,512,8,153]{1,0,2,3:T(2,128)(2,1)} %reshape.170) | copy-start | bytes 7520260
  96.7 2.8 %copy-start.7 = (pred[16,64,128]{2,1,0:T(8,128)(4,1)S(1)}, pred[16,64,128]{2,1,0:T(8,128)(4,1)}, u32[]{:S(2)}) copy-start(pred[16,64,128]{2,1,0:T(8,128)(4,1)} %broadcast_and_fusion) | copy-start | bytes 393220
  99.6 11.8 %copy-start.3 = (bf16[2,512,8,16]{1,0,3,2:T(2,128)(2,1)S(1)}, bf16[2,512,8,16]{1,0,3,2:T(2,128)(2,1)}, u32[]{:S(2)}) copy-start(bf16[2,512,8,16]{1,0,3,2:T(2,128)(2,1)} %reshape.165) | copy-start | bytes 786436
  99.6 11.8 %copy-start.6 = (pred[512,512]{1,0:T(8,128)(4,1)S(1)}, pred[512,512]{1,0:T(8,128)(4,1)}, u32[]{:S(2)}) copy-start(pred[512,512]{1,0:T(8,128)(4,1)} %iota_compare_fusion) | copy-start | bytes 786436
  108.3 11.9 %collective-permute-start = (bf16[64,8,128]{2,1,0:T(8,128)(2,1)}, bf16[64,8,128]{2,1,0:T(8,128)(2,1)S(1)}, u32[]{:S(2)}, u32[]{:S(2)}) collective-permute-start(bf16[64,8,128]{2,1,0:T(8,128)(2,1)} %slice.475), channel_id=1, source_target_pairs={{0,4},{4,8},{8,12},{1,5},{5,9},{9,13},{2,6},{6,10},{10,14},{3,7},{... | collective-permute-start | bytes 393224 | tf_op jit(solution)/shard_map/ppermute | solution.py:21
  118.8 1.3 copy-start.4
  120.2 0.8 copy-start.11
  120.4 2.2 %copy-start.10 = (f32[16,8,64,128]{3,2,1,0:T(8,128)S(1)}, f32[16,8,64,128]{3,2,1,0:T(8,128)}, u32[]{:S(2)}) copy-start(f32[16,8,64,128]{3,2,1,0:T(8,128)} %get-tuple-element.40) | copy-start | bytes 12582916
  125.3 21.2 %copy-start.9 = (pred[4]{0:T(512)(128)(4,1)S(1)}, pred[4]{0:T(512)(128)(4,1)}, u32[]{:S(2)}) copy-start(pred[4]{0:T(512)(128)(4,1)} %iota_compare_fusion.5) | copy-start | bytes 16
  146.5 2.9 %copy-start.1 = (f32[2,8,512,128]{3,2,1,0:T(8,128)S(1)}, f32[2,8,512,128]{3,2,1,0:T(8,128)}, u32[]{:S(2)}) copy-start(f32[2,8,512,128]{3,2,1,0:T(8,128)} %fusion.1) | copy-start | bytes 12582916
  154.3 4.6 %copy-start.8 = (f32[1024]{0:T(1024)S(1)}, f32[1024]{0:T(1024)}, u32[]{:S(2)}) copy-start(f32[1024]{0:T(1024)} %param.7) | copy-start | bytes 12292
Sparse Core Ops, SparseCore 0:
  93.3 53.0 all-gather.2

commit v2 on v1

--- a/solution.py
+++ b/solution.py
@@ -1,6 +1,7 @@
 import math
 
 import jax
+import numpy as np
 import jax.numpy as jnp
 from jax import lax
 from jax.sharding import PartitionSpec as P
@@ -22,14 +23,18 @@
 
 
 def unique_features(vector, doubled):
+    rows, cols = np.triu_indices(KD)
+    pick_rows = jnp.asarray(np.eye(KD)[:, rows], jnp.bfloat16)
+    pick_cols = jnp.asarray(np.eye(KD)[:, cols], jnp.bfloat16)
+    first = jnp.einsum("...d,df->...f", vector, pick_rows, preferred_element_type=jnp.float32)
+    second = jnp.einsum("...d,df->...f", vector, pick_cols, preferred_element_type=jnp.float32)
+    prod = ((first * second) * outer_scale).astype(jnp.bfloat16)
+    if doubled:
+        prod = prod * jnp.asarray(np.where(rows == cols, 1.0, 2.0), jnp.bfloat16)
     lead = vector.shape[:-1]
-    pieces = [jnp.ones(lead + (1,), jnp.bfloat16), (vector * 0.5).astype(jnp.bfloat16)]
-    for i in range(KD):
-        prod = ((vector[..., i : i + 1] * vector[..., i:]) * outer_scale).astype(jnp.bfloat16)
-        if doubled and i + 1 < KD:
-            prod = jnp.concatenate([prod[..., :1], prod[..., 1:] * 2], axis=-1)
-        pieces.append(prod)
-    return jnp.concatenate(pieces, axis=-1)
+    unit = jnp.ones(lead + (1,), jnp.bfloat16)
+    half = (vector.astype(jnp.float32) * 0.5).astype(jnp.bfloat16)
+    return jnp.concatenate([unit, half, prod], axis=-1)
 
 
 def per_device(queries, keys, values, gain):
@@ -48,7 +53,7 @@
     block_count = span_rows // block_rows
     first_span = lax.axis_index("ctx") == 0
 
-    key_feat = unique_features(key_head.astype(jnp.float32), False)
+    key_feat = unique_features(key_head, False)
     feat = key_feat.shape[-1]
     block_states = jnp.einsum(
         "nrhf,nrhv->nhfv",
@@ -84,7 +89,7 @@
         jnp.bfloat16
     )
     intra = jnp.einsum("nhrs,nshv->nrhv", kernel, value_blocks, preferred_element_type=jnp.float32)
-    query_feat = unique_features(query_blocks.astype(jnp.float32), True)
+    query_feat = unique_features(query_blocks, True)
     inter = jnp.einsum("nrhf,nhfv->nrhv", query_feat, states, preferred_element_type=jnp.float32)
     linear = (intra + inter).reshape(span_rows, heads_here, VD)
 

time: 206 us -> 174 us (0.84)
  other arithmetic: 36.7 us -> 10.3 us
  local copies, waits for them, and re-layouts: 58.9 us -> 41.7 us
  waiting for transfers between devices: 21.1 us -> 30.2 us
    unnamed x30 -> x0, other arithmetic: 20.6 us -> none
    all_to_all x1, waiting for transfers between devices: 0.01 us -> 19.5 us  [per_device(): lax.all_to_all(value_tok, 'head', split_axis=1, concat_axis=0, tiled=True)]
    unnamed x44 -> x31, local copies, waits for them, and re-layouts: 20.3 us -> 7.96 us
    all_gather x1, waiting for transfers between devices: 16 us -> 10.7 us  [per_device(): everything = lax.all_gather(span_state, 'ctx')]
    all_to_all x1, waiting for transfers between devices: 5.11 us -> 0.01 us  [per_device(): lax.all_to_all(key_tok, 'head', split_axis=1, concat_axis=0, tiled=True)]
    dot_general x0 -> x4, matrix products: none -> 4.49 us  [the longest x2 2.98 us: unique_features(): jnp.einsum('...d,df->...f', vector, pick_cols, preferred_element_type=jnp...]
    reshape x1, local copies, waits for them, and re-layouts: 7.01 us -> 2.77 us  [per_device(): key_feat.reshape(block_count, block_rows, heads_here, feat)]
    convert_element_type x17 -> x2, other arithmetic: 5.01 us -> 0.79 us  [unique_features(): half = (vector.astype(jnp.float32) * 0.5).astype(jnp.bfloat16)]
  transfers between devices with their start and end apart: 6 -> 6, of which waited for: 2 -> 2; matrix products, arithmetic and copies ran while one was open for 46% -> 31% of each run, Pallas kernels for 0% -> 0%
where the time goes in v2:
time: 174 us; the launch traced here: 173 us
  local copies, waits for them, and re-layouts  41.7 us (24%)
  waiting for transfers between devices  30.2 us (17%)
  blocking collectives  28.8 us (17%)
  matrix products  28.6 us (16%)
  starting transfers between devices  20.2 us (12%)
  between operations  13.8 us (8%)
  other arithmetic  10.3 us (6%)
    all_to_all x1, blocking collectives, per_device(): lax.all_to_all(mixed, 'head', split_axis=0, concat_axis=1, tiled=True)  28.8 us
    all_to_all x1, waiting for transfers between devices, per_device(): lax.all_to_all(value_tok, 'head', split_axis=1, concat_axis=0, tiled=True)  19.5 us
    all_gather x1, waiting for transfers between devices, per_device(): everything = lax.all_gather(span_state, 'ctx')  10.7 us
    ppermute x2, starting transfers between devices, shifted(): return lax.ppermute(shard, axis, pairs)  8.05 us
    unnamed x31, local copies, waits for them, and re-layouts  7.96 us
    sub x1, matrix products, per_device(): expo = jnp.where(valid, jnp.exp(window_scores - highest_score), 0.0)  7.55 us
    dot_general x1, matrix products, per_device(): jnp.einsum('nhrs,nshv->nrhv', kernel, value_blocks, preferred_element_typ...  7.31 us
    transpose x1, local copies, waits for them, and re-layouts, per_device(): jnp.einsum('chrp,cphv->crhv', weights, value_win, preferred_element_type=...  5.23 us
  transfers between devices with their start and end apart: 6, of which 2 were waited for; matrix products, arithmetic and copies ran while one was open for 31% of the time, Pallas kernels for 0%

profile of v2, /device:TPU:0, one launch (start us, length us, event | category | flops | bytes accessed | tf_op | source)
XLA Modules:
  0.0 173.4 jit_solution(13907406029088128837)
XLA Ops:
  6.5 1.8 %copy.125 = bf16[256,512]{0,1:T(8,128)(2,1)} copy(bf16[256,512]{1,0:T(8,128)(2,1)} %param.10) | data formatting | bytes 524288 | tf_op args[1]
  8.3 4.2 %all-to-all-start.1 = ((bf16[256,32,16]{0,2,1:T(8,128)(2,1)}), bf16[256,32,16]{0,2,1:T(8,128)(2,1)S(1)}, u32[]{:S(2)}, u32[]{:S(2)}) async-start(bf16[256,32,16]{0,2,1:T(8,128)(2,1)} %bitcast.3), calls=%async_computation.1 | async-start | bytes 524288 | tf_op jit(solution)/shard_map/all_to_all | solution.py:47
  12.6 3.3 %copy.129 = bf16[256,4096]{0,1:T(8,128)(2,1)S(1)} copy(bf16[256,4096]{1,0:T(8,128)(2,1)} %param.11) | data formatting | bytes 4194304 | tf_op args[2]
  15.9 2.9 %copy.130 = bf16[256,32,128]{2,0,1:T(8,128)(2,1)} copy(bf16[256,32,128]{0,2,1:T(8,128)(2,1)S(1)} %bitcast.103) | data formatting | bytes 4194304 | tf_op jit(solution)/shard_map/reshape | solution.py:44
  19.8 4.5 %all-to-all-start.2 = ((bf16[256,32,128]{2,0,1:T(8,128)(2,1)}), bf16[256,32,128]{2,0,1:T(8,128)(2,1)}, u32[]{:S(2)}, u32[]{:S(2)}) async-start(bf16[256,32,128]{2,0,1:T(8,128)(2,1)} %copy.130), calls=%async_computation.2 | async-start | bytes 4194304 | tf_op jit(solution)/shard_map/all_to_all | solution.py:48
  26.8 1.0 pad_maximum_fusion
  27.8 2.8 %reshape.185 = bf16[2,512,8,153]{1,0,3,2:T(2,128)(2,1)} reshape(bf16[1024,8,153]{0,2,1:T(8,128)(2,1)S(1)} %pad_maximum_fusion) | data formatting | bytes 5013504 | tf_op jit(solution)/shard_map/reshape | solution.py:60
  30.6 19.5 %all-to-all-done.2 = bf16[256,32,128]{2,0,1:T(8,128)(2,1)} async-done(((bf16[256,32,128]{2,0,1:T(8,128)(2,1)}), bf16[256,32,128]{2,0,1:T(8,128)(2,1)}, u32[]{:S(2)}, u32[]{:S(2)}) %all-to-all-start.2) | async-done | bytes 2097184 | tf_op jit(solution)/shard_map/all_to_all | solution.py:48
  50.0 3.4 %all-to-all-start = ((bf16[256,32,16]{0,2,1:T(8,128)(2,1)}), bf16[256,32,16]{0,2,1:T(8,128)(2,1)S(1)}, u32[]{:S(2)}, u32[]{:S(2)}) async-start(bf16[256,32,16]{0,2,1:T(8,128)(2,1)} %bitcast), calls=%async_computation | async-start | bytes 524288 | tf_op jit(solution)/shard_map/all_to_all | solution.py:46
  53.5 3.1 %copy.132 = bf16[4,256,8,128]{3,2,1,0:T(8,128)(2,1)S(1)} copy(bf16[4,256,8,128]{3,1,2,0:T(8,128)(2,1)} %bitcast.9) | data formatting | bytes 4194304 | tf_op jit(solution)/shard_map/all_to_all | solution.py:48
  56.6 2.1 %fusion.74 = (f32[8,153,128]{2,1,0:T(8,128)S(1)}, f32[2,8,153,128]{3,2,1,0:T(8,128)}) fusion(bf16[2,512,8,128]{3,2,1,0:T(8,128)(2,1)S(1)} %bitcast.95, bf16[2,512,8,153]{1,0,3,2:T(2,128)(2,1)S(1)} %copy-done.1), kind=kOutput, calls=%fused_computation.85 | convolution fusion | flops 321020928 | bytes 6483968 | tf_op jit(solution)/shard_map/nrhf,nrhv->nhfv/dot_general | solution.py:58
  58.7 1.2 copy.138
  60.9 4.7 %collective-permute-start.1 = (bf16[64,8,16]{0,2,1:T(8,128)(2,1)}, bf16[64,8,16]{0,2,1:T(8,128)(2,1)}, u32[]{:S(2)}, u32[]{:S(2)}) collective-permute-start(bf16[64,8,16]{0,2,1:T(8,128)(2,1)} %slice.21), channel_id=1, source_target_pairs={{0,4},{4,8},{8,12},{1,5},{5,9},{9,13},{2,6},{6,10},{10,14},{3,7},{... | collective-permute-start | bytes 49160 | tf_op jit(solution)/shard_map/ppermute | solution.py:22
  66.6 2.2 %fusion.25 = bf16[2,512,8,136]{1,3,2,0:T(8,128)(2,1)} fusion(f32[136,2,512,8]{2,0,3,1:T(8,128)S(1)} %fusion.51, bf16[16,136,1,1]{1,0,3,2:T(8,128)(2,1)S(1)} %copy-done.7, bf16[136]{0:T(256)(128)(2,1)S(1)} %copy-done.12, bf16[2,512,8,16]{1,0,3,2:T(2,128)(2,1)S(1)} %reshape.166), kind=kOutput, calls=%fused_computation.36 | convolution fusion | flops 40108032 | bytes 6951440 | tf_op jit(solution)/shard_map/...d,df->...f/dot_general | solution.py:30
  69.5 1.1 reshape.177
  72.0 0.9 copy.152
  72.9 0.9 pad_maximum_fusion.3
  74.2 1.0 copy.151
  75.2 7.6 %fusion.69 = (f32[16,8,64]{2,1,0:T(8,128)S(1)}, f32[16,8,64,128]{3,2,1,0:T(8,128)}) fusion(pred[16,64,128]{2,1,0:T(8,128)(4,1)S(1)} %broadcast_and_fusion, bf16[16,64,8,16]{1,0,3,2:T(8,128)(2,1)} %reshape.177, bf16[16,64,8,16]{1,3,2,0:T(8,128)(2,1)} %copy.152, bf16[16,64,8,16]{1,3,2,0:T(8,128)(2,1)} %copy.151), kind=kOutput, calls=%fused_computation.84 | convolution fusion | flops 75497600 | bytes 5144576 | tf_op jit(solution)/shard_map/sub | solution.py:128
  82.7 3.3 %collective-permute-start = (bf16[64,8,128]{2,1,0:T(8,128)(2,1)S(1)}, bf16[64,8,128]{2,1,0:T(8,128)(2,1)S(1)}, u32[]{:S(2)}, u32[]{:S(2)}) collective-permute-start(bf16[64,8,128]{2,1,0:T(8,128)(2,1)S(1)} %slice.23), channel_id=1, source_target_pairs={{0,4},{4,8},{8,12},{1,5},{5,9},{9,13},{2,6},{6,10},{10,14},{3,7},{... | collective-permute-start | bytes 393224 | tf_op jit(solution)/shard_map/ppermute | solution.py:22
  86.1 7.3 %fusion.1 = f32[2,8,512,128]{3,2,1,0:T(8,128)} fusion(pred[512,512]{1,0:T(8,128)(4,1)S(1)} %copy-done.5, bf16[2,512,8,128]{3,2,1,0:T(8,128)(2,1)S(1)} %bitcast.97, bf16[2,512,8,16]{1,0,3,2:T(2,128)(2,1)S(1)} %copy-done.6, bf16[2,512,8,16]{1,0,3,2:T(2,128)(2,1)S(1)} %reshape.166), kind=kOutput, calls=%fused_computation.2 | convolution fusion | flops 1237319680 | bytes 7077888 | tf_op jit(solution)/shard_map/nhrs,nshv->nrhv/dot_general | solution.py:91
  95.6 1.4 copy-done.13
  96.9 2.7 %fusion.28 = f32[16,64,8,128]{3,1,2,0:T(8,128)S(1)} fusion(bf16[16,64,8,128]{3,1,2,0:T(8,128)(2,1)S(1)} %copy.149, bf16[16,64,8,128]{3,1,2,0:T(8,128)(2,1)S(1)} %copy.148, f32[16,8,64,128]{3,2,1,0:T(8,128)S(1)} %copy-done.13, f32[16,8,64]{2,1,0:T(8,128)S(1)} %get-tuple-element.5), kind=kOutput, calls=%fused_computation.37 | convolution fusion | flops 278921216 | bytes 12615680 | tf_op jit(solution)/shard_map/chrp,cphv->crhv/dot_general | solution.py:130
  99.6 5.2 %copy.154 = f32[16,64,8,128]{3,2,1,0:T(8,128)} copy(f32[16,64,8,128]{3,1,2,0:T(8,128)S(1)} %fusion.28) | data formatting | bytes 8388608 | tf_op jit(solution)/shard_map/chrp,cphv->crhv/transpose | solution.py:130
  104.8 10.7 %all-gather.3.cloned.1.call-done = f32[32,153,128]{2,0,1:T(8,128)} async-done(((f32[8,153,128]{2,0,1:T(8,128)}), f32[32,153,128]{2,0,1:T(8,128)}) %all-gather.3.cloned.1.call-update) | async-done | bytes 2506768 | tf_op jit(solution)/shard_map/all_gather | solution.py:65
  115.5 2.2 %fusion.22 = f32[8,153,128]{2,0,1:T(8,128)S(1)} fusion(f32[32,153,128]{2,0,1:T(8,128)} %all-gather.3.cloned.1.call-done, pred[4]{0:T(512)(128)(4,1)S(1)} %iota_compare_fusion.5), kind=kLoop, calls=%fused_computation.33 | loop fusion | flops 1096704 | bytes 3133444 | tf_op jit(solution)/shard_map/reduce_sum | solution.py:68
  117.9 4.5 %multiply_reduce_fusion = (f32[2,512,8]{1,2,0:T(8,128)S(1)}, f32[2,512,8,128]{3,1,2,0:T(8,128)S(1)}) fusion(bf16[2,512,8,136]{1,3,2,0:T(8,128)(2,1)S(1)} %copy-done, bf16[2,512,8,16]{1,3,2,0:T(8,128)(2,1)S(1)} %copy-done.2, bf16[153]{0:T(256)(128)(2,1)S(1)} %pad.12.clone, f32[1,8,153,128]{3,2,1,0:T(8,128)S(1)} %slice.20, f32[8,153,128]{2,1,0:T(8,128)S(1)} %copy.139, ...), kind=kOutput, calls=%fused_computation.21 | convolution fusion | flops 332148736 | bytes 12165426 | tf_op jit(solution)/shard_map/nrhf,nhfv->nrhv/dot_general | solution.py:93
  122.4 4.4 %copy.144 = f32[2,512,8,128]{3,2,1,0:T(8,128)} copy(f32[2,512,8,128]{3,1,2,0:T(8,128)S(1)} %get-tuple-element.10) | data formatting | bytes 8388608 | tf_op jit(solution)/shard_map/add | solution.py:94
  127.0 4.1 %fusion.9 = bf16[1024,8,128]{2,1,0:T(8,128)(2,1)S(1)} fusion(f32[16,64,8,128]{3,2,1,0:T(8,128)} %copy.154, f32[2,512,8,128]{3,2,1,0:T(8,128)} %copy.144, f32[8,128]{1,0:T(8,128)S(1)} %bitcast.115, f32[1024,8]{1,0:T(8,128)S(1)} %copy.145), kind=kLoop, calls=%fused_computation.12 | loop fusion | flops 4194304 | bytes 10522624 | tf_op jit(solution)/shard_map/convert_element_type | solution.py:136
  131.1 28.8 %all_to_all.66 = bf16[1024,8,128]{2,1,0:T(8,128)(2,1)S(1)} all-to-all(bf16[1024,8,128]{2,1,0:T(8,128)(2,1)S(1)} %fusion.9), channel_id=1, replica_groups=mesh['groups'=2,'ctx'=4,'head'=4] {'head'}, dimensions={0} | all-to-all | bytes 4194304 | tf_op jit(solution)/shard_map/all_to_all | solution.py:137
  159.9 2.6 %copy.155 = bf16[256,4,8,128]{0,3,2,1:T(8,128)(2,1)} copy(bf16[256,4,8,128]{3,2,0,1:T(8,128)(2,1)S(1)} %bitcast.101) | data formatting | bytes 4194304 | tf_op jit(solution)/shard_map/all_to_all | solution.py:137
  162.5 4.1 %copy.156 = bf16[256,4096]{1,0:T(8,128)(2,1)} copy(bf16[256,4096]{0,1:T(8,128)(2,1)} %bitcast.102) | data formatting | bytes 4194304 | tf_op jit(solution)/shard_map/reshape | solution.py:138
  (65 shorter events, 10.4 us)
Async XLA Ops:
  8.3 11.5 %all-to-all-start.1 = ((bf16[256,32,16]{0,2,1:T(8,128)(2,1)}), bf16[256,32,16]{0,2,1:T(8,128)(2,1)S(1)}, u32[]{:S(2)}, u32[]{:S(2)}) async-start(bf16[256,32,16]{0,2,1:T(8,128)(2,1)} %bitcast.3), calls=%async_computation.1 | async-start | bytes 524288 | tf_op jit(solution)/shard_map/all_to_all | solution.py:47
  12.5 6.3 %copy-start.4 = (bf16[256,512]{1,0:T(8,128)(2,1)S(1)}, bf16[256,512]{1,0:T(8,128)(2,1)}, u32[]{:S(2)}) copy-start(bf16[256,512]{1,0:T(8,128)(2,1)} %param.9) | copy-start | bytes 786436
  15.9 9.4 %copy-start.10 = (bf16[16,136,1]{1,0,2:T(8,128)(2,1)S(1)}, bf16[16,136,1]{1,0,2:T(8,128)(2,1)}, u32[]{:S(2)}) copy-start(bf16[16,136,1]{1,0,2:T(8,128)(2,1)} %constant.53) | copy-start | bytes 13060
  19.8 6.2 %copy-start.9 = (bf16[16,136,1]{1,0,2:T(8,128)(2,1)S(1)}, bf16[16,136,1]{1,0,2:T(8,128)(2,1)}, u32[]{:S(2)}) copy-start(bf16[16,136,1]{1,0,2:T(8,128)(2,1)} %constant.54) | copy-start | bytes 13060
  19.8 30.2 %all-to-all-start.2 = ((bf16[256,32,128]{2,0,1:T(8,128)(2,1)}), bf16[256,32,128]{2,0,1:T(8,128)(2,1)}, u32[]{:S(2)}, u32[]{:S(2)}) async-start(bf16[256,32,128]{2,0,1:T(8,128)(2,1)} %copy.130), calls=%async_computation.2 | async-start | bytes 4194304 | tf_op jit(solution)/shard_map/all_to_all | solution.py:48
  50.0 10.6 %all-to-all-start = ((bf16[256,32,16]{0,2,1:T(8,128)(2,1)}), bf16[256,32,16]{0,2,1:T(8,128)(2,1)S(1)}, u32[]{:S(2)}, u32[]{:S(2)}) async-start(bf16[256,32,16]{0,2,1:T(8,128)(2,1)} %bitcast), calls=%async_computation | async-start | bytes 524288 | tf_op jit(solution)/shard_map/all_to_all | solution.py:46
  53.5 62.0 %all-gather.3.cloned.1.call-start = ((), (), s32[]{:S(2)}) async-start(), calls=%async_computation.4 | async-start | bytes 3133440 | tf_op jit(solution)/shard_map/all_gather | solution.py:65
  53.5 3.1 %copy-start.1 = (bf16[2,512,8,153]{1,0,3,2:T(2,128)(2,1)S(1)}, bf16[2,512,8,153]{1,0,3,2:T(2,128)(2,1)}, u32[]{:S(2)}) copy-start(bf16[2,512,8,153]{1,0,3,2:T(2,128)(2,1)} %reshape.185) | copy-start | bytes 7520260
  56.6 9.2 %copy-start.8 = (bf16[16,136,1,1]{1,0,3,2:T(8,128)(2,1)S(1)}, bf16[16,136,1,1]{1,0,3,2:T(8,128)(2,1)}, u32[]{:S(2)}) copy-start(bf16[16,136,1,1]{1,0,3,2:T(8,128)(2,1)} %constant.55) | copy-start | bytes 13060
  58.7 7.8 %copy-start.7 = (bf16[16,136,1,1]{1,0,3,2:T(8,128)(2,1)S(1)}, bf16[16,136,1,1]{1,0,3,2:T(8,128)(2,1)}, u32[]{:S(2)}) copy-start(bf16[16,136,1,1]{1,0,3,2:T(8,128)(2,1)} %constant.56) | copy-start | bytes 13060
  58.7 7.9 %copy-start.12 = (bf16[136]{0:T(256)(128)(2,1)S(1)}, bf16[136]{0:T(256)(128)(2,1)}, u32[]{:S(2)}) copy-start(bf16[136]{0:T(256)(128)(2,1)} %constant.50.clone) | copy-start | bytes 820
  60.9 12.1 %collective-permute-start.1 = (bf16[64,8,16]{0,2,1:T(8,128)(2,1)}, bf16[64,8,16]{0,2,1:T(8,128)(2,1)}, u32[]{:S(2)}, u32[]{:S(2)}) collective-permute-start(bf16[64,8,16]{0,2,1:T(8,128)(2,1)} %slice.21), channel_id=1, source_target_pairs={{0,4},{4,8},{8,12},{1,5},{5,9},{9,13},{2,6},{6,10},{10,14},{3,7},{... | collective-permute-start | bytes 49160 | tf_op jit(solution)/shard_map/ppermute | solution.py:22
  75.2 10.9 %copy-start.5 = (pred[512,512]{1,0:T(8,128)(4,1)S(1)}, pred[512,512]{1,0:T(8,128)(4,1)}, u32[]{:S(2)}) copy-start(pred[512,512]{1,0:T(8,128)(4,1)} %iota_compare_fusion) | copy-start | bytes 786436
  75.2 10.9 %copy-start.6 = (bf16[2,512,8,16]{1,0,3,2:T(2,128)(2,1)S(1)}, bf16[2,512,8,16]{1,0,3,2:T(2,128)(2,1)}, u32[]{:S(2)}) copy-start(bf16[2,512,8,16]{1,0,3,2:T(2,128)(2,1)} %reshape.168) | copy-start | bytes 786436
  82.7 12.0 %collective-permute-start = (bf16[64,8,128]{2,1,0:T(8,128)(2,1)S(1)}, bf16[64,8,128]{2,1,0:T(8,128)(2,1)S(1)}, u32[]{:S(2)}, u32[]{:S(2)}) collective-permute-start(bf16[64,8,128]{2,1,0:T(8,128)(2,1)S(1)} %slice.23), channel_id=1, source_target_pairs={{0,4},{4,8},{8,12},{1,5},{5,9},{9,13},{2,6},{6,10},{10,14},{3,7},{... | collective-permute-start | bytes 393224 | tf_op jit(solution)/shard_map/ppermute | solution.py:22
  93.4 1.3 copy-start.3
  94.7 2.2 %copy-start.13 = (f32[16,8,64,128]{3,2,1,0:T(8,128)S(1)}, f32[16,8,64,128]{3,2,1,0:T(8,128)}, u32[]{:S(2)}) copy-start(f32[16,8,64,128]{3,2,1,0:T(8,128)} %get-tuple-element.6) | copy-start | bytes 12582916
  104.8 13.0 %copy-start = (bf16[2,512,8,136]{1,3,2,0:T(8,128)(2,1)S(1)}, bf16[2,512,8,136]{1,3,2,0:T(8,128)(2,1)}, u32[]{:S(2)}) copy-start(bf16[2,512,8,136]{1,3,2,0:T(8,128)(2,1)} %fusion.25) | copy-start | bytes 6684676
  104.8 13.0 %copy-start.2 = (bf16[2,512,8,16]{1,3,2,0:T(8,128)(2,1)S(1)}, bf16[2,512,8,16]{1,3,2,0:T(8,128)(2,1)}, u32[]{:S(2)}) copy-start(bf16[2,512,8,16]{1,3,2,0:T(8,128)(2,1)} %multiply_convert_fusion.2) | copy-start | bytes 786436
  122.3 4.6 %copy-start.11 = (f32[1024]{0:T(1024)S(1)}, f32[1024]{0:T(1024)}, u32[]{:S(2)}) copy-start(f32[1024]{0:T(1024)} %param.12) | copy-start | bytes 12292
Sparse Core Ops, SparseCore 0:
  60.1 55.3 all-gather.2

commit v3 on v2

--- a/solution.py
+++ b/solution.py
@@ -42,11 +42,11 @@
     query_tok = queries.reshape(local_tokens, HEADS, KD)
     key_tok = keys.reshape(local_tokens, HEADS, KD)
     value_tok = values.reshape(local_tokens, HEADS, VD)
-    query_head, key_head, value_head = (
-        lax.all_to_all(query_tok, "head", split_axis=1, concat_axis=0, tiled=True),
-        lax.all_to_all(key_tok, "head", split_axis=1, concat_axis=0, tiled=True),
-        lax.all_to_all(value_tok, "head", split_axis=1, concat_axis=0, tiled=True),
-    )
+    packed = jnp.concatenate([query_tok, key_tok, value_tok], axis=2)
+    packed = lax.all_to_all(packed, "head", split_axis=1, concat_axis=0, tiled=True)
+    query_head = packed[:, :, :KD]
+    key_head = packed[:, :, KD : 2 * KD]
+    value_head = packed[:, :, 2 * KD :]
     span_rows = query_head.shape[0]
     heads_here = query_head.shape[1]
     block_rows = min(512, span_rows)
@@ -62,7 +62,7 @@
         preferred_element_type=jnp.float32,
     )
     span_state = jnp.sum(block_states, axis=0)
-    everything = lax.all_gather(span_state, "ctx")
+    everything = lax.all_gather(span_state.astype(jnp.bfloat16), "ctx").astype(jnp.float32)
     peers = everything.shape[0]
     here = lax.axis_index("ctx")
     entering = jnp.sum(

time: 174 us -> 195 us (1.12)
  matrix products: 28.6 us -> 40.4 us
  local copies, waits for them, and re-layouts: 41.7 us -> 51.5 us
  starting transfers between devices: 20.2 us -> 13.1 us
  other arithmetic: 10.3 us -> 16.4 us
    all_to_all x3 -> x1, waiting for transfers between devices: 19.5 us -> 30.5 us  [per_device(): lax.all_to_all(packed, 'head', split_axis=1, concat_axis=0, tiled=True)]
    all_gather x1, waiting for transfers between devices: 10.7 us -> 0.01 us  [per_device(): lax.all_gather(span_state.astype(jnp.bfloat16), 'ctx').astype(jnp.float32)]
    all_to_all x3 -> x1, starting transfers between devices: 12.1 us -> 4.21 us  [per_device(): lax.all_to_all(packed, 'head', split_axis=1, concat_axis=0, tiled=True)]
    slice x0 -> x4, local copies, waits for them, and re-layouts: none -> 6.56 us  [the longest x2 5.79 us: per_device(): value_head = packed[:, :, 2 * KD:]]
    reshape x3 -> x0, local copies, waits for them, and re-layouts: 3.9 us -> none  [the longest x1 2.86 us: per_device(): value_tok = values.reshape(local_tokens, HEADS, VD)]
    concatenate x0 -> x1, local copies, waits for them, and re-layouts: none -> 3.37 us  [per_device(): jnp.concatenate([tail_values, value_head[:span_rows - WINDOW]], axis=0)]
    concatenate x1, other arithmetic: 0.18 us -> 3.54 us  [per_device(): jnp.concatenate([tail_values, value_head[:span_rows - WINDOW]], axis=0)]
    dot_general x2, matrix products: 2.98 us -> 5.79 us  [unique_features(): jnp.einsum('...d,df->...f', vector, pick_cols, preferred_element_type=jnp...]
  transfers between devices with their start and end apart: 6 -> 4, of which waited for: 2 -> 1; matrix products, arithmetic and copies ran while one was open for 31% -> 28% of each run, Pallas kernels for 0% -> 0%
where the time goes in v3:
time: 195 us; the launch traced here: 194 us
  local copies, waits for them, and re-layouts  51.5 us (26%)
  matrix products  40.4 us (21%)
  waiting for transfers between devices  30.5 us (16%)
  blocking collectives  28.2 us (14%)
  other arithmetic  16.4 us (8%)
  between operations  13.7 us (7%)
  starting transfers between devices  13.1 us (7%)
    all_to_all x1, waiting for transfers between devices, per_device(): lax.all_to_all(packed, 'head', split_axis=1, concat_axis=0, tiled=True)  30.5 us
    all_to_all x1, blocking collectives, per_device(): lax.all_to_all(mixed, 'head', split_axis=0, concat_axis=1, tiled=True)  28.2 us
    dot_general x1, matrix products, per_device(): jnp.einsum('nhrs,nshv->nrhv', kernel, value_blocks, preferred_element_typ...  9.46 us
    ppermute x2, starting transfers between devices, shifted(): return lax.ppermute(shard, axis, pairs)  8.87 us
    sub x1, matrix products, per_device(): expo = jnp.where(valid, jnp.exp(window_scores - highest_score), 0.0)  7.41 us
    unnamed x41, local copies, waits for them, and re-layouts  6.13 us
    dot_general x1, matrix products, per_device(): jnp.einsum('nrhf,nhfv->nrhv', query_feat, states, preferred_element_type=...  5.81 us
    dot_general x2, matrix products, unique_features(): jnp.einsum('...d,df->...f', vector, pick_cols, preferred_element_type=jnp...  5.79 us
  transfers between devices with their start and end apart: 4, of which 1 were waited for; matrix products, arithmetic and copies ran while one was open for 28% of the time, Pallas kernels for 0%

profile of v3, /device:TPU:0, one launch (start us, length us, event | category | flops | bytes accessed | tf_op | source)
XLA Modules:
  0.0 193.8 jit_solution(3157501746191368267)
XLA Ops:
  6.5 3.3 %copy.144 = bf16[256,4096]{0,1:T(8,128)(2,1)S(1)} copy(bf16[256,4096]{1,0:T(8,128)(2,1)} %param.11) | data formatting | bytes 4194304 | tf_op args[2]
  10.2 1.8 pad_maximum_fusion
  11.9 4.2 %all-to-all-start = ((bf16[256,32,160]{0,2,1:T(8,128)(2,1)}), bf16[256,32,160]{0,2,1:T(8,128)(2,1)S(1)}, u32[]{:S(2)}, u32[]{:S(2)}) async-start(bf16[256,32,160]{0,2,1:T(8,128)(2,1)} %pad_maximum_fusion), calls=%async_computation | async-start | bytes 5242880 | tf_op jit(solution)/shard_map/all_to_all | solution.py:46
  17.0 30.5 %all-to-all-done = bf16[256,32,160]{0,2,1:T(8,128)(2,1)S(1)} async-done(((bf16[256,32,160]{0,2,1:T(8,128)(2,1)}), bf16[256,32,160]{0,2,1:T(8,128)(2,1)S(1)}, u32[]{:S(2)}, u32[]{:S(2)}) %all-to-all-start) | async-done | bytes 2621472 | tf_op jit(solution)/shard_map/all_to_all | solution.py:46
  47.5 1.5 copy-done
  49.0 2.1 %copy.176 = bf16[4,8,20,8,256]{4,3,0,2,1:T(8,128)(2,1)S(1)} copy(bf16[4,8,20,8,256]{4,3,2,1,0:T(8,128)(2,1)} %bitcast.84) | data formatting | bytes 5242880 | tf_op jit(solution)/shard_map/all_to_all | solution.py:46
  51.2 1.6 slice.36
  55.5 2.5 %pad_maximum_fusion.1 = bf16[1024,8,153]{0,2,1:T(8,128)(2,1)} fusion(bf16[1024,8,136]{0,2,1:T(8,128)(2,1)S(1)} %multiply_convert_fusion.1, bf16[1024,8,16]{0,2,1:T(8,128)(2,1)S(1)} %multiply_convert_fusion.3, bf16[153]{0:T(256)(128)(2,1)S(1)} %pad.12.clone), kind=kLoop, calls=%fused_computation.23 | loop fusion | flops 7520256 | bytes 4997426 | tf_op jit(solution)/shard_map/concatenate | solution.py:37
  58.0 4.6 %reshape.188 = bf16[2,512,8,153]{1,0,3,2:T(2,128)(2,1)} reshape(bf16[1024,8,153]{0,2,1:T(8,128)(2,1)} %pad_maximum_fusion.1) | data formatting | bytes 5013504 | tf_op jit(solution)/shard_map/reshape | solution.py:60
  62.6 4.2 %copy.146 = bf16[1024,8,128]{2,1,0:T(8,128)(2,1)} copy(bf16[1024,8,128]{0,2,1:T(8,128)(2,1)} %slice.36) | data formatting | bytes 4194304 | tf_op jit(solution)/shard_map/slice | solution.py:49
  66.7 4.4 %fusion.82 = (bf16[8,153,128]{2,1,0:T(8,128)(2,1)S(1)}, f32[2,8,153,128]{3,2,1,0:T(8,128)}) fusion(bf16[2,512,8,128]{3,2,1,0:T(8,128)(2,1)} %bitcast.85, bf16[2,512,8,153]{1,0,3,2:T(2,128)(2,1)} %reshape.188), kind=kOutput, calls=%fused_computation.90 | convolution fusion | flops 321020928 | bytes 6170624 | tf_op jit(solution)/shard_map/nrhf,nrhv->nhfv/dot_general | solution.py:58
  72.0 5.0 %collective-permute-start.1 = (bf16[64,8,16]{0,2,1:T(8,128)(2,1)}, bf16[64,8,16]{0,2,1:T(8,128)(2,1)}, u32[]{:S(2)}, u32[]{:S(2)}) collective-permute-start(bf16[64,8,16]{0,2,1:T(8,128)(2,1)} %slice.40), channel_id=1, source_target_pairs={{0,4},{4,8},{8,12},{1,5},{5,9},{9,13},{2,6},{6,10},{10,14},{3,7},{... | collective-permute-start | bytes 49160 | tf_op jit(solution)/shard_map/ppermute | solution.py:22
  77.0 2.8 %fusion.51 = f32[2,512,8,136]{1,3,2,0:T(8,128)} fusion(bf16[16,136,1,1]{1,0,3,2:T(8,128)(2,1)S(1)} %copy-done.13, bf16[8,2,2,8,512]{4,3,2,1,0:T(8,128)(2,1)S(1)} %bitcast.80), kind=kOutput, calls=%fused_computation.57 | convolution fusion | flops 35651584 | bytes 4722944 | tf_op jit(solution)/shard_map/...d,df->...f/dot_general | solution.py:29
  79.8 9.5 %fusion.1 = f32[2,8,128,512]{3,2,1,0:T(8,128)} fusion(pred[512,512]{1,0:T(8,128)(4,1)S(1)} %iota_compare_fusion, bf16[2,512,8,128]{3,2,1,0:T(8,128)(2,1)} %bitcast.86, bf16[8,2,2,8,512]{4,3,2,1,0:T(8,128)(2,1)S(1)} %bitcast.94, bf16[8,2,2,8,512]{4,3,2,1,0:T(8,128)(2,1)S(1)} %bitcast.81), kind=kOutput, calls=%fused_computation.2 | convolution fusion | flops 1237319680 | bytes 7077888 | tf_op jit(solution)/shard_map/nhrs,nshv->nrhv/dot_general | solution.py:91
  89.3 4.7 %fusion.23 = bf16[2,512,8,136]{1,3,2,0:T(8,128)(2,1)} fusion(f32[2,512,8,136]{1,3,2,0:T(8,128)} %fusion.51, bf16[16,136,1,1]{1,0,3,2:T(8,128)(2,1)S(1)} %copy-done.12, bf16[136]{0:T(256)(128)(2,1)S(1)} %copy-done.17, bf16[8,2,2,8,512]{4,3,2,1,0:T(8,128)(2,1)S(1)} %bitcast.82), kind=kOutput, calls=%fused_computation.33 | convolution fusion | flops 40108032 | bytes 6951440 | tf_op jit(solution)/shard_map/...d,df->...f/dot_general | solution.py:30
  95.5 1.3 reshape.179
  96.8 1.2 reshape.177
  97.9 1.6 slice.43
  101.4 3.9 %collective-permute-start = (bf16[64,8,128]{0,2,1:T(8,128)(2,1)}, bf16[64,8,128]{0,2,1:T(8,128)(2,1)}, u32[]{:S(2)}, u32[]{:S(2)}) collective-permute-start(bf16[64,8,128]{0,2,1:T(8,128)(2,1)} %slice.42), channel_id=1, source_target_pairs={{0,4},{4,8},{8,12},{1,5},{5,9},{9,13},{2,6},{6,10},{10,14},{3,7},{... | collective-permute-start | bytes 393224 | tf_op jit(solution)/shard_map/ppermute | solution.py:22
  105.3 1.9 copy.163
  109.4 7.4 %fusion.77 = (f32[16,8,64]{2,1,0:T(8,128)S(1)}, f32[16,8,64,128]{3,2,1,0:T(8,128)}) fusion(pred[16,64,128]{2,1,0:T(8,128)(4,1)S(1)} %broadcast_and_fusion, bf16[16,64,8,16]{1,0,3,2:T(8,128)(2,1)} %reshape.177, bf16[16,64,8,16]{1,3,2,0:T(8,128)(2,1)S(1)} %copy-done.8, bf16[16,64,8,16]{1,3,2,0:T(8,128)(2,1)} %copy.164), kind=kOutput, calls=%fused_computation.89 | convolution fusion | flops 75497600 | bytes 5144576 | tf_op jit(solution)/shard_map/sub | solution.py:128
  116.8 3.5 %pad_maximum_fusion.2 = bf16[1024,8,128]{0,2,1:T(8,128)(2,1)} fusion(bf16[960,8,128]{0,2,1:T(8,128)(2,1)S(1)} %copy-done.3, bf16[64,8,128]{0,2,1:T(8,128)(2,1)} %collective-permute-done), kind=kLoop, calls=%fused_computation.35 | loop fusion | flops 4194304 | bytes 4194304 | tf_op jit(solution)/shard_map/concatenate | solution.py:101
  120.3 3.4 %copy.160 = bf16[1024,8,128]{2,1,0:T(8,128)(2,1)S(1)} copy(bf16[1024,8,128]{0,2,1:T(8,128)(2,1)} %pad_maximum_fusion.2) | data formatting | bytes 4194304 | tf_op jit(solution)/shard_map/concatenate | solution.py:101
  125.3 4.0 %fusion.26 = f32[16,64,8,128]{3,1,2,0:T(8,128)S(1)} fusion(bf16[16,64,8,128]{3,1,2,0:T(8,128)(2,1)S(1)} %copy-done.4, bf16[16,64,8,128]{3,1,2,0:T(8,128)(2,1)S(1)} %copy.162, f32[16,8,64,128]{3,2,1,0:T(8,128)} %get-tuple-element.8, f32[16,8,64]{2,1,0:T(8,128)S(1)} %get-tuple-element.7), kind=kOutput, calls=%fused_computation.34 | convolution fusion | flops 278921216 | bytes 12615680 | tf_op jit(solution)/shard_map/chrp,cphv->crhv/dot_general | solution.py:130
  129.3 5.3 %copy.167 = f32[16,64,8,128]{3,2,1,0:T(8,128)} copy(f32[16,64,8,128]{3,1,2,0:T(8,128)S(1)} %fusion.26) | data formatting | bytes 8388608 | tf_op jit(solution)/shard_map/chrp,cphv->crhv/transpose | solution.py:130
  134.6 1.9 fusion.22
  136.7 5.8 %multiply_reduce_fusion = (f32[2,512,8]{1,2,0:T(8,128)S(1)}, f32[2,512,8,128]{1,3,2,0:T(8,128)}) fusion(f32[2,8,128,512]{3,2,1,0:T(8,128)} %fusion.1, bf16[2,512,8,136]{1,3,2,0:T(8,128)(2,1)S(1)} %copy-done.1, bf16[2,512,8,16]{1,3,2,0:T(8,128)(2,1)S(1)} %copy-done.5, bf16[153]{0:T(256)(128)(2,1)S(1)} %pad.12.clone, f32[1,8,153,128]{3,2,1,0:T(8,128)S(1)} %slice.39, ...), kind=kOutput, calls=%fused_computation.19 | convolution fusion | flops 332148736 | bytes 12165426 | tf_op jit(solution)/shard_map/nrhf,nhfv->nrhv/dot_general | solution.py:93
  142.5 5.3 %copy.158 = f32[2,512,8,128]{3,2,1,0:T(8,128)} copy(f32[2,512,8,128]{1,3,2,0:T(8,128)} %get-tuple-element.12) | data formatting | bytes 8388608 | tf_op jit(solution)/shard_map/add | solution.py:94
  148.0 4.1 %fusion.9 = bf16[1024,8,128]{2,1,0:T(8,128)(2,1)S(1)} fusion(f32[16,64,8,128]{3,2,1,0:T(8,128)} %copy.167, f32[2,512,8,128]{3,2,1,0:T(8,128)} %copy.158, f32[8,128]{1,0:T(8,128)S(1)} %bitcast.96, f32[1024,8]{1,0:T(8,128)S(1)} %copy.159), kind=kLoop, calls=%fused_computation.12 | loop fusion | flops 4194304 | bytes 10522624 | tf_op jit(solution)/shard_map/convert_element_type | solution.py:136
  152.1 28.2 %all_to_all.33 = bf16[1024,8,128]{2,1,0:T(8,128)(2,1)S(1)} all-to-all(bf16[1024,8,128]{2,1,0:T(8,128)(2,1)S(1)} %fusion.9), channel_id=1, replica_groups=mesh['groups'=2,'ctx'=4,'head'=4] {'head'}, dimensions={0} | all-to-all | bytes 4194304 | tf_op jit(solution)/shard_map/all_to_all | solution.py:137
  180.3 2.6 %copy.168 = bf16[256,4,8,128]{0,3,2,1:T(8,128)(2,1)} copy(bf16[256,4,8,128]{3,2,0,1:T(8,128)(2,1)S(1)} %bitcast.90) | data formatting | bytes 4194304 | tf_op jit(solution)/shard_map/all_to_all | solution.py:137
  182.8 4.1 %copy.169 = bf16[256,4096]{1,0:T(8,128)(2,1)} copy(bf16[256,4096]{0,1:T(8,128)(2,1)} %bitcast.91) | data formatting | bytes 4194304 | tf_op jit(solution)/shard_map/reshape | solution.py:138
  (71 shorter events, 12.2 us)
Async XLA Ops:
  6.5 3.3 %copy-start.10 = (bf16[256,512]{1,0:T(8,128)(2,1)S(1)}, bf16[256,512]{1,0:T(8,128)(2,1)}, u32[]{:S(2)}) copy-start(bf16[256,512]{1,0:T(8,128)(2,1)} %param.9) | copy-start | bytes 786436
  6.5 3.5 %copy-start.11 = (bf16[256,512]{1,0:T(8,128)(2,1)S(1)}, bf16[256,512]{1,0:T(8,128)(2,1)}, u32[]{:S(2)}) copy-start(bf16[256,512]{1,0:T(8,128)(2,1)} %param.10) | copy-start | bytes 786436
  11.9 35.5 %all-to-all-start = ((bf16[256,32,160]{0,2,1:T(8,128)(2,1)}), bf16[256,32,160]{0,2,1:T(8,128)(2,1)S(1)}, u32[]{:S(2)}, u32[]{:S(2)}) async-start(bf16[256,32,160]{0,2,1:T(8,128)(2,1)} %pad_maximum_fusion), calls=%async_computation | async-start | bytes 5242880 | tf_op jit(solution)/shard_map/all_to_all | solution.py:46
  16.1 118.4 %all-gather.3.cloned.1.call-start = ((), (), s32[]{:S(2)}) async-start(), calls=%async_computation.2 | async-start | bytes 1566720 | tf_op jit(solution)/shard_map/all_gather | solution.py:65
  47.5 1.5 copy-start
  51.1 2.5 %copy-start.15 = (bf16[16,136,1]{1,0,2:T(8,128)(2,1)S(1)}, bf16[16,136,1]{1,0,2:T(8,128)(2,1)}, u32[]{:S(2)}) copy-start(bf16[16,136,1]{1,0,2:T(8,128)(2,1)} %constant.53) | copy-start | bytes 13060
  51.1 3.2 %copy-start.14 = (bf16[16,136,1]{1,0,2:T(8,128)(2,1)S(1)}, bf16[16,136,1]{1,0,2:T(8,128)(2,1)}, u32[]{:S(2)}) copy-start(bf16[16,136,1]{1,0,2:T(8,128)(2,1)} %constant.54) | copy-start | bytes 13060
  52.8 27.0 %copy-start.6 = (bf16[1024,8,16]{0,2,1:T(8,128)(2,1)}, bf16[1024,8,16]{0,2,1:T(8,128)(2,1)S(1)}, u32[]{:S(2)}) copy-start(bf16[1024,8,16]{0,2,1:T(8,128)(2,1)S(1)} %get-tuple-element.5) | copy-start | bytes 786436
  66.7 10.2 %copy-start.13 = (bf16[16,136,1,1]{1,0,3,2:T(8,128)(2,1)S(1)}, bf16[16,136,1,1]{1,0,3,2:T(8,128)(2,1)}, u32[]{:S(2)}) copy-start(bf16[16,136,1,1]{1,0,3,2:T(8,128)(2,1)} %constant.55) | copy-start | bytes 13060
  72.0 35.2 %collective-permute-start.1 = (bf16[64,8,16]{0,2,1:T(8,128)(2,1)}, bf16[64,8,16]{0,2,1:T(8,128)(2,1)}, u32[]{:S(2)}, u32[]{:S(2)}) collective-permute-start(bf16[64,8,16]{0,2,1:T(8,128)(2,1)} %slice.40), channel_id=1, source_target_pairs={{0,4},{4,8},{8,12},{1,5},{5,9},{9,13},{2,6},{6,10},{10,14},{3,7},{... | collective-permute-start | bytes 49160 | tf_op jit(solution)/shard_map/ppermute | solution.py:22
  79.8 9.5 %copy-start.12 = (bf16[16,136,1,1]{1,0,3,2:T(8,128)(2,1)S(1)}, bf16[16,136,1,1]{1,0,3,2:T(8,128)(2,1)}, u32[]{:S(2)}) copy-start(bf16[16,136,1,1]{1,0,3,2:T(8,128)(2,1)} %constant.56) | copy-start | bytes 13060
  79.8 9.5 %copy-start.17 = (bf16[136]{0:T(256)(128)(2,1)S(1)}, bf16[136]{0:T(256)(128)(2,1)}, u32[]{:S(2)}) copy-start(bf16[136]{0:T(256)(128)(2,1)} %constant.50.clone) | copy-start | bytes 820
  97.9 2.4 %copy-start.9 = (f32[2,8,153,128]{3,2,1,0:T(8,128)S(1)}, f32[2,8,153,128]{3,2,1,0:T(8,128)}, u32[]{:S(2)}) copy-start(f32[2,8,153,128]{3,2,1,0:T(8,128)} %get-tuple-element.10) | copy-start | bytes 3760132
  97.9 7.3 %copy-start.2 = (bf16[1024,8,128]{2,1,0:T(8,128)(2,1)S(1)}, bf16[1024,8,128]{2,1,0:T(8,128)(2,1)}, u32[]{:S(2)}) copy-start(bf16[1024,8,128]{2,1,0:T(8,128)(2,1)} %copy.146) | copy-start | bytes 6291460
  99.5 7.7 %copy-start.7 = (bf16[960,8,16]{0,2,1:T(8,128)(2,1)S(1)}, bf16[960,8,16]{0,2,1:T(8,128)(2,1)}, u32[]{:S(2)}) copy-start(bf16[960,8,16]{0,2,1:T(8,128)(2,1)} %slice.41) | copy-start | bytes 737284
  101.4 8.0 %copy-start.8 = (bf16[16,64,8,16]{1,3,2,0:T(8,128)(2,1)S(1)}, bf16[16,64,8,16]{1,3,2,0:T(8,128)(2,1)}, u32[]{:S(2)}) copy-start(bf16[16,64,8,16]{1,3,2,0:T(8,128)(2,1)} %copy.165) | copy-start | bytes 786436
  101.4 15.4 %collective-permute-start = (bf16[64,8,128]{0,2,1:T(8,128)(2,1)}, bf16[64,8,128]{0,2,1:T(8,128)(2,1)}, u32[]{:S(2)}, u32[]{:S(2)}) collective-permute-start(bf16[64,8,128]{0,2,1:T(8,128)(2,1)} %slice.42), channel_id=1, source_target_pairs={{0,4},{4,8},{8,12},{1,5},{5,9},{9,13},{2,6},{6,10},{10,14},{3,7},{... | collective-permute-start | bytes 393224 | tf_op jit(solution)/shard_map/ppermute | solution.py:22
  109.4 7.4 %copy-start.3 = (bf16[960,8,128]{0,2,1:T(8,128)(2,1)S(1)}, bf16[960,8,128]{0,2,1:T(8,128)(2,1)}, u32[]{:S(2)}) copy-start(bf16[960,8,128]{0,2,1:T(8,128)(2,1)} %slice.43) | copy-start | bytes 5898244
  123.7 1.6 copy-start.4
  129.3 5.3 %copy-start.18 = (pred[4]{0:T(512)(128)(4,1)S(1)}, pred[4]{0:T(512)(128)(4,1)}, u32[]{:S(2)}) copy-start(pred[4]{0:T(512)(128)(4,1)} %iota_compare_fusion.5) | copy-start | bytes 16
  129.3 7.4 %copy-start.1 = (bf16[2,512,8,136]{1,3,2,0:T(8,128)(2,1)S(1)}, bf16[2,512,8,136]{1,3,2,0:T(8,128)(2,1)}, u32[]{:S(2)}) copy-start(bf16[2,512,8,136]{1,3,2,0:T(8,128)(2,1)} %fusion.23) | copy-start | bytes 6684676
  129.3 7.4 %copy-start.5 = (bf16[2,512,8,16]{1,3,2,0:T(8,128)(2,1)S(1)}, bf16[2,512,8,16]{1,3,2,0:T(8,128)(2,1)}, u32[]{:S(2)}) copy-start(bf16[2,512,8,16]{1,3,2,0:T(8,128)(2,1)} %multiply_convert_fusion.2) | copy-start | bytes 786436
  142.5 5.5 %copy-start.16 = (f32[1024]{0:T(1024)S(1)}, f32[1024]{0:T(1024)}, u32[]{:S(2)}) copy-start(f32[1024]{0:T(1024)} %param.12) | copy-start | bytes 12292
Sparse Core Ops, SparseCore 0:
  72.1 35.3 all-gather.2

commit v4 on v2

--- a/solution.py
+++ b/solution.py
@@ -37,21 +37,11 @@
     return jnp.concatenate([unit, half, prod], axis=-1)
 
 
-def per_device(queries, keys, values, gain):
-    local_tokens = queries.shape[0]
-    query_tok = queries.reshape(local_tokens, HEADS, KD)
-    key_tok = keys.reshape(local_tokens, HEADS, KD)
-    value_tok = values.reshape(local_tokens, HEADS, VD)
-    query_head, key_head, value_head = (
-        lax.all_to_all(query_tok, "head", split_axis=1, concat_axis=0, tiled=True),
-        lax.all_to_all(key_tok, "head", split_axis=1, concat_axis=0, tiled=True),
-        lax.all_to_all(value_tok, "head", split_axis=1, concat_axis=0, tiled=True),
-    )
+def attend(query_head, key_head, value_head, gains, first_span):
     span_rows = query_head.shape[0]
     heads_here = query_head.shape[1]
     block_rows = min(512, span_rows)
     block_count = span_rows // block_rows
-    first_span = lax.axis_index("ctx") == 0
 
     key_feat = unique_features(key_head, False)
     feat = key_feat.shape[-1]
@@ -93,9 +83,11 @@
     inter = jnp.einsum("nrhf,nhfv->nrhv", query_feat, states, preferred_element_type=jnp.float32)
     linear = (intra + inter).reshape(span_rows, heads_here, VD)
 
-    tail_keys, tail_values = shifted(
-        (key_head[span_rows - WINDOW :], value_head[span_rows - WINDOW :]), "ctx", 1
+    tails = shifted(
+        jnp.concatenate([key_head, value_head], axis=2)[span_rows - WINDOW :], "ctx", 1
     )
+    tail_keys = tails[:, :, :KD]
+    tail_values = tails[:, :, KD:]
     chunks = span_rows // WINDOW
     key_prev = jnp.concatenate([tail_keys, key_head[: span_rows - WINDOW]], axis=0)
     value_prev = jnp.concatenate([tail_values, value_head[: span_rows - WINDOW]], axis=0)
@@ -132,10 +124,39 @@
     ).reshape(span_rows, heads_here, VD)
 
     scale = lax.rsqrt(jnp.mean(linear * linear, axis=2, keepdims=True) + epsilon)
-    gains = gain.reshape(heads_here, VD)
-    mixed = (linear * scale * gains + window).astype(jnp.bfloat16)
-    tokens_back = lax.all_to_all(mixed, "head", split_axis=0, concat_axis=1, tiled=True)
-    return tokens_back.reshape(tokens_back.shape[0], HEADS * VD)
+    return (linear * scale * gains + window).astype(jnp.bfloat16)
+
+
+def per_device(queries, keys, values, gain):
+    local_tokens = queries.shape[0]
+    peers = lax.axis_size("head")
+    heads_here = HEADS // peers
+    groups = 2 if heads_here % 2 == 0 else 1
+    group_heads = heads_here // groups
+    query_tok = queries.reshape(local_tokens, peers, groups, group_heads, KD)
+    key_tok = keys.reshape(local_tokens, peers, groups, group_heads, KD)
+    value_tok = values.reshape(local_tokens, peers, groups, group_heads, VD)
+    gains = gain.reshape(groups, group_heads, VD)
+    first_span = lax.axis_index("ctx") == 0
+    span_rows = local_tokens * peers
+
+    def gathered(tok, g, width):
+        moved = lax.all_to_all(tok[:, :, g], "head", split_axis=1, concat_axis=0, tiled=True)
+        return moved.reshape(span_rows, group_heads, width)
+
+    outs = []
+    for g in range(groups):
+        mixed = attend(
+            gathered(query_tok, g, KD),
+            gathered(key_tok, g, KD),
+            gathered(value_tok, g, VD),
+            gains[g],
+            first_span,
+        )
+        back = lax.all_to_all(mixed, "head", split_axis=0, concat_axis=1, tiled=True)
+        outs.append(back.reshape(local_tokens, peers, group_heads, VD))
+    tokens_back = jnp.stack(outs, axis=2)
+    return tokens_back.reshape(local_tokens, HEADS * VD)
 
 
 def solution(mesh):

time: 174 us -> 219 us (1.26)
  blocking collectives: 28.8 us -> 0 us
  starting transfers between devices: 20.2 us -> 36.8 us
  local copies, waits for them, and re-layouts: 41.7 us -> 58.2 us
  waiting for transfers between devices: 30.2 us -> 46.3 us
  other arithmetic: 10.3 us -> 24.9 us
  matrix products: 28.6 us -> 36.7 us
    all_to_all x1 -> x0, blocking collectives: 28.8 us -> none  [per_device(): lax.all_to_all(mixed, 'head', split_axis=0, concat_axis=1, tiled=True)]
    all_to_all x3 -> x8, waiting for transfers between devices: 19.5 us -> 39.3 us  [the longest x2 21.3 us: per_device(): lax.all_to_all(mixed, 'head', split_axis=0, concat_axis=1, tiled=True)]
    another operation x0 -> x11, local copies, waits for them, and re-layouts: none -> 16.6 us  [the longest x4 7.11 us: attend(): key_head.reshape(chunks, WINDOW, heads_here, KD)]
    all_to_all x3 -> x8, starting transfers between devices: 12.1 us -> 28.3 us  [the longest x6 21.2 us: gathered(): lax.all_to_all(tok[:, :, g], 'head', split_axis=1, concat_axis=0, tiled=T...]
    dot_general x4 -> x10, matrix products: 16.5 us -> 28.8 us  [the longest x2 11.1 us: attend(): jnp.einsum('nhrs,nshv->nrhv', kernel, value_blocks, preferred_element_typ...]
    sub x1 -> x0, matrix products: 7.55 us -> none  [per_device(): expo = jnp.where(valid, jnp.exp(window_scores - highest_score), 0.0)]
    sub x0 -> x2, other arithmetic: none -> 5.38 us  [attend(): expo = jnp.where(valid, jnp.exp(window_scores - highest_score), 0.0)]
    add x1 -> x2, local copies, waits for them, and re-layouts: 4.4 us -> 0.27 us  [attend(): linear = (intra + inter).reshape(span_rows, heads_here, VD)]
  transfers between devices with their start and end apart: 6 -> 12, of which waited for: 2 -> 7; matrix products, arithmetic and copies ran while one was open for 31% -> 47% of each run, Pallas kernels for 0% -> 0%
where the time goes in v4:
time: 219 us; the launch traced here: 217 us
  local copies, waits for them, and re-layouts  58.2 us (27%)
  waiting for transfers between devices  46.3 us (21%)
  starting transfers between devices  36.8 us (17%)
  matrix products  36.7 us (17%)
  other arithmetic  24.9 us (11%)
  between operations  14.1 us (6%)
    all_to_all x2, waiting for transfers between devices, per_device(): lax.all_to_all(mixed, 'head', split_axis=0, concat_axis=1, tiled=True)  21.3 us
    all_to_all x6, starting transfers between devices, gathered(): lax.all_to_all(tok[:, :, g], 'head', split_axis=1, concat_axis=0, tiled=T...  21.2 us
    all_to_all x6, waiting for transfers between devices, gathered(): lax.all_to_all(tok[:, :, g], 'head', split_axis=1, concat_axis=0, tiled=T...  18 us
    dot_general x2, matrix products, attend(): jnp.einsum('nhrs,nshv->nrhv', kernel, value_blocks, preferred_element_typ...  11.1 us
    ppermute x2, starting transfers between devices, shifted(): return lax.ppermute(shard, axis, pairs)  8.49 us
    another operation x4, local copies, waits for them, and re-layouts, attend(): key_head.reshape(chunks, WINDOW, heads_here, KD)  7.11 us
    all_to_all x2, starting transfers between devices, per_device(): lax.all_to_all(mixed, 'head', split_axis=0, concat_axis=1, tiled=True)  7.03 us
    all_gather x2, waiting for transfers between devices, attend(): everything = lax.all_gather(span_state, 'ctx')  6.98 us
  transfers between devices with their start and end apart: 12, of which 7 were waited for; matrix products, arithmetic and copies ran while one was open for 47% of the time, Pallas kernels for 0%

profile of v4, /device:TPU:0, one launch (start us, length us, event | category | flops | bytes accessed | tf_op | source)
XLA Modules:
  0.0 217.1 jit_solution(292104657550504875)
XLA Ops:
  8.4 4.2 %all-to-all-start.5 = ((bf16[256,4,4,16]{0,3,2,1:T(8,128)(2,1)}), bf16[256,4,4,16]{0,3,2,1:T(8,128)(2,1)S(1)}, u32[]{:S(2)}, u32[]{:S(2)}) async-start(bf16[256,4,4,16]{0,3,2,1:T(8,128)(2,1)} %get-tuple-element.12), calls=%async_computation.5 | async-start | bytes 262144 | tf_op jit(solution)/shard_map/all_to_all | solution.py:144
  12.6 3.3 %copy.132 = bf16[256,4096]{0,1:T(8,128)(2,1)S(1)} copy(bf16[256,4096]{1,0:T(8,128)(2,1)} %param.16) | data formatting | bytes 4194304 | tf_op args[2]
  20.0 3.3 %all-to-all-start.1 = ((bf16[256,4,4,16]{0,3,2,1:T(8,128)(2,1)}), bf16[256,4,4,16]{0,3,2,1:T(8,128)(2,1)S(1)}, u32[]{:S(2)}, u32[]{:S(2)}) async-start(bf16[256,4,4,16]{0,3,2,1:T(8,128)(2,1)} %get-tuple-element.11), calls=%async_computation.1 | async-start | bytes 262144 | tf_op jit(solution)/shard_map/all_to_all | solution.py:144
  23.5 4.4 %all-to-all-done.1 = bf16[256,4,4,16]{0,3,2,1:T(8,128)(2,1)S(1)} async-done(((bf16[256,4,4,16]{0,3,2,1:T(8,128)(2,1)}), bf16[256,4,4,16]{0,3,2,1:T(8,128)(2,1)S(1)}, u32[]{:S(2)}, u32[]{:S(2)}) %all-to-all-start.1) | async-done | bytes 131104 | tf_op jit(solution)/shard_map/all_to_all | solution.py:144
  27.9 3.3 %all-to-all-start.4 = ((bf16[256,4,4,16]{0,3,2,1:T(8,128)(2,1)}), bf16[256,4,4,16]{0,3,2,1:T(8,128)(2,1)S(1)}, u32[]{:S(2)}, u32[]{:S(2)}) async-start(bf16[256,4,4,16]{0,3,2,1:T(8,128)(2,1)} %get-tuple-element.10), calls=%async_computation.4 | async-start | bytes 262144 | tf_op jit(solution)/shard_map/all_to_all | solution.py:144
  35.9 3.3 %all-to-all-start = ((bf16[256,4,4,16]{0,3,2,1:T(8,128)(2,1)}), bf16[256,4,4,16]{0,3,2,1:T(8,128)(2,1)S(1)}, u32[]{:S(2)}, u32[]{:S(2)}) async-start(bf16[256,4,4,16]{0,3,2,1:T(8,128)(2,1)} %get-tuple-element.9), calls=%async_computation | async-start | bytes 262144 | tf_op jit(solution)/shard_map/all_to_all | solution.py:144
  40.1 3.7 %all-to-all-done = bf16[256,4,4,16]{0,3,2,1:T(8,128)(2,1)S(1)} async-done(((bf16[256,4,4,16]{0,3,2,1:T(8,128)(2,1)}), bf16[256,4,4,16]{0,3,2,1:T(8,128)(2,1)S(1)}, u32[]{:S(2)}, u32[]{:S(2)}) %all-to-all-start) | async-done | bytes 131104 | tf_op jit(solution)/shard_map/all_to_all | solution.py:144
  43.8 3.5 %all-to-all-start.2 = ((bf16[256,4,4,128]{0,3,2,1:T(8,128)(2,1)}), bf16[256,4,4,128]{0,3,2,1:T(8,128)(2,1)S(1)}, u32[]{:S(2)}, u32[]{:S(2)}) async-start(bf16[256,4,4,128]{0,3,2,1:T(8,128)(2,1)} %get-tuple-element.7), calls=%async_computation.2 | async-start | bytes 2097152 | tf_op jit(solution)/shard_map/all_to_all | solution.py:144
  52.3 9.4 %all-to-all-done.2 = bf16[256,4,4,128]{0,3,2,1:T(8,128)(2,1)S(1)} async-done(((bf16[256,4,4,128]{0,3,2,1:T(8,128)(2,1)}), bf16[256,4,4,128]{0,3,2,1:T(8,128)(2,1)S(1)}, u32[]{:S(2)}, u32[]{:S(2)}) %all-to-all-start.2) | async-done | bytes 1048608 | tf_op jit(solution)/shard_map/all_to_all | solution.py:144
  61.7 3.5 %all-to-all-start.6 = ((bf16[256,4,4,128]{0,3,2,1:T(8,128)(2,1)}), bf16[256,4,4,128]{0,3,2,1:T(8,128)(2,1)S(1)}, u32[]{:S(2)}, u32[]{:S(2)}) async-start(bf16[256,4,4,128]{0,3,2,1:T(8,128)(2,1)} %get-tuple-element.8), calls=%async_computation.6 | async-start | bytes 2097152 | tf_op jit(solution)/shard_map/all_to_all | solution.py:144
  65.3 3.7 %pad_maximum_fusion.3 = (bf16[1024,4,153]{0,2,1:T(8,128)(2,1)}, bf16[1024,4,153]{0,2,1:T(8,128)(2,1)S(1)}) fusion(bf16[1024,4,136]{0,2,1:T(8,128)(2,1)} %fusion.32, bf16[1024,4,16]{0,2,1:T(8,128)(2,1)} %multiply_convert_fusion.7, bf16[153]{0:T(256)(128)(2,1)S(1)} %pad.33.clone, bf16[1024,4,136]{0,2,1:T(8,128)(2,1)} %fusion.35, ...), kind=kLoop, calls=%fused_computation.55 | loop fusion | flops 6893568 | bytes 4997426 | tf_op jit(solution)/shard_map/concatenate | solution.py:37
  69.0 2.7 %reshape.229 = bf16[2,512,4,153]{1,0,3,2:T(2,128)(2,1)} reshape(bf16[1024,4,153]{0,2,1:T(8,128)(2,1)} %get-tuple-element.15) | data formatting | bytes 2506752 | tf_op jit(solution)/shard_map/reshape | solution.py:50
  74.6 3.7 %fusion.110 = (f32[4,153,128]{2,1,0:T(8,128)}, f32[2,4,153,128]{3,2,1,0:T(8,128)}) fusion(bf16[2,512,4,128]{3,1,0,2:T(8,128)(2,1)} %bitcast.198, bf16[2,512,4,153]{1,0,3,2:T(2,128)(2,1)} %reshape.229), kind=kOutput, calls=%fused_computation.158 | convolution fusion | flops 160510464 | bytes 3241984 | tf_op jit(solution)/shard_map/nrhf,nrhv->nhfv/dot_general | solution.py:48
  85.2 1.8 reshape_reshape.42
  102.0 4.7 %collective-permute-start.1 = (bf16[64,4,144]{0,2,1:T(8,128)(2,1)}, bf16[64,4,144]{0,2,1:T(8,128)(2,1)}, u32[]{:S(2)}, u32[]{:S(2)}) collective-permute-start(bf16[64,4,144]{0,2,1:T(8,128)(2,1)} %pad_maximum_fusion.7), channel_id=1, source_target_pairs={{0,4},{4,8},{8,12},{1,5},{5,9},{9,13},{2,6},{6,10},{10,14},{3,7},{... | collective-permute-start | bytes 221192 | tf_op jit(solution)/shard_map/ppermute | solution.py:22
  108.2 3.8 %collective-permute-start = (bf16[64,4,144]{0,2,1:T(8,128)(2,1)}, bf16[64,4,144]{0,2,1:T(8,128)(2,1)}, u32[]{:S(2)}, u32[]{:S(2)}) collective-permute-start(bf16[64,4,144]{0,2,1:T(8,128)(2,1)} %pad_maximum_fusion.8), channel_id=1, source_target_pairs={{0,4},{4,8},{8,12},{1,5},{5,9},{9,13},{2,6},{6,10},{10,14},{3,7},{... | collective-permute-start | bytes 221192 | tf_op jit(solution)/shard_map/ppermute | solution.py:22
  112.1 5.5 %fusion.2 = f32[2,4,512,128]{3,2,1,0:T(8,128)} fusion(pred[512,512]{1,0:T(8,128)(4,1)} %iota_compare_fusion, bf16[2,512,4,128]{3,1,0,2:T(8,128)(2,1)} %bitcast.199, bf16[2,512,4,16]{1,0,3,2:T(2,128)(2,1)} %reshape_reshape.39, bf16[2,512,4,16]{1,0,3,2:T(2,128)(2,1)S(1)} %copy-done.9), kind=kOutput, calls=%fused_computation.4 | convolution fusion | flops 618659840 | bytes 3670016 | tf_op jit(solution)/shard_map/nhrs,nshv->nrhv/dot_general | solution.py:81
  117.6 5.6 %fusion.3 = f32[2,4,512,128]{3,2,1,0:T(8,128)} fusion(pred[512,512]{1,0:T(8,128)(4,1)} %iota_compare_fusion, bf16[2,512,4,128]{3,1,0,2:T(8,128)(2,1)} %bitcast.201, bf16[2,512,4,16]{1,0,3,2:T(2,128)(2,1)} %reshape_reshape.45, bf16[2,512,4,16]{1,0,3,2:T(2,128)(2,1)S(1)} %copy-done.7), kind=kOutput, calls=%fused_computation.5 | convolution fusion | flops 618659840 | bytes 3670016 | tf_op jit(solution)/shard_map/nhrs,nshv->nrhv/dot_general | solution.py:81
  123.2 2.6 %fusion.111 = (f32[4,153,128]{2,1,0:T(8,128)}, f32[2,4,153,128]{3,2,1,0:T(8,128)S(1)}) fusion(bf16[2,512,4,128]{3,1,0,2:T(8,128)(2,1)S(1)} %bitcast.202, bf16[2,512,4,153]{1,0,3,2:T(2,128)(2,1)} %reshape.236), kind=kOutput, calls=%fused_computation.159 | convolution fusion | flops 160510464 | bytes 3241984 | tf_op jit(solution)/shard_map/nrhf,nrhv->nhfv/dot_general | solution.py:48
  129.1 2.0 fusion.109
  134.1 2.4 %fusion.29 = f32[16,64,4,128]{3,1,2,0:T(8,128)S(1)} fusion(f32[16,4,64,128]{3,2,1,0:T(8,128)} %get-tuple-element.18, f32[16,4,64]{2,1,0:T(4,128)S(1)} %get-tuple-element.17, bf16[16,64,4,128]{3,1,0,2:T(8,128)(2,1)S(1)} %bitcast.203, bf16[16,64,4,128]{3,1,0,2:T(8,128)(2,1)} %bitcast.205), kind=kOutput, calls=%fused_computation.48 | convolution fusion | flops 139460608 | bytes 6307840 | tf_op jit(solution)/shard_map/chrp,cphv->crhv/dot_general | solution.py:122
  145.9 3.3 %fusion.112 = (f32[16,4,64]{2,1,0:T(4,128)S(1)}, f32[16,4,64,128]{3,2,1,0:T(8,128)S(1)}) fusion(f32[16,4,128,64]{2,3,1,0:T(8,128)S(1)} %fusion.66, pred[16,64,128]{2,1,0:T(8,128)(4,1)S(1)} %copy-done.27), kind=kOutput, calls=%fused_computation.160 | output fusion | flops 3145855 | bytes 4341760 | tf_op jit(solution)/shard_map/sub | solution.py:120
  152.2 7.0 %all-gather.7.cloned.1.call-done = f32[16,153,128]{2,1,0:T(8,128)} async-done(((f32[4,153,128]{2,1,0:T(8,128)}), f32[16,153,128]{2,1,0:T(8,128)}) %all-gather.7.cloned.1.call-update) | async-done | bytes 1253392 | tf_op jit(solution)/shard_map/all_gather | solution.py:55
  159.2 3.0 %select_reduce_fusion.1 = (f32[4,153,128]{2,1,0:T(8,128)}, f32[4,153,128]{2,1,0:T(8,128)S(1)}) fusion(f32[4,4,153,128]{3,2,1,0:T(8,128)} %bitcast.196, pred[4]{0:T(512)(128)(4,1)S(1)} %iota_compare_fusion.5, f32[4,4,153,128]{3,2,1,0:T(8,128)} %bitcast.197), kind=kLoop, calls=%fused_computation.70 | loop fusion | flops 1096704 | bytes 3133444 | tf_op jit(solution)/shard_map/reduce_sum | solution.py:58
  162.2 2.4 %multiply_reduce_fusion = (f32[2,512,4]{1,2,0:T(4,128)S(1)}, f32[2,512,4,128]{3,1,2,0:T(8,128)S(1)}) fusion(bf16[2,512,4,136]{1,3,2,0:T(8,128)(2,1)S(1)} %copy-done.4, bf16[2,512,4,16]{1,3,2,0:T(8,128)(2,1)S(1)} %copy-done.23, bf16[153]{0:T(256)(128)(2,1)S(1)} %pad.33.clone, f32[1,4,153,128]{3,2,1,0:T(8,128)} %slice.115, ...), kind=kOutput, calls=%fused_computation.40 | convolution fusion | flops 166074368 | bytes 6082866 | tf_op jit(solution)/shard_map/nrhf,nhfv->nrhv/dot_general | solution.py:83
  167.6 3.5 %all-to-all-start.7 = ((bf16[1024,4,128]{2,1,0:T(4,128)(2,1)}), bf16[1024,4,128]{2,1,0:T(4,128)(2,1)S(1)}, u32[]{:S(2)}, u32[]{:S(2)}) async-start(bf16[1024,4,128]{2,1,0:T(4,128)(2,1)} %copy.181), calls=%async_computation.7 | async-start | bytes 2097152 | tf_op jit(solution)/shard_map/all_to_all | solution.py:156
  171.2 3.0 %multiply_reduce_fusion.1 = (f32[2,512,4]{1,2,0:T(4,128)S(1)}, f32[2,512,4,128]{3,1,2,0:T(8,128)S(1)}) fusion(bf16[2,512,4,136]{1,3,2,0:T(8,128)(2,1)S(1)} %copy-done.3, bf16[2,512,4,16]{1,3,2,0:T(8,128)(2,1)S(1)} %copy-done.22, bf16[153]{0:T(256)(128)(2,1)S(1)} %pad.33.clone, f32[1,4,153,128]{3,2,1,0:T(8,128)S(1)} %copy-done.13, ...), kind=kOutput, calls=%fused_computation.42 | convolution fusion | flops 166074368 | bytes 6082866 | tf_op jit(solution)/shard_map/nrhf,nhfv->nrhv/dot_general | solution.py:83
  178.5 7.0 %all-to-all-done.7 = bf16[1024,4,128]{2,1,0:T(4,128)(2,1)S(1)} async-done(((bf16[1024,4,128]{2,1,0:T(4,128)(2,1)}), bf16[1024,4,128]{2,1,0:T(4,128)(2,1)S(1)}, u32[]{:S(2)}, u32[]{:S(2)}) %all-to-all-start.7) | async-done | bytes 1048608 | tf_op jit(solution)/shard_map/all_to_all | solution.py:156
  185.5 3.5 %all-to-all-start.3 = ((bf16[1024,4,128]{2,1,0:T(4,128)(2,1)}), bf16[1024,4,128]{2,1,0:T(4,128)(2,1)S(1)}, u32[]{:S(2)}, u32[]{:S(2)}) async-start(bf16[1024,4,128]{2,1,0:T(4,128)(2,1)} %copy.154), calls=%async_computation.3 | async-start | bytes 2097152 | tf_op jit(solution)/shard_map/all_to_all | solution.py:156
  189.2 14.3 %all-to-all-done.3 = bf16[1024,4,128]{2,1,0:T(4,128)(2,1)S(1)} async-done(((bf16[1024,4,128]{2,1,0:T(4,128)(2,1)}), bf16[1024,4,128]{2,1,0:T(4,128)(2,1)S(1)}, u32[]{:S(2)}, u32[]{:S(2)}) %all-to-all-start.3) | async-done | bytes 1048608 | tf_op jit(solution)/shard_map/all_to_all | solution.py:156
  203.8 2.4 %copy.183 = bf16[256,4,2,4,128]{0,4,3,2,1:T(8,128)(2,1)} copy(bf16[256,4,2,4,128]{4,0,1,3,2:T(8,128)(2,1)S(1)} %pad_maximum_fusion.2) | data formatting | bytes 4194304 | tf_op jit(solution)/shard_map/stack | solution.py:158
  206.2 4.1 %copy.184 = bf16[256,4096]{1,0:T(8,128)(2,1)} copy(bf16[256,4096]{0,1:T(8,128)(2,1)} %bitcast.191) | data formatting | bytes 4194304 | tf_op jit(solution)/shard_map/reshape | solution.py:159
  (161 shorter events, 69.0 us)
Async XLA Ops:
  8.4 11.6 %all-to-all-start.5 = ((bf16[256,4,4,16]{0,3,2,1:T(8,128)(2,1)}), bf16[256,4,4,16]{0,3,2,1:T(8,128)(2,1)S(1)}, u32[]{:S(2)}, u32[]{:S(2)}) async-start(bf16[256,4,4,16]{0,3,2,1:T(8,128)(2,1)} %get-tuple-element.12), calls=%async_computation.5 | async-start | bytes 262144 | tf_op jit(solution)/shard_map/all_to_all | solution.py:144
  17.4 14.1 %copy-start.31 = (bf16[16,136,1]{1,0,2:T(8,128)(2,1)S(1)}, bf16[16,136,1]{1,0,2:T(8,128)(2,1)}, u32[]{:S(2)}) copy-start(bf16[16,136,1]{1,0,2:T(8,128)(2,1)} %constant.58) | copy-start | bytes 13060
  20.0 8.0 %all-to-all-start.1 = ((bf16[256,4,4,16]{0,3,2,1:T(8,128)(2,1)}), bf16[256,4,4,16]{0,3,2,1:T(8,128)(2,1)S(1)}, u32[]{:S(2)}, u32[]{:S(2)}) async-start(bf16[256,4,4,16]{0,3,2,1:T(8,128)(2,1)} %get-tuple-element.11), calls=%async_computation.1 | async-start | bytes 262144 | tf_op jit(solution)/shard_map/all_to_all | solution.py:144
  23.4 7.8 %copy-start.10 = (bf16[4,256,1,4,16]{1,0,4,3,2:T(4,128)(2,1)}, bf16[4,256,1,4,16]{1,0,4,3,2:T(4,128)(2,1)S(1)}, u32[]{:S(2)}) copy-start(bf16[4,256,1,4,16]{1,0,4,3,2:T(4,128)(2,1)S(1)} %copy.157) | copy-start | bytes 393220
  23.5 25.0 %copy-start.1 = (bf16[1024,4,16]{0,2,1:T(8,128)(2,1)}, bf16[1024,4,16]{0,2,1:T(8,128)(2,1)S(1)}, u32[]{:S(2)}) copy-start(bf16[1024,4,16]{0,2,1:T(8,128)(2,1)S(1)} %reshape.235) | copy-start | bytes 393220
  27.9 7.9 %all-to-all-start.4 = ((bf16[256,4,4,16]{0,3,2,1:T(8,128)(2,1)}), bf16[256,4,4,16]{0,3,2,1:T(8,128)(2,1)S(1)}, u32[]{:S(2)}, u32[]{:S(2)}) async-start(bf16[256,4,4,16]{0,3,2,1:T(8,128)(2,1)} %get-tuple-element.10), calls=%async_computation.4 | async-start | bytes 262144 | tf_op jit(solution)/shard_map/all_to_all | solution.py:144
  35.4 12.1 %copy-start.29 = (bf16[16,136,1,1]{1,0,3,2:T(8,128)(2,1)S(1)}, bf16[16,136,1,1]{1,0,3,2:T(8,128)(2,1)}, u32[]{:S(2)}) copy-start(bf16[16,136,1,1]{1,0,3,2:T(8,128)(2,1)} %constant.60) | copy-start | bytes 13060
  35.9 7.9 %all-to-all-start = ((bf16[256,4,4,16]{0,3,2,1:T(8,128)(2,1)}), bf16[256,4,4,16]{0,3,2,1:T(8,128)(2,1)S(1)}, u32[]{:S(2)}, u32[]{:S(2)}) async-start(bf16[256,4,4,16]{0,3,2,1:T(8,128)(2,1)} %get-tuple-element.9), calls=%async_computation | async-start | bytes 262144 | tf_op jit(solution)/shard_map/all_to_all | solution.py:144
  40.0 3.8 %copy-start.14 = (bf16[4,256,1,4,16]{1,0,4,3,2:T(4,128)(2,1)}, bf16[4,256,1,4,16]{1,0,4,3,2:T(4,128)(2,1)S(1)}, u32[]{:S(2)}) copy-start(bf16[4,256,1,4,16]{1,0,4,3,2:T(4,128)(2,1)S(1)} %copy.156) | copy-start | bytes 393220
  40.1 9.1 %copy-start.6 = (bf16[2,512,4,16]{1,0,3,2:T(2,128)(2,1)}, bf16[2,512,4,16]{1,0,3,2:T(2,128)(2,1)S(1)}, u32[]{:S(2)}) copy-start(bf16[2,512,4,16]{1,0,3,2:T(2,128)(2,1)S(1)} %reshape_reshape.44) | copy-start | bytes 393220
  43.8 18.0 %all-to-all-start.2 = ((bf16[256,4,4,128]{0,3,2,1:T(8,128)(2,1)}), bf16[256,4,4,128]{0,3,2,1:T(8,128)(2,1)S(1)}, u32[]{:S(2)}, u32[]{:S(2)}) async-start(bf16[256,4,4,128]{0,3,2,1:T(8,128)(2,1)} %get-tuple-element.7), calls=%async_computation.2 | async-start | bytes 2097152 | tf_op jit(solution)/shard_map/all_to_all | solution.py:144
  47.5 3.2 %copy-start.8 = (bf16[2,512,4,16]{1,0,3,2:T(2,128)(2,1)}, bf16[2,512,4,16]{1,0,3,2:T(2,128)(2,1)S(1)}, u32[]{:S(2)}) copy-start(bf16[2,512,4,16]{1,0,3,2:T(2,128)(2,1)S(1)} %reshape_reshape.38) | copy-start | bytes 393220
  61.7 33.8 %all-to-all-start.6 = ((bf16[256,4,4,128]{0,3,2,1:T(8,128)(2,1)}), bf16[256,4,4,128]{0,3,2,1:T(8,128)(2,1)S(1)}, u32[]{:S(2)}, u32[]{:S(2)}) async-start(bf16[256,4,4,128]{0,3,2,1:T(8,128)(2,1)} %get-tuple-element.8), calls=%async_computation.6 | async-start | bytes 2097152 | tf_op jit(solution)/shard_map/all_to_all | solution.py:144
  65.3 86.9 %all-gather.5.cloned.1.call-start = ((), (), s32[]{:S(2)}) async-start(), calls=%async_computation.8 | async-start | bytes 1638400 | tf_op jit(solution)/shard_map/all_gather | solution.py:55
  78.3 80.9 %all-gather.7.cloned.1.call-start = ((), (), s32[]{:S(2)}) async-start(), calls=%async_computation.9 | async-start | bytes 1638400 | tf_op jit(solution)/shard_map/all_gather | solution.py:55
  101.3 10.8 %copy-start.9 = (bf16[2,512,4,16]{1,0,3,2:T(2,128)(2,1)S(1)}, bf16[2,512,4,16]{1,0,3,2:T(2,128)(2,1)}, u32[]{:S(2)}) copy-start(bf16[2,512,4,16]{1,0,3,2:T(2,128)(2,1)} %copy-done.8) | copy-start | bytes 393220
  102.0 25.3 %collective-permute-start.1 = (bf16[64,4,144]{0,2,1:T(8,128)(2,1)}, bf16[64,4,144]{0,2,1:T(8,128)(2,1)}, u32[]{:S(2)}, u32[]{:S(2)}) collective-permute-start(bf16[64,4,144]{0,2,1:T(8,128)(2,1)} %pad_maximum_fusion.7), channel_id=1, source_target_pairs={{0,4},{4,8},{8,12},{1,5},{5,9},{9,13},{2,6},{6,10},{10,14},{3,7},{... | collective-permute-start | bytes 221192 | tf_op jit(solution)/shard_map/ppermute | solution.py:22
  108.2 9.3 %copy-start.7 = (bf16[2,512,4,16]{1,0,3,2:T(2,128)(2,1)S(1)}, bf16[2,512,4,16]{1,0,3,2:T(2,128)(2,1)}, u32[]{:S(2)}) copy-start(bf16[2,512,4,16]{1,0,3,2:T(2,128)(2,1)} %copy-done.6) | copy-start | bytes 393220
  108.2 28.5 %collective-permute-start = (bf16[64,4,144]{0,2,1:T(8,128)(2,1)}, bf16[64,4,144]{0,2,1:T(8,128)(2,1)}, u32[]{:S(2)}, u32[]{:S(2)}) collective-permute-start(bf16[64,4,144]{0,2,1:T(8,128)(2,1)} %pad_maximum_fusion.8), channel_id=1, source_target_pairs={{0,4},{4,8},{8,12},{1,5},{5,9},{9,13},{2,6},{6,10},{10,14},{3,7},{... | collective-permute-start | bytes 221192 | tf_op jit(solution)/shard_map/ppermute | solution.py:22
  117.6 5.6 %copy-start.17 = (bf16[4,256,1,4,128]{4,1,0,3,2:T(8,128)(2,1)S(1)}, bf16[4,256,1,4,128]{4,1,0,3,2:T(8,128)(2,1)}, u32[]{:S(2)}) copy-start(bf16[4,256,1,4,128]{4,1,0,3,2:T(8,128)(2,1)} %copy.160) | copy-start | bytes 3145732
  123.2 3.3 %copy-start.25 = (f32[2,4,153,128]{3,2,1,0:T(8,128)S(1)}, f32[2,4,153,128]{3,2,1,0:T(8,128)}, u32[]{:S(2)}) copy-start(f32[2,4,153,128]{3,2,1,0:T(8,128)} %get-tuple-element.20) | copy-start | bytes 1880068
  141.1 3.2 %copy-start.19 = (bf16[16,64,4,16]{1,0,3,2:T(8,128)(2,1)S(1)}, bf16[16,64,4,16]{1,0,3,2:T(8,128)(2,1)}, u32[]{:S(2)}) copy-start(bf16[16,64,4,16]{1,0,3,2:T(8,128)(2,1)} %reshape_reshape.43) | copy-start | bytes 393220
  142.6 3.3 %copy-start.27 = (pred[16,64,128]{2,1,0:T(8,128)(4,1)S(1)}, pred[16,64,128]{2,1,0:T(8,128)(4,1)}, u32[]{:S(2)}) copy-start(pred[16,64,128]{2,1,0:T(8,128)(4,1)} %broadcast_and_fusion) | copy-start | bytes 393220
  145.9 3.4 %copy-start.16 = (bf16[4,256,1,4,128]{4,1,0,3,2:T(8,128)(2,1)S(1)}, bf16[4,256,1,4,128]{4,1,0,3,2:T(8,128)(2,1)}, u32[]{:S(2)}) copy-start(bf16[4,256,1,4,128]{4,1,0,3,2:T(8,128)(2,1)} %copy.133) | copy-start | bytes 3145732
  150.6 11.5 %copy-start.23 = (bf16[2,512,4,16]{1,3,2,0:T(8,128)(2,1)S(1)}, bf16[2,512,4,16]{1,3,2,0:T(8,128)(2,1)}, u32[]{:S(2)}) copy-start(bf16[2,512,4,16]{1,3,2,0:T(8,128)(2,1)} %multiply_convert_fusion.4) | copy-start | bytes 393220
  152.2 9.9 %copy-start.4 = (bf16[2,512,4,136]{1,3,2,0:T(8,128)(2,1)S(1)}, bf16[2,512,4,136]{1,3,2,0:T(8,128)(2,1)}, u32[]{:S(2)}) copy-start(bf16[2,512,4,136]{1,3,2,0:T(8,128)(2,1)} %fusion.37) | copy-start | bytes 3342340
  165.8 5.4 %copy-start.3 = (bf16[2,512,4,136]{1,3,2,0:T(8,128)(2,1)S(1)}, bf16[2,512,4,136]{1,3,2,0:T(8,128)(2,1)}, u32[]{:S(2)}) copy-start(bf16[2,512,4,136]{1,3,2,0:T(8,128)(2,1)} %fusion.34) | copy-start | bytes 3342340
  165.8 5.4 %copy-start.5 = (f32[4,153,128]{2,1,0:T(8,128)S(1)}, f32[4,153,128]{2,1,0:T(8,128)}, u32[]{:S(2)}) copy-start(f32[4,153,128]{2,1,0:T(8,128)} %get-tuple-element.5) | copy-start | bytes 940036
  165.8 5.4 %copy-start.13 = (f32[1,4,153,128]{3,2,1,0:T(8,128)S(1)}, f32[1,4,153,128]{3,2,1,0:T(8,128)}, u32[]{:S(2)}) copy-start(f32[1,4,153,128]{3,2,1,0:T(8,128)} %slice.107) | copy-start | bytes 940036
  165.8 5.4 %copy-start.22 = (bf16[2,512,4,16]{1,3,2,0:T(8,128)(2,1)S(1)}, bf16[2,512,4,16]{1,3,2,0:T(8,128)(2,1)}, u32[]{:S(2)}) copy-start(bf16[2,512,4,16]{1,3,2,0:T(8,128)(2,1)} %multiply_convert_fusion.6) | copy-start | bytes 393220
  167.6 18.0 %all-to-all-start.7 = ((bf16[1024,4,128]{2,1,0:T(4,128)(2,1)}), bf16[1024,4,128]{2,1,0:T(4,128)(2,1)S(1)}, u32[]{:S(2)}, u32[]{:S(2)}) async-start(bf16[1024,4,128]{2,1,0:T(4,128)(2,1)} %copy.181), calls=%async_computation.7 | async-start | bytes 2097152 | tf_op jit(solution)/shard_map/all_to_all | solution.py:156
  185.5 18.0 %all-to-all-start.3 = ((bf16[1024,4,128]{2,1,0:T(4,128)(2,1)}), bf16[1024,4,128]{2,1,0:T(4,128)(2,1)S(1)}, u32[]{:S(2)}, u32[]{:S(2)}) async-start(bf16[1024,4,128]{2,1,0:T(4,128)(2,1)} %copy.154), calls=%async_computation.3 | async-start | bytes 2097152 | tf_op jit(solution)/shard_map/all_to_all | solution.py:156
  (14 other events, 26.3 us)
Sparse Core Ops, SparseCore 0:
  78.4 34.9 all-gather.4
  127.4 31.7 all-gather.6

commit v5 on v2

--- a/solution.py
+++ b/solution.py
@@ -4,6 +4,8 @@
 import numpy as np
 import jax.numpy as jnp
 from jax import lax
+from jax.experimental import pallas as pl
+from jax.experimental.pallas import tpu as pltpu
 from jax.sharding import PartitionSpec as P
 
 HEADS = 32
@@ -35,6 +37,71 @@
     unit = jnp.ones(lead + (1,), jnp.bfloat16)
     half = (vector.astype(jnp.float32) * 0.5).astype(jnp.bfloat16)
     return jnp.concatenate([unit, half, prod], axis=-1)
+
+
+CHUNK = 128
+
+
+def local_attention_kernel(flag_ref, q_ref, kx_ref, vx_ref, intra_ref, win_ref, *, span_rows, block_rows):
+    first_span = flag_ref[0] == 1
+    for i in range(span_rows // CHUNK):
+        r0 = i * CHUNK
+        q_c = q_ref[0, r0 : r0 + CHUNK, :]
+        bs = (r0 // block_rows) * block_rows
+        width = r0 + CHUNK - bs
+        k_i = kx_ref[0, WINDOW + bs : WINDOW + r0 + CHUNK, :]
+        v_i = vx_ref[WINDOW + bs : WINDOW + r0 + CHUNK, :]
+        scores = (
+            lax.dot_general(q_c, k_i, (((1,), (1,)), ((), ())), preferred_element_type=jnp.float32)
+            * 0.25
+        )
+        row = lax.broadcasted_iota(jnp.int32, (CHUNK, width), 0)
+        col = lax.broadcasted_iota(jnp.int32, (CHUNK, width), 1)
+        kernel = jnp.where(
+            col <= row + (r0 - bs), 1.0 + scores + 0.5 * scores * scores, 0.0
+        ).astype(jnp.bfloat16)
+        intra_ref[r0 : r0 + CHUNK, :] = jnp.dot(kernel, v_i, preferred_element_type=jnp.float32)
+
+        k_w = kx_ref[0, r0 : r0 + CHUNK + WINDOW, :]
+        v_w = vx_ref[r0 : r0 + CHUNK + WINDOW, :]
+        ws = (
+            lax.dot_general(q_c, k_w, (((1,), (1,)), ((), ())), preferred_element_type=jnp.float32)
+            * 0.25
+        )
+        wrow = lax.broadcasted_iota(jnp.int32, (CHUNK, CHUNK + WINDOW), 0)
+        wcol = lax.broadcasted_iota(jnp.int32, (CHUNK, CHUNK + WINDOW), 1)
+        valid = (wcol > wrow) & (wcol <= wrow + WINDOW)
+        if i == 0:
+            valid = valid & ((wcol >= WINDOW) | jnp.logical_not(first_span))
+        masked = jnp.where(valid, ws, -jnp.inf)
+        highest = jnp.max(masked, axis=1, keepdims=True)
+        expo = jnp.where(valid, jnp.exp(ws - highest), 0.0)
+        weights = (expo / jnp.sum(expo, axis=1, keepdims=True)).astype(jnp.bfloat16)
+        win_ref[r0 : r0 + CHUNK, :] = jnp.dot(weights, v_w, preferred_element_type=jnp.float32)
+
+
+def local_attention(flag, q_hm, kx_hm, vx, block_rows):
+    heads_here, span_rows, _ = q_hm.shape
+    ext = kx_hm.shape[1]
+    body = lambda *refs: local_attention_kernel(*refs, span_rows=span_rows, block_rows=block_rows)
+    out = jax.ShapeDtypeStruct((span_rows, heads_here * VD), jnp.float32)
+    return pl.pallas_call(
+        body,
+        grid_spec=pltpu.PrefetchScalarGridSpec(
+            num_scalar_prefetch=1,
+            grid=(heads_here,),
+            in_specs=[
+                pl.BlockSpec((1, span_rows, KD), lambda h, f: (h, 0, 0)),
+                pl.BlockSpec((1, ext, KD), lambda h, f: (h, 0, 0)),
+                pl.BlockSpec((ext, VD), lambda h, f: (0, h)),
+            ],
+            out_specs=[
+                pl.BlockSpec((span_rows, VD), lambda h, f: (0, h)),
+                pl.BlockSpec((span_rows, VD), lambda h, f: (0, h)),
+            ],
+        ),
+        out_shape=(out, out),
+    )(flag, q_hm, kx_hm, vx)
 
 
 def per_device(queries, keys, values, gain):
@@ -77,59 +144,24 @@
     states = (before + entering[None]).astype(jnp.bfloat16)
 
     query_blocks = query_head.reshape(block_count, block_rows, heads_here, KD)
-    key_blocks = key_head.reshape(block_count, block_rows, heads_here, KD)
-    value_blocks = value_head.reshape(block_count, block_rows, heads_here, VD)
-    scores = (
-        jnp.einsum("nrhd,nshd->nhrs", query_blocks, key_blocks, preferred_element_type=jnp.float32)
-        * 0.25
-    )
-    row_pos = jnp.arange(block_rows)[:, None]
-    col_pos = jnp.arange(block_rows)[None, :]
-    kernel = jnp.where(col_pos <= row_pos, 1.0 + scores + 0.5 * scores * scores, 0.0).astype(
-        jnp.bfloat16
-    )
-    intra = jnp.einsum("nhrs,nshv->nrhv", kernel, value_blocks, preferred_element_type=jnp.float32)
     query_feat = unique_features(query_blocks, True)
     inter = jnp.einsum("nrhf,nhfv->nrhv", query_feat, states, preferred_element_type=jnp.float32)
-    linear = (intra + inter).reshape(span_rows, heads_here, VD)
 
-    tail_keys, tail_values = shifted(
-        (key_head[span_rows - WINDOW :], value_head[span_rows - WINDOW :]), "ctx", 1
+    tails = shifted(
+        jnp.concatenate([key_head, value_head], axis=2)[span_rows - WINDOW :], "ctx", 1
     )
-    chunks = span_rows // WINDOW
-    key_prev = jnp.concatenate([tail_keys, key_head[: span_rows - WINDOW]], axis=0)
-    value_prev = jnp.concatenate([tail_values, value_head[: span_rows - WINDOW]], axis=0)
-    key_win = jnp.concatenate(
-        [
-            key_prev.reshape(chunks, WINDOW, heads_here, KD),
-            key_head.reshape(chunks, WINDOW, heads_here, KD),
-        ],
-        axis=1,
+    key_ext = jnp.concatenate([tails[:, :, :KD], key_head], axis=0)
+    value_ext = jnp.concatenate([tails[:, :, KD:], value_head], axis=0)
+    flag = first_span.astype(jnp.int32).reshape(1)
+    intra, window = local_attention(
+        flag,
+        jnp.transpose(query_head, (1, 0, 2)),
+        jnp.transpose(key_ext, (1, 0, 2)),
+        value_ext.reshape(span_rows + WINDOW, heads_here * VD),
+        block_rows,
     )
-    value_win = jnp.concatenate(
-        [
-            value_prev.reshape(chunks, WINDOW, heads_here, VD),
-            value_head.reshape(chunks, WINDOW, heads_here, VD),
-        ],
-        axis=1,
-    )
-    query_chunks = query_head.reshape(chunks, WINDOW, heads_here, KD)
-    window_scores = (
-        jnp.einsum("crhd,cphd->chrp", query_chunks, key_win, preferred_element_type=jnp.float32)
-        * 0.25
-    )
-    r_pos = jnp.arange(WINDOW)[:, None]
-    p_pos = jnp.arange(2 * WINDOW)[None, :]
-    chunk_pos = jnp.arange(chunks)[:, None, None, None]
-    valid = (p_pos > r_pos) & (p_pos <= r_pos + WINDOW)
-    valid = valid[None, None] & ((chunk_pos > 0) | (p_pos >= WINDOW) | jnp.logical_not(first_span))
-    masked = jnp.where(valid, window_scores, -jnp.inf)
-    highest_score = jnp.max(masked, axis=3, keepdims=True)
-    expo = jnp.where(valid, jnp.exp(window_scores - highest_score), 0.0)
-    weights = (expo / jnp.sum(expo, axis=3, keepdims=True)).astype(jnp.bfloat16)
-    window = jnp.einsum(
-        "chrp,cphv->crhv", weights, value_win, preferred_element_type=jnp.float32
-    ).reshape(span_rows, heads_here, VD)
+    linear = intra.reshape(span_rows, heads_here, VD) + inter.reshape(span_rows, heads_here, VD)
+    window = window.reshape(span_rows, heads_here, VD)
 
     scale = lax.rsqrt(jnp.mean(linear * linear, axis=2, keepdims=True) + epsilon)
     gains = gain.reshape(heads_here, VD)

time: 174 us -> 196 us (1.13)
  the two profiles are of different devices: /device:TPU:0 before, /device:TPU:20 now
where the time goes in v5:
time: 196 us
  local copies, waits for them, and re-layouts  42.4 us (22%)
  waiting for transfers between devices  34.1 us (17%)
  Pallas kernels  31.4 us (16%)
  blocking collectives  28.2 us (14%)
  other arithmetic  19.5 us (10%)
  starting transfers between devices  15.1 us (8%)
  between operations  13.7 us (7%)
  matrix products  11.1 us (6%)
    pallas_call x1, Pallas kernels, local_attention(): pl.pallas_call(body, grid_spec=pltpu.PrefetchScalarGridSpec(num_scalar_pr...  31.4 us
    all_to_all x1, blocking collectives, per_device(): lax.all_to_all(mixed, 'head', split_axis=0, concat_axis=1, tiled=True)  28.2 us
    unnamed x35, local copies, waits for them, and re-layouts  19.2 us
    ppermute x1, waiting for transfers between devices, shifted(): return lax.ppermute(shard, axis, pairs)  17.4 us
    all_to_all x1, waiting for transfers between devices, per_device(): lax.all_to_all(value_tok, 'head', split_axis=1, concat_axis=0, tiled=True)  10.7 us
    all_to_all x1, waiting for transfers between devices, per_device(): lax.all_to_all(query_tok, 'head', split_axis=1, concat_axis=0, tiled=True)  5.98 us
    transpose x1, local copies, waits for them, and re-layouts, per_device(): jnp.einsum('nrhf,nhfv->nrhv', query_feat, states, preferred_element_type=...  5.29 us
    reshape x1, local copies, waits for them, and re-layouts, per_device(): key_feat.reshape(block_count, block_rows, heads_here, feat)  4.59 us
  transfers between devices with their start and end apart: 5, of which 3 were waited for; matrix products, arithmetic and copies ran while one was open for 20% of the time, Pallas kernels for 16%

profile of v5, /device:TPU:20, one launch (start us, length us, event | category | flops | bytes accessed | tf_op | source)
XLA Modules:
  0.0 195.6 jit_solution(15510792635633435998)
XLA Ops:
  6.5 1.8 copy.154
  8.3 3.4 %all-to-all-start.1 = ((bf16[256,32,16]{0,2,1:T(8,128)(2,1)}), bf16[256,32,16]{0,2,1:T(8,128)(2,1)S(1)}, u32[]{:S(2)}, u32[]{:S(2)}) async-start(bf16[256,32,16]{0,2,1:T(8,128)(2,1)} %bitcast.6), calls=%async_computation.1 | async-start | bytes 524288 | tf_op jit(solution)/shard_map/all_to_all | solution.py:114
  11.7 3.3 %copy.156 = bf16[256,4096]{0,1:T(8,128)(2,1)S(1)} copy(bf16[256,4096]{1,0:T(8,128)(2,1)} %param.11) | data formatting | bytes 4194304 | tf_op args[2]
  15.0 2.9 %copy.157 = bf16[256,32,128]{2,0,1:T(8,128)(2,1)} copy(bf16[256,32,128]{0,2,1:T(8,128)(2,1)S(1)} %bitcast.95) | data formatting | bytes 4194304 | tf_op jit(solution)/shard_map/reshape | solution.py:111
  17.9 4.5 %all-to-all-start.2 = ((bf16[256,32,128]{2,0,1:T(8,128)(2,1)}), bf16[256,32,128]{2,0,1:T(8,128)(2,1)}, u32[]{:S(2)}, u32[]{:S(2)}) async-start(bf16[256,32,128]{2,0,1:T(8,128)(2,1)} %copy.157), calls=%async_computation.2 | async-start | bytes 4194304 | tf_op jit(solution)/shard_map/all_to_all | solution.py:115
  23.5 1.9 convert_multiply_fusion
  25.4 1.8 copy.163
  28.8 1.5 fusion.9
  30.3 2.5 %pad_maximum_fusion = bf16[1024,8,153]{0,2,1:T(8,128)(2,1)} fusion(bf16[1024,8,136]{0,2,1:T(8,128)(2,1)S(1)} %fusion.9, bf16[1024,8,16]{0,2,1:T(8,128)(2,1)S(1)} %copy.163, bf16[153]{0:T(256)(128)(2,1)S(1)} %pad.4.clone), kind=kLoop, calls=%fused_computation.7 | loop fusion | flops 7520256 | bytes 4997426 | tf_op jit(solution)/shard_map/concatenate | solution.py:39
  32.8 4.6 %reshape.76 = bf16[2,512,8,153]{1,0,3,2:T(2,128)(2,1)} reshape(bf16[1024,8,153]{0,2,1:T(8,128)(2,1)} %pad_maximum_fusion) | data formatting | bytes 5013504 | tf_op jit(solution)/shard_map/reshape | solution.py:127
  37.4 10.7 %all-to-all-done.2 = bf16[256,32,128]{2,0,1:T(8,128)(2,1)} async-done(((bf16[256,32,128]{2,0,1:T(8,128)(2,1)}), bf16[256,32,128]{2,0,1:T(8,128)(2,1)}, u32[]{:S(2)}, u32[]{:S(2)}) %all-to-all-start.2) | async-done | bytes 2097184 | tf_op jit(solution)/shard_map/all_to_all | solution.py:115
  48.1 3.1 %copy.159 = bf16[4,256,8,128]{3,2,1,0:T(8,128)(2,1)S(1)} copy(bf16[4,256,8,128]{3,1,2,0:T(8,128)(2,1)} %bitcast.13) | data formatting | bytes 4194304 | tf_op jit(solution)/shard_map/all_to_all | solution.py:115
  51.3 2.1 %fusion.23 = (f32[8,153,128]{2,1,0:T(8,128)S(1)}, f32[2,8,153,128]{3,2,1,0:T(8,128)}) fusion(bf16[2,512,8,128]{3,2,1,0:T(8,128)(2,1)S(1)} %bitcast.88, bf16[2,512,8,153]{1,0,3,2:T(2,128)(2,1)S(1)} %copy-done.5), kind=kOutput, calls=%fused_computation.40 | convolution fusion | flops 321020928 | bytes 6483968 | tf_op jit(solution)/shard_map/nrhf,nrhv->nhfv/dot_general | solution.py:125
  55.4 3.4 %all-to-all-start = ((bf16[256,32,16]{0,2,1:T(8,128)(2,1)}), bf16[256,32,16]{0,2,1:T(8,128)(2,1)S(1)}, u32[]{:S(2)}, u32[]{:S(2)}) async-start(bf16[256,32,16]{0,2,1:T(8,128)(2,1)} %bitcast.1), calls=%async_computation | async-start | bytes 524288 | tf_op jit(solution)/shard_map/all_to_all | solution.py:113
  58.9 6.0 %all-to-all-done = bf16[256,32,16]{0,2,1:T(8,128)(2,1)S(1)} async-done(((bf16[256,32,16]{0,2,1:T(8,128)(2,1)}), bf16[256,32,16]{0,2,1:T(8,128)(2,1)S(1)}, u32[]{:S(2)}, u32[]{:S(2)}) %all-to-all-start) | async-done | bytes 262176 | tf_op jit(solution)/shard_map/all_to_all | solution.py:113
  65.0 1.7 copy.153
  67.7 2.1 %fusion.11 = bf16[2,512,8,136]{1,3,2,0:T(8,128)(2,1)} fusion(f32[136,2,512,8]{2,0,3,1:T(8,128)S(1)} %fusion.19, bf16[16,136,1,1]{1,0,3,2:T(8,128)(2,1)S(1)} %copy-done.8, bf16[136]{0:T(256)(128)(2,1)S(1)} %copy-done.13, bf16[2,512,8,16]{1,0,3,2:T(2,128)(2,1)S(1)} %reshape.65), kind=kOutput, calls=%fused_computation.19 | convolution fusion | flops 40108032 | bytes 6951440 | tf_op jit(solution)/shard_map/...d,df->...f/dot_general | solution.py:32
  70.3 3.8 %collective-permute-start = (bf16[64,8,144]{2,0,1:T(8,128)(2,1)S(1)}, bf16[64,8,144]{2,0,1:T(8,128)(2,1)S(1)}, u32[]{:S(2)}, u32[]{:S(2)}) collective-permute-start(bf16[64,8,144]{2,0,1:T(8,128)(2,1)S(1)} %pad_maximum_fusion.2), channel_id=1, source_target_pairs={{0,4},{4,8},{8,12},{1,5},{5,9},{9,13},{2,6},{6,10},{10,14},{3,7},{... | collective-permute-start | bytes 442376 | tf_op jit(solution)/shard_map/ppermute | solution.py:24
  74.8 17.4 %collective-permute-done = bf16[64,8,144]{2,0,1:T(8,128)(2,1)S(1)} collective-permute-done((bf16[64,8,144]{2,0,1:T(8,128)(2,1)S(1)}, bf16[64,8,144]{2,0,1:T(8,128)(2,1)S(1)}, u32[]{:S(2)}, u32[]{:S(2)}) %collective-permute-start) | collective-permute-done | bytes 147488 | tf_op jit(solution)/shard_map/ppermute | solution.py:24
  92.4 1.8 maximum_bitcast_fusion.refs_2_
  94.2 1.6 pad_maximum_fusion.1.refs_3_
  95.8 31.4 %shard_map.91 = (f32[1024,1024]{1,0:T(8,128)}, f32[1024,1024]{1,0:T(8,128)}) custom-call(s32[1]{0:T(128)} %bitcast.refs_0_, bf16[8,1024,16]{2,1,0:T(8,128)(2,1)} %bitcast.91, bf16[8,1088,16]{2,1,0:T(8,128)(2,1)} %maximum_bitcast_fusion.refs_2_, bf16[1088,1024]{1,0:T(8,128)(2,1)} %pad_maximum_fusion.1.refs_3_), custom_call_target="tpu_custom_call" | custom-call | tf_op jit(solution)/shard_map/pallas_call | solution.py:88
  127.2 5.3 %copy.191 = f32[128,8,8,128]{3,2,1,0:T(8,128)} copy(f32[128,8,8,128]{3,1,2,0:T(8,128)} %bitcast.97) | data formatting | bytes 8388608
  132.6 3.0 %copy.192 = f32[128,8,8,128]{3,2,1,0:T(8,128)} copy(f32[128,8,8,128]{3,1,2,0:T(8,128)S(1)} %bitcast.96) | data formatting | bytes 8388608
  135.5 2.4 %fusion.8 = f32[8,153,128]{2,0,1:T(8,128)S(1)} fusion(f32[32,153,128]{2,0,1:T(8,128)} %all-gather.3.cloned.1.call-done, pred[4]{0:T(512)(128)(4,1)S(1)} %iota_compare_fusion), kind=kLoop, calls=%fused_computation.16 | loop fusion | flops 1096704 | bytes 3133444 | tf_op jit(solution)/shard_map/reduce_sum | solution.py:135
  138.0 3.1 %fusion.12 = f32[2,512,8,128]{1,3,2,0:T(8,128)} fusion(bf16[2,512,8,136]{1,3,2,0:T(8,128)(2,1)S(1)} %copy-done.3, bf16[2,512,8,16]{1,3,2,0:T(8,128)(2,1)S(1)} %multiply_convert_fusion.2, bf16[153]{0:T(256)(128)(2,1)S(1)} %pad.4.clone, f32[1,8,153,128]{3,2,1,0:T(8,128)S(1)} %slice.18, f32[8,153,128]{2,1,0:T(8,128)S(1)} %copy.171), kind=kOutput, calls=%fused_computation.22 | convolution fusion | flops 329011200 | bytes 7938354 | tf_op jit(solution)/shard_map/nrhf,nhfv->nrhv/dot_general | solution.py:148
  141.1 5.3 %copy.176 = f32[2,512,8,128]{3,2,1,0:T(8,128)} copy(f32[2,512,8,128]{1,3,2,0:T(8,128)} %fusion.12) | data formatting | bytes 8388608 | tf_op jit(solution)/shard_map/nrhf,nhfv->nrhv/transpose | solution.py:148
  146.4 3.9 %bitcast_add_fusion.1 = f32[1024,8,128]{2,1,0:T(8,128)S(1)} fusion(f32[128,8,8,128]{3,2,1,0:T(8,128)} %copy.191, f32[2,512,8,128]{3,2,1,0:T(8,128)} %copy.176), kind=kLoop, calls=%fused_computation.4 | loop fusion | flops 1048576 | bytes 12582912 | tf_op jit(solution)/shard_map/add | solution.py:163
  150.3 2.0 %copy-done = f32[1024,8,128]{2,1,0:T(8,128)} copy-done((f32[1024,8,128]{2,1,0:T(8,128)}, f32[1024,8,128]{2,1,0:T(8,128)S(1)}, u32[]{:S(2)}) %copy-start) | copy-done | bytes 4194328
  153.8 4.1 %fusion = bf16[1024,8,128]{2,1,0:T(8,128)(2,1)S(1)} fusion(f32[128,8,8,128]{3,2,1,0:T(8,128)} %copy.192, f32[1024,8,128]{2,1,0:T(8,128)} %copy-done, f32[8,128]{1,0:T(8,128)S(1)} %bitcast.101, f32[1024,8]{1,0:T(8,128)S(1)} %copy.178), kind=kLoop, calls=%fused_computation.3 | loop fusion | flops 4194304 | bytes 10522624 | tf_op jit(solution)/shard_map/convert_element_type | solution.py:168
  158.0 28.2 %all_to_all.69 = bf16[1024,8,128]{2,1,0:T(8,128)(2,1)S(1)} all-to-all(bf16[1024,8,128]{2,1,0:T(8,128)(2,1)S(1)} %fusion), channel_id=1, replica_groups=mesh['groups'=2,'ctx'=4,'head'=4] {'head'}, dimensions={0} | all-to-all | bytes 4194304 | tf_op jit(solution)/shard_map/all_to_all | solution.py:169
  186.5 2.3 %copy.210 = bf16[32,8,32,128]{3,1,2,0:T(8,128)(2,1)} copy(bf16[32,8,32,128]{3,2,1,0:T(8,128)(2,1)S(1)} %bitcast.94) | data formatting | bytes 4194304
  (53 shorter events, 9.1 us)
Async XLA Ops:
  8.3 9.6 %all-to-all-start.1 = ((bf16[256,32,16]{0,2,1:T(8,128)(2,1)}), bf16[256,32,16]{0,2,1:T(8,128)(2,1)S(1)}, u32[]{:S(2)}, u32[]{:S(2)}) async-start(bf16[256,32,16]{0,2,1:T(8,128)(2,1)} %bitcast.6), calls=%async_computation.1 | async-start | bytes 524288 | tf_op jit(solution)/shard_map/all_to_all | solution.py:114
  17.9 30.3 %all-to-all-start.2 = ((bf16[256,32,128]{2,0,1:T(8,128)(2,1)}), bf16[256,32,128]{2,0,1:T(8,128)(2,1)}, u32[]{:S(2)}, u32[]{:S(2)}) async-start(bf16[256,32,128]{2,0,1:T(8,128)(2,1)} %copy.157), calls=%async_computation.2 | async-start | bytes 4194304 | tf_op jit(solution)/shard_map/all_to_all | solution.py:115
  22.4 113.2 %all-gather.3.cloned.1.call-start = ((), (), s32[]{:S(2)}) async-start(), calls=%async_computation.4 | async-start | bytes 3133440 | tf_op jit(solution)/shard_map/all_gather | solution.py:132
  23.5 3.7 %copy-start.11 = (bf16[16,136,1]{1,0,2:T(8,128)(2,1)S(1)}, bf16[16,136,1]{1,0,2:T(8,128)(2,1)}, u32[]{:S(2)}) copy-start(bf16[16,136,1]{1,0,2:T(8,128)(2,1)} %constant.39) | copy-start | bytes 13060
  27.2 1.5 copy-start.10
  48.1 3.1 %copy-start.5 = (bf16[2,512,8,153]{1,0,3,2:T(2,128)(2,1)S(1)}, bf16[2,512,8,153]{1,0,3,2:T(2,128)(2,1)}, u32[]{:S(2)}) copy-start(bf16[2,512,8,153]{1,0,3,2:T(2,128)(2,1)} %reshape.76) | copy-start | bytes 7520260
  51.2 2.1 %copy-start.1 = (bf16[4,256,8,128]{3,2,1,0:T(8,128)(2,1)}, bf16[4,256,8,128]{3,2,1,0:T(8,128)(2,1)S(1)}, u32[]{:S(2)}) copy-start(bf16[4,256,8,128]{3,2,1,0:T(8,128)(2,1)S(1)} %copy.159) | copy-start | bytes 6291460
  51.2 3.3 %copy-start.7 = (bf16[256,512]{1,0:T(8,128)(2,1)S(1)}, bf16[256,512]{1,0:T(8,128)(2,1)}, u32[]{:S(2)}) copy-start(bf16[256,512]{1,0:T(8,128)(2,1)} %param.9) | copy-start | bytes 786436
  54.5 12.4 %copy-start.9 = (bf16[16,136,1,1]{1,0,3,2:T(8,128)(2,1)S(1)}, bf16[16,136,1,1]{1,0,3,2:T(8,128)(2,1)}, u32[]{:S(2)}) copy-start(bf16[16,136,1,1]{1,0,3,2:T(8,128)(2,1)} %constant.41) | copy-start | bytes 13060
  55.4 9.4 %all-to-all-start = ((bf16[256,32,16]{0,2,1:T(8,128)(2,1)}), bf16[256,32,16]{0,2,1:T(8,128)(2,1)S(1)}, u32[]{:S(2)}, u32[]{:S(2)}) async-start(bf16[256,32,16]{0,2,1:T(8,128)(2,1)} %bitcast.1), calls=%async_computation | async-start | bytes 524288 | tf_op jit(solution)/shard_map/all_to_all | solution.py:113
  66.8 0.9 copy-start.8
  66.8 1.0 copy-start.13
  67.7 2.1 %copy-start.2 = (bf16[4,256,8,128]{3,2,1,0:T(8,128)(2,1)S(1)}, bf16[4,256,8,128]{3,2,1,0:T(8,128)(2,1)}, u32[]{:S(2)}) copy-start(bf16[4,256,8,128]{3,2,1,0:T(8,128)(2,1)} %copy-done.1) | copy-start | bytes 6291460
  70.1 4.0 %copy-start.6 = (f32[2,8,153,128]{3,2,1,0:T(8,128)S(1)}, f32[2,8,153,128]{3,2,1,0:T(8,128)}, u32[]{:S(2)}) copy-start(f32[2,8,153,128]{3,2,1,0:T(8,128)} %get-tuple-element.10) | copy-start | bytes 3760132
  70.3 22.0 %collective-permute-start = (bf16[64,8,144]{2,0,1:T(8,128)(2,1)S(1)}, bf16[64,8,144]{2,0,1:T(8,128)(2,1)S(1)}, u32[]{:S(2)}, u32[]{:S(2)}) collective-permute-start(bf16[64,8,144]{2,0,1:T(8,128)(2,1)S(1)} %pad_maximum_fusion.2), channel_id=1, source_target_pairs={{0,4},{4,8},{8,12},{1,5},{5,9},{9,13},{2,6},{6,10},{10,14},{3,7},{... | collective-permute-start | bytes 442376 | tf_op jit(solution)/shard_map/ppermute | solution.py:24
  127.2 5.3 %copy-start.4 = (f32[1024,1024]{1,0:T(8,128)S(1)}, f32[1024,1024]{1,0:T(8,128)}, u32[]{:S(2)}) copy-start(f32[1024,1024]{1,0:T(8,128)} %get-tuple-element.8) | copy-start | bytes 12582916
  135.5 2.5 %copy-start.3 = (bf16[2,512,8,136]{1,3,2,0:T(8,128)(2,1)S(1)}, bf16[2,512,8,136]{1,3,2,0:T(8,128)(2,1)}, u32[]{:S(2)}) copy-start(bf16[2,512,8,136]{1,3,2,0:T(8,128)(2,1)} %fusion.11) | copy-start | bytes 6684676
  150.3 2.0 %copy-start = (f32[1024,8,128]{2,1,0:T(8,128)}, f32[1024,8,128]{2,1,0:T(8,128)S(1)}, u32[]{:S(2)}) copy-start(f32[1024,8,128]{2,1,0:T(8,128)S(1)} %bitcast_add_fusion.1) | copy-start | bytes 12582916
  152.3 1.6 copy-start.12
Sparse Core Ops, SparseCore 0:
  54.7 53.9 all-gather.2

commit v6 on v5

v6 whole, which is shorter than its diff:
```python
import math

import jax
import numpy as np
import jax.numpy as jnp
from jax import lax
from jax.experimental import pallas as pl
from jax.experimental.pallas import tpu as pltpu
from jax.sharding import PartitionSpec as P

HEADS = 32
KD = 16
VD = 128
WINDOW = 64


outer_scale = 1.0 / (4.0 * math.sqrt(2.0))
epsilon = 1e-06


def shifted(shard, axis, by):
    peers = lax.axis_size(axis)
    pairs = [(i, i + by) for i in range(peers) if 0 <= i + by < peers]
    return lax.ppermute(shard, axis, pairs)


def unique_features(vector, doubled):
    rows, cols = np.triu_indices(KD)
    pick_rows = jnp.asarray(np.eye(KD)[:, rows], jnp.bfloat16)
    pick_cols = jnp.asarray(np.eye(KD)[:, cols], jnp.bfloat16)
    first = jnp.einsum("...d,df->...f", vector, pick_rows, preferred_element_type=jnp.float32)
    second = jnp.einsum("...d,df->...f", vector, pick_cols, preferred_element_type=jnp.float32)
    prod = ((first * second) * outer_scale).astype(jnp.bfloat16)
    if doubled:
        prod = prod * jnp.asarray(np.where(rows == cols, 1.0, 2.0), jnp.bfloat16)
    lead = vector.shape[:-1]
    unit = jnp.ones(lead + (1,), jnp.bfloat16)
    half = (vector.astype(jnp.float32) * 0.5).astype(jnp.bfloat16)
    return jnp.concatenate([unit, half, prod], axis=-1)


CHUNK = 128
LEAD = 128


def local_attention_kernel(flag_ref, q_ref, kt_ref, vx_ref, intra_ref, win_ref, *, span_rows, block_rows):
    first_span = flag_ref[0] == 1
    for i in range(span_rows // CHUNK):
        r0 = i * CHUNK
        q_c = q_ref[0, r0 : r0 + CHUNK, :]
        bs = (r0 // block_rows) * block_rows
        width = r0 + CHUNK - bs
        k_i = kt_ref[0, :, LEAD + bs : LEAD + r0 + CHUNK]
        v_i = vx_ref[LEAD + bs : LEAD + r0 + CHUNK, :]
        scores = jnp.dot(q_c, k_i, preferred_element_type=jnp.float32) * 0.25
        row = lax.broadcasted_iota(jnp.int32, (CHUNK, width), 0)
        col = lax.broadcasted_iota(jnp.int32, (CHUNK, width), 1)
        kernel = jnp.where(
            col <= row + (r0 - bs), 1.0 + scores + 0.5 * scores * scores, 0.0
        ).astype(jnp.bfloat16)
        intra_ref[r0 : r0 + CHUNK, :] = jnp.dot(kernel, v_i, preferred_element_type=jnp.float32)

        k_w = kt_ref[0, :, r0 : r0 + CHUNK + LEAD]
        v_w = vx_ref[r0 : r0 + CHUNK + LEAD, :]
        ws = jnp.dot(q_c, k_w, preferred_element_type=jnp.float32) * 0.25
        wrow = lax.broadcasted_iota(jnp.int32, (CHUNK, CHUNK + LEAD), 0)
        wcol = lax.broadcasted_iota(jnp.int32, (CHUNK, CHUNK + LEAD), 1)
        valid = (wcol > wrow + LEAD - WINDOW) & (wcol <= wrow + LEAD)
        if i == 0:
            valid = valid & ((wcol >= LEAD) | jnp.logical_not(first_span))
        masked = jnp.where(valid, ws, -jnp.inf)
        highest = jnp.max(masked, axis=1, keepdims=True)
        expo = jnp.where(valid, jnp.exp(ws - highest), 0.0)
        weights = (expo / jnp.sum(expo, axis=1, keepdims=True)).astype(jnp.bfloat16)
        win_ref[r0 : r0 + CHUNK, :] = jnp.dot(weights, v_w, preferred_element_type=jnp.float32)


def local_attention(flag, q_hm, kt_hm, vx, block_rows):
    heads_here, span_rows, _ = q_hm.shape
    ext = kt_hm.shape[2]
    body = lambda *refs: local_attention_kernel(*refs, span_rows=span_rows, block_rows=block_rows)
    out = jax.ShapeDtypeStruct((span_rows, heads_here * VD), jnp.float32)
    return pl.pallas_call(
        body,
        grid_spec=pltpu.PrefetchScalarGridSpec(
            num_scalar_prefetch=1,
            grid=(heads_here,),
            in_specs=[
                pl.BlockSpec((1, span_rows, KD), lambda h, f: (h, 0, 0)),
                pl.BlockSpec((1, KD, ext), lambda h, f: (h, 0, 0)),
                pl.BlockSpec((ext, VD), lambda h, f: (0, h)),
            ],
            out_specs=[
                pl.BlockSpec((span_rows, VD), lambda h, f: (0, h)),
                pl.BlockSpec((span_rows, VD), lambda h, f: (0, h)),
            ],
        ),
        out_shape=(out, out),
    )(flag, q_hm, kt_hm, vx)


def mix_kernel(intra_ref, inter_ref, win_ref, gain_ref, out_ref):
    linear = intra_ref[...] + inter_ref[0]
    scale = lax.rsqrt(jnp.mean(linear * linear, axis=1, keepdims=True) + epsilon)
    out_ref[...] = (linear * scale * gain_ref[...] + win_ref[...]).astype(jnp.bfloat16)


def mix(intra, inter_hm, window, gain):
    heads_here, span_rows, _ = inter_hm.shape
    tile = pl.BlockSpec((span_rows, VD), lambda h: (0, h))
    return pl.pallas_call(
        mix_kernel,
        grid=(heads_here,),
        in_specs=[
            tile,
            pl.BlockSpec((1, span_rows, VD), lambda h: (h, 0, 0)),
            tile,
            pl.BlockSpec((1, VD), lambda h: (0, h)),
        ],
        out_specs=tile,
        out_shape=jax.ShapeDtypeStruct((span_rows, heads_here * VD), jnp.bfloat16),
    )(intra, inter_hm, window, gain.reshape(1, heads_here * VD))


def per_device(queries, keys, values, gain):
    local_tokens = queries.shape[0]
    query_tok = queries.reshape(local_tokens, HEADS, KD)
    key_tok = keys.reshape(local_tokens, HEADS, KD)
    value_tok = values.reshape(local_tokens, HEADS, VD)
    query_head, key_head, value_head = (
        lax.all_to_all(query_tok, "head", split_axis=1, concat_axis=0, tiled=True),
        lax.all_to_all(key_tok, "head", split_axis=1, concat_axis=0, tiled=True),
        lax.all_to_all(value_tok, "head", split_axis=1, concat_axis=0, tiled=True),
    )
    span_rows = query_head.shape[0]
    heads_here = query_head.shape[1]
    block_rows = min(512, span_rows)
    block_count = span_rows // block_rows
    first_span = lax.axis_index("ctx") == 0
    query_hm = jnp.transpose(query_head, (1, 0, 2))
    key_hm = jnp.transpose(key_head, (1, 0, 2))

    tails = shifted(
        jnp.concatenate([key_head, value_head], axis=2)[span_rows - WINDOW :], "ctx", 1
    )

    key_feat = unique_features(key_hm, False)
    feat = key_feat.shape[-1]
    block_states = jnp.einsum(
        "hnrf,nrhv->hnfv",
        key_feat.reshape(heads_here, block_count, block_rows, feat),
        value_head.reshape(block_count, block_rows, heads_here, VD),
        preferred_element_type=jnp.float32,
    )
    span_state = jnp.sum(block_states, axis=1)
    tails, span_state = lax.optimization_barrier((tails, span_state))
    everything = lax.all_gather(span_state, "ctx")
    peers = everything.shape[0]
    here = lax.axis_index("ctx")
    entering = jnp.sum(
        jnp.where(
            (jnp.arange(peers) < here)[:, None, None, None], everything, jnp.zeros_like(everything)
        ),
        axis=0,
    )
    before = jnp.concatenate(
        [jnp.zeros_like(block_states[:, :1]), jnp.cumsum(block_states[:, :-1], axis=1)], axis=1
    )
    states = (before + entering[:, None]).astype(jnp.bfloat16)

    query_feat = unique_features(query_hm, True)
    inter = jnp.einsum(
        "hnrf,hnfv->hnrv",
        query_feat.reshape(heads_here, block_count, block_rows, feat),
        states,
        preferred_element_type=jnp.float32,
    ).reshape(heads_here, span_rows, VD)

    lead = jnp.zeros((LEAD - WINDOW, heads_here, KD + VD), jnp.bfloat16)
    key_ext = jnp.concatenate([lead[:, :, :KD], tails[:, :, :KD], key_head], axis=0)
    value_ext = jnp.concatenate([lead[:, :, KD:], tails[:, :, KD:], value_head], axis=0)
    flag = first_span.astype(jnp.int32).reshape(1)
    intra, window = local_attention(
        flag,
        query_hm,
        jnp.transpose(key_ext, (1, 2, 0)),
        value_ext.reshape(span_rows + LEAD, heads_here * VD),
        block_rows,
    )
    mixed = mix(intra, inter, window, gain)
    tokens_back = lax.all_to_all(mixed, "head", split_axis=0, concat_axis=1, tiled=True)
    return tokens_back


def solution(mesh):
    placed = (
        P(("groups", "ctx", "head"), None),
        P(("groups", "ctx", "head"), None),
        P(("groups", "ctx", "head"), None),
        P("head"),
    )
    return jax.shard_map(
        per_device,
        mesh=mesh,
        in_specs=placed,
        out_specs=P(("groups", "ctx", "head"), None),
        check_vma=False,
    )
```

time: 196 us -> 186 us (0.949)
  the two profiles are of different devices: /device:TPU:20 before, /device:TPU:0 now
where the time goes in v6:
time: 186 us; the launch traced here: 185 us
  waiting for transfers between devices  41.5 us (22%)
  local copies, waits for them, and re-layouts  36.8 us (20%)
  blocking collectives  29.3 us (16%)
  Pallas kernels  29.2 us (16%)
  starting transfers between devices  15.6 us (8%)
  between operations  13.7 us (7%)
  matrix products  9.97 us (5%)
  other arithmetic  8.87 us (5%)
    all_to_all x1, blocking collectives, per_device(): lax.all_to_all(mixed, 'head', split_axis=0, concat_axis=1, tiled=True)  29.3 us
    pallas_call x1, Pallas kernels, local_attention(): pl.pallas_call(body, grid_spec=pltpu.PrefetchScalarGridSpec(num_scalar_pr...  20.8 us
    all_gather x1, waiting for transfers between devices, per_device(): everything = lax.all_gather(span_state, 'ctx')  20.6 us
    all_to_all x1, waiting for transfers between devices, per_device(): lax.all_to_all(value_tok, 'head', split_axis=1, concat_axis=0, tiled=True)  14.3 us
    all_to_all x4, local copies, waits for them, and re-layouts, per_device(): lax.all_to_all(value_tok, 'head', split_axis=1, concat_axis=0, tiled=True)  9.83 us
    pallas_call x1, Pallas kernels, mix(): pl.pallas_call(mix_kernel, grid=(heads_here,), in_specs=[tile, pl.BlockSp...  8.42 us
    unnamed x18, local copies, waits for them, and re-layouts  8.28 us
    reshape x1, local copies, waits for them, and re-layouts, per_device(): query_feat.reshape(heads_here, block_count, block_rows, feat)  4.65 us
  transfers between devices with their start and end apart: 5, of which 4 were waited for; matrix products, arithmetic and copies ran while one was open for 19% of the time, Pallas kernels for 11%

profile of v6, /device:TPU:0, one launch (start us, length us, event | category | flops | bytes accessed | tf_op | source)
XLA Modules:
  0.0 184.8 jit_solution(7889327928121794154)
XLA Ops:
  6.5 1.8 copy.63
  8.3 4.2 %all-to-all-start = ((bf16[256,32,16]{0,2,1:T(8,128)(2,1)}), bf16[256,32,16]{0,2,1:T(8,128)(2,1)S(1)}, u32[]{:S(2)}, u32[]{:S(2)}) async-start(bf16[256,32,16]{0,2,1:T(8,128)(2,1)} %bitcast.1), calls=%async_computation | async-start | bytes 524288 | tf_op jit(solution)/shard_map/all_to_all | solution.py:131
  12.5 1.8 copy.65
  14.3 4.2 %all-to-all-done = bf16[256,32,16]{0,2,1:T(8,128)(2,1)S(1)} async-done(((bf16[256,32,16]{0,2,1:T(8,128)(2,1)}), bf16[256,32,16]{0,2,1:T(8,128)(2,1)S(1)}, u32[]{:S(2)}, u32[]{:S(2)}) %all-to-all-start) | async-done | bytes 262176 | tf_op jit(solution)/shard_map/all_to_all | solution.py:131
  18.6 3.4 %all-to-all-start.1 = ((bf16[256,32,16]{0,2,1:T(8,128)(2,1)}), bf16[256,32,16]{0,2,1:T(8,128)(2,1)S(1)}, u32[]{:S(2)}, u32[]{:S(2)}) async-start(bf16[256,32,16]{0,2,1:T(8,128)(2,1)} %bitcast.5), calls=%async_computation.1 | async-start | bytes 524288 | tf_op jit(solution)/shard_map/all_to_all | solution.py:132
  22.0 3.3 %copy.67 = bf16[256,4096]{0,1:T(8,128)(2,1)S(1)} copy(bf16[256,4096]{1,0:T(8,128)(2,1)} %param.11) | data formatting | bytes 4194304 | tf_op args[2]
  25.3 2.9 %copy.68 = bf16[256,32,128]{2,0,1:T(8,128)(2,1)} copy(bf16[256,32,128]{0,2,1:T(8,128)(2,1)S(1)} %bitcast.82) | data formatting | bytes 4194304 | tf_op jit(solution)/shard_map/reshape | solution.py:129
  28.2 3.6 %all-to-all-start.2 = ((bf16[256,32,128]{2,0,1:T(8,128)(2,1)}), bf16[256,32,128]{2,0,1:T(8,128)(2,1)S(1)}, u32[]{:S(2)}, u32[]{:S(2)}) async-start(bf16[256,32,128]{2,0,1:T(8,128)(2,1)} %copy.68), calls=%async_computation.2 | async-start | bytes 4194304 | tf_op jit(solution)/shard_map/all_to_all | solution.py:133
  35.1 3.5 %pad_maximum_fusion.1 = (bf16[8,1024,153]{1,2,0:T(8,128)(2,1)}, bf16[8,1024,153]{1,2,0:T(8,128)(2,1)}) fusion(bf16[8,1024,136]{1,2,0:T(8,128)(2,1)S(1)} %fusion.7, bf16[8,1024,16]{1,2,0:T(8,128)(2,1)S(1)} %multiply_convert_fusion.2, bf16[153]{0:T(256)(128)(2,1)S(1)} %pad.7.clone, bf16[8,1024,136]{1,2,0:T(8,128)(2,1)S(1)} %fusion.5, ...), kind=kLoop, calls=%fused_computation.3 | loop fusion | flops 13787136 | bytes 9994546 | tf_op jit(solution)/shard_map/concatenate | solution.py:39
  38.6 4.6 %reshape.59 = bf16[8,2,512,153]{2,1,3,0:T(2,128)(2,1)} reshape(bf16[8,1024,153]{1,2,0:T(8,128)(2,1)} %get-tuple-element.14) | data formatting | bytes 5013504 | tf_op jit(solution)/shard_map/reshape | solution.py:151
  43.2 14.3 %all-to-all-done.2 = bf16[256,32,128]{2,0,1:T(8,128)(2,1)S(1)} async-done(((bf16[256,32,128]{2,0,1:T(8,128)(2,1)}), bf16[256,32,128]{2,0,1:T(8,128)(2,1)S(1)}, u32[]{:S(2)}, u32[]{:S(2)}) %all-to-all-start.2) | async-done | bytes 2097184 | tf_op jit(solution)/shard_map/all_to_all | solution.py:133
  57.5 1.5 copy.72
  58.9 2.5 %copy.70 = bf16[4,256,8,128]{1,0,3,2:T(4,128)(2,1)} copy(bf16[4,256,8,128]{3,1,2,0:T(8,128)(2,1)S(1)} %bitcast.70) | data formatting | bytes 4194304 | tf_op jit(solution)/shard_map/all_to_all | solution.py:133
  61.5 4.5 %all_to_all.64 = bf16[1024,8,128]{0,2,1:T(8,128)(2,1)} reshape(bf16[4,256,8,128]{1,0,3,2:T(4,128)(2,1)} %copy.70) | data formatting | bytes 4194304 | tf_op jit(solution)/shard_map/all_to_all | solution.py:133
  66.0 1.3 pad_maximum_fusion.3
  67.2 4.3 %collective-permute-start = (bf16[64,8,144]{0,2,1:T(8,128)(2,1)S(1)}, bf16[64,8,144]{0,2,1:T(8,128)(2,1)S(1)}, u32[]{:S(2)}, u32[]{:S(2)}) collective-permute-start(bf16[64,8,144]{0,2,1:T(8,128)(2,1)S(1)} %pad_maximum_fusion.3), channel_id=1, source_target_pairs={{0,4},{4,8},{8,12},{1,5},{5,9},{9,13},{2,6},{6,10},{10,14},{3,7},{... | collective-permute-start | bytes 442376 | tf_op jit(solution)/shard_map/ppermute | solution.py:24
  71.5 3.6 %fusion.16 = (f32[8,153,128]{2,1,0:T(8,128)S(1)}, f32[8,2,153,128]{3,2,1,0:T(8,128)}) fusion(bf16[2,512,8,128]{3,1,0,2:T(8,128)(2,1)} %bitcast.78, bf16[8,2,512,153]{2,1,3,0:T(2,128)(2,1)S(1)} %copy-done), kind=kOutput, calls=%fused_computation.28 | convolution fusion | flops 321020928 | bytes 6483968 | tf_op jit(solution)/shard_map/hnrf,nrhv->hnfv/dot_general | solution.py:149
  75.1 2.3 %collective-permute-done = bf16[64,8,144]{0,2,1:T(8,128)(2,1)S(1)} collective-permute-done((bf16[64,8,144]{0,2,1:T(8,128)(2,1)S(1)}, bf16[64,8,144]{0,2,1:T(8,128)(2,1)S(1)}, u32[]{:S(2)}, u32[]{:S(2)}) %collective-permute-start) | collective-permute-done | bytes 147488 | tf_op jit(solution)/shard_map/ppermute | solution.py:24
  77.4 1.2 copy.78
  78.7 1.7 copy.76.refs_1_
  80.4 4.6 %reshape.60 = bf16[8,2,512,153]{2,1,3,0:T(2,128)(2,1)} reshape(bf16[8,1024,153]{1,2,0:T(8,128)(2,1)} %get-tuple-element.13) | data formatting | bytes 5013504 | tf_op jit(solution)/shard_map/reshape | solution.py:174
  85.0 1.4 copy.75
  87.9 1.0 slice.22
  89.0 0.8 concatenate.25
  89.8 1.8 pad_maximum_fusion.2.refs_3_
  91.6 20.8 %shard_map.91 = (f32[1024,1024]{1,0:T(8,128)}, f32[1024,1024]{1,0:T(8,128)}) custom-call(s32[1]{0:T(128)} %bitcast.refs_0_, bf16[8,1024,16]{2,1,0:T(8,128)(2,1)} %copy.76.refs_1_, bf16[8,16,1152]{2,1,0:T(8,128)(2,1)} %bitcast.88, bf16[1152,1024]{1,0:T(8,128)(2,1)} %pad_maximum_fusion.2.refs_3_), custom_call_target="tpu_custom_call" | custom-call | tf_op jit(solution)/shard_map/pallas_call | solution.py:83
  112.4 20.6 %all-gather.3.cloned.1.call-done = f32[32,153,128]{2,0,1:T(8,128)} async-done(((f32[8,153,128]{2,0,1:T(8,128)}), f32[32,153,128]{2,0,1:T(8,128)}) %all-gather.3.cloned.1.call-update) | async-done | bytes 2506768 | tf_op jit(solution)/shard_map/all_gather | solution.py:157
  133.0 2.2 %fusion.4 = f32[8,153,128]{2,0,1:T(8,128)S(1)} fusion(f32[32,153,128]{2,0,1:T(8,128)} %all-gather.3.cloned.1.call-done, pred[4]{0:T(512)(128)(4,1)S(1)} %iota_compare_fusion), kind=kLoop, calls=%fused_computation.9 | loop fusion | flops 1096704 | bytes 3133444 | tf_op jit(solution)/shard_map/reduce_sum | solution.py:160
  135.4 3.4 %fusion = f32[8,2,512,128]{3,2,1,0:T(8,128)} fusion(bf16[8,2,512,153]{2,1,3,0:T(2,128)(2,1)S(1)} %copy-done.1, f32[8,1,153,128]{3,2,1,0:T(8,128)S(1)} %slice.24, f32[8,153,128]{2,1,0:T(8,128)S(1)} %copy.79), kind=kOutput, calls=%fused_computation.4 | convolution fusion | flops 321490944 | bytes 7954432 | tf_op jit(solution)/shard_map/hnrf,hnfv->hnrv/dot_general | solution.py:172
  138.8 8.4 %shard_map.92 = bf16[1024,1024]{1,0:T(8,128)(2,1)} custom-call(f32[1024,1024]{1,0:T(8,128)} %get-tuple-element.10.intra_ref, f32[8,1024,128]{2,1,0:T(8,128)} %bitcast.72, f32[1024,1024]{1,0:T(8,128)} %get-tuple-element.12.win_ref, f32[1,1024]{1,0:T(1,128)} %bitcast.92), custom_call_target="tpu_custom_call" | custom-call | tf_op jit(solution)/shard_map/pallas_call | solution.py:111
  147.2 29.3 %all_to_all.73 = bf16[4,256,1024]{2,1,0:T(8,128)(2,1)S(1)} all-to-all(bf16[4,256,1024]{2,1,0:T(8,128)(2,1)} %bitcast.83), channel_id=1, replica_groups=mesh['groups'=2,'ctx'=4,'head'=4] {'head'}, dimensions={0} | all-to-all | bytes 4194304 | tf_op jit(solution)/shard_map/all_to_all | solution.py:191
  176.5 1.5 copy.92
  (35 shorter events, 5.0 us)
Async XLA Ops:
  8.3 10.2 %all-to-all-start = ((bf16[256,32,16]{0,2,1:T(8,128)(2,1)}), bf16[256,32,16]{0,2,1:T(8,128)(2,1)S(1)}, u32[]{:S(2)}, u32[]{:S(2)}) async-start(bf16[256,32,16]{0,2,1:T(8,128)(2,1)} %bitcast.1), calls=%async_computation | async-start | bytes 524288 | tf_op jit(solution)/shard_map/all_to_all | solution.py:131
  18.6 9.6 %all-to-all-start.1 = ((bf16[256,32,16]{0,2,1:T(8,128)(2,1)}), bf16[256,32,16]{0,2,1:T(8,128)(2,1)S(1)}, u32[]{:S(2)}, u32[]{:S(2)}) async-start(bf16[256,32,16]{0,2,1:T(8,128)(2,1)} %bitcast.5), calls=%async_computation.1 | async-start | bytes 524288 | tf_op jit(solution)/shard_map/all_to_all | solution.py:132
  28.2 3.8 %copy-start.5 = (bf16[16,136,1]{1,0,2:T(8,128)(2,1)S(1)}, bf16[16,136,1]{1,0,2:T(8,128)(2,1)}, u32[]{:S(2)}) copy-start(bf16[16,136,1]{1,0,2:T(8,128)(2,1)} %constant.34) | copy-start | bytes 13060
  28.2 29.3 %all-to-all-start.2 = ((bf16[256,32,128]{2,0,1:T(8,128)(2,1)}), bf16[256,32,128]{2,0,1:T(8,128)(2,1)S(1)}, u32[]{:S(2)}, u32[]{:S(2)}) async-start(bf16[256,32,128]{2,0,1:T(8,128)(2,1)} %copy.68), calls=%async_computation.2 | async-start | bytes 4194304 | tf_op jit(solution)/shard_map/all_to_all | solution.py:133
  31.8 101.2 %all-gather.3.cloned.1.call-start = ((), (), s32[]{:S(2)}) async-start(), calls=%async_computation.4 | async-start | bytes 3133440 | tf_op jit(solution)/shard_map/all_gather | solution.py:157
  32.7 0.8 copy-start.4
  33.5 0.8 copy-start.6
  66.0 5.6 %copy-start = (bf16[8,2,512,153]{2,1,3,0:T(2,128)(2,1)S(1)}, bf16[8,2,512,153]{2,1,3,0:T(2,128)(2,1)}, u32[]{:S(2)}) copy-start(bf16[8,2,512,153]{2,1,3,0:T(2,128)(2,1)} %reshape.59) | copy-start | bytes 7520260
  67.2 10.2 %collective-permute-start = (bf16[64,8,144]{0,2,1:T(8,128)(2,1)S(1)}, bf16[64,8,144]{0,2,1:T(8,128)(2,1)S(1)}, u32[]{:S(2)}, u32[]{:S(2)}) collective-permute-start(bf16[64,8,144]{0,2,1:T(8,128)(2,1)S(1)} %pad_maximum_fusion.3), channel_id=1, source_target_pairs={{0,4},{4,8},{8,12},{1,5},{5,9},{9,13},{2,6},{6,10},{10,14},{3,7},{... | collective-permute-start | bytes 442376 | tf_op jit(solution)/shard_map/ppermute | solution.py:24
  77.4 10.4 %copy-start.3 = (bf16[64,8,144]{0,2,1:T(8,128)(2,1)}, bf16[64,8,144]{0,2,1:T(8,128)(2,1)S(1)}, u32[]{:S(2)}) copy-start(bf16[64,8,144]{0,2,1:T(8,128)(2,1)S(1)} %collective-permute-done) | copy-start | bytes 442372
  86.4 1.4 copy-start.2
  112.4 23.0 %copy-start.1 = (bf16[8,2,512,153]{2,1,3,0:T(2,128)(2,1)S(1)}, bf16[8,2,512,153]{2,1,3,0:T(2,128)(2,1)}, u32[]{:S(2)}) copy-start(bf16[8,2,512,153]{2,1,3,0:T(2,128)(2,1)} %reshape.60) | copy-start | bytes 7520260
Sparse Core Ops, SparseCore 0:
  78.7 54.2 all-gather.2

commit v7 on v6

--- a/solution.py
+++ b/solution.py
@@ -51,7 +51,7 @@
         bs = (r0 // block_rows) * block_rows
         width = r0 + CHUNK - bs
         k_i = kt_ref[0, :, LEAD + bs : LEAD + r0 + CHUNK]
-        v_i = vx_ref[LEAD + bs : LEAD + r0 + CHUNK, :]
+        v_i = vx_ref[0, LEAD + bs : LEAD + r0 + CHUNK, :]
         scores = jnp.dot(q_c, k_i, preferred_element_type=jnp.float32) * 0.25
         row = lax.broadcasted_iota(jnp.int32, (CHUNK, width), 0)
         col = lax.broadcasted_iota(jnp.int32, (CHUNK, width), 1)
@@ -61,7 +61,7 @@
         intra_ref[r0 : r0 + CHUNK, :] = jnp.dot(kernel, v_i, preferred_element_type=jnp.float32)
 
         k_w = kt_ref[0, :, r0 : r0 + CHUNK + LEAD]
-        v_w = vx_ref[r0 : r0 + CHUNK + LEAD, :]
+        v_w = vx_ref[0, r0 : r0 + CHUNK + LEAD, :]
         ws = jnp.dot(q_c, k_w, preferred_element_type=jnp.float32) * 0.25
         wrow = lax.broadcasted_iota(jnp.int32, (CHUNK, CHUNK + LEAD), 0)
         wcol = lax.broadcasted_iota(jnp.int32, (CHUNK, CHUNK + LEAD), 1)
@@ -88,7 +88,7 @@
             in_specs=[
                 pl.BlockSpec((1, span_rows, KD), lambda h, f: (h, 0, 0)),
                 pl.BlockSpec((1, KD, ext), lambda h, f: (h, 0, 0)),
-                pl.BlockSpec((ext, VD), lambda h, f: (0, h)),
+                pl.BlockSpec((1, ext, VD), lambda h, f: (h, 0, 0)),
             ],
             out_specs=[
                 pl.BlockSpec((span_rows, VD), lambda h, f: (0, h)),
@@ -124,36 +124,32 @@
 
 def per_device(queries, keys, values, gain):
     local_tokens = queries.shape[0]
-    query_tok = queries.reshape(local_tokens, HEADS, KD)
-    key_tok = keys.reshape(local_tokens, HEADS, KD)
-    value_tok = values.reshape(local_tokens, HEADS, VD)
-    query_head, key_head, value_head = (
-        lax.all_to_all(query_tok, "head", split_axis=1, concat_axis=0, tiled=True),
-        lax.all_to_all(key_tok, "head", split_axis=1, concat_axis=0, tiled=True),
-        lax.all_to_all(value_tok, "head", split_axis=1, concat_axis=0, tiled=True),
-    )
-    span_rows = query_head.shape[0]
-    heads_here = query_head.shape[1]
+
+    def to_heads(tok, width):
+        tok = jnp.transpose(tok.reshape(local_tokens, HEADS, width), (1, 0, 2))
+        return lax.all_to_all(tok, "head", split_axis=0, concat_axis=1, tiled=True)
+
+    query_hm = to_heads(queries, KD)
+    key_hm = to_heads(keys, KD)
+    value_hm = to_heads(values, VD)
+    heads_here, span_rows, _ = query_hm.shape
     block_rows = min(512, span_rows)
     block_count = span_rows // block_rows
     first_span = lax.axis_index("ctx") == 0
-    query_hm = jnp.transpose(query_head, (1, 0, 2))
-    key_hm = jnp.transpose(key_head, (1, 0, 2))
 
     tails = shifted(
-        jnp.concatenate([key_head, value_head], axis=2)[span_rows - WINDOW :], "ctx", 1
+        jnp.concatenate([key_hm, value_hm], axis=2)[:, span_rows - WINDOW :], "ctx", 1
     )
 
     key_feat = unique_features(key_hm, False)
     feat = key_feat.shape[-1]
     block_states = jnp.einsum(
-        "hnrf,nrhv->hnfv",
+        "hnrf,hnrv->hnfv",
         key_feat.reshape(heads_here, block_count, block_rows, feat),
-        value_head.reshape(block_count, block_rows, heads_here, VD),
+        value_hm.reshape(heads_here, block_count, block_rows, VD),
         preferred_element_type=jnp.float32,
     )
     span_state = jnp.sum(block_states, axis=1)
-    tails, span_state = lax.optimization_barrier((tails, span_state))
     everything = lax.all_gather(span_state, "ctx")
     peers = everything.shape[0]
     here = lax.axis_index("ctx")
@@ -176,16 +172,12 @@
         preferred_element_type=jnp.float32,
     ).reshape(heads_here, span_rows, VD)
 
-    lead = jnp.zeros((LEAD - WINDOW, heads_here, KD + VD), jnp.bfloat16)
-    key_ext = jnp.concatenate([lead[:, :, :KD], tails[:, :, :KD], key_head], axis=0)
-    value_ext = jnp.concatenate([lead[:, :, KD:], tails[:, :, KD:], value_head], axis=0)
+    lead = jnp.zeros((heads_here, LEAD - WINDOW, KD + VD), jnp.bfloat16)
+    key_ext = jnp.concatenate([lead[:, :, :KD], tails[:, :, :KD], key_hm], axis=1)
+    value_ext = jnp.concatenate([lead[:, :, KD:], tails[:, :, KD:], value_hm], axis=1)
     flag = first_span.astype(jnp.int32).reshape(1)
     intra, window = local_attention(
-        flag,
-        query_hm,
-        jnp.transpose(key_ext, (1, 2, 0)),
-        value_ext.reshape(span_rows + LEAD, heads_here * VD),
-        block_rows,
+        flag, query_hm, jnp.transpose(key_ext, (0, 2, 1)), value_ext, block_rows
     )
     mixed = mix(intra, inter, window, gain)
     tokens_back = lax.all_to_all(mixed, "head", split_axis=0, concat_axis=1, tiled=True)

time: 186 us -> 178 us (0.957)
  waiting for transfers between devices: 41.5 us -> 25.1 us
  other arithmetic: 8.87 us -> 14.6 us
  matrix products: 9.97 us -> 12.8 us
    all_to_all x3, waiting for transfers between devices: 18.5 us -> 7.43 us  [to_heads(): return lax.all_to_all(tok, 'head', split_axis=0, concat_axis=1, tiled=True)]
    mul x0 -> x2, other arithmetic: none -> 5.21 us  [unique_features(): half = (vector.astype(jnp.float32) * 0.5).astype(jnp.bfloat16)]
    mul x0 -> x2, local copies, waits for them, and re-layouts: none -> 3.69 us  [unique_features(): half = (vector.astype(jnp.float32) * 0.5).astype(jnp.bfloat16)]
    all_gather x1, waiting for transfers between devices: 20.6 us -> 17.2 us  [per_device(): everything = lax.all_gather(span_state, 'ctx')]
    reshape x1 -> x0, local copies, waits for them, and re-layouts: 2.86 us -> none  [per_device(): value_tok = values.reshape(local_tokens, HEADS, VD)]
    unnamed x18 -> x19, local copies, waits for them, and re-layouts: 8.28 us -> 6.3 us
    all_to_all x6 -> x4, local copies, waits for them, and re-layouts: 9.87 us -> 8.1 us  [to_heads(): return lax.all_to_all(tok, 'head', split_axis=0, concat_axis=1, tiled=True)]
  transfers between devices with their start and end apart: 5 -> 5, of which waited for: 4 -> 5; matrix products, arithmetic and copies ran while one was open for 19% -> 25% of each run, Pallas kernels for 11% -> 12%
where the time goes in v7:
time: 178 us; the launch traced here: 176 us
  local copies, waits for them, and re-layouts  35 us (20%)
  blocking collectives  29.3 us (16%)
  Pallas kernels  29.2 us (16%)
  waiting for transfers between devices  25.1 us (14%)
  starting transfers between devices  16.9 us (9%)
  other arithmetic  14.6 us (8%)
  between operations  13.6 us (8%)
  matrix products  12.8 us (7%)
    all_to_all x1, blocking collectives, per_device(): lax.all_to_all(mixed, 'head', split_axis=0, concat_axis=1, tiled=True)  29.3 us
    pallas_call x1, Pallas kernels, local_attention(): pl.pallas_call(body, grid_spec=pltpu.PrefetchScalarGridSpec(num_scalar_pr...  20.8 us
    all_gather x1, waiting for transfers between devices, per_device(): everything = lax.all_gather(span_state, 'ctx')  17.2 us
    all_to_all x3, starting transfers between devices, to_heads(): return lax.all_to_all(tok, 'head', split_axis=0, concat_axis=1, tiled=True)  12.1 us
    pallas_call x1, Pallas kernels, mix(): pl.pallas_call(mix_kernel, grid=(heads_here,), in_specs=[tile, pl.BlockSp...  8.42 us
    all_to_all x4, local copies, waits for them, and re-layouts, to_heads(): return lax.all_to_all(tok, 'head', split_axis=0, concat_axis=1, tiled=True)  8.1 us
    all_to_all x3, waiting for transfers between devices, to_heads(): return lax.all_to_all(tok, 'head', split_axis=0, concat_axis=1, tiled=True)  7.43 us
    unnamed x19, local copies, waits for them, and re-layouts  6.3 us
  transfers between devices with their start and end apart: 5, of which 5 were waited for; matrix products, arithmetic and copies ran while one was open for 25% of the time, Pallas kernels for 12%

profile of v7, /device:TPU:0, one launch (start us, length us, event | category | flops | bytes accessed | tf_op | source)
XLA Modules:
  0.0 176.4 jit_solution(1154463031708502896)
XLA Ops:
  6.5 1.9 %copy.104 = bf16[256,512]{0,1:T(8,128)(2,1)} copy(bf16[256,512]{1,0:T(8,128)(2,1)} %param.10) | data formatting | bytes 524288 | tf_op args[1]
  8.5 4.2 %all-to-all-start.1 = ((bf16[32,256,16]{1,2,0:T(8,128)(2,1)}), bf16[32,256,16]{1,2,0:T(8,128)(2,1)S(1)}, u32[]{:S(2)}, u32[]{:S(2)}) async-start(bf16[32,256,16]{1,2,0:T(8,128)(2,1)} %bitcast.7), calls=%async_computation.1 | async-start | bytes 524288 | tf_op jit(solution)/shard_map/all_to_all | solution.py:130
  12.7 1.8 %copy.102 = bf16[256,512]{0,1:T(8,128)(2,1)} copy(bf16[256,512]{1,0:T(8,128)(2,1)} %param.9) | data formatting | bytes 524288 | tf_op args[0]
  14.5 4.2 %all-to-all-done.1 = bf16[32,256,16]{1,2,0:T(8,128)(2,1)S(1)} async-done(((bf16[32,256,16]{1,2,0:T(8,128)(2,1)}), bf16[32,256,16]{1,2,0:T(8,128)(2,1)S(1)}, u32[]{:S(2)}, u32[]{:S(2)}) %all-to-all-start.1) | async-done | bytes 262176 | tf_op jit(solution)/shard_map/all_to_all | solution.py:130
  18.7 3.4 %all-to-all-start = ((bf16[32,256,16]{1,2,0:T(8,128)(2,1)}), bf16[32,256,16]{1,2,0:T(8,128)(2,1)S(1)}, u32[]{:S(2)}, u32[]{:S(2)}) async-start(bf16[32,256,16]{1,2,0:T(8,128)(2,1)} %bitcast.2), calls=%async_computation | async-start | bytes 524288 | tf_op jit(solution)/shard_map/all_to_all | solution.py:130
  22.1 2.5 %copy.106 = bf16[256,4096]{0,1:T(8,128)(2,1)} copy(bf16[256,4096]{1,0:T(8,128)(2,1)S(1)} %copy-done.4) | data formatting | bytes 4194304 | tf_op args[2]
  25.7 2.5 %all-to-all-done = bf16[32,256,16]{1,2,0:T(8,128)(2,1)S(1)} async-done(((bf16[32,256,16]{1,2,0:T(8,128)(2,1)}), bf16[32,256,16]{1,2,0:T(8,128)(2,1)S(1)}, u32[]{:S(2)}, u32[]{:S(2)}) %all-to-all-start) | async-done | bytes 262176 | tf_op jit(solution)/shard_map/all_to_all | solution.py:130
  28.1 4.5 %all-to-all-start.2 = ((bf16[32,256,128]{1,2,0:T(8,128)(2,1)}), bf16[32,256,128]{1,2,0:T(8,128)(2,1)}, u32[]{:S(2)}, u32[]{:S(2)}) async-start(bf16[32,256,128]{1,2,0:T(8,128)(2,1)} %bitcast.69), calls=%async_computation.2 | async-start | bytes 4194304 | tf_op jit(solution)/shard_map/all_to_all | solution.py:130
  32.7 1.7 copy.103
  34.4 3.3 %convert_multiply_fusion.1 = bf16[8,1024,16]{2,1,0:T(8,128)(2,1)} fusion(bf16[8,4,256,16]{3,2,1,0:T(8,128)(2,1)} %copy.103), kind=kLoop, calls=%fused_computation.3 | loop fusion | flops 393216 | bytes 524288 | tf_op jit(solution)/shard_map/mul | solution.py:38
  37.7 1.8 %copy.111 = bf16[8,1024,16]{1,2,0:T(8,128)(2,1)S(1)} copy(bf16[8,1024,16]{2,1,0:T(8,128)(2,1)} %convert_multiply_fusion.1) | data formatting | bytes 524288 | tf_op jit(solution)/shard_map/mul | solution.py:38
  39.6 1.9 %convert_multiply_fusion = bf16[8,1024,16]{2,1,0:T(8,128)(2,1)} fusion(bf16[8,4,256,16]{3,2,1,0:T(8,128)(2,1)S(1)} %copy.105), kind=kLoop, calls=%fused_computation.2 | loop fusion | flops 393216 | bytes 524288 | tf_op jit(solution)/shard_map/mul | solution.py:38
  41.5 1.8 %copy.115 = bf16[8,1024,16]{1,2,0:T(8,128)(2,1)S(1)} copy(bf16[8,1024,16]{2,1,0:T(8,128)(2,1)} %convert_multiply_fusion) | data formatting | bytes 524288 | tf_op jit(solution)/shard_map/mul | solution.py:38
  43.3 1.5 fusion.12
  44.9 1.5 fusion.11
  46.5 1.5 fusion.7
  48.0 1.6 fusion.6
  49.6 3.5 %pad_maximum_fusion.1 = (bf16[8,1024,153]{1,2,0:T(8,128)(2,1)}, bf16[8,1024,153]{1,2,0:T(8,128)(2,1)}) fusion(bf16[8,1024,136]{1,2,0:T(8,128)(2,1)S(1)} %fusion.7, bf16[8,1024,16]{1,2,0:T(8,128)(2,1)S(1)} %copy.115, bf16[153]{0:T(256)(128)(2,1)S(1)} %pad.4.clone, bf16[8,1024,136]{1,2,0:T(8,128)(2,1)S(1)} %fusion.6, bf16[8,1024,16]{1,2,0:T(8,128)(2,1)S(1)} %copy.111), kind=kLoop, calls=%fused_computation.5 | loop fusion | flops 13787136 | bytes 9994546 | tf_op jit(solution)/shard_map/concatenate | solution.py:39
  53.1 4.6 %reshape.55 = bf16[8,2,512,153]{2,1,3,0:T(2,128)(2,1)} reshape(bf16[8,1024,153]{1,2,0:T(8,128)(2,1)} %get-tuple-element.9) | data formatting | bytes 5013504 | tf_op jit(solution)/shard_map/reshape | solution.py:148
  58.4 3.9 %copy.108 = bf16[8,4,256,128]{3,2,1,0:T(8,128)(2,1)} copy(bf16[8,4,256,128]{2,3,0,1:T(8,128)(2,1)} %bitcast.15) | data formatting | bytes 4194304 | tf_op jit(solution)/shard_map/all_to_all | solution.py:130
  62.3 3.2 %fusion.10 = (f32[8,153,128]{2,1,0:T(8,128)S(1)}, f32[8,2,153,128]{3,2,1,0:T(8,128)S(1)}) fusion(bf16[8,2,512,128]{3,2,1,0:T(8,128)(2,1)} %bitcast.65, bf16[8,2,512,153]{2,1,3,0:T(2,128)(2,1)} %reshape.55), kind=kOutput, calls=%fused_computation.21 | convolution fusion | flops 321020928 | bytes 6483968 | tf_op jit(solution)/shard_map/hnrf,hnrv->hnfv/dot_general | solution.py:146
  66.8 1.7 pad_maximum_fusion.3
  68.6 4.8 %collective-permute-start = (bf16[8,64,144]{2,1,0:T(8,128)(2,1)}, bf16[8,64,144]{2,1,0:T(8,128)(2,1)}, u32[]{:S(2)}, u32[]{:S(2)}) collective-permute-start(bf16[8,64,144]{2,1,0:T(8,128)(2,1)} %pad_maximum_fusion.3), channel_id=1, source_target_pairs={{0,4},{4,8},{8,12},{1,5},{5,9},{9,13},{2,6},{6,10},{10,14},{3,7},{... | collective-permute-start | bytes 442376 | tf_op jit(solution)/shard_map/ppermute | solution.py:24
  74.8 4.7 %reshape.54 = bf16[8,2,512,153]{2,1,3,0:T(2,128)(2,1)} reshape(bf16[8,1024,153]{1,2,0:T(8,128)(2,1)} %get-tuple-element.10) | data formatting | bytes 5013504 | tf_op jit(solution)/shard_map/reshape | solution.py:170
  82.0 1.8 concatenate.19
  84.8 1.9 %pad_maximum_fusion.2.refs_3_ = bf16[8,1152,128]{2,1,0:T(8,128)(2,1)} fusion(bf16[8,1024,128]{2,1,0:T(8,128)(2,1)S(1)} %bitcast.67, bf16[8,64,128]{2,1,0:T(8,128)(2,1)S(1)} %slice.25, bf16[1152]{0:T(1024)(128)(2,1)S(1)} %pad.7.clone), kind=kLoop, calls=%fused_computation.12 | loop fusion | flops 7077888 | bytes 4589824 | tf_op jit(solution)/shard_map/concatenate | solution.py:177
  86.7 20.8 %shard_map.91 = (f32[1024,1024]{1,0:T(8,128)}, f32[1024,1024]{1,0:T(8,128)}) custom-call(s32[1]{0:T(128)} %bitcast.refs_0_, bf16[8,1024,16]{2,1,0:T(8,128)(2,1)} %bitcast.62, bf16[8,16,1152]{2,1,0:T(8,128)(2,1)} %bitcast.72, bf16[8,1152,128]{2,1,0:T(8,128)(2,1)} %pad_maximum_fusion.2.refs_3_), custom_call_target="tpu_custom_call" | custom-call | tf_op jit(solution)/shard_map/pallas_call | solution.py:83
  107.5 17.2 %all-gather.3.cloned.1.call-done = f32[32,153,128]{2,0,1:T(8,128)} async-done(((f32[8,153,128]{2,0,1:T(8,128)}), f32[32,153,128]{2,0,1:T(8,128)}) %all-gather.3.cloned.1.call-update) | async-done | bytes 2506768 | tf_op jit(solution)/shard_map/all_gather | solution.py:153
  124.6 2.2 %fusion.4 = f32[8,153,128]{2,0,1:T(8,128)S(1)} fusion(f32[32,153,128]{2,0,1:T(8,128)} %all-gather.3.cloned.1.call-done, pred[4]{0:T(512)(128)(4,1)S(1)} %iota_compare_fusion), kind=kLoop, calls=%fused_computation.11 | loop fusion | flops 1096704 | bytes 3133444 | tf_op jit(solution)/shard_map/reduce_sum | solution.py:156
  127.0 3.4 %fusion.2 = f32[8,2,512,128]{3,2,1,0:T(8,128)} fusion(bf16[8,2,512,153]{2,1,3,0:T(2,128)(2,1)S(1)} %copy-done.2, f32[8,1,153,128]{3,2,1,0:T(8,128)S(1)} %copy-done.3, f32[8,153,128]{2,1,0:T(8,128)S(1)} %copy.122), kind=kOutput, calls=%fused_computation.8 | convolution fusion | flops 321490944 | bytes 7954432 | tf_op jit(solution)/shard_map/hnrf,hnfv->hnrv/dot_general | solution.py:168
  130.4 8.4 %shard_map.92 = bf16[1024,1024]{1,0:T(8,128)(2,1)} custom-call(f32[1024,1024]{1,0:T(8,128)} %get-tuple-element.7.intra_ref, f32[8,1024,128]{2,1,0:T(8,128)} %bitcast.68, f32[1024,1024]{1,0:T(8,128)} %get-tuple-element.8.win_ref, f32[1,1024]{1,0:T(1,128)} %bitcast.75), custom_call_target="tpu_custom_call" | custom-call | tf_op jit(solution)/shard_map/pallas_call | solution.py:111
  138.8 29.3 %all_to_all.73 = bf16[4,256,1024]{2,1,0:T(8,128)(2,1)S(1)} all-to-all(bf16[4,256,1024]{2,1,0:T(8,128)(2,1)} %bitcast.71), channel_id=1, replica_groups=mesh['groups'=2,'ctx'=4,'head'=4] {'head'}, dimensions={0} | all-to-all | bytes 4194304 | tf_op jit(solution)/shard_map/all_to_all | solution.py:183
  (34 shorter events, 9.6 us)
Async XLA Ops:
  6.5 15.6 %copy-start.4 = (bf16[256,4096]{1,0:T(8,128)(2,1)S(1)}, bf16[256,4096]{1,0:T(8,128)(2,1)}, u32[]{:S(2)}) copy-start(bf16[256,4096]{1,0:T(8,128)(2,1)} %param.11) | copy-start | bytes 6291460
  8.5 10.2 %all-to-all-start.1 = ((bf16[32,256,16]{1,2,0:T(8,128)(2,1)}), bf16[32,256,16]{1,2,0:T(8,128)(2,1)S(1)}, u32[]{:S(2)}, u32[]{:S(2)}) async-start(bf16[32,256,16]{1,2,0:T(8,128)(2,1)} %bitcast.7), calls=%async_computation.1 | async-start | bytes 524288 | tf_op jit(solution)/shard_map/all_to_all | solution.py:130
  18.7 9.4 %all-to-all-start = ((bf16[32,256,16]{1,2,0:T(8,128)(2,1)}), bf16[32,256,16]{1,2,0:T(8,128)(2,1)S(1)}, u32[]{:S(2)}, u32[]{:S(2)}) async-start(bf16[32,256,16]{1,2,0:T(8,128)(2,1)} %bitcast.2), calls=%async_computation | async-start | bytes 524288 | tf_op jit(solution)/shard_map/all_to_all | solution.py:130
  28.1 30.3 %all-to-all-start.2 = ((bf16[32,256,128]{1,2,0:T(8,128)(2,1)}), bf16[32,256,128]{1,2,0:T(8,128)(2,1)}, u32[]{:S(2)}, u32[]{:S(2)}) async-start(bf16[32,256,128]{1,2,0:T(8,128)(2,1)} %bitcast.69), calls=%async_computation.2 | async-start | bytes 4194304 | tf_op jit(solution)/shard_map/all_to_all | solution.py:130
  32.6 92.0 %all-gather.3.cloned.1.call-start = ((), (), s32[]{:S(2)}) async-start(), calls=%async_computation.4 | async-start | bytes 3133440 | tf_op jit(solution)/shard_map/all_gather | solution.py:153
  39.6 3.7 %copy-start.6 = (bf16[16,136,1]{1,0,2:T(8,128)(2,1)S(1)}, bf16[16,136,1]{1,0,2:T(8,128)(2,1)}, u32[]{:S(2)}) copy-start(bf16[16,136,1]{1,0,2:T(8,128)(2,1)} %constant.34) | copy-start | bytes 13060
  43.3 1.6 copy-start
  44.9 1.5 copy-start.5
  46.5 1.6 copy-start.7
  68.6 12.4 %collective-permute-start = (bf16[8,64,144]{2,1,0:T(8,128)(2,1)}, bf16[8,64,144]{2,1,0:T(8,128)(2,1)}, u32[]{:S(2)}, u32[]{:S(2)}) collective-permute-start(bf16[8,64,144]{2,1,0:T(8,128)(2,1)} %pad_maximum_fusion.3), channel_id=1, source_target_pairs={{0,4},{4,8},{8,12},{1,5},{5,9},{9,13},{2,6},{6,10},{10,14},{3,7},{... | collective-permute-start | bytes 442376 | tf_op jit(solution)/shard_map/ppermute | solution.py:24
  79.5 5.3 %copy-start.1 = (bf16[8,4,256,128]{3,2,1,0:T(8,128)(2,1)S(1)}, bf16[8,4,256,128]{3,2,1,0:T(8,128)(2,1)}, u32[]{:S(2)}) copy-start(bf16[8,4,256,128]{3,2,1,0:T(8,128)(2,1)} %copy.108) | copy-start | bytes 6291460
  107.5 19.5 %copy-start.2 = (bf16[8,2,512,153]{2,1,3,0:T(2,128)(2,1)S(1)}, bf16[8,2,512,153]{2,1,3,0:T(2,128)(2,1)}, u32[]{:S(2)}) copy-start(bf16[8,2,512,153]{2,1,3,0:T(2,128)(2,1)} %reshape.54) | copy-start | bytes 7520260
  107.5 19.5 %copy-start.3 = (f32[8,1,153,128]{3,2,1,0:T(8,128)S(1)}, f32[8,1,153,128]{3,2,1,0:T(8,128)}, u32[]{:S(2)}) copy-start(f32[8,1,153,128]{3,2,1,0:T(8,128)} %slice.26) | copy-start | bytes 1880068
Sparse Core Ops, SparseCore 0:
  66.9 57.6 all-gather.2

commit v8 on v7

--- a/solution.py
+++ b/solution.py
@@ -129,10 +129,9 @@
         tok = jnp.transpose(tok.reshape(local_tokens, HEADS, width), (1, 0, 2))
         return lax.all_to_all(tok, "head", split_axis=0, concat_axis=1, tiled=True)
 
-    query_hm = to_heads(queries, KD)
+    value_hm = to_heads(values, VD)
     key_hm = to_heads(keys, KD)
-    value_hm = to_heads(values, VD)
-    heads_here, span_rows, _ = query_hm.shape
+    heads_here, span_rows, _ = key_hm.shape
     block_rows = min(512, span_rows)
     block_count = span_rows // block_rows
     first_span = lax.axis_index("ctx") == 0
@@ -151,6 +150,8 @@
     )
     span_state = jnp.sum(block_states, axis=1)
     everything = lax.all_gather(span_state, "ctx")
+    queries, span_state = lax.optimization_barrier((queries, span_state))
+    query_hm = to_heads(queries, KD)
     peers = everything.shape[0]
     here = lax.axis_index("ctx")
     entering = jnp.sum(

time: 178 us -> 169 us (0.949)
  waiting for transfers between devices: 25.1 us -> 18 us
    all_gather x1, waiting for transfers between devices: 17.2 us -> 4.51 us  [per_device(): everything = lax.all_gather(span_state, 'ctx')]
    all_to_all x3, waiting for transfers between devices: 7.43 us -> 13.1 us  [to_heads(): return lax.all_to_all(tok, 'head', split_axis=0, concat_axis=1, tiled=True)]
    optimization_barrier x0 -> x1, local copies, waits for them, and re-layouts: none -> 1.86 us  [per_device(): queries, span_state = lax.optimization_barrier((queries, span_state))]
    concatenate x1 -> x2, other arithmetic: 3.48 us -> 5.02 us  [unique_features(): return jnp.concatenate([unit, half, prod], axis=-1)]
    unnamed x19 -> x16, local copies, waits for them, and re-layouts: 6.3 us -> 5.89 us
where the time goes in v8:
time: 169 us; the launch traced here: 167 us
  local copies, waits for them, and re-layouts  33.3 us (20%)
  blocking collectives  29.3 us (17%)
  Pallas kernels  29.2 us (17%)
  waiting for transfers between devices  18 us (11%)
  starting transfers between devices  17.1 us (10%)
  other arithmetic  14.9 us (9%)
  between operations  13.6 us (8%)
  matrix products  11.2 us (7%)
    all_to_all x1, blocking collectives, per_device(): lax.all_to_all(mixed, 'head', split_axis=0, concat_axis=1, tiled=True)  29.3 us
    pallas_call x1, Pallas kernels, local_attention(): pl.pallas_call(body, grid_spec=pltpu.PrefetchScalarGridSpec(num_scalar_pr...  20.8 us
    all_to_all x3, waiting for transfers between devices, to_heads(): return lax.all_to_all(tok, 'head', split_axis=0, concat_axis=1, tiled=True)  13.1 us
    all_to_all x3, starting transfers between devices, to_heads(): return lax.all_to_all(tok, 'head', split_axis=0, concat_axis=1, tiled=True)  12.2 us
    pallas_call x1, Pallas kernels, mix(): pl.pallas_call(mix_kernel, grid=(heads_here,), in_specs=[tile, pl.BlockSp...  8.42 us
    all_to_all x4, local copies, waits for them, and re-layouts, to_heads(): return lax.all_to_all(tok, 'head', split_axis=0, concat_axis=1, tiled=True)  7.41 us
    unnamed x16, local copies, waits for them, and re-layouts  5.89 us
    concatenate x2, other arithmetic, unique_features(): return jnp.concatenate([unit, half, prod], axis=-1)  5.02 us
  transfers between devices with their start and end apart: 5, of which 5 were waited for; matrix products, arithmetic and copies ran while one was open for 25% of the time, Pallas kernels for 12%

profile of v8, /device:TPU:0, one launch (start us, length us, event | category | flops | bytes accessed | tf_op | source)
XLA Modules:
  0.0 166.7 jit_solution(14895608057743914588)
XLA Ops:
  6.5 1.8 %copy.102 = bf16[256,512]{0,1:T(8,128)(2,1)} copy(bf16[256,512]{1,0:T(8,128)(2,1)} %param.10) | data formatting | bytes 524288 | tf_op args[1]
  8.3 4.2 %all-to-all-start = ((bf16[32,256,16]{1,2,0:T(8,128)(2,1)}), bf16[32,256,16]{1,2,0:T(8,128)(2,1)S(1)}, u32[]{:S(2)}, u32[]{:S(2)}) async-start(bf16[32,256,16]{1,2,0:T(8,128)(2,1)} %bitcast.2), calls=%async_computation | async-start | bytes 524288 | tf_op jit(solution)/shard_map/all_to_all | solution.py:130
  12.5 4.1 %copy.108 = bf16[256,4096]{0,1:T(8,128)(2,1)} copy(bf16[256,4096]{1,0:T(8,128)(2,1)} %param.11) | data formatting | bytes 4194304 | tf_op args[2]
  16.6 2.0 %all-to-all-done = bf16[32,256,16]{1,2,0:T(8,128)(2,1)S(1)} async-done(((bf16[32,256,16]{1,2,0:T(8,128)(2,1)}), bf16[32,256,16]{1,2,0:T(8,128)(2,1)S(1)}, u32[]{:S(2)}, u32[]{:S(2)}) %all-to-all-start) | async-done | bytes 262176 | tf_op jit(solution)/shard_map/all_to_all | solution.py:130
  18.6 4.5 %all-to-all-start.1 = ((bf16[32,256,128]{1,2,0:T(8,128)(2,1)}), bf16[32,256,128]{1,2,0:T(8,128)(2,1)}, u32[]{:S(2)}, u32[]{:S(2)}) async-start(bf16[32,256,128]{1,2,0:T(8,128)(2,1)} %bitcast.10), calls=%async_computation.1 | async-start | bytes 4194304 | tf_op jit(solution)/shard_map/all_to_all | solution.py:130
  24.1 1.9 %convert_multiply_fusion.1 = bf16[8,1024,16]{2,1,0:T(8,128)(2,1)} fusion(bf16[8,4,256,16]{3,2,1,0:T(8,128)(2,1)S(1)} %copy.103), kind=kLoop, calls=%fused_computation.3 | loop fusion | flops 393216 | bytes 524288 | tf_op jit(solution)/shard_map/mul | solution.py:38
  26.0 1.8 %copy.104 = bf16[8,1024,16]{1,2,0:T(8,128)(2,1)S(1)} copy(bf16[8,1024,16]{2,1,0:T(8,128)(2,1)} %convert_multiply_fusion.1) | data formatting | bytes 524288 | tf_op jit(solution)/shard_map/mul | solution.py:38
  27.9 1.5 fusion.10
  29.4 1.5 fusion.6
  31.0 2.5 %pad_maximum_fusion = bf16[8,1024,153]{1,2,0:T(8,128)(2,1)} fusion(bf16[8,1024,136]{1,2,0:T(8,128)(2,1)S(1)} %fusion.6, bf16[8,1024,16]{1,2,0:T(8,128)(2,1)S(1)} %copy.104, bf16[153]{0:T(256)(128)(2,1)S(1)} %pad.9.clone), kind=kLoop, calls=%fused_computation.4 | loop fusion | flops 7520256 | bytes 4997426 | tf_op jit(solution)/shard_map/concatenate | solution.py:39
  33.5 4.6 %reshape.54 = bf16[8,2,512,153]{2,1,3,0:T(2,128)(2,1)} reshape(bf16[8,1024,153]{1,2,0:T(8,128)(2,1)} %pad_maximum_fusion) | data formatting | bytes 5013504 | tf_op jit(solution)/shard_map/reshape | solution.py:147
  38.1 10.7 %all-to-all-done.1 = bf16[32,256,128]{1,2,0:T(8,128)(2,1)} async-done(((bf16[32,256,128]{1,2,0:T(8,128)(2,1)}), bf16[32,256,128]{1,2,0:T(8,128)(2,1)}, u32[]{:S(2)}, u32[]{:S(2)}) %all-to-all-start.1) | async-done | bytes 2097184 | tf_op jit(solution)/shard_map/all_to_all | solution.py:130
  48.8 3.9 %copy.110 = bf16[8,4,256,128]{3,2,1,0:T(8,128)(2,1)} copy(bf16[8,4,256,128]{2,3,0,1:T(8,128)(2,1)} %bitcast.13) | data formatting | bytes 4194304 | tf_op jit(solution)/shard_map/all_to_all | solution.py:130
  52.7 3.2 %fusion.9 = (f32[8,153,128]{2,1,0:T(8,128)S(1)}, f32[8,2,153,128]{3,2,1,0:T(8,128)S(1)}) fusion(bf16[8,2,512,128]{3,2,1,0:T(8,128)(2,1)} %bitcast.63, bf16[8,2,512,153]{2,1,3,0:T(2,128)(2,1)} %reshape.54), kind=kOutput, calls=%fused_computation.20 | convolution fusion | flops 321020928 | bytes 6483968 | tf_op jit(solution)/shard_map/hnrf,hnrv->hnfv/dot_general | solution.py:145
  56.0 1.2 copy.121
  57.2 1.8 %pad_maximum_fusion.3 = bf16[8,64,144]{2,1,0:T(8,128)(2,1)} fusion(bf16[8,1024,128]{2,1,0:T(8,128)(2,1)} %bitcast.64, bf16[8,1024,16]{2,1,0:T(8,128)(2,1)S(1)} %bitcast.58), kind=kLoop, calls=%fused_computation.17 | loop fusion | flops 294912 | bytes 2506752 | tf_op jit(solution)/shard_map/concatenate | solution.py:140
  58.9 4.8 %collective-permute-start = (bf16[8,64,144]{2,1,0:T(8,128)(2,1)}, bf16[8,64,144]{2,1,0:T(8,128)(2,1)}, u32[]{:S(2)}, u32[]{:S(2)}) collective-permute-start(bf16[8,64,144]{2,1,0:T(8,128)(2,1)} %pad_maximum_fusion.3), channel_id=1, source_target_pairs={{0,4},{4,8},{8,12},{1,5},{5,9},{9,13},{2,6},{6,10},{10,14},{3,7},{... | collective-permute-start | bytes 442376 | tf_op jit(solution)/shard_map/ppermute | solution.py:24
  63.8 1.4 copy.116
  66.1 1.9 %copy.112 = bf16[256,512]{0,1:T(8,128)(2,1)} copy(bf16[256,512]{1,0:T(8,128)(2,1)} %param.9) | data formatting | bytes 524288 | tf_op jit(solution)/shard_map/optimization_barrier | solution.py:153
  67.9 3.6 %all-to-all-start.2 = ((bf16[32,256,16]{1,2,0:T(8,128)(2,1)}), bf16[32,256,16]{1,2,0:T(8,128)(2,1)S(1)}, u32[]{:S(2)}, u32[]{:S(2)}) async-start(bf16[32,256,16]{1,2,0:T(8,128)(2,1)} %bitcast.16), calls=%async_computation.2 | async-start | bytes 524288 | tf_op jit(solution)/shard_map/all_to_all | solution.py:130
  73.0 2.0 %pad_maximum_fusion.2.refs_3_ = bf16[8,1152,128]{2,1,0:T(8,128)(2,1)} fusion(bf16[8,1024,128]{2,1,0:T(8,128)(2,1)S(1)} %bitcast.65, bf16[8,64,128]{2,1,0:T(8,128)(2,1)S(1)} %slice.25, bf16[1152]{0:T(1024)(128)(2,1)S(1)} %pad.4.clone), kind=kLoop, calls=%fused_computation.12 | loop fusion | flops 7077888 | bytes 4589824 | tf_op jit(solution)/shard_map/concatenate | solution.py:178
  78.4 2.0 %convert_multiply_fusion = bf16[8,1024,16]{2,1,0:T(8,128)(2,1)} fusion(bf16[8,4,256,16]{3,2,1,0:T(8,128)(2,1)S(1)} %copy.113), kind=kLoop, calls=%fused_computation.2 | loop fusion | flops 393216 | bytes 524288 | tf_op jit(solution)/shard_map/mul | solution.py:38
  80.4 1.8 %copy.117 = bf16[8,1024,16]{1,2,0:T(8,128)(2,1)S(1)} copy(bf16[8,1024,16]{2,1,0:T(8,128)(2,1)} %convert_multiply_fusion) | data formatting | bytes 524288 | tf_op jit(solution)/shard_map/mul | solution.py:38
  83.9 2.5 %pad_maximum_fusion.1 = bf16[8,1024,153]{1,2,0:T(8,128)(2,1)} fusion(bf16[8,1024,136]{1,2,0:T(8,128)(2,1)S(1)} %fusion.5, bf16[8,1024,16]{1,2,0:T(8,128)(2,1)S(1)} %copy.117, bf16[153]{0:T(256)(128)(2,1)S(1)} %pad.9.clone), kind=kLoop, calls=%fused_computation.5 | loop fusion | flops 7520256 | bytes 4997426 | tf_op jit(solution)/shard_map/concatenate | solution.py:39
  86.4 3.3 %reshape.55 = bf16[8,2,512,153]{2,1,3,0:T(2,128)(2,1)S(1)} reshape(bf16[8,1024,153]{1,2,0:T(8,128)(2,1)} %pad_maximum_fusion.1) | data formatting | bytes 5013504 | tf_op jit(solution)/shard_map/reshape | solution.py:171
  89.7 20.8 %shard_map.91 = (f32[1024,1024]{1,0:T(8,128)}, f32[1024,1024]{1,0:T(8,128)}) custom-call(s32[1]{0:T(128)} %bitcast.refs_0_, bf16[8,1024,16]{2,1,0:T(8,128)(2,1)} %bitcast.62, bf16[8,16,1152]{2,1,0:T(8,128)(2,1)} %bitcast.69, bf16[8,1152,128]{2,1,0:T(8,128)(2,1)} %pad_maximum_fusion.2.refs_3_), custom_call_target="tpu_custom_call" | custom-call | tf_op jit(solution)/shard_map/pallas_call | solution.py:83
  110.4 4.5 %all-gather.3.cloned.1.call-done = f32[32,153,128]{2,0,1:T(8,128)} async-done(((f32[8,153,128]{2,0,1:T(8,128)}), f32[32,153,128]{2,0,1:T(8,128)}) %all-gather.3.cloned.1.call-update) | async-done | bytes 2506768 | tf_op jit(solution)/shard_map/all_gather | solution.py:152
  115.0 2.2 %fusion.4 = f32[8,153,128]{2,0,1:T(8,128)S(1)} fusion(f32[32,153,128]{2,0,1:T(8,128)} %all-gather.3.cloned.1.call-done, pred[4]{0:T(512)(128)(4,1)S(1)} %iota_compare_fusion), kind=kLoop, calls=%fused_computation.11 | loop fusion | flops 1096704 | bytes 3133444 | tf_op jit(solution)/shard_map/reduce_sum | solution.py:157
  117.3 3.4 %fusion = f32[8,2,512,128]{3,2,1,0:T(8,128)} fusion(bf16[8,2,512,153]{2,1,3,0:T(2,128)(2,1)S(1)} %reshape.55, f32[8,1,153,128]{3,2,1,0:T(8,128)S(1)} %copy-done.2, f32[8,153,128]{2,1,0:T(8,128)S(1)} %copy.122), kind=kOutput, calls=%fused_computation.6 | convolution fusion | flops 321490944 | bytes 7954432 | tf_op jit(solution)/shard_map/hnrf,hnfv->hnrv/dot_general | solution.py:169
  120.7 8.4 %shard_map.92 = bf16[1024,1024]{1,0:T(8,128)(2,1)} custom-call(f32[1024,1024]{1,0:T(8,128)} %get-tuple-element.9.intra_ref, f32[8,1024,128]{2,1,0:T(8,128)} %bitcast.66, f32[1024,1024]{1,0:T(8,128)} %get-tuple-element.10.win_ref, f32[1,1024]{1,0:T(1,128)} %bitcast.72), custom_call_target="tpu_custom_call" | custom-call | tf_op jit(solution)/shard_map/pallas_call | solution.py:111
  129.1 29.3 %all_to_all.73 = bf16[4,256,1024]{2,1,0:T(8,128)(2,1)S(1)} all-to-all(bf16[4,256,1024]{2,1,0:T(8,128)(2,1)} %bitcast.68), channel_id=1, replica_groups=mesh['groups'=2,'ctx'=4,'head'=4] {'head'}, dimensions={0} | all-to-all | bytes 4194304 | tf_op jit(solution)/shard_map/all_to_all | solution.py:184
  158.4 1.5 copy.135
  (33 shorter events, 8.4 us)
Async XLA Ops:
  8.3 10.2 %all-to-all-start = ((bf16[32,256,16]{1,2,0:T(8,128)(2,1)}), bf16[32,256,16]{1,2,0:T(8,128)(2,1)S(1)}, u32[]{:S(2)}, u32[]{:S(2)}) async-start(bf16[32,256,16]{1,2,0:T(8,128)(2,1)} %bitcast.2), calls=%async_computation | async-start | bytes 524288 | tf_op jit(solution)/shard_map/all_to_all | solution.py:130
  18.6 30.2 %all-to-all-start.1 = ((bf16[32,256,128]{1,2,0:T(8,128)(2,1)}), bf16[32,256,128]{1,2,0:T(8,128)(2,1)}, u32[]{:S(2)}, u32[]{:S(2)}) async-start(bf16[32,256,128]{1,2,0:T(8,128)(2,1)} %bitcast.10), calls=%async_computation.1 | async-start | bytes 4194304 | tf_op jit(solution)/shard_map/all_to_all | solution.py:130
  23.0 91.9 %all-gather.3.cloned.1.call-start = ((), (), s32[]{:S(2)}) async-start(), calls=%async_computation.4 | async-start | bytes 3133440 | tf_op jit(solution)/shard_map/all_gather | solution.py:152
  24.1 3.7 %copy-start.5 = (bf16[16,136,1]{1,0,2:T(8,128)(2,1)S(1)}, bf16[16,136,1]{1,0,2:T(8,128)(2,1)}, u32[]{:S(2)}) copy-start(bf16[16,136,1]{1,0,2:T(8,128)(2,1)} %constant.34) | copy-start | bytes 13060
  27.9 1.5 copy-start.4
  58.9 13.0 %collective-permute-start = (bf16[8,64,144]{2,1,0:T(8,128)(2,1)}, bf16[8,64,144]{2,1,0:T(8,128)(2,1)}, u32[]{:S(2)}, u32[]{:S(2)}) collective-permute-start(bf16[8,64,144]{2,1,0:T(8,128)(2,1)} %pad_maximum_fusion.3), channel_id=1, source_target_pairs={{0,4},{4,8},{8,12},{1,5},{5,9},{9,13},{2,6},{6,10},{10,14},{3,7},{... | collective-permute-start | bytes 442376 | tf_op jit(solution)/shard_map/ppermute | solution.py:24
  65.2 7.8 %copy-start.1 = (bf16[8,4,256,128]{3,2,1,0:T(8,128)(2,1)S(1)}, bf16[8,4,256,128]{3,2,1,0:T(8,128)(2,1)}, u32[]{:S(2)}) copy-start(bf16[8,4,256,128]{3,2,1,0:T(8,128)(2,1)} %copy.110) | copy-start | bytes 6291460
  67.9 9.4 %all-to-all-start.2 = ((bf16[32,256,16]{1,2,0:T(8,128)(2,1)}), bf16[32,256,16]{1,2,0:T(8,128)(2,1)S(1)}, u32[]{:S(2)}, u32[]{:S(2)}) async-start(bf16[32,256,16]{1,2,0:T(8,128)(2,1)} %bitcast.16), calls=%async_computation.2 | async-start | bytes 524288 | tf_op jit(solution)/shard_map/all_to_all | solution.py:130
  73.0 3.1 %copy-start.3 = (bf16[8,1024,16]{1,2,0:T(8,128)(2,1)S(1)}, bf16[8,1024,16]{1,2,0:T(8,128)(2,1)}, u32[]{:S(2)}) copy-start(bf16[8,1024,16]{1,2,0:T(8,128)(2,1)} %copy.116) | copy-start | bytes 786436
  78.4 4.7 %copy-start = (bf16[8,4,256,16]{3,2,1,0:T(8,128)(2,1)}, bf16[8,4,256,16]{3,2,1,0:T(8,128)(2,1)S(1)}, u32[]{:S(2)}) copy-start(bf16[8,4,256,16]{3,2,1,0:T(8,128)(2,1)S(1)} %copy.113) | copy-start | bytes 786436
  82.2 0.8 copy-start.6
  110.4 6.9 %copy-start.2 = (f32[8,1,153,128]{3,2,1,0:T(8,128)S(1)}, f32[8,1,153,128]{3,2,1,0:T(8,128)}, u32[]{:S(2)}) copy-start(f32[8,1,153,128]{3,2,1,0:T(8,128)} %slice.26) | copy-start | bytes 1880068
Sparse Core Ops, SparseCore 0:
  57.3 57.6 all-gather.2

commit v9 on v8

--- a/solution.py
+++ b/solution.py
@@ -99,27 +99,32 @@
     )(flag, q_hm, kt_hm, vx)
 
 
-def mix_kernel(intra_ref, inter_ref, win_ref, gain_ref, out_ref):
-    linear = intra_ref[...] + inter_ref[0]
-    scale = lax.rsqrt(jnp.mean(linear * linear, axis=1, keepdims=True) + epsilon)
-    out_ref[...] = (linear * scale * gain_ref[...] + win_ref[...]).astype(jnp.bfloat16)
+def mix_kernel(intra_ref, qf_ref, st_ref, win_ref, gain_ref, out_ref, *, block_rows):
+    for n in range(qf_ref.shape[1]):
+        rows = slice(n * block_rows, (n + 1) * block_rows)
+        inter = jnp.dot(qf_ref[0, n], st_ref[0, n], preferred_element_type=jnp.float32)
+        linear = intra_ref[rows, :] + inter
+        scale = lax.rsqrt(jnp.mean(linear * linear, axis=1, keepdims=True) + epsilon)
+        out_ref[rows, :] = (linear * scale * gain_ref[...] + win_ref[rows, :]).astype(jnp.bfloat16)
 
 
-def mix(intra, inter_hm, window, gain):
-    heads_here, span_rows, _ = inter_hm.shape
+def mix(intra, query_feat, states, window, gain):
+    heads_here, block_count, block_rows, feat = query_feat.shape
+    span_rows = block_count * block_rows
     tile = pl.BlockSpec((span_rows, VD), lambda h: (0, h))
     return pl.pallas_call(
-        mix_kernel,
+        lambda *refs: mix_kernel(*refs, block_rows=block_rows),
         grid=(heads_here,),
         in_specs=[
             tile,
-            pl.BlockSpec((1, span_rows, VD), lambda h: (h, 0, 0)),
+            pl.BlockSpec((1, block_count, block_rows, feat), lambda h: (h, 0, 0, 0)),
+            pl.BlockSpec((1, block_count, feat, VD), lambda h: (h, 0, 0, 0)),
             tile,
             pl.BlockSpec((1, VD), lambda h: (0, h)),
         ],
         out_specs=tile,
         out_shape=jax.ShapeDtypeStruct((span_rows, heads_here * VD), jnp.bfloat16),
-    )(intra, inter_hm, window, gain.reshape(1, heads_here * VD))
+    )(intra, query_feat, states, window, gain.reshape(1, heads_here * VD))
 
 
 def per_device(queries, keys, values, gain):
@@ -140,11 +145,10 @@
         jnp.concatenate([key_hm, value_hm], axis=2)[:, span_rows - WINDOW :], "ctx", 1
     )
 
-    key_feat = unique_features(key_hm, False)
-    feat = key_feat.shape[-1]
+    key_feat = unique_features(key_hm.reshape(heads_here, block_count, block_rows, KD), False)
     block_states = jnp.einsum(
         "hnrf,hnrv->hnfv",
-        key_feat.reshape(heads_here, block_count, block_rows, feat),
+        key_feat,
         value_hm.reshape(heads_here, block_count, block_rows, VD),
         preferred_element_type=jnp.float32,
     )
@@ -165,13 +169,7 @@
     )
     states = (before + entering[:, None]).astype(jnp.bfloat16)
 
-    query_feat = unique_features(query_hm, True)
-    inter = jnp.einsum(
-        "hnrf,hnfv->hnrv",
-        query_feat.reshape(heads_here, block_count, block_rows, feat),
-        states,
-        preferred_element_type=jnp.float32,
-    ).reshape(heads_here, span_rows, VD)
+    query_feat = unique_features(query_hm.reshape(heads_here, block_count, block_rows, KD), True)
 
     lead = jnp.zeros((heads_here, LEAD - WINDOW, KD + VD), jnp.bfloat16)
     key_ext = jnp.concatenate([lead[:, :, :KD], tails[:, :, :KD], key_hm], axis=1)
@@ -180,7 +178,7 @@
     intra, window = local_attention(
         flag, query_hm, jnp.transpose(key_ext, (0, 2, 1)), value_ext, block_rows
     )
-    mixed = mix(intra, inter, window, gain)
+    mixed = mix(intra, query_feat, states, window, gain)
     tokens_back = lax.all_to_all(mixed, "head", split_axis=0, concat_axis=1, tiled=True)
     return tokens_back
 

time: 169 us -> 180 us (1.065)
  the two profiles are of different devices: /device:TPU:0 before, /device:TPU:16 now
where the time goes in v9:
time: 180 us; the launch traced here: 179 us
  waiting for transfers between devices  32.8 us (18%)
  local copies, waits for them, and re-layouts  30.2 us (17%)
  Pallas kernels  30 us (17%)
  blocking collectives  29.3 us (16%)
  other arithmetic  17.2 us (10%)
  starting transfers between devices  14.4 us (8%)
  between operations  13.7 us (8%)
  matrix products  11.2 us (6%)
    all_to_all x1, blocking collectives, per_device(): lax.all_to_all(mixed, 'head', split_axis=0, concat_axis=1, tiled=True)  29.3 us
    all_to_all x3, waiting for transfers between devices, to_heads(): return lax.all_to_all(tok, 'head', split_axis=0, concat_axis=1, tiled=True)  24.2 us
    pallas_call x1, Pallas kernels, local_attention(): pl.pallas_call(body, grid_spec=pltpu.PrefetchScalarGridSpec(num_scalar_pr...  20.9 us
    all_to_all x3, starting transfers between devices, to_heads(): return lax.all_to_all(tok, 'head', split_axis=0, concat_axis=1, tiled=True)  10.9 us
    pallas_call x1, Pallas kernels, mix(): pl.pallas_call(lambda *refs: mix_kernel(*refs, block_rows=block_rows), gr...  9.07 us
    ppermute x1, waiting for transfers between devices, shifted(): return lax.ppermute(shard, axis, pairs)  8.6 us
    mul x1, local copies, waits for them, and re-layouts, unique_features(): prod = (first * second * outer_scale).astype(jnp.bfloat16)  7.85 us
    unnamed x26, local copies, waits for them, and re-layouts  7.84 us
  transfers between devices with their start and end apart: 5, of which 3 were waited for; matrix products, arithmetic and copies ran while one was open for 23% of the time, Pallas kernels for 12%

profile of v9, /device:TPU:16, one launch (start us, length us, event | category | flops | bytes accessed | tf_op | source)
XLA Modules:
  0.0 178.6 jit_solution(4169097532877263179)
XLA Ops:
  6.5 1.8 %copy.117 = bf16[256,512]{0,1:T(8,128)(2,1)} copy(bf16[256,512]{1,0:T(8,128)(2,1)} %param.10) | data formatting | bytes 524288 | tf_op args[1]
  8.3 3.4 %all-to-all-start = ((bf16[32,256,16]{1,2,0:T(8,128)(2,1)}), bf16[32,256,16]{1,2,0:T(8,128)(2,1)S(1)}, u32[]{:S(2)}, u32[]{:S(2)}) async-start(bf16[32,256,16]{1,2,0:T(8,128)(2,1)} %bitcast.2), calls=%async_computation | async-start | bytes 524288 | tf_op jit(solution)/shard_map/all_to_all | solution.py:135
  11.7 4.1 %copy.124 = bf16[256,4096]{0,1:T(8,128)(2,1)} copy(bf16[256,4096]{1,0:T(8,128)(2,1)} %param.11) | data formatting | bytes 4194304 | tf_op args[2]
  15.8 1.9 %all-to-all-done = bf16[32,256,16]{1,2,0:T(8,128)(2,1)S(1)} async-done(((bf16[32,256,16]{1,2,0:T(8,128)(2,1)}), bf16[32,256,16]{1,2,0:T(8,128)(2,1)S(1)}, u32[]{:S(2)}, u32[]{:S(2)}) %all-to-all-start) | async-done | bytes 262176 | tf_op jit(solution)/shard_map/all_to_all | solution.py:135
  17.7 3.7 %all-to-all-start.1 = ((bf16[32,256,128]{1,2,0:T(8,128)(2,1)}), bf16[32,256,128]{1,2,0:T(8,128)(2,1)S(1)}, u32[]{:S(2)}, u32[]{:S(2)}) async-start(bf16[32,256,128]{1,2,0:T(8,128)(2,1)} %bitcast.11), calls=%async_computation.1 | async-start | bytes 4194304 | tf_op jit(solution)/shard_map/all_to_all | solution.py:135
  22.8 2.1 %fusion.7 = bf16[8,2,512,136]{2,3,1,0:T(8,128)(2,1)} fusion(f32[136,8,2,512]{3,0,2,1:T(8,128)S(1)} %fusion.10, bf16[16,136,1,1]{1,0,3,2:T(8,128)(2,1)S(1)} %copy-done.6, bf16[8,2,512,16]{2,1,3,0:T(2,128)(2,1)S(1)} %reshape.41), kind=kOutput, calls=%fused_computation.13 | convolution fusion | flops 38993920 | bytes 6951168 | tf_op jit(solution)/shard_map/...d,df->...f/dot_general | solution.py:32
  24.9 22.2 %all-to-all-done.1 = bf16[32,256,128]{1,2,0:T(8,128)(2,1)S(1)} async-done(((bf16[32,256,128]{1,2,0:T(8,128)(2,1)}), bf16[32,256,128]{1,2,0:T(8,128)(2,1)S(1)}, u32[]{:S(2)}, u32[]{:S(2)}) %all-to-all-start.1) | async-done | bytes 2097184 | tf_op jit(solution)/shard_map/all_to_all | solution.py:135
  47.2 1.3 copy-done.4
  48.5 3.0 %copy.126 = bf16[8,4,256,128]{3,2,1,0:T(8,128)(2,1)S(1)} copy(bf16[8,4,256,128]{2,3,0,1:T(8,128)(2,1)} %bitcast.66) | data formatting | bytes 4194304 | tf_op jit(solution)/shard_map/all_to_all | solution.py:135
  51.5 4.7 %fusion.13 = (f32[8,153,128]{2,1,0:T(8,128)S(1)}, f32[8,2,153,128]{3,2,1,0:T(8,128)}) fusion(bf16[8,2,512,128]{3,2,1,0:T(8,128)(2,1)S(1)} %bitcast.63, bf16[8,2,512,136]{2,3,1,0:T(8,128)(2,1)} %fusion.7, bf16[8,2,512,16]{2,3,1,0:T(8,128)(2,1)S(1)} %multiply_convert_fusion.3, bf16[153]{0:T(256)(128)(2,1)S(1)} %pad.9.clone), kind=kOutput, calls=%fused_computation.24 | convolution fusion | flops 328541184 | bytes 6467890 | tf_op jit(solution)/shard_map/hnrf,hnrv->hnfv/dot_general | solution.py:149
  56.2 1.2 copy.137
  57.4 1.0 copy.129
  58.5 1.1 pad_maximum_fusion.2
  59.6 3.5 %collective-permute-start = (bf16[8,64,144]{2,1,0:T(8,128)(2,1)S(1)}, bf16[8,64,144]{2,1,0:T(8,128)(2,1)}, u32[]{:S(2)}, u32[]{:S(2)}) collective-permute-start(bf16[8,64,144]{2,1,0:T(8,128)(2,1)S(1)} %pad_maximum_fusion.2), channel_id=1, source_target_pairs={{0,4},{4,8},{8,12},{1,5},{5,9},{9,13},{2,6},{6,10},{10,14},{3,7},{... | collective-permute-start | bytes 442376 | tf_op jit(solution)/shard_map/ppermute | solution.py:24
  65.0 0.8 copy.127
  65.8 3.7 %all-to-all-start.2 = ((bf16[32,256,16]{1,2,0:T(8,128)(2,1)}), bf16[32,256,16]{1,2,0:T(8,128)(2,1)S(1)}, u32[]{:S(2)}, u32[]{:S(2)}) async-start(bf16[32,256,16]{1,2,0:T(8,128)(2,1)} %bitcast.17), calls=%async_computation.2 | async-start | bytes 524288 | tf_op jit(solution)/shard_map/all_to_all | solution.py:135
  69.5 1.1 slice.26
  70.7 8.6 %collective-permute-done = bf16[8,64,144]{2,1,0:T(8,128)(2,1)} collective-permute-done((bf16[8,64,144]{2,1,0:T(8,128)(2,1)S(1)}, bf16[8,64,144]{2,1,0:T(8,128)(2,1)}, u32[]{:S(2)}, u32[]{:S(2)}) %collective-permute-start) | collective-permute-done | bytes 147488 | tf_op jit(solution)/shard_map/ppermute | solution.py:24
  79.3 1.1 slice.25
  80.4 2.7 %pad_maximum_fusion.1.refs_3_ = bf16[8,1152,128]{2,1,0:T(8,128)(2,1)} fusion(bf16[8,1024,128]{2,1,0:T(8,128)(2,1)S(1)} %bitcast.65, bf16[8,64,128]{2,1,0:T(8,128)(2,1)S(1)} %slice.25, bf16[1152]{0:T(1024)(128)(2,1)} %pad.4.clone), kind=kLoop, calls=%fused_computation.12 | loop fusion | flops 7077888 | bytes 4589824 | tf_op jit(solution)/shard_map/concatenate | solution.py:176
  83.0 0.9 slice.24
  84.9 1.0 copy.128
  87.2 2.9 %convolution_multiply_fusion = f32[8,2,512,136]{2,3,1,0:T(8,128)} fusion(f32[8,2,512,136]{2,3,1,0:T(8,128)S(1)} %fusion.14, bf16[8,2,512,16]{3,2,1,0:T(8,128)(2,1)S(1)} %bitcast.58, bf16[16,136,1,1]{1,0,3,2:T(8,128)(2,1)S(1)} %copy-done.6), kind=kOutput, calls=%fused_computation.14 | convolution fusion | flops 36765696 | bytes 9179392 | tf_op jit(solution)/shard_map/...d,df->...f/dot_general | solution.py:32
  90.1 7.8 %copy.136 = f32[8,2,512,136]{3,2,1,0:T(8,128)} copy(f32[8,2,512,136]{2,3,1,0:T(8,128)} %convolution_multiply_fusion) | data formatting | bytes 8912896 | tf_op jit(solution)/shard_map/mul | solution.py:33
  97.9 20.9 %shard_map.91 = (f32[1024,1024]{1,0:T(8,128)}, f32[1024,1024]{1,0:T(8,128)}) custom-call(s32[1]{0:T(128)} %bitcast.refs_0_, bf16[8,1024,16]{2,1,0:T(8,128)(2,1)} %bitcast.59, bf16[8,16,1152]{2,1,0:T(8,128)(2,1)} %bitcast.71, bf16[8,1152,128]{2,1,0:T(8,128)(2,1)} %pad_maximum_fusion.1.refs_3_), custom_call_target="tpu_custom_call" | custom-call | tf_op jit(solution)/shard_map/pallas_call | solution.py:83
  119.5 4.4 %fusion = bf16[8,2,512,136]{3,2,1,0:T(8,128)(2,1)S(1)} fusion(f32[8,2,512,136]{3,2,1,0:T(8,128)} %copy.136, bf16[136]{0:T(256)(128)(2,1)S(1)} %copy-done.8), kind=kLoop, calls=%fused_computation.2 | loop fusion | flops 3342336 | bytes 6684944 | tf_op jit(solution)/shard_map/mul | solution.py:35
  123.9 4.7 %pad_maximum_fusion.refs_1_ = bf16[8,2,512,153]{3,2,1,0:T(8,128)(2,1)} fusion(bf16[8,2,512,136]{3,2,1,0:T(8,128)(2,1)S(1)} %fusion, bf16[8,2,512,16]{3,2,1,0:T(8,128)(2,1)S(1)} %multiply_convert_fusion.2, bf16[153]{0:T(256)(128)(2,1)S(1)} %copy-done.11), kind=kLoop, calls=%fused_computation.3 | loop fusion | flops 7520256 | bytes 4997426 | tf_op jit(solution)/shard_map/concatenate | solution.py:39
  128.7 2.2 %fusion.6 = f32[8,153,128]{2,0,1:T(8,128)S(1)} fusion(f32[32,153,128]{2,0,1:T(8,128)} %all-gather.3.cloned.1.call-done, pred[4]{0:T(512)(128)(4,1)S(1)} %copy-done.9), kind=kLoop, calls=%fused_computation.11 | loop fusion | flops 1096704 | bytes 3133444 | tf_op jit(solution)/shard_map/reduce_sum | solution.py:161
  131.0 0.9 add_convert_fusion.refs_2_
  132.0 9.1 %shard_map.92 = bf16[1024,1024]{1,0:T(8,128)(2,1)} custom-call(f32[1024,1024]{1,0:T(8,128)} %get-tuple-element.9.refs_0_, bf16[8,2,512,153]{3,2,1,0:T(8,128)(2,1)} %pad_maximum_fusion.refs_1_, bf16[8,2,153,128]{3,2,1,0:T(8,128)(2,1)} %add_convert_fusion.refs_2_, f32[1024,1024]{1,0:T(8,128)} %get-tuple-element.10.refs_3_, f32[1,1024]{1,0:T(1,128)} %bitcast.73), custom_call_target="tpu_custom_call" | custom-call | tf_op jit(solution)/shard_map/pallas_call | solution.py:115
  141.0 29.3 %all_to_all.73 = bf16[4,256,1024]{2,1,0:T(8,128)(2,1)S(1)} all-to-all(bf16[4,256,1024]{2,1,0:T(8,128)(2,1)} %bitcast.68), channel_id=1, replica_groups=mesh['groups'=2,'ctx'=4,'head'=4] {'head'}, dimensions={0} | all-to-all | bytes 4194304 | tf_op jit(solution)/shard_map/all_to_all | solution.py:182
  170.3 1.5 copy.146
  (42 shorter events, 6.2 us)
Async XLA Ops:
  8.3 9.4 %all-to-all-start = ((bf16[32,256,16]{1,2,0:T(8,128)(2,1)}), bf16[32,256,16]{1,2,0:T(8,128)(2,1)S(1)}, u32[]{:S(2)}, u32[]{:S(2)}) async-start(bf16[32,256,16]{1,2,0:T(8,128)(2,1)} %bitcast.2), calls=%async_computation | async-start | bytes 524288 | tf_op jit(solution)/shard_map/all_to_all | solution.py:135
  17.7 4.3 %copy-start.7 = (bf16[16,136,1,1]{1,0,3,2:T(8,128)(2,1)S(1)}, bf16[16,136,1,1]{1,0,3,2:T(8,128)(2,1)}, u32[]{:S(2)}) copy-start(bf16[16,136,1,1]{1,0,3,2:T(8,128)(2,1)} %constant.34) | copy-start | bytes 13060
  17.7 29.4 %all-to-all-start.1 = ((bf16[32,256,128]{1,2,0:T(8,128)(2,1)}), bf16[32,256,128]{1,2,0:T(8,128)(2,1)S(1)}, u32[]{:S(2)}, u32[]{:S(2)}) async-start(bf16[32,256,128]{1,2,0:T(8,128)(2,1)} %bitcast.11), calls=%async_computation.1 | async-start | bytes 4194304 | tf_op jit(solution)/shard_map/all_to_all | solution.py:135
  21.5 107.2 %all-gather.3.cloned.1.call-start = ((), (), s32[]{:S(2)}) async-start(), calls=%async_computation.4 | async-start | bytes 3133440 | tf_op jit(solution)/shard_map/all_gather | solution.py:156
  21.6 30.0 %copy-start.10 = (bf16[153]{0:T(256)(128)(2,1)}, bf16[153]{0:T(256)(128)(2,1)S(1)}, u32[]{:S(2)}) copy-start(bf16[153]{0:T(256)(128)(2,1)S(1)} %pad.9.clone) | copy-start | bytes 922
  22.0 0.8 copy-start.6
  47.2 1.3 copy-start.4
  51.5 4.7 %copy-start.2 = (bf16[8,4,256,128]{3,2,1,0:T(8,128)(2,1)}, bf16[8,4,256,128]{3,2,1,0:T(8,128)(2,1)S(1)}, u32[]{:S(2)}) copy-start(bf16[8,4,256,128]{3,2,1,0:T(8,128)(2,1)S(1)} %copy.126) | copy-start | bytes 6291460
  58.5 6.5 %copy-start.5 = (bf16[256,512]{1,0:T(8,128)(2,1)S(1)}, bf16[256,512]{1,0:T(8,128)(2,1)}, u32[]{:S(2)}) copy-start(bf16[256,512]{1,0:T(8,128)(2,1)} %param.9) | copy-start | bytes 786436
  59.6 19.7 %collective-permute-start = (bf16[8,64,144]{2,1,0:T(8,128)(2,1)S(1)}, bf16[8,64,144]{2,1,0:T(8,128)(2,1)}, u32[]{:S(2)}, u32[]{:S(2)}) collective-permute-start(bf16[8,64,144]{2,1,0:T(8,128)(2,1)S(1)} %pad_maximum_fusion.2), channel_id=1, source_target_pairs={{0,4},{4,8},{8,12},{1,5},{5,9},{9,13},{2,6},{6,10},{10,14},{3,7},{... | collective-permute-start | bytes 442376 | tf_op jit(solution)/shard_map/ppermute | solution.py:24
  65.0 15.4 %copy-start.3 = (bf16[8,4,256,128]{3,2,1,0:T(8,128)(2,1)S(1)}, bf16[8,4,256,128]{3,2,1,0:T(8,128)(2,1)}, u32[]{:S(2)}) copy-start(bf16[8,4,256,128]{3,2,1,0:T(8,128)(2,1)} %copy-done.2) | copy-start | bytes 6291460
  65.8 19.1 %all-to-all-start.2 = ((bf16[32,256,16]{1,2,0:T(8,128)(2,1)}), bf16[32,256,16]{1,2,0:T(8,128)(2,1)S(1)}, u32[]{:S(2)}, u32[]{:S(2)}) async-start(bf16[32,256,16]{1,2,0:T(8,128)(2,1)} %bitcast.17), calls=%async_computation.2 | async-start | bytes 524288 | tf_op jit(solution)/shard_map/all_to_all | solution.py:135
  85.9 1.3 copy-start
  97.9 20.9 %copy-start.1 = (bf16[8,4,256,16]{3,2,1,0:T(8,128)(2,1)S(1)}, bf16[8,4,256,16]{3,2,1,0:T(8,128)(2,1)}, u32[]{:S(2)}) copy-start(bf16[8,4,256,16]{3,2,1,0:T(8,128)(2,1)} %copy-done) | copy-start | bytes 786436
  118.8 0.7 copy-start.8
  119.5 4.4 %copy-start.11 = (bf16[153]{0:T(256)(128)(2,1)S(1)}, bf16[153]{0:T(256)(128)(2,1)}, u32[]{:S(2)}) copy-start(bf16[153]{0:T(256)(128)(2,1)} %copy-done.10) | copy-start | bytes 922
  123.9 4.8 %copy-start.9 = (pred[4]{0:T(512)(128)(4,1)S(1)}, pred[4]{0:T(512)(128)(4,1)}, u32[]{:S(2)}) copy-start(pred[4]{0:T(512)(128)(4,1)} %iota_compare_fusion) | copy-start | bytes 16
Sparse Core Ops, SparseCore 0:
  57.6 55.2 all-gather.2

commit v10 on v8

--- a/solution.py
+++ b/solution.py
@@ -140,11 +140,10 @@
         jnp.concatenate([key_hm, value_hm], axis=2)[:, span_rows - WINDOW :], "ctx", 1
     )
 
-    key_feat = unique_features(key_hm, False)
-    feat = key_feat.shape[-1]
+    key_feat = unique_features(key_hm.reshape(heads_here, block_count, block_rows, KD), False)
     block_states = jnp.einsum(
         "hnrf,hnrv->hnfv",
-        key_feat.reshape(heads_here, block_count, block_rows, feat),
+        key_feat,
         value_hm.reshape(heads_here, block_count, block_rows, VD),
         preferred_element_type=jnp.float32,
     )
@@ -165,10 +164,10 @@
     )
     states = (before + entering[:, None]).astype(jnp.bfloat16)
 
-    query_feat = unique_features(query_hm, True)
+    query_feat = unique_features(query_hm.reshape(heads_here, block_count, block_rows, KD), True)
     inter = jnp.einsum(
         "hnrf,hnfv->hnrv",
-        query_feat.reshape(heads_here, block_count, block_rows, feat),
+        query_feat,
         states,
         preferred_element_type=jnp.float32,
     ).reshape(heads_here, span_rows, VD)

time: 169 us -> 169 us (level)
  waiting for transfers between devices: 18 us -> 36.1 us
  local copies, waits for them, and re-layouts: 33.3 us -> 23.9 us
  other arithmetic: 14.9 us -> 6.69 us
  matrix products: 11.2 us -> 13 us
    all_to_all x3, waiting for transfers between devices: 13.1 us -> 24.4 us  [to_heads(): return lax.all_to_all(tok, 'head', split_axis=0, concat_axis=1, tiled=True)]
    reshape x2, local copies, waits for them, and re-layouts: 7.9 us -> 0.34 us  [the longest x1 0.17 us: per_device(): key_hm.reshape(heads_here, block_count, block_rows, KD)]
    all_gather x1, waiting for transfers between devices: 4.51 us -> 11.7 us  [per_device(): everything = lax.all_gather(span_state, 'ctx')]
    concatenate x2 -> x0, other arithmetic: 5.02 us -> none  [unique_features(): return jnp.concatenate([unit, half, prod], axis=-1)]
    mul x2 -> x0, other arithmetic: 3.87 us -> none  [unique_features(): half = (vector.astype(jnp.float32) * 0.5).astype(jnp.bfloat16)]
    mul x2 -> x0, local copies, waits for them, and re-layouts: 3.69 us -> none  [unique_features(): half = (vector.astype(jnp.float32) * 0.5).astype(jnp.bfloat16)]
    dot_general x2, matrix products: 6.61 us -> 8.3 us  [the longest x1 4.64 us: per_device(): jnp.einsum('hnrf,hnrv->hnfv', key_feat, value_hm.reshape(heads_here, bloc...]
    unnamed x16 -> x20, local copies, waits for them, and re-layouts: 5.89 us -> 7.21 us
  transfers between devices with their start and end apart: 5 -> 5, of which waited for: 5 -> 4; matrix products, arithmetic and copies ran while one was open for 25% -> 14% of each run, Pallas kernels for 12% -> 12%
where the time goes in v10:
time: 169 us; the launch traced here: 168 us
  waiting for transfers between devices  36.1 us (21%)
  blocking collectives  29.3 us (17%)
  Pallas kernels  29.2 us (17%)
  local copies, waits for them, and re-layouts  23.9 us (14%)
  starting transfers between devices  16.4 us (10%)
  between operations  13.7 us (8%)
  matrix products  13 us (8%)
  other arithmetic  6.69 us (4%)
    all_to_all x1, blocking collectives, per_device(): lax.all_to_all(mixed, 'head', split_axis=0, concat_axis=1, tiled=True)  29.3 us
    all_to_all x3, waiting for transfers between devices, to_heads(): return lax.all_to_all(tok, 'head', split_axis=0, concat_axis=1, tiled=True)  24.4 us
    pallas_call x1, Pallas kernels, local_attention(): pl.pallas_call(body, grid_spec=pltpu.PrefetchScalarGridSpec(num_scalar_pr...  20.8 us
    all_gather x1, waiting for transfers between devices, per_device(): everything = lax.all_gather(span_state, 'ctx')  11.7 us
    all_to_all x3, starting transfers between devices, to_heads(): return lax.all_to_all(tok, 'head', split_axis=0, concat_axis=1, tiled=True)  11.5 us
    pallas_call x1, Pallas kernels, mix(): pl.pallas_call(mix_kernel, grid=(heads_here,), in_specs=[tile, pl.BlockSp...  8.42 us
    unnamed x20, local copies, waits for them, and re-layouts  7.21 us
    all_to_all x6, local copies, waits for them, and re-layouts, to_heads(): return lax.all_to_all(tok, 'head', split_axis=0, concat_axis=1, tiled=True)  6.95 us
  transfers between devices with their start and end apart: 5, of which 4 were waited for; matrix products, arithmetic and copies ran while one was open for 14% of the time, Pallas kernels for 12%

profile of v10, /device:TPU:0, one launch (start us, length us, event | category | flops | bytes accessed | tf_op | source)
XLA Modules:
  0.0 168.2 jit_solution(6929803435106707570)
XLA Ops:
  6.5 1.8 %copy.61 = bf16[256,512]{0,1:T(8,128)(2,1)} copy(bf16[256,512]{1,0:T(8,128)(2,1)} %param.10) | data formatting | bytes 524288 | tf_op args[1]
  8.3 4.2 %all-to-all-start = ((bf16[32,256,16]{1,2,0:T(8,128)(2,1)}), bf16[32,256,16]{1,2,0:T(8,128)(2,1)S(1)}, u32[]{:S(2)}, u32[]{:S(2)}) async-start(bf16[32,256,16]{1,2,0:T(8,128)(2,1)} %bitcast.2), calls=%async_computation | async-start | bytes 524288 | tf_op jit(solution)/shard_map/all_to_all | solution.py:130
  12.5 4.1 %copy.66 = bf16[256,4096]{0,1:T(8,128)(2,1)} copy(bf16[256,4096]{1,0:T(8,128)(2,1)} %param.11) | data formatting | bytes 4194304 | tf_op args[2]
  16.6 2.0 %all-to-all-done = bf16[32,256,16]{1,2,0:T(8,128)(2,1)S(1)} async-done(((bf16[32,256,16]{1,2,0:T(8,128)(2,1)}), bf16[32,256,16]{1,2,0:T(8,128)(2,1)S(1)}, u32[]{:S(2)}, u32[]{:S(2)}) %all-to-all-start) | async-done | bytes 262176 | tf_op jit(solution)/shard_map/all_to_all | solution.py:130
  18.6 3.7 %all-to-all-start.1 = ((bf16[32,256,128]{1,2,0:T(8,128)(2,1)}), bf16[32,256,128]{1,2,0:T(8,128)(2,1)S(1)}, u32[]{:S(2)}, u32[]{:S(2)}) async-start(bf16[32,256,128]{1,2,0:T(8,128)(2,1)} %bitcast.11), calls=%async_computation.1 | async-start | bytes 4194304 | tf_op jit(solution)/shard_map/all_to_all | solution.py:130
  23.6 2.1 %fusion.12 = bf16[8,2,512,136]{2,3,1,0:T(8,128)(2,1)} fusion(f32[136,8,2,512]{3,0,2,1:T(8,128)S(1)} %fusion.20, bf16[16,136,1,1]{1,0,3,2:T(8,128)(2,1)S(1)} %copy-done.3, bf16[8,2,512,16]{2,1,3,0:T(2,128)(2,1)S(1)} %reshape.44), kind=kOutput, calls=%fused_computation.16 | convolution fusion | flops 38993920 | bytes 6951168 | tf_op jit(solution)/shard_map/...d,df->...f/dot_general | solution.py:32
  25.8 22.2 %all-to-all-done.1 = bf16[32,256,128]{1,2,0:T(8,128)(2,1)S(1)} async-done(((bf16[32,256,128]{1,2,0:T(8,128)(2,1)}), bf16[32,256,128]{1,2,0:T(8,128)(2,1)S(1)}, u32[]{:S(2)}, u32[]{:S(2)}) %all-to-all-start.1) | async-done | bytes 2097184 | tf_op jit(solution)/shard_map/all_to_all | solution.py:130
  48.0 1.3 copy-done.2
  49.3 3.0 %copy.68 = bf16[8,4,256,128]{3,2,1,0:T(8,128)(2,1)S(1)} copy(bf16[8,4,256,128]{2,3,0,1:T(8,128)(2,1)} %bitcast.61) | data formatting | bytes 4194304 | tf_op jit(solution)/shard_map/all_to_all | solution.py:130
  52.4 4.6 %fusion.25 = (f32[8,153,128]{2,1,0:T(8,128)S(1)}, f32[8,2,153,128]{3,2,1,0:T(8,128)}) fusion(bf16[8,2,512,128]{3,2,1,0:T(8,128)(2,1)S(1)} %bitcast.56, bf16[8,2,512,136]{2,3,1,0:T(8,128)(2,1)} %fusion.12, bf16[8,2,512,16]{2,3,1,0:T(8,128)(2,1)S(1)} %multiply_convert_fusion.3, bf16[153]{0:T(256)(128)(2,1)S(1)} %pad.9.clone), kind=kOutput, calls=%fused_computation.34 | convolution fusion | flops 328541184 | bytes 6467890 | tf_op jit(solution)/shard_map/hnrf,hnrv->hnfv/dot_general | solution.py:144
  57.0 1.2 copy.79
  58.2 1.0 copy.71
  59.2 1.1 pad_maximum_fusion.1
  60.3 4.8 %collective-permute-start = (bf16[8,64,144]{2,1,0:T(8,128)(2,1)S(1)}, bf16[8,64,144]{2,1,0:T(8,128)(2,1)}, u32[]{:S(2)}, u32[]{:S(2)}) collective-permute-start(bf16[8,64,144]{2,1,0:T(8,128)(2,1)S(1)} %pad_maximum_fusion.1), channel_id=1, source_target_pairs={{0,4},{4,8},{8,12},{1,5},{5,9},{9,13},{2,6},{6,10},{10,14},{3,7},{... | collective-permute-start | bytes 442376 | tf_op jit(solution)/shard_map/ppermute | solution.py:24
  66.3 0.8 copy.74
  67.1 1.3 slice.26
  68.4 1.8 %copy.69 = bf16[256,512]{0,1:T(8,128)(2,1)} copy(bf16[256,512]{1,0:T(8,128)(2,1)} %param.9) | data formatting | bytes 524288 | tf_op jit(solution)/shard_map/optimization_barrier | solution.py:152
  70.2 3.6 %all-to-all-start.2 = ((bf16[32,256,16]{1,2,0:T(8,128)(2,1)}), bf16[32,256,16]{1,2,0:T(8,128)(2,1)S(1)}, u32[]{:S(2)}, u32[]{:S(2)}) async-start(bf16[32,256,16]{1,2,0:T(8,128)(2,1)} %bitcast.17), calls=%async_computation.2 | async-start | bytes 524288 | tf_op jit(solution)/shard_map/all_to_all | solution.py:130
  73.8 1.1 slice.25
  74.9 2.7 %pad_maximum_fusion.refs_3_ = bf16[8,1152,128]{2,1,0:T(8,128)(2,1)} fusion(bf16[8,1024,128]{2,1,0:T(8,128)(2,1)S(1)} %bitcast.58, bf16[8,64,128]{2,1,0:T(8,128)(2,1)S(1)} %slice.25, bf16[1152]{0:T(1024)(128)(2,1)} %pad.4.clone), kind=kLoop, calls=%fused_computation.14 | loop fusion | flops 7077888 | bytes 4589824 | tf_op jit(solution)/shard_map/concatenate | solution.py:177
  77.6 0.9 slice.24
  78.6 0.8 concatenate.20
  79.8 1.7 %copy.70 = bf16[8,4,256,16]{3,2,1,0:T(8,128)(2,1)} copy(bf16[8,4,256,16]{2,3,0,1:T(8,128)(2,1)S(1)} %bitcast.67) | data formatting | bytes 524288 | tf_op jit(solution)/shard_map/all_to_all | solution.py:130
  81.7 20.8 %shard_map.91 = (f32[1024,1024]{1,0:T(8,128)}, f32[1024,1024]{1,0:T(8,128)}) custom-call(s32[1]{0:T(128)} %bitcast.refs_0_, bf16[8,1024,16]{2,1,0:T(8,128)(2,1)} %bitcast.60, bf16[8,16,1152]{2,1,0:T(8,128)(2,1)} %bitcast.68, bf16[8,1152,128]{2,1,0:T(8,128)(2,1)} %pad_maximum_fusion.refs_3_), custom_call_target="tpu_custom_call" | custom-call | tf_op jit(solution)/shard_map/pallas_call | solution.py:83
  102.5 0.8 fusion.17
  103.3 1.0 fusion.11
  104.4 11.7 %all-gather.3.cloned.1.call-done = f32[32,153,128]{2,0,1:T(8,128)} async-done(((f32[8,153,128]{2,0,1:T(8,128)}), f32[32,153,128]{2,0,1:T(8,128)}) %all-gather.3.cloned.1.call-update) | async-done | bytes 2506768 | tf_op jit(solution)/shard_map/all_gather | solution.py:151
  116.1 2.2 %fusion.10 = f32[8,153,128]{2,0,1:T(8,128)S(1)} fusion(f32[32,153,128]{2,0,1:T(8,128)} %all-gather.3.cloned.1.call-done, pred[4]{0:T(512)(128)(4,1)S(1)} %copy-done.8), kind=kLoop, calls=%fused_computation.13 | loop fusion | flops 1096704 | bytes 3133444 | tf_op jit(solution)/shard_map/reduce_sum | solution.py:156
  118.5 3.7 %fusion.5 = f32[8,2,512,128]{3,2,1,0:T(8,128)} fusion(bf16[8,2,512,136]{2,3,1,0:T(8,128)(2,1)S(1)} %fusion.11, bf16[8,2,512,16]{2,3,1,0:T(8,128)(2,1)S(1)} %multiply_convert_fusion.2, bf16[153]{0:T(256)(128)(2,1)S(1)} %copy-done.7, f32[8,1,153,128]{3,2,1,0:T(8,128)S(1)} %slice.26, f32[8,153,128]{2,1,0:T(8,128)S(1)} %copy.80), kind=kOutput, calls=%fused_computation.7 | convolution fusion | flops 329011200 | bytes 7938354 | tf_op jit(solution)/shard_map/hnrf,hnfv->hnrv/dot_general | solution.py:168
  122.2 8.4 %shard_map.92 = bf16[1024,1024]{1,0:T(8,128)(2,1)} custom-call(f32[1024,1024]{1,0:T(8,128)} %get-tuple-element.9.intra_ref, f32[8,1024,128]{2,1,0:T(8,128)} %bitcast.59, f32[1024,1024]{1,0:T(8,128)} %get-tuple-element.10.win_ref, f32[1,1024]{1,0:T(1,128)} %bitcast.69), custom_call_target="tpu_custom_call" | custom-call | tf_op jit(solution)/shard_map/pallas_call | solution.py:111
  130.6 29.3 %all_to_all.73 = bf16[4,256,1024]{2,1,0:T(8,128)(2,1)S(1)} all-to-all(bf16[4,256,1024]{2,1,0:T(8,128)(2,1)} %bitcast.63), channel_id=1, replica_groups=mesh['groups'=2,'ctx'=4,'head'=4] {'head'}, dimensions={0} | all-to-all | bytes 4194304 | tf_op jit(solution)/shard_map/all_to_all | solution.py:183
  159.9 1.5 copy.86
  (35 shorter events, 3.3 us)
Async XLA Ops:
  8.3 10.2 %all-to-all-start = ((bf16[32,256,16]{1,2,0:T(8,128)(2,1)}), bf16[32,256,16]{1,2,0:T(8,128)(2,1)S(1)}, u32[]{:S(2)}, u32[]{:S(2)}) async-start(bf16[32,256,16]{1,2,0:T(8,128)(2,1)} %bitcast.2), calls=%async_computation | async-start | bytes 524288 | tf_op jit(solution)/shard_map/all_to_all | solution.py:130
  18.6 4.3 %copy-start.4 = (bf16[16,136,1,1]{1,0,3,2:T(8,128)(2,1)S(1)}, bf16[16,136,1,1]{1,0,3,2:T(8,128)(2,1)}, u32[]{:S(2)}) copy-start(bf16[16,136,1,1]{1,0,3,2:T(8,128)(2,1)} %constant.34) | copy-start | bytes 13060
  18.6 29.4 %all-to-all-start.1 = ((bf16[32,256,128]{1,2,0:T(8,128)(2,1)}), bf16[32,256,128]{1,2,0:T(8,128)(2,1)S(1)}, u32[]{:S(2)}, u32[]{:S(2)}) async-start(bf16[32,256,128]{1,2,0:T(8,128)(2,1)} %bitcast.11), calls=%async_computation.1 | async-start | bytes 4194304 | tf_op jit(solution)/shard_map/all_to_all | solution.py:130
  22.3 93.8 %all-gather.3.cloned.1.call-start = ((), (), s32[]{:S(2)}) async-start(), calls=%async_computation.4 | async-start | bytes 3133440 | tf_op jit(solution)/shard_map/all_gather | solution.py:151
  22.4 30.0 %copy-start.6 = (bf16[153]{0:T(256)(128)(2,1)}, bf16[153]{0:T(256)(128)(2,1)S(1)}, u32[]{:S(2)}) copy-start(bf16[153]{0:T(256)(128)(2,1)S(1)} %pad.9.clone) | copy-start | bytes 922
  22.8 0.8 copy-start.3
  48.0 1.3 copy-start.2
  52.3 4.7 %copy-start = (bf16[8,4,256,128]{3,2,1,0:T(8,128)(2,1)}, bf16[8,4,256,128]{3,2,1,0:T(8,128)(2,1)S(1)}, u32[]{:S(2)}) copy-start(bf16[8,4,256,128]{3,2,1,0:T(8,128)(2,1)S(1)} %copy.68) | copy-start | bytes 6291460
  60.3 13.5 %collective-permute-start = (bf16[8,64,144]{2,1,0:T(8,128)(2,1)S(1)}, bf16[8,64,144]{2,1,0:T(8,128)(2,1)}, u32[]{:S(2)}, u32[]{:S(2)}) collective-permute-start(bf16[8,64,144]{2,1,0:T(8,128)(2,1)S(1)} %pad_maximum_fusion.1), channel_id=1, source_target_pairs={{0,4},{4,8},{8,12},{1,5},{5,9},{9,13},{2,6},{6,10},{10,14},{3,7},{... | collective-permute-start | bytes 442376 | tf_op jit(solution)/shard_map/ppermute | solution.py:24
  67.1 7.8 %copy-start.1 = (bf16[8,4,256,128]{3,2,1,0:T(8,128)(2,1)S(1)}, bf16[8,4,256,128]{3,2,1,0:T(8,128)(2,1)}, u32[]{:S(2)}) copy-start(bf16[8,4,256,128]{3,2,1,0:T(8,128)(2,1)} %copy-done) | copy-start | bytes 6291460
  70.2 9.4 %all-to-all-start.2 = ((bf16[32,256,16]{1,2,0:T(8,128)(2,1)}), bf16[32,256,16]{1,2,0:T(8,128)(2,1)S(1)}, u32[]{:S(2)}, u32[]{:S(2)}) async-start(bf16[32,256,16]{1,2,0:T(8,128)(2,1)} %bitcast.17), calls=%async_computation.2 | async-start | bytes 524288 | tf_op jit(solution)/shard_map/all_to_all | solution.py:130
  102.5 0.9 copy-start.5
  103.3 12.8 %copy-start.8 = (pred[4]{0:T(512)(128)(4,1)S(1)}, pred[4]{0:T(512)(128)(4,1)}, u32[]{:S(2)}) copy-start(pred[4]{0:T(512)(128)(4,1)} %iota_compare_fusion) | copy-start | bytes 16
  104.4 14.1 %copy-start.7 = (bf16[153]{0:T(256)(128)(2,1)S(1)}, bf16[153]{0:T(256)(128)(2,1)}, u32[]{:S(2)}) copy-start(bf16[153]{0:T(256)(128)(2,1)} %copy-done.6) | copy-start | bytes 922
Sparse Core Ops, SparseCore 0:
  58.3 57.7 all-gather.2

commit v11 on v9

--- a/solution.py
+++ b/solution.py
@@ -36,7 +36,7 @@
     lead = vector.shape[:-1]
     unit = jnp.ones(lead + (1,), jnp.bfloat16)
     half = (vector.astype(jnp.float32) * 0.5).astype(jnp.bfloat16)
-    return jnp.concatenate([unit, half, prod], axis=-1)
+    return jnp.concatenate([prod, half, unit], axis=-1)
 
 
 CHUNK = 128
@@ -99,32 +99,71 @@
     )(flag, q_hm, kt_hm, vx)
 
 
-def mix_kernel(intra_ref, qf_ref, st_ref, win_ref, gain_ref, out_ref, *, block_rows):
-    for n in range(qf_ref.shape[1]):
+def mix_kernel(
+    here_ref, intra_ref, win_ref, q_ref, every_ref, before_ref, pr_ref, pc_ref, w2_ref, gain_ref,
+    out_ref, *, block_rows
+):
+    here = here_ref[0]
+    entering = jnp.zeros(every_ref.shape[2:], jnp.float32)
+    for k in range(every_ref.shape[0]):
+        entering = entering + jnp.where(k < here, every_ref[k, 0], 0.0)
+    q = q_ref[0]
+    first = jnp.dot(q, pr_ref[...], preferred_element_type=jnp.float32)
+    second = jnp.dot(q, pc_ref[...], preferred_element_type=jnp.float32)
+    prod = ((first * second) * outer_scale).astype(jnp.bfloat16) * w2_ref[...]
+    half = (q.astype(jnp.float32) * 0.5).astype(jnp.bfloat16)
+    pairs = prod.shape[1]
+    for n in range(before_ref.shape[1]):
         rows = slice(n * block_rows, (n + 1) * block_rows)
-        inter = jnp.dot(qf_ref[0, n], st_ref[0, n], preferred_element_type=jnp.float32)
+        state = before_ref[0, n] + entering
+        inter = (
+            jnp.dot(prod[rows], state[:pairs].astype(jnp.bfloat16), preferred_element_type=jnp.float32)
+            + jnp.dot(
+                half[rows],
+                state[pairs : pairs + KD].astype(jnp.bfloat16),
+                preferred_element_type=jnp.float32,
+            )
+            + state[pairs + KD :].astype(jnp.bfloat16).astype(jnp.float32)
+        )
         linear = intra_ref[rows, :] + inter
         scale = lax.rsqrt(jnp.mean(linear * linear, axis=1, keepdims=True) + epsilon)
         out_ref[rows, :] = (linear * scale * gain_ref[...] + win_ref[rows, :]).astype(jnp.bfloat16)
 
 
-def mix(intra, query_feat, states, window, gain):
-    heads_here, block_count, block_rows, feat = query_feat.shape
-    span_rows = block_count * block_rows
-    tile = pl.BlockSpec((span_rows, VD), lambda h: (0, h))
+def mix(here, intra, window, query_hm, everything, before, gain):
+    heads_here, span_rows, _ = query_hm.shape
+    peers, _, feat, _ = everything.shape
+    block_count = before.shape[1]
+    rows, cols = np.triu_indices(KD)
+    pick_rows = jnp.asarray(np.eye(KD)[:, rows], jnp.bfloat16)
+    pick_cols = jnp.asarray(np.eye(KD)[:, cols], jnp.bfloat16)
+    doubled = jnp.asarray(np.where(rows == cols, 1.0, 2.0)[None, :], jnp.bfloat16)
+    pairs = rows.shape[0]
+    tile = pl.BlockSpec((span_rows, VD), lambda h, c: (0, h))
+    whole = lambda shape: pl.BlockSpec(shape, lambda h, c: (0, 0))
     return pl.pallas_call(
-        lambda *refs: mix_kernel(*refs, block_rows=block_rows),
-        grid=(heads_here,),
-        in_specs=[
-            tile,
-            pl.BlockSpec((1, block_count, block_rows, feat), lambda h: (h, 0, 0, 0)),
-            pl.BlockSpec((1, block_count, feat, VD), lambda h: (h, 0, 0, 0)),
-            tile,
-            pl.BlockSpec((1, VD), lambda h: (0, h)),
-        ],
-        out_specs=tile,
+        lambda *refs: mix_kernel(*refs, block_rows=span_rows // block_count),
+        grid_spec=pltpu.PrefetchScalarGridSpec(
+            num_scalar_prefetch=1,
+            grid=(heads_here,),
+            in_specs=[
+                tile,
+                tile,
+                pl.BlockSpec((1, span_rows, KD), lambda h, c: (h, 0, 0)),
+                pl.BlockSpec((peers, 1, feat, VD), lambda h, c: (0, h, 0, 0)),
+                pl.BlockSpec((1, block_count, feat, VD), lambda h, c: (h, 0, 0, 0)),
+                whole((KD, pairs)),
+                whole((KD, pairs)),
+                whole((1, pairs)),
+                pl.BlockSpec((1, VD), lambda h, c: (0, h)),
+            ],
+            out_specs=tile,
+        ),
         out_shape=jax.ShapeDtypeStruct((span_rows, heads_here * VD), jnp.bfloat16),
-    )(intra, query_feat, states, window, gain.reshape(1, heads_here * VD))
+    )(
+        here, intra, window, query_hm, everything, before, pick_rows, pick_cols, doubled,
+        gain.reshape(1, heads_here * VD),
+    )
 
 
 def per_device(queries, keys, values, gain):
@@ -156,20 +195,9 @@
     everything = lax.all_gather(span_state, "ctx")
     queries, span_state = lax.optimization_barrier((queries, span_state))
     query_hm = to_heads(queries, KD)
-    peers = everything.shape[0]
-    here = lax.axis_index("ctx")
-    entering = jnp.sum(
-        jnp.where(
-            (jnp.arange(peers) < here)[:, None, None, None], everything, jnp.zeros_like(everything)
-        ),
-        axis=0,
-    )
     before = jnp.concatenate(
         [jnp.zeros_like(block_states[:, :1]), jnp.cumsum(block_states[:, :-1], axis=1)], axis=1
     )
-    states = (before + entering[:, None]).astype(jnp.bfloat16)
-
-    query_feat = unique_features(query_hm.reshape(heads_here, block_count, block_rows, KD), True)
 
     lead = jnp.zeros((heads_here, LEAD - WINDOW, KD + VD), jnp.bfloat16)
     key_ext = jnp.concatenate([lead[:, :, :KD], tails[:, :, :KD], key_hm], axis=1)
@@ -178,7 +206,8 @@
     intra, window = local_attention(
         flag, query_hm, jnp.transpose(key_ext, (0, 2, 1)), value_ext, block_rows
     )
-    mixed = mix(intra, query_feat, states, window, gain)
+    here = lax.axis_index("ctx").astype(jnp.int32).reshape(1)
+    mixed = mix(here, intra, window, query_hm, everything, before, gain)
     tokens_back = lax.all_to_all(mixed, "head", split_axis=0, concat_axis=1, tiled=True)
     return tokens_back
 

time: 180 us -> 170 us (0.944)
  the two profiles are of different devices: /device:TPU:16 before, /device:TPU:0 now
where the time goes in v11:
time: 170 us; the launch traced here: 169 us
  waiting for transfers between devices  42.8 us (25%)
  Pallas kernels  31.6 us (19%)
  blocking collectives  29.3 us (17%)
  local copies, waits for them, and re-layouts  25.8 us (15%)
  starting transfers between devices  15.6 us (9%)
  between operations  13.6 us (8%)
  matrix products  7.25 us (4%)
  other arithmetic  3.08 us (2%)
    all_to_all x1, blocking collectives, per_device(): lax.all_to_all(mixed, 'head', split_axis=0, concat_axis=1, tiled=True)  29.3 us
    all_to_all x3, waiting for transfers between devices, to_heads(): return lax.all_to_all(tok, 'head', split_axis=0, concat_axis=1, tiled=True)  24.2 us
    pallas_call x1, Pallas kernels, local_attention(): pl.pallas_call(body, grid_spec=pltpu.PrefetchScalarGridSpec(num_scalar_pr...  20.7 us
    all_gather x1, waiting for transfers between devices, per_device(): everything = lax.all_gather(span_state, 'ctx')  17.5 us
    all_to_all x3, starting transfers between devices, to_heads(): return lax.all_to_all(tok, 'head', split_axis=0, concat_axis=1, tiled=True)  11.5 us
    pallas_call x1, Pallas kernels, mix(): pl.pallas_call(lambda *refs: mix_kernel(*refs, block_rows=span_rows // bl...  10.9 us
    unnamed x14, local copies, waits for them, and re-layouts  7.2 us
    all_to_all x5, local copies, waits for them, and re-layouts, to_heads(): return lax.all_to_all(tok, 'head', split_axis=0, concat_axis=1, tiled=True)  6.74 us
  transfers between devices with their start and end apart: 5, of which 4 were waited for; matrix products, arithmetic and copies ran while one was open for 11% of the time, Pallas kernels for 12%

profile of v11, /device:TPU:0, one launch (start us, length us, event | category | flops | bytes accessed | tf_op | source)
XLA Modules:
  0.0 169.0 jit_solution(6486277829004186773)
XLA Ops:
  6.5 1.8 %copy.52 = bf16[256,512]{0,1:T(8,128)(2,1)} copy(bf16[256,512]{1,0:T(8,128)(2,1)} %param.10) | data formatting | bytes 524288 | tf_op args[1]
  8.3 4.2 %all-to-all-start = ((bf16[32,256,16]{1,2,0:T(8,128)(2,1)}), bf16[32,256,16]{1,2,0:T(8,128)(2,1)S(1)}, u32[]{:S(2)}, u32[]{:S(2)}) async-start(bf16[32,256,16]{1,2,0:T(8,128)(2,1)} %bitcast.5), calls=%async_computation | async-start | bytes 524288 | tf_op jit(solution)/shard_map/all_to_all | solution.py:174
  12.5 4.1 %copy.57 = bf16[256,4096]{0,1:T(8,128)(2,1)} copy(bf16[256,4096]{1,0:T(8,128)(2,1)} %param.11) | data formatting | bytes 4194304 | tf_op args[2]
  16.6 2.0 %all-to-all-done = bf16[32,256,16]{1,2,0:T(8,128)(2,1)S(1)} async-done(((bf16[32,256,16]{1,2,0:T(8,128)(2,1)}), bf16[32,256,16]{1,2,0:T(8,128)(2,1)S(1)}, u32[]{:S(2)}, u32[]{:S(2)}) %all-to-all-start) | async-done | bytes 262176 | tf_op jit(solution)/shard_map/all_to_all | solution.py:174
  18.6 3.7 %all-to-all-start.1 = ((bf16[32,256,128]{1,2,0:T(8,128)(2,1)}), bf16[32,256,128]{1,2,0:T(8,128)(2,1)S(1)}, u32[]{:S(2)}, u32[]{:S(2)}) async-start(bf16[32,256,128]{1,2,0:T(8,128)(2,1)} %bitcast.12), calls=%async_computation.1 | async-start | bytes 4194304 | tf_op jit(solution)/shard_map/all_to_all | solution.py:174
  22.4 0.2 copy.53
  22.7 0.2 reshape.35
  22.9 0.8 fusion.8
  23.7 2.1 %fusion.5 = bf16[8,2,512,136]{2,3,1,0:T(8,128)(2,1)} fusion(f32[136,8,2,512]{3,0,2,1:T(8,128)S(1)} %fusion.8, bf16[16,136,1,1]{1,0,3,2:T(8,128)(2,1)S(1)} %copy-done.4, bf16[8,2,512,16]{2,1,3,0:T(2,128)(2,1)S(1)} %reshape.35), kind=kOutput, calls=%fused_computation.7 | convolution fusion | flops 38993920 | bytes 6951168 | tf_op jit(solution)/shard_map/...d,df->...f/dot_general | solution.py:32
  25.8 22.2 %all-to-all-done.1 = bf16[32,256,128]{1,2,0:T(8,128)(2,1)S(1)} async-done(((bf16[32,256,128]{1,2,0:T(8,128)(2,1)}), bf16[32,256,128]{1,2,0:T(8,128)(2,1)S(1)}, u32[]{:S(2)}, u32[]{:S(2)}) %all-to-all-start.1) | async-done | bytes 2097184 | tf_op jit(solution)/shard_map/all_to_all | solution.py:174
  48.0 1.3 copy-done.2
  49.3 3.0 %copy.59 = bf16[8,4,256,128]{3,2,1,0:T(8,128)(2,1)S(1)} copy(bf16[8,4,256,128]{2,3,0,1:T(8,128)(2,1)} %bitcast.56) | data formatting | bytes 4194304 | tf_op jit(solution)/shard_map/all_to_all | solution.py:174
  52.4 4.4 %fusion.11 = (f32[8,153,128]{2,1,0:T(8,128)S(1)}, f32[8,2,153,128]{3,2,1,0:T(8,128)}) fusion(bf16[8,2,512,128]{3,2,1,0:T(8,128)(2,1)S(1)} %bitcast.51, bf16[8,2,512,16]{2,3,1,0:T(8,128)(2,1)S(1)} %multiply_convert_fusion.1, bf16[8,2,512,136]{2,3,1,0:T(8,128)(2,1)} %fusion.5, bf16[153]{0:T(256)(128)(2,1)S(1)} %pad.8.clone), kind=kOutput, calls=%fused_computation.15 | convolution fusion | flops 328541184 | bytes 6467890 | tf_op jit(solution)/shard_map/hnrf,hnrv->hnfv/dot_general | solution.py:188
  56.7 1.2 copy.66
  58.0 1.0 copy.62
  59.0 1.1 pad_maximum_fusion.1
  60.1 4.1 %collective-permute-start = (bf16[8,64,144]{2,1,0:T(8,128)(2,1)S(1)}, bf16[8,64,144]{2,1,0:T(8,128)(2,1)S(1)}, u32[]{:S(2)}, u32[]{:S(2)}) collective-permute-start(bf16[8,64,144]{2,1,0:T(8,128)(2,1)S(1)} %pad_maximum_fusion.1), channel_id=1, source_target_pairs={{0,4},{4,8},{8,12},{1,5},{5,9},{9,13},{2,6},{6,10},{10,14},{3,7},{... | collective-permute-start | bytes 442376 | tf_op jit(solution)/shard_map/ppermute | solution.py:24
  64.3 0.8 copy.65
  65.1 0.8 copy.60
  65.9 3.5 %all-to-all-start.2 = ((bf16[32,256,16]{1,2,0:T(8,128)(2,1)}), bf16[32,256,16]{1,2,0:T(8,128)(2,1)S(1)}, u32[]{:S(2)}, u32[]{:S(2)}) async-start(bf16[32,256,16]{1,2,0:T(8,128)(2,1)} %bitcast.18), calls=%async_computation.2 | async-start | bytes 524288 | tf_op jit(solution)/shard_map/all_to_all | solution.py:174
  69.5 1.1 slice.26
  70.6 1.2 concatenate.19.refs_5_
  71.8 1.2 collective-permute-done
  73.1 1.9 %pad_maximum_fusion.refs_3_ = bf16[8,1152,128]{2,1,0:T(8,128)(2,1)} fusion(bf16[8,1024,128]{2,1,0:T(8,128)(2,1)S(1)} %bitcast.53, bf16[8,64,128]{2,1,0:T(8,128)(2,1)S(1)} %slice.25, bf16[1152]{0:T(1024)(128)(2,1)S(1)} %pad.1.clone), kind=kLoop, calls=%fused_computation.6 | loop fusion | flops 7077888 | bytes 4589824 | tf_op jit(solution)/shard_map/concatenate | solution.py:204
  75.2 0.8 concatenate.17
  76.0 1.7 %copy.61 = bf16[8,4,256,16]{3,2,1,0:T(8,128)(2,1)} copy(bf16[8,4,256,16]{2,3,0,1:T(8,128)(2,1)S(1)} %bitcast.61) | data formatting | bytes 524288 | tf_op jit(solution)/shard_map/all_to_all | solution.py:174
  77.7 20.7 %shard_map.91 = (f32[1024,1024]{1,0:T(8,128)}, f32[1024,1024]{1,0:T(8,128)}) custom-call(s32[1]{0:T(128)} %bitcast.1.refs_0_, bf16[8,1024,16]{2,1,0:T(8,128)(2,1)} %bitcast.47, bf16[8,16,1152]{2,1,0:T(8,128)(2,1)} %bitcast.60, bf16[8,1152,128]{2,1,0:T(8,128)(2,1)} %pad_maximum_fusion.refs_3_), custom_call_target="tpu_custom_call" | custom-call | tf_op jit(solution)/shard_map/pallas_call | solution.py:83
  98.5 17.5 %all-gather.3.cloned.1.call-done = f32[32,153,128]{2,0,1:T(8,128)} async-done(((f32[8,153,128]{2,0,1:T(8,128)}), f32[32,153,128]{2,0,1:T(8,128)}) %all-gather.3.cloned.1.call-update) | async-done | bytes 2506768 | tf_op jit(solution)/shard_map/all_gather | solution.py:195
  115.9 4.6 %copy.67 = f32[32,153,128]{2,1,0:T(8,128)} copy(f32[32,153,128]{2,0,1:T(8,128)} %all-gather.3.cloned.1.call-done) | data formatting | bytes 5013504 | tf_op jit(solution)/shard_map/all_gather | solution.py:195
  120.6 10.9 %shard_map.92 = bf16[1024,1024]{1,0:T(8,128)(2,1)} custom-call(s32[1]{0:T(128)} %bitcast.refs_0_, f32[1024,1024]{1,0:T(8,128)} %get-tuple-element.9.refs_1_, f32[1024,1024]{1,0:T(8,128)} %get-tuple-element.10.refs_2_, bf16[8,1024,16]{2,1,0:T(8,128)(2,1)} %bitcast.48, f32[4,8,153,128]{3,2,1,0:T(8,128)} %bitcast.54, f32[8,2,153,128]{3,2,1,0:T(8,128)} %concatenate.19.refs_5_, ...), custom_call_target="tpu_custom_call" | custom-call | tf_op jit(solution)/shard_map/pallas_call | solution.py:144
  131.4 29.3 %all_to_all.73 = bf16[4,256,1024]{2,1,0:T(8,128)(2,1)S(1)} all-to-all(bf16[4,256,1024]{2,1,0:T(8,128)(2,1)} %bitcast.55), channel_id=1, replica_groups=mesh['groups'=2,'ctx'=4,'head'=4] {'head'}, dimensions={0} | all-to-all | bytes 4194304 | tf_op jit(solution)/shard_map/all_to_all | solution.py:211
  160.7 1.5 copy.73
  (22 shorter events, 0.5 us)
Async XLA Ops:
  8.3 10.2 %all-to-all-start = ((bf16[32,256,16]{1,2,0:T(8,128)(2,1)}), bf16[32,256,16]{1,2,0:T(8,128)(2,1)S(1)}, u32[]{:S(2)}, u32[]{:S(2)}) async-start(bf16[32,256,16]{1,2,0:T(8,128)(2,1)} %bitcast.5), calls=%async_computation | async-start | bytes 524288 | tf_op jit(solution)/shard_map/all_to_all | solution.py:174
  18.6 4.3 %copy-start.5 = (bf16[16,136,1,1]{1,0,3,2:T(8,128)(2,1)S(1)}, bf16[16,136,1,1]{1,0,3,2:T(8,128)(2,1)}, u32[]{:S(2)}) copy-start(bf16[16,136,1,1]{1,0,3,2:T(8,128)(2,1)} %constant.33) | copy-start | bytes 13060
  18.6 29.4 %all-to-all-start.1 = ((bf16[32,256,128]{1,2,0:T(8,128)(2,1)}), bf16[32,256,128]{1,2,0:T(8,128)(2,1)S(1)}, u32[]{:S(2)}, u32[]{:S(2)}) async-start(bf16[32,256,128]{1,2,0:T(8,128)(2,1)} %bitcast.12), calls=%async_computation.1 | async-start | bytes 4194304 | tf_op jit(solution)/shard_map/all_to_all | solution.py:174
  22.3 93.6 %all-gather.3.cloned.1.call-start = ((), (), s32[]{:S(2)}) async-start(), calls=%async_computation.4 | async-start | bytes 3133440 | tf_op jit(solution)/shard_map/all_gather | solution.py:195
  22.9 0.8 copy-start.4
  48.0 1.3 copy-start.2
  52.3 4.4 %copy-start = (bf16[8,4,256,128]{3,2,1,0:T(8,128)(2,1)}, bf16[8,4,256,128]{3,2,1,0:T(8,128)(2,1)S(1)}, u32[]{:S(2)}) copy-start(bf16[8,4,256,128]{3,2,1,0:T(8,128)(2,1)S(1)} %copy.59) | copy-start | bytes 6291460
  59.0 6.1 %copy-start.3 = (bf16[256,512]{1,0:T(8,128)(2,1)S(1)}, bf16[256,512]{1,0:T(8,128)(2,1)}, u32[]{:S(2)}) copy-start(bf16[256,512]{1,0:T(8,128)(2,1)} %param.9) | copy-start | bytes 786436
  60.1 12.9 %collective-permute-start = (bf16[8,64,144]{2,1,0:T(8,128)(2,1)S(1)}, bf16[8,64,144]{2,1,0:T(8,128)(2,1)S(1)}, u32[]{:S(2)}, u32[]{:S(2)}) collective-permute-start(bf16[8,64,144]{2,1,0:T(8,128)(2,1)S(1)} %pad_maximum_fusion.1), channel_id=1, source_target_pairs={{0,4},{4,8},{8,12},{1,5},{5,9},{9,13},{2,6},{6,10},{10,14},{3,7},{... | collective-permute-start | bytes 442376 | tf_op jit(solution)/shard_map/ppermute | solution.py:24
  65.0 8.0 %copy-start.1 = (bf16[8,4,256,128]{3,2,1,0:T(8,128)(2,1)S(1)}, bf16[8,4,256,128]{3,2,1,0:T(8,128)(2,1)}, u32[]{:S(2)}) copy-start(bf16[8,4,256,128]{3,2,1,0:T(8,128)(2,1)} %copy-done) | copy-start | bytes 6291460
  65.9 10.1 %all-to-all-start.2 = ((bf16[32,256,16]{1,2,0:T(8,128)(2,1)}), bf16[32,256,16]{1,2,0:T(8,128)(2,1)S(1)}, u32[]{:S(2)}, u32[]{:S(2)}) async-start(bf16[32,256,16]{1,2,0:T(8,128)(2,1)} %bitcast.18), calls=%async_computation.2 | async-start | bytes 524288 | tf_op jit(solution)/shard_map/all_to_all | solution.py:174
Sparse Core Ops, SparseCore 0:
  58.1 57.7 all-gather.2

commit v12 on v10

--- a/solution.py
+++ b/solution.py
@@ -105,21 +105,21 @@
     out_ref[...] = (linear * scale * gain_ref[...] + win_ref[...]).astype(jnp.bfloat16)
 
 
-def mix(intra, inter_hm, window, gain):
-    heads_here, span_rows, _ = inter_hm.shape
-    tile = pl.BlockSpec((span_rows, VD), lambda h: (0, h))
+def mix(intra, inter_hm, window, gain, offset):
+    heads_group, span_rows, _ = inter_hm.shape
+    tile = pl.BlockSpec((span_rows, VD), lambda h: (0, h + offset))
     return pl.pallas_call(
         mix_kernel,
-        grid=(heads_here,),
+        grid=(heads_group,),
         in_specs=[
             tile,
             pl.BlockSpec((1, span_rows, VD), lambda h: (h, 0, 0)),
             tile,
-            pl.BlockSpec((1, VD), lambda h: (0, h)),
+            pl.BlockSpec((1, VD), lambda h: (0, h + offset)),
         ],
-        out_specs=tile,
-        out_shape=jax.ShapeDtypeStruct((span_rows, heads_here * VD), jnp.bfloat16),
-    )(intra, inter_hm, window, gain.reshape(1, heads_here * VD))
+        out_specs=pl.BlockSpec((span_rows, VD), lambda h: (0, h)),
+        out_shape=jax.ShapeDtypeStruct((span_rows, heads_group * VD), jnp.bfloat16),
+    )(intra, inter_hm, window, gain.reshape(1, gain.shape[0]))
 
 
 def per_device(queries, keys, values, gain):
@@ -148,29 +148,17 @@
         preferred_element_type=jnp.float32,
     )
     span_state = jnp.sum(block_states, axis=1)
-    everything = lax.all_gather(span_state, "ctx")
+    groups = 2 if heads_here % 2 == 0 else 1
+    group_heads = heads_here // groups
+    everything = [lax.all_gather(span_state[:group_heads], "ctx")]
     queries, span_state = lax.optimization_barrier((queries, span_state))
     query_hm = to_heads(queries, KD)
-    peers = everything.shape[0]
+    peers = everything[0].shape[0]
     here = lax.axis_index("ctx")
-    entering = jnp.sum(
-        jnp.where(
-            (jnp.arange(peers) < here)[:, None, None, None], everything, jnp.zeros_like(everything)
-        ),
-        axis=0,
-    )
     before = jnp.concatenate(
         [jnp.zeros_like(block_states[:, :1]), jnp.cumsum(block_states[:, :-1], axis=1)], axis=1
     )
-    states = (before + entering[:, None]).astype(jnp.bfloat16)
-
     query_feat = unique_features(query_hm.reshape(heads_here, block_count, block_rows, KD), True)
-    inter = jnp.einsum(
-        "hnrf,hnfv->hnrv",
-        query_feat,
-        states,
-        preferred_element_type=jnp.float32,
-    ).reshape(heads_here, span_rows, VD)
 
     lead = jnp.zeros((heads_here, LEAD - WINDOW, KD + VD), jnp.bfloat16)
     key_ext = jnp.concatenate([lead[:, :, :KD], tails[:, :, :KD], key_hm], axis=1)
@@ -179,9 +167,34 @@
     intra, window = local_attention(
         flag, query_hm, jnp.transpose(key_ext, (0, 2, 1)), value_ext, block_rows
     )
-    mixed = mix(intra, inter, window, gain)
-    tokens_back = lax.all_to_all(mixed, "head", split_axis=0, concat_axis=1, tiled=True)
-    return tokens_back
+
+    outs = []
+    for g in range(groups):
+        heads = slice(g * group_heads, (g + 1) * group_heads)
+        if g > 0:
+            span_part, _ = lax.optimization_barrier((span_state[heads], intra))
+            everything.append(lax.all_gather(span_part, "ctx"))
+        gathered = everything[g]
+        if g > 0:
+            gathered, outs[-1] = lax.optimization_barrier((gathered, outs[-1]))
+        entering = jnp.sum(
+            jnp.where(
+                (jnp.arange(peers) < here)[:, None, None, None], gathered, jnp.zeros_like(gathered)
+            ),
+            axis=0,
+        )
+        states = (before[heads] + entering[:, None]).astype(jnp.bfloat16)
+        inter = jnp.einsum(
+            "hnrf,hnfv->hnrv", query_feat[heads], states, preferred_element_type=jnp.float32
+        ).reshape(group_heads, span_rows, VD)
+        mixed = mix(intra, inter, window, gain, g * group_heads)
+        back = lax.all_to_all(mixed, "head", split_axis=0, concat_axis=1, tiled=True)
+        outs.append(back)
+    peers_head = lax.axis_size("head")
+    tokens_back = jnp.stack(
+        [o.reshape(local_tokens, peers_head, group_heads * VD) for o in outs], axis=2
+    )
+    return tokens_back.reshape(local_tokens, HEADS * VD)
 
 
 def solution(mesh):

time: 169 us -> 181 us (1.071)
  blocking collectives: 29.3 us -> 17 us
  waiting for transfers between devices: 36.1 us -> 42.6 us
  matrix products: 13 us -> 19.3 us
  local copies, waits for them, and re-layouts: 23.9 us -> 29.6 us
  starting transfers between devices: 16.4 us -> 19.9 us
    all_to_all x1, blocking collectives: 29.3 us -> 17 us  [per_device(): lax.all_to_all(mixed, 'head', split_axis=0, concat_axis=1, tiled=True)]
    all_gather x1 -> x2, waiting for transfers between devices: 11.7 us -> 18.8 us  [the longest x1 18.8 us: per_device(): everything.append(lax.all_gather(span_part, 'ctx'))]
    all_to_all x0 -> x1, starting transfers between devices: none -> 3.7 us  [per_device(): lax.all_to_all(mixed, 'head', split_axis=0, concat_axis=1, tiled=True)]
    reshape x0 -> x1, local copies, waits for them, and re-layouts: none -> 2.86 us  [per_device(): return tokens_back.reshape(local_tokens, HEADS * VD)]
    dot_general x2, matrix products: 3.17 us -> 5.45 us  [unique_features(): jnp.einsum('...d,df->...f', vector, pick_cols, preferred_element_type=jnp...]
    all_to_all x1 -> x2, local copies, waits for them, and re-layouts: 1.49 us -> 3.76 us  [per_device(): lax.all_to_all(mixed, 'head', split_axis=0, concat_axis=1, tiled=True)]
    dot_general x2, matrix products: 1.55 us -> 3.59 us  [unique_features(): jnp.einsum('...d,df->...f', vector, pick_rows, preferred_element_type=jnp...]
    dot_general x1 -> x2, matrix products: 3.67 us -> 5.66 us  [per_device(): jnp.einsum('hnrf,hnfv->hnrv', query_feat[heads], states, preferred_elemen...]
  transfers between devices with their start and end apart: 5 -> 7, of which waited for: 4 -> 3; matrix products, arithmetic and copies ran while one was open for 14% -> 20% of each run, Pallas kernels for 12% -> 14%
where the time goes in v12:
time: 181 us; the launch traced here: 180 us
  waiting for transfers between devices  42.6 us (24%)
  Pallas kernels  30.3 us (17%)
  local copies, waits for them, and re-layouts  29.6 us (16%)
  starting transfers between devices  19.9 us (11%)
  matrix products  19.3 us (11%)
  blocking collectives  17 us (9%)
  between operations  13.7 us (8%)
  other arithmetic  7.65 us (4%)
    all_to_all x3, waiting for transfers between devices, to_heads(): return lax.all_to_all(tok, 'head', split_axis=0, concat_axis=1, tiled=True)  23.7 us
    pallas_call x1, Pallas kernels, local_attention(): pl.pallas_call(body, grid_spec=pltpu.PrefetchScalarGridSpec(num_scalar_pr...  20.8 us
    all_gather x1, waiting for transfers between devices, per_device(): everything.append(lax.all_gather(span_part, 'ctx'))  18.8 us
    all_to_all x1, blocking collectives, per_device(): lax.all_to_all(mixed, 'head', split_axis=0, concat_axis=1, tiled=True)  17 us
    all_to_all x3, starting transfers between devices, to_heads(): return lax.all_to_all(tok, 'head', split_axis=0, concat_axis=1, tiled=True)  11.4 us
    pallas_call x2, Pallas kernels, mix(): pl.pallas_call(mix_kernel, grid=(heads_group,), in_specs=[tile, pl.BlockS...  9.52 us
    unnamed x24, local copies, waits for them, and re-layouts  7.21 us
    all_to_all x6, local copies, waits for them, and re-layouts, to_heads(): return lax.all_to_all(tok, 'head', split_axis=0, concat_axis=1, tiled=True)  6.94 us
  transfers between devices with their start and end apart: 7, of which 3 were waited for; matrix products, arithmetic and copies ran while one was open for 20% of the time, Pallas kernels for 14%

profile of v12, /device:TPU:0, one launch (start us, length us, event | category | flops | bytes accessed | tf_op | source)
XLA Modules:
  0.0 180.1 jit_solution(610278035464677341)
XLA Ops:
  6.5 1.8 copy.48
  8.3 4.2 %all-to-all-start = ((bf16[32,256,16]{1,2,0:T(8,128)(2,1)}), bf16[32,256,16]{1,2,0:T(8,128)(2,1)S(1)}, u32[]{:S(2)}, u32[]{:S(2)}) async-start(bf16[32,256,16]{1,2,0:T(8,128)(2,1)} %bitcast.1), calls=%async_computation | async-start | bytes 524288 | tf_op jit(solution)/shard_map/all_to_all | solution.py:130
  12.5 4.1 %copy.53 = bf16[256,4096]{0,1:T(8,128)(2,1)} copy(bf16[256,4096]{1,0:T(8,128)(2,1)} %param.11) | data formatting | bytes 4194304 | tf_op args[2]
  16.6 2.0 %all-to-all-done = bf16[32,256,16]{1,2,0:T(8,128)(2,1)S(1)} async-done(((bf16[32,256,16]{1,2,0:T(8,128)(2,1)}), bf16[32,256,16]{1,2,0:T(8,128)(2,1)S(1)}, u32[]{:S(2)}, u32[]{:S(2)}) %all-to-all-start) | async-done | bytes 262176 | tf_op jit(solution)/shard_map/all_to_all | solution.py:130
  18.6 3.7 %all-to-all-start.1 = ((bf16[32,256,128]{1,2,0:T(8,128)(2,1)}), bf16[32,256,128]{1,2,0:T(8,128)(2,1)S(1)}, u32[]{:S(2)}, u32[]{:S(2)}) async-start(bf16[32,256,128]{1,2,0:T(8,128)(2,1)} %bitcast.10), calls=%async_computation.1 | async-start | bytes 4194304 | tf_op jit(solution)/shard_map/all_to_all | solution.py:130
  24.1 2.1 %fusion.6 = bf16[8,2,512,136]{2,3,1,0:T(8,128)(2,1)} fusion(f32[136,8,2,512]{3,0,2,1:T(8,128)S(1)} %fusion.24, bf16[16,136,1,1]{1,0,3,2:T(8,128)(2,1)S(1)} %copy-done.5, bf16[8,2,512,16]{2,1,3,0:T(2,128)(2,1)S(1)} %reshape.54), kind=kOutput, calls=%fused_computation.10 | convolution fusion | flops 38993920 | bytes 6951168 | tf_op jit(solution)/shard_map/...d,df->...f/dot_general | solution.py:32
  26.2 21.7 %all-to-all-done.1 = bf16[32,256,128]{1,2,0:T(8,128)(2,1)S(1)} async-done(((bf16[32,256,128]{1,2,0:T(8,128)(2,1)}), bf16[32,256,128]{1,2,0:T(8,128)(2,1)S(1)}, u32[]{:S(2)}, u32[]{:S(2)}) %all-to-all-start.1) | async-done | bytes 2097184 | tf_op jit(solution)/shard_map/all_to_all | solution.py:130
  48.0 1.3 copy-done.2
  49.3 3.0 %copy.55 = bf16[8,4,256,128]{3,2,1,0:T(8,128)(2,1)S(1)} copy(bf16[8,4,256,128]{2,3,0,1:T(8,128)(2,1)} %bitcast.65) | data formatting | bytes 4194304 | tf_op jit(solution)/shard_map/all_to_all | solution.py:130
  52.4 4.6 %fusion.31 = (f32[8,153,128]{2,1,0:T(8,128)S(1)}, f32[8,2,153,128]{3,2,1,0:T(8,128)}) fusion(bf16[8,2,512,128]{3,2,1,0:T(8,128)(2,1)S(1)} %bitcast.61, bf16[8,2,512,136]{2,3,1,0:T(8,128)(2,1)} %fusion.6, bf16[8,2,512,16]{2,3,1,0:T(8,128)(2,1)S(1)} %multiply_convert_fusion.3, bf16[153]{0:T(256)(128)(2,1)S(1)} %copy-done.9), kind=kOutput, calls=%fused_computation.42 | convolution fusion | flops 328541184 | bytes 6467890 | tf_op jit(solution)/shard_map/hnrf,hnrv->hnfv/dot_general | solution.py:144
  58.8 1.1 pad_maximum_fusion.5
  59.9 4.8 %collective-permute-start = (bf16[8,64,144]{2,1,0:T(8,128)(2,1)S(1)}, bf16[8,64,144]{2,1,0:T(8,128)(2,1)}, u32[]{:S(2)}, u32[]{:S(2)}) collective-permute-start(bf16[8,64,144]{2,1,0:T(8,128)(2,1)S(1)} %pad_maximum_fusion.5), channel_id=1, source_target_pairs={{0,4},{4,8},{8,12},{1,5},{5,9},{9,13},{2,6},{6,10},{10,14},{3,7},{... | collective-permute-start | bytes 442376 | tf_op jit(solution)/shard_map/ppermute | solution.py:24
  67.6 3.4 %all-to-all-start.2 = ((bf16[32,256,16]{1,2,0:T(8,128)(2,1)}), bf16[32,256,16]{1,2,0:T(8,128)(2,1)S(1)}, u32[]{:S(2)}, u32[]{:S(2)}) async-start(bf16[32,256,16]{1,2,0:T(8,128)(2,1)} %bitcast.17), calls=%async_computation.2 | async-start | bytes 524288 | tf_op jit(solution)/shard_map/all_to_all | solution.py:130
  71.0 2.0 %slice.50 = f32[8,1,153,128]{3,2,1,0:T(8,128)} slice(f32[8,2,153,128]{3,2,1,0:T(8,128)} %get-tuple-element.20), slice={[0:8], [0:1], [0:153], [0:128]} | slice | bytes 1253376 | tf_op jit(solution)/shard_map/slice | solution.py:159
  73.8 1.1 slice.49
  74.8 2.6 %pad_maximum_fusion.1.refs_3_ = bf16[8,1152,128]{2,1,0:T(8,128)(2,1)} fusion(bf16[8,1024,128]{2,1,0:T(8,128)(2,1)S(1)} %bitcast.63, bf16[8,64,128]{2,1,0:T(8,128)(2,1)S(1)} %slice.49, bf16[1152]{0:T(1024)(128)(2,1)} %pad.6.clone), kind=kLoop, calls=%fused_computation.8 | loop fusion | flops 7077888 | bytes 4589824 | tf_op jit(solution)/shard_map/concatenate | solution.py:165
  79.3 1.7 copy.57
  81.4 20.8 %shard_map.91 = (f32[1024,1024]{1,0:T(8,128)}, f32[1024,1024]{1,0:T(8,128)}) custom-call(s32[1]{0:T(128)} %bitcast.15.refs_0_, bf16[8,1024,16]{2,1,0:T(8,128)(2,1)} %bitcast.64, bf16[8,16,1152]{2,1,0:T(8,128)(2,1)} %bitcast.79, bf16[8,1152,128]{2,1,0:T(8,128)(2,1)} %pad_maximum_fusion.1.refs_3_), custom_call_target="tpu_custom_call" | custom-call | tf_op jit(solution)/shard_map/pallas_call | solution.py:83
  102.2 2.8 %fusion.21 = f32[8,2,512,136]{2,3,1,0:T(8,128)} fusion(bf16[16,136,1,1]{1,0,3,2:T(8,128)(2,1)S(1)} %copy-done.6, bf16[8,2,512,16]{2,1,3,0:T(2,128)(2,1)S(1)} %reshape.60), kind=kOutput, calls=%fused_computation.31 | convolution fusion | flops 35651584 | bytes 4722944 | tf_op jit(solution)/shard_map/...d,df->...f/dot_general | solution.py:31
  105.1 3.3 %fusion.5 = bf16[8,2,512,136]{2,3,1,0:T(8,128)(2,1)S(1)} fusion(f32[8,2,512,136]{2,3,1,0:T(8,128)} %fusion.21, bf16[16,136,1,1]{1,0,3,2:T(8,128)(2,1)S(1)} %copy-done.5, bf16[136]{0:T(256)(128)(2,1)S(1)} %copy-done.8, bf16[8,2,512,16]{2,1,3,0:T(2,128)(2,1)S(1)} %reshape.60), kind=kOutput, calls=%fused_computation.9 | convolution fusion | flops 40108032 | bytes 6951440 | tf_op jit(solution)/shard_map/...d,df->...f/dot_general | solution.py:32
  108.5 1.5 select_reduce_fusion.1
  110.0 2.3 %fusion.8 = f32[4,2,512,128]{3,2,1,0:T(8,128)} fusion(bf16[8,2,512,136]{2,3,1,0:T(8,128)(2,1)S(1)} %fusion.5, bf16[8,2,512,16]{2,3,1,0:T(8,128)(2,1)S(1)} %multiply_convert_fusion.2, bf16[153]{0:T(256)(128)(2,1)S(1)} %copy-done.10, f32[8,1,153,128]{3,2,1,0:T(8,128)S(1)} %copy-done.3, f32[4,153,128]{2,1,0:T(8,128)S(1)} %select_reduce_fusion.1), kind=kOutput, calls=%fused_computation.15 | convolution fusion | flops 168265728 | bytes 5527858 | tf_op jit(solution)/shard_map/hnrf,hnfv->hnrv/dot_general | solution.py:187
  112.4 4.8 %shard_map.92 = bf16[1024,512]{1,0:T(8,128)(2,1)} custom-call(f32[1024,1024]{1,0:T(8,128)} %get-tuple-element.14.intra_ref, f32[4,1024,128]{2,1,0:T(8,128)} %bitcast.76, f32[1024,1024]{1,0:T(8,128)} %get-tuple-element.16.win_ref, f32[1,1024]{1,0:T(1,128)} %bitcast.80), custom_call_target="tpu_custom_call" | custom-call | tf_op jit(solution)/shard_map/pallas_call | solution.py:111
  117.2 2.3 %copy.66 = bf16[4,256,512]{1,2,0:T(8,128)(2,1)} copy(bf16[4,256,512]{2,1,0:T(8,128)(2,1)} %bitcast.70) | data formatting | bytes 2097152 | tf_op jit(solution)/shard_map/all_to_all | solution.py:191
  119.5 3.7 %all-to-all-start.3 = ((bf16[4,256,512]{1,2,0:T(8,128)(2,1)}), bf16[4,256,512]{1,2,0:T(8,128)(2,1)S(1)}, u32[]{:S(2)}, u32[]{:S(2)}) async-start(bf16[4,256,512]{1,2,0:T(8,128)(2,1)} %copy.66), calls=%async_computation.3 | async-start | bytes 2097152 | tf_op jit(solution)/shard_map/all_to_all | solution.py:191
  123.2 18.8 %all-gather.5.cloned.1.call-done = f32[16,153,128]{2,1,0:T(8,128)} async-done(((f32[4,153,128]{2,1,0:T(8,128)}), f32[16,153,128]{2,1,0:T(8,128)}) %all-gather.5.cloned.1.call-update) | async-done | bytes 1253392 | tf_op jit(solution)/shard_map/all_gather | solution.py:176
  142.0 1.5 select_reduce_fusion
  143.5 3.3 %fusion.7 = f32[4,2,512,128]{3,2,1,0:T(8,128)} fusion(bf16[8,2,512,136]{2,3,1,0:T(8,128)(2,1)S(1)} %fusion.5, bf16[8,2,512,16]{2,3,1,0:T(8,128)(2,1)S(1)} %multiply_convert_fusion.2, bf16[153]{0:T(256)(128)(2,1)S(1)} %copy-done.10, f32[8,1,153,128]{3,2,1,0:T(8,128)} %slice.50, f32[4,153,128]{2,1,0:T(8,128)S(1)} %select_reduce_fusion), kind=kOutput, calls=%fused_computation.14 | convolution fusion | flops 168265728 | bytes 5527858 | tf_op jit(solution)/shard_map/hnrf,hnfv->hnrv/dot_general | solution.py:187
  146.8 4.7 %shard_map.93 = bf16[1024,512]{1,0:T(8,128)(2,1)} custom-call(f32[1024,1024]{1,0:T(8,128)} %get-tuple-element.14.intra_ref, f32[4,1024,128]{2,1,0:T(8,128)} %bitcast.75, f32[1024,1024]{1,0:T(8,128)} %get-tuple-element.16.win_ref, f32[1,1024]{1,0:T(1,128)} %bitcast.81), custom_call_target="tpu_custom_call" | custom-call | tf_op jit(solution)/shard_map/pallas_call | solution.py:111
  151.6 1.5 copy.67
  153.0 17.0 %all_to_all.89 = bf16[4,256,512]{1,2,0:T(8,128)(2,1)S(1)} all-to-all(bf16[4,256,512]{1,2,0:T(8,128)(2,1)S(1)} %copy.67), channel_id=1, replica_groups=mesh['groups'=2,'ctx'=4,'head'=4] {'head'}, dimensions={0} | all-to-all | bytes 2097152 | tf_op jit(solution)/shard_map/all_to_all | solution.py:191
  170.4 2.9 %copy.69 = bf16[256,4096]{1,0:T(8,128)(2,1)} copy(bf16[256,4096]{0,1:T(8,128)(2,1)S(1)} %bitcast.66) | data formatting | bytes 4194304 | tf_op jit(solution)/shard_map/reshape | solution.py:197
  (51 shorter events, 9.8 us)
Async XLA Ops:
  8.3 10.2 %all-to-all-start = ((bf16[32,256,16]{1,2,0:T(8,128)(2,1)}), bf16[32,256,16]{1,2,0:T(8,128)(2,1)S(1)}, u32[]{:S(2)}, u32[]{:S(2)}) async-start(bf16[32,256,16]{1,2,0:T(8,128)(2,1)} %bitcast.1), calls=%async_computation | async-start | bytes 524288 | tf_op jit(solution)/shard_map/all_to_all | solution.py:130
  18.6 4.8 %copy-start.6 = (bf16[16,136,1,1]{1,0,3,2:T(8,128)(2,1)S(1)}, bf16[16,136,1,1]{1,0,3,2:T(8,128)(2,1)}, u32[]{:S(2)}) copy-start(bf16[16,136,1,1]{1,0,3,2:T(8,128)(2,1)} %constant.34) | copy-start | bytes 13060
  18.6 29.4 %all-to-all-start.1 = ((bf16[32,256,128]{1,2,0:T(8,128)(2,1)}), bf16[32,256,128]{1,2,0:T(8,128)(2,1)S(1)}, u32[]{:S(2)}, u32[]{:S(2)}) async-start(bf16[32,256,128]{1,2,0:T(8,128)(2,1)} %bitcast.10), calls=%async_computation.1 | async-start | bytes 4194304 | tf_op jit(solution)/shard_map/all_to_all | solution.py:130
  22.3 86.2 %all-gather.7.cloned.1.call-start = ((), (), s32[]{:S(2)}) async-start(), calls=%async_computation.6 | async-start | bytes 1638400 | tf_op jit(solution)/shard_map/all_gather | solution.py:153
  23.3 0.8 copy-start.5
  26.2 26.1 %copy-start.9 = (bf16[153]{0:T(256)(128)(2,1)S(1)}, bf16[153]{0:T(256)(128)(2,1)}, u32[]{:S(2)}) copy-start(bf16[153]{0:T(256)(128)(2,1)} %pad.11.clone) | copy-start | bytes 922
  48.0 1.3 copy-start.2
  52.3 4.7 %copy-start = (bf16[8,4,256,128]{3,2,1,0:T(8,128)(2,1)}, bf16[8,4,256,128]{3,2,1,0:T(8,128)(2,1)S(1)}, u32[]{:S(2)}) copy-start(bf16[8,4,256,128]{3,2,1,0:T(8,128)(2,1)S(1)} %copy.55) | copy-start | bytes 6291460
  58.8 7.9 %copy-start.4 = (bf16[256,512]{1,0:T(8,128)(2,1)S(1)}, bf16[256,512]{1,0:T(8,128)(2,1)}, u32[]{:S(2)}) copy-start(bf16[256,512]{1,0:T(8,128)(2,1)} %param.9) | copy-start | bytes 786436
  59.9 13.8 %collective-permute-start = (bf16[8,64,144]{2,1,0:T(8,128)(2,1)S(1)}, bf16[8,64,144]{2,1,0:T(8,128)(2,1)}, u32[]{:S(2)}, u32[]{:S(2)}) collective-permute-start(bf16[8,64,144]{2,1,0:T(8,128)(2,1)S(1)} %pad_maximum_fusion.5), channel_id=1, source_target_pairs={{0,4},{4,8},{8,12},{1,5},{5,9},{9,13},{2,6},{6,10},{10,14},{3,7},{... | collective-permute-start | bytes 442376 | tf_op jit(solution)/shard_map/ppermute | solution.py:24
  66.7 8.1 %copy-start.1 = (bf16[8,4,256,128]{3,2,1,0:T(8,128)(2,1)S(1)}, bf16[8,4,256,128]{3,2,1,0:T(8,128)(2,1)}, u32[]{:S(2)}) copy-start(bf16[8,4,256,128]{3,2,1,0:T(8,128)(2,1)} %copy-done) | copy-start | bytes 6291460
  67.6 11.8 %all-to-all-start.2 = ((bf16[32,256,16]{1,2,0:T(8,128)(2,1)}), bf16[32,256,16]{1,2,0:T(8,128)(2,1)S(1)}, u32[]{:S(2)}, u32[]{:S(2)}) async-start(bf16[32,256,16]{1,2,0:T(8,128)(2,1)} %bitcast.17), calls=%async_computation.2 | async-start | bytes 524288 | tf_op jit(solution)/shard_map/all_to_all | solution.py:130
  71.0 71.0 %all-gather.5.cloned.1.call-start = ((), (), s32[]{:S(2)}) async-start(), calls=%async_computation.5 | async-start | bytes 1638400 | tf_op jit(solution)/shard_map/all_gather | solution.py:176
  102.2 2.9 %copy-start.8 = (bf16[136]{0:T(256)(128)(2,1)S(1)}, bf16[136]{0:T(256)(128)(2,1)}, u32[]{:S(2)}) copy-start(bf16[136]{0:T(256)(128)(2,1)} %constant.31.clone) | copy-start | bytes 820
  105.1 3.4 %copy-start.7 = (pred[4]{0:T(512)(128)(4,1)S(1)}, pred[4]{0:T(512)(128)(4,1)}, u32[]{:S(2)}) copy-start(pred[4]{0:T(512)(128)(4,1)} %iota_compare_fusion) | copy-start | bytes 16
  105.1 4.9 %copy-start.3 = (f32[8,1,153,128]{3,2,1,0:T(8,128)S(1)}, f32[8,1,153,128]{3,2,1,0:T(8,128)}, u32[]{:S(2)}) copy-start(f32[8,1,153,128]{3,2,1,0:T(8,128)} %slice.50) | copy-start | bytes 1880068
  105.1 4.9 %copy-start.10 = (bf16[153]{0:T(256)(128)(2,1)S(1)}, bf16[153]{0:T(256)(128)(2,1)}, u32[]{:S(2)}) copy-start(bf16[153]{0:T(256)(128)(2,1)} %pad.11.clone) | copy-start | bytes 922
  119.5 22.5 %all-to-all-start.3 = ((bf16[4,256,512]{1,2,0:T(8,128)(2,1)}), bf16[4,256,512]{1,2,0:T(8,128)(2,1)S(1)}, u32[]{:S(2)}, u32[]{:S(2)}) async-start(bf16[4,256,512]{1,2,0:T(8,128)(2,1)} %copy.66), calls=%async_computation.3 | async-start | bytes 2097152 | tf_op jit(solution)/shard_map/all_to_all | solution.py:191
Sparse Core Ops, SparseCore 0:
  57.9 33.6 all-gather.6
  105.2 36.7 all-gather.4

commit v13 on v10

--- a/solution.py
+++ b/solution.py
@@ -148,17 +148,24 @@
         preferred_element_type=jnp.float32,
     )
     span_state = jnp.sum(block_states, axis=1)
-    everything = lax.all_gather(span_state, "ctx")
+    peers = lax.axis_size("ctx")
+    running = span_state
+    entering = None
+    first_round = span_state
+    shift = 1
+    while shift < peers:
+        received = shifted(running, "ctx", shift)
+        entering = received if entering is None else entering + received
+        if shift == 1:
+            first_round = received
+        shift *= 2
+        if shift < peers:
+            running = running + received
+    if entering is None:
+        entering = jnp.zeros_like(span_state)
     queries, span_state = lax.optimization_barrier((queries, span_state))
     query_hm = to_heads(queries, KD)
-    peers = everything.shape[0]
-    here = lax.axis_index("ctx")
-    entering = jnp.sum(
-        jnp.where(
-            (jnp.arange(peers) < here)[:, None, None, None], everything, jnp.zeros_like(everything)
-        ),
-        axis=0,
-    )
+    query_hm, first_round = lax.optimization_barrier((query_hm, first_round))
     before = jnp.concatenate(
         [jnp.zeros_like(block_states[:, :1]), jnp.cumsum(block_states[:, :-1], axis=1)], axis=1
     )

time: 169 us -> 156 us (0.923)
  between operations: 13.7 us -> 0.23 us
  waiting for transfers between devices: 36.1 us -> 23.6 us
  starting transfers between devices: 16.4 us -> 24.2 us
  matrix products: 13 us -> 14.8 us
  local copies, waits for them, and re-layouts: 23.9 us -> 25.7 us
    all_gather x1 -> x0, waiting for transfers between devices: 11.7 us -> none  [per_device(): everything = lax.all_gather(span_state, 'ctx')]
    ppermute x1 -> x3, starting transfers between devices: 4.8 us -> 11.5 us  [shifted(): return lax.ppermute(shard, axis, pairs)]
    add x0 -> x2, other arithmetic: none -> 3.61 us  [the longest x1 2.28 us: per_device(): running = running + received]
    dot_general x1, matrix products: 4.64 us -> 2.35 us  [per_device(): jnp.einsum('hnrf,hnrv->hnfv', key_feat, value_hm.reshape(heads_here, bloc...]
    dot_general x2, matrix products: 1.55 us -> 3.8 us  [unique_features(): jnp.einsum('...d,df->...f', vector, pick_rows, preferred_element_type=jnp...]
    reduce_sum x1 -> x0, other arithmetic: 2.23 us -> none  [per_device(): jnp.sum(jnp.where((jnp.arange(peers) < here)[:, None, None, None], everyt...]
    dot_general x2, matrix products: 3.17 us -> 4.96 us  [unique_features(): jnp.einsum('...d,df->...f', vector, pick_cols, preferred_element_type=jnp...]
    all_to_all x6 -> x5, local copies, waits for them, and re-layouts: 6.95 us -> 8.49 us  [to_heads(): return lax.all_to_all(tok, 'head', split_axis=0, concat_axis=1, tiled=True)]
  transfers between devices with their start and end apart: 5 -> 6, of which waited for: 4 -> 3; matrix products, arithmetic and copies ran while one was open for 14% -> 18% of each run, Pallas kernels for 12% -> 13%
where the time goes in v13:
time: 156 us; the launch traced here: 155 us
  Pallas kernels  29.3 us (19%)
  blocking collectives  29.3 us (19%)
  local copies, waits for them, and re-layouts  25.7 us (16%)
  starting transfers between devices  24.2 us (16%)
  waiting for transfers between devices  23.6 us (15%)
  matrix products  14.8 us (9%)
  other arithmetic  7.54 us (5%)
    all_to_all x1, blocking collectives, per_device(): lax.all_to_all(mixed, 'head', split_axis=0, concat_axis=1, tiled=True)  29.3 us
    all_to_all x3, waiting for transfers between devices, to_heads(): return lax.all_to_all(tok, 'head', split_axis=0, concat_axis=1, tiled=True)  23.6 us
    pallas_call x1, Pallas kernels, local_attention(): pl.pallas_call(body, grid_spec=pltpu.PrefetchScalarGridSpec(num_scalar_pr...  20.9 us
    all_to_all x3, starting transfers between devices, to_heads(): return lax.all_to_all(tok, 'head', split_axis=0, concat_axis=1, tiled=True)  12.7 us
    ppermute x3, starting transfers between devices, shifted(): return lax.ppermute(shard, axis, pairs)  11.5 us
    all_to_all x5, local copies, waits for them, and re-layouts, to_heads(): return lax.all_to_all(tok, 'head', split_axis=0, concat_axis=1, tiled=True)  8.49 us
    pallas_call x1, Pallas kernels, mix(): pl.pallas_call(mix_kernel, grid=(heads_here,), in_specs=[tile, pl.BlockSp...  8.42 us
    unnamed x20, local copies, waits for them, and re-layouts  5.88 us
  transfers between devices with their start and end apart: 6, of which 3 were waited for; matrix products, arithmetic and copies ran while one was open for 18% of the time, Pallas kernels for 13%

profile of v13, /device:TPU:0, one launch (start us, length us, event | category | flops | bytes accessed | tf_op | source)
XLA Modules:
  0.0 154.7 jit_solution(6882842110424860770)
XLA Ops:
  0.0 1.8 %copy.82 = bf16[256,512]{0,1:T(8,128)(2,1)} copy(bf16[256,512]{1,0:T(8,128)(2,1)} %param.10) | data formatting | bytes 524288 | tf_op args[1]
  1.8 4.2 %all-to-all-start = ((bf16[32,256,16]{1,2,0:T(8,128)(2,1)}), bf16[32,256,16]{1,2,0:T(8,128)(2,1)S(1)}, u32[]{:S(2)}, u32[]{:S(2)}) async-start(bf16[32,256,16]{1,2,0:T(8,128)(2,1)} %bitcast.2), calls=%async_computation | async-start | bytes 524288 | tf_op jit(solution)/shard_map/all_to_all | solution.py:130
  6.0 4.1 %copy.87 = bf16[256,4096]{0,1:T(8,128)(2,1)} copy(bf16[256,4096]{1,0:T(8,128)(2,1)} %param.11) | data formatting | bytes 4194304 | tf_op args[2]
  10.1 2.0 %all-to-all-done = bf16[32,256,16]{1,2,0:T(8,128)(2,1)S(1)} async-done(((bf16[32,256,16]{1,2,0:T(8,128)(2,1)}), bf16[32,256,16]{1,2,0:T(8,128)(2,1)S(1)}, u32[]{:S(2)}, u32[]{:S(2)}) %all-to-all-start) | async-done | bytes 262176 | tf_op jit(solution)/shard_map/all_to_all | solution.py:130
  12.0 4.4 %all-to-all-start.1 = ((bf16[32,256,128]{1,2,0:T(8,128)(2,1)}), bf16[32,256,128]{1,2,0:T(8,128)(2,1)}, u32[]{:S(2)}, u32[]{:S(2)}) async-start(bf16[32,256,128]{1,2,0:T(8,128)(2,1)} %bitcast.11), calls=%async_computation.1 | async-start | bytes 4194304 | tf_op jit(solution)/shard_map/all_to_all | solution.py:130
  18.8 2.1 %fusion.11 = bf16[8,2,512,136]{2,3,1,0:T(8,128)(2,1)} fusion(f32[136,8,2,512]{3,0,2,1:T(8,128)S(1)} %fusion.16, bf16[16,136,1,1]{1,0,3,2:T(8,128)(2,1)S(1)} %copy-done.7, bf16[8,2,512,16]{2,1,3,0:T(2,128)(2,1)S(1)} %reshape.39), kind=kOutput, calls=%fused_computation.14 | convolution fusion | flops 38993920 | bytes 6951168 | tf_op jit(solution)/shard_map/...d,df->...f/dot_general | solution.py:32
  20.9 21.3 %all-to-all-done.1 = bf16[32,256,128]{1,2,0:T(8,128)(2,1)} async-done(((bf16[32,256,128]{1,2,0:T(8,128)(2,1)}), bf16[32,256,128]{1,2,0:T(8,128)(2,1)}, u32[]{:S(2)}, u32[]{:S(2)}) %all-to-all-start.1) | async-done | bytes 2097184 | tf_op jit(solution)/shard_map/all_to_all | solution.py:130
  42.2 3.9 %copy.89 = bf16[8,4,256,128]{3,2,1,0:T(8,128)(2,1)} copy(bf16[8,4,256,128]{2,3,0,1:T(8,128)(2,1)} %bitcast.14) | data formatting | bytes 4194304 | tf_op jit(solution)/shard_map/all_to_all | solution.py:130
  46.2 1.9 %pad_maximum_fusion.1 = bf16[8,64,144]{2,1,0:T(8,128)(2,1)} fusion(bf16[8,1024,128]{2,1,0:T(8,128)(2,1)} %bitcast.57, bf16[8,1024,16]{2,1,0:T(8,128)(2,1)S(1)} %bitcast.55), kind=kLoop, calls=%fused_computation.21 | loop fusion | flops 294912 | bytes 2506752 | tf_op jit(solution)/shard_map/concatenate | solution.py:140
  48.1 4.8 %collective-permute-start.1 = (bf16[8,64,144]{2,1,0:T(8,128)(2,1)}, bf16[8,64,144]{2,1,0:T(8,128)(2,1)}, u32[]{:S(2)}, u32[]{:S(2)}) collective-permute-start(bf16[8,64,144]{2,1,0:T(8,128)(2,1)} %pad_maximum_fusion.1), channel_id=1, source_target_pairs={{0,4},{4,8},{8,12},{1,5},{5,9},{9,13},{2,6},{6,10},{10,14},{3,7},{... | collective-permute-start | bytes 442376 | tf_op jit(solution)/shard_map/ppermute | solution.py:24
  52.9 2.4 %fusion.21 = (f32[8,153,128]{2,1,0:T(8,128)S(1)}, f32[8,2,153,128]{3,2,1,0:T(8,128)}) fusion(bf16[8,2,512,128]{3,2,1,0:T(8,128)(2,1)S(1)} %bitcast.58, bf16[8,2,512,136]{2,3,1,0:T(8,128)(2,1)S(1)} %copy-done.4, bf16[8,2,512,16]{2,3,1,0:T(8,128)(2,1)S(1)} %multiply_convert_fusion.3, bf16[153]{0:T(256)(128)(2,1)S(1)} %pad.9.clone), kind=kOutput, calls=%fused_computation.28 | convolution fusion | flops 328541184 | bytes 6467890 | tf_op jit(solution)/shard_map/hnrf,hnrv->hnfv/dot_general | solution.py:144
  55.2 1.2 copy.92
  56.4 3.6 %collective-permute-start = (f32[8,153,128]{2,0,1:T(8,128)}, f32[8,153,128]{2,0,1:T(8,128)}, u32[]{:S(2)}, u32[]{:S(2)}) collective-permute-start(f32[8,153,128]{2,0,1:T(8,128)} %copy.92), channel_id=1, source_target_pairs={{0,4},{4,8},{8,12},{1,5},{5,9},{9,13},{2,6},{6,10},{10,14},{3,7},{... | collective-permute-start | bytes 1880072 | tf_op jit(solution)/shard_map/ppermute | solution.py:24
  60.1 1.4 copy.96
  61.5 1.3 slice.26
  62.8 1.8 %copy.90 = bf16[256,512]{0,1:T(8,128)(2,1)} copy(bf16[256,512]{1,0:T(8,128)(2,1)} %param.9) | data formatting | bytes 524288 | tf_op jit(solution)/shard_map/optimization_barrier | solution.py:166
  64.6 4.0 %all-to-all-start.2 = ((bf16[32,256,16]{1,2,0:T(8,128)(2,1)}), bf16[32,256,16]{1,2,0:T(8,128)(2,1)}, u32[]{:S(2)}, u32[]{:S(2)}) async-start(bf16[32,256,16]{1,2,0:T(8,128)(2,1)} %bitcast.66), calls=%async_computation.2 | async-start | bytes 524288 | tf_op jit(solution)/shard_map/all_to_all | solution.py:130
  68.7 1.1 slice.25
  69.7 1.9 %pad_maximum_fusion.refs_3_ = bf16[8,1152,128]{2,1,0:T(8,128)(2,1)} fusion(bf16[8,1024,128]{2,1,0:T(8,128)(2,1)S(1)} %bitcast.59, bf16[8,64,128]{2,1,0:T(8,128)(2,1)S(1)} %slice.25, bf16[1152]{0:T(1024)(128)(2,1)S(1)} %pad.4.clone), kind=kLoop, calls=%fused_computation.12 | loop fusion | flops 7077888 | bytes 4589824 | tf_op jit(solution)/shard_map/concatenate | solution.py:184
  72.7 1.8 %concatenate.20 = bf16[8,1152,16]{1,2,0:T(8,128)(2,1)} concatenate(bf16[8,64,16]{1,2,0:T(8,128)(2,1)S(1)} %slice.18, bf16[8,64,16]{1,2,0:T(8,128)(2,1)S(1)} %copy.95, bf16[8,1024,16]{1,2,0:T(8,128)(2,1)} %copy.96), dimensions={1} | concatenate | bytes 589824 | tf_op jit(solution)/shard_map/concatenate | solution.py:183
  74.7 1.9 %copy.91 = bf16[8,4,256,16]{3,2,1,0:T(8,128)(2,1)S(1)} copy(bf16[8,4,256,16]{2,3,0,1:T(8,128)(2,1)} %bitcast.19) | data formatting | bytes 524288 | tf_op jit(solution)/shard_map/all_to_all | solution.py:130
  76.7 1.4 copy.97
  78.1 2.8 %fusion.22 = f32[8,2,512,136]{2,3,1,0:T(8,128)} fusion(bf16[8,2,512,16]{3,2,1,0:T(8,128)(2,1)S(1)} %bitcast.52, bf16[16,136,1,1]{1,0,3,2:T(8,128)(2,1)S(1)} %copy-done.7), kind=kOutput, calls=%fused_computation.29 | convolution fusion | flops 35651584 | bytes 4722944 | tf_op jit(solution)/shard_map/...d,df->...f/dot_general | solution.py:32
  80.9 2.3 %copy_add_fusion = f32[8,153,128]{2,0,1:T(8,128)} fusion(f32[8,153,128]{2,0,1:T(8,128)} %collective-permute-done, f32[8,153,128]{2,1,0:T(8,128)S(1)} %get-tuple-element.13), kind=kLoop, calls=%fused_computation.30 | loop fusion | flops 156672 | bytes 1880064 | tf_op jit(solution)/shard_map/add | solution.py:163
  83.2 3.1 %collective-permute-start.2 = (f32[8,153,128]{2,0,1:T(8,128)}, f32[8,153,128]{2,0,1:T(8,128)}, u32[]{:S(2)}, u32[]{:S(2)}) collective-permute-start(f32[8,153,128]{2,0,1:T(8,128)} %copy_add_fusion), channel_id=1, source_target_pairs={{0,8},{4,12},{1,9},{5,13},{2,10},{6,14},{3,11},{7,15},{16,24},{20,... | collective-permute-start | bytes 1880072 | tf_op jit(solution)/shard_map/ppermute | solution.py:24
  86.3 20.9 %shard_map.91 = (f32[1024,1024]{1,0:T(8,128)}, f32[1024,1024]{1,0:T(8,128)}) custom-call(s32[1]{0:T(128)} %bitcast.refs_0_, bf16[8,1024,16]{2,1,0:T(8,128)(2,1)} %bitcast.53, bf16[8,16,1152]{2,1,0:T(8,128)(2,1)} %bitcast.65, bf16[8,1152,128]{2,1,0:T(8,128)(2,1)} %pad_maximum_fusion.refs_3_), custom_call_target="tpu_custom_call" | custom-call | tf_op jit(solution)/shard_map/pallas_call | solution.py:83
  107.3 3.0 %fusion.10 = bf16[8,2,512,136]{2,3,1,0:T(8,128)(2,1)S(1)} fusion(f32[8,2,512,136]{2,3,1,0:T(8,128)} %fusion.22, bf16[8,2,512,16]{3,2,1,0:T(8,128)(2,1)S(1)} %bitcast.54, bf16[16,136,1,1]{1,0,3,2:T(8,128)(2,1)S(1)} %copy-done.6, bf16[136]{0:T(256)(128)(2,1)S(1)} %copy-done.8), kind=kOutput, calls=%fused_computation.13 | convolution fusion | flops 40108032 | bytes 6951440 | tf_op jit(solution)/shard_map/...d,df->...f/dot_general | solution.py:31
  110.3 1.3 add.18
  111.8 3.7 %fusion.5 = f32[8,2,512,128]{3,2,1,0:T(8,128)} fusion(bf16[8,2,512,136]{2,3,1,0:T(8,128)(2,1)S(1)} %fusion.10, bf16[8,2,512,16]{2,3,1,0:T(8,128)(2,1)S(1)} %multiply_convert_fusion.2, bf16[153]{0:T(256)(128)(2,1)S(1)} %pad.9.clone, f32[8,1,153,128]{3,2,1,0:T(8,128)S(1)} %slice.26, f32[8,153,128]{2,1,0:T(8,128)S(1)} %copy.101), kind=kOutput, calls=%fused_computation.7 | convolution fusion | flops 329011200 | bytes 7938354 | tf_op jit(solution)/shard_map/hnrf,hnfv->hnrv/dot_general | solution.py:175
  115.5 8.4 %shard_map.92 = bf16[1024,1024]{1,0:T(8,128)(2,1)} custom-call(f32[1024,1024]{1,0:T(8,128)} %get-tuple-element.11.intra_ref, f32[8,1024,128]{2,1,0:T(8,128)} %bitcast.60, f32[1024,1024]{1,0:T(8,128)} %get-tuple-element.12.win_ref, f32[1,1024]{1,0:T(1,128)} %bitcast.67), custom_call_target="tpu_custom_call" | custom-call | tf_op jit(solution)/shard_map/pallas_call | solution.py:111
  123.9 29.3 %all_to_all.73 = bf16[4,256,1024]{2,1,0:T(8,128)(2,1)S(1)} all-to-all(bf16[4,256,1024]{2,1,0:T(8,128)(2,1)} %bitcast.62), channel_id=1, replica_groups=mesh['groups'=2,'ctx'=4,'head'=4] {'head'}, dimensions={0} | all-to-all | bytes 4194304 | tf_op jit(solution)/shard_map/all_to_all | solution.py:190
  153.2 1.5 copy.109
  (35 shorter events, 3.7 us)
Async XLA Ops:
  1.8 10.2 %all-to-all-start = ((bf16[32,256,16]{1,2,0:T(8,128)(2,1)}), bf16[32,256,16]{1,2,0:T(8,128)(2,1)S(1)}, u32[]{:S(2)}, u32[]{:S(2)}) async-start(bf16[32,256,16]{1,2,0:T(8,128)(2,1)} %bitcast.2), calls=%async_computation | async-start | bytes 524288 | tf_op jit(solution)/shard_map/all_to_all | solution.py:130
  12.0 30.2 %all-to-all-start.1 = ((bf16[32,256,128]{1,2,0:T(8,128)(2,1)}), bf16[32,256,128]{1,2,0:T(8,128)(2,1)}, u32[]{:S(2)}, u32[]{:S(2)}) async-start(bf16[32,256,128]{1,2,0:T(8,128)(2,1)} %bitcast.11), calls=%async_computation.1 | async-start | bytes 4194304 | tf_op jit(solution)/shard_map/all_to_all | solution.py:130
  16.5 1.5 copy-start.6
  17.9 0.8 copy-start.7
  46.2 6.7 %copy-start.2 = (bf16[8,4,256,128]{3,2,1,0:T(8,128)(2,1)S(1)}, bf16[8,4,256,128]{3,2,1,0:T(8,128)(2,1)}, u32[]{:S(2)}) copy-start(bf16[8,4,256,128]{3,2,1,0:T(8,128)(2,1)} %copy.89) | copy-start | bytes 6291460
  46.2 6.7 %copy-start.4 = (bf16[8,2,512,136]{2,3,1,0:T(8,128)(2,1)S(1)}, bf16[8,2,512,136]{2,3,1,0:T(8,128)(2,1)}, u32[]{:S(2)}) copy-start(bf16[8,2,512,136]{2,3,1,0:T(8,128)(2,1)} %fusion.11) | copy-start | bytes 6684676
  48.1 20.6 %collective-permute-start.1 = (bf16[8,64,144]{2,1,0:T(8,128)(2,1)}, bf16[8,64,144]{2,1,0:T(8,128)(2,1)}, u32[]{:S(2)}, u32[]{:S(2)}) collective-permute-start(bf16[8,64,144]{2,1,0:T(8,128)(2,1)} %pad_maximum_fusion.1), channel_id=1, source_target_pairs={{0,4},{4,8},{8,12},{1,5},{5,9},{9,13},{2,6},{6,10},{10,14},{3,7},{... | collective-permute-start | bytes 442376 | tf_op jit(solution)/shard_map/ppermute | solution.py:24
  56.4 20.2 %collective-permute-start = (f32[8,153,128]{2,0,1:T(8,128)}, f32[8,153,128]{2,0,1:T(8,128)}, u32[]{:S(2)}, u32[]{:S(2)}) collective-permute-start(f32[8,153,128]{2,0,1:T(8,128)} %copy.92), channel_id=1, source_target_pairs={{0,4},{4,8},{8,12},{1,5},{5,9},{9,13},{2,6},{6,10},{10,14},{3,7},{... | collective-permute-start | bytes 1880072 | tf_op jit(solution)/shard_map/ppermute | solution.py:24
  61.5 8.2 %copy-start.3 = (bf16[8,4,256,128]{3,2,1,0:T(8,128)(2,1)S(1)}, bf16[8,4,256,128]{3,2,1,0:T(8,128)(2,1)}, u32[]{:S(2)}) copy-start(bf16[8,4,256,128]{3,2,1,0:T(8,128)(2,1)} %copy.89) | copy-start | bytes 6291460
  64.6 10.1 %all-to-all-start.2 = ((bf16[32,256,16]{1,2,0:T(8,128)(2,1)}), bf16[32,256,16]{1,2,0:T(8,128)(2,1)}, u32[]{:S(2)}, u32[]{:S(2)}) async-start(bf16[32,256,16]{1,2,0:T(8,128)(2,1)} %bitcast.66), calls=%async_computation.2 | async-start | bytes 524288 | tf_op jit(solution)/shard_map/all_to_all | solution.py:130
  76.6 4.3 %copy-start = (bf16[8,4,256,16]{3,2,1,0:T(8,128)(2,1)}, bf16[8,4,256,16]{3,2,1,0:T(8,128)(2,1)S(1)}, u32[]{:S(2)}) copy-start(bf16[8,4,256,16]{3,2,1,0:T(8,128)(2,1)S(1)} %copy.91) | copy-start | bytes 786436
  83.2 24.0 %copy-start.5 = (bf16[8,2,512,16]{2,3,1,0:T(8,128)(2,1)S(1)}, bf16[8,2,512,16]{2,3,1,0:T(8,128)(2,1)}, u32[]{:S(2)}) copy-start(bf16[8,2,512,16]{2,3,1,0:T(8,128)(2,1)} %copy.97) | copy-start | bytes 786436
  83.2 27.1 %collective-permute-start.2 = (f32[8,153,128]{2,0,1:T(8,128)}, f32[8,153,128]{2,0,1:T(8,128)}, u32[]{:S(2)}, u32[]{:S(2)}) collective-permute-start(f32[8,153,128]{2,0,1:T(8,128)} %copy_add_fusion), channel_id=1, source_target_pairs={{0,8},{4,12},{1,9},{5,13},{2,10},{6,14},{3,11},{7,15},{16,24},{20,... | collective-permute-start | bytes 1880072 | tf_op jit(solution)/shard_map/ppermute | solution.py:24
  86.3 20.9 %copy-start.1 = (bf16[8,4,256,16]{3,2,1,0:T(8,128)(2,1)S(1)}, bf16[8,4,256,16]{3,2,1,0:T(8,128)(2,1)}, u32[]{:S(2)}) copy-start(bf16[8,4,256,16]{3,2,1,0:T(8,128)(2,1)} %copy-done) | copy-start | bytes 786436
  86.3 20.9 %copy-start.8 = (bf16[136]{0:T(256)(128)(2,1)S(1)}, bf16[136]{0:T(256)(128)(2,1)}, u32[]{:S(2)}) copy-start(bf16[136]{0:T(256)(128)(2,1)} %constant.30.clone) | copy-start | bytes 820

commit v14 on v13

--- a/solution.py
+++ b/solution.py
@@ -129,8 +129,10 @@
         tok = jnp.transpose(tok.reshape(local_tokens, HEADS, width), (1, 0, 2))
         return lax.all_to_all(tok, "head", split_axis=0, concat_axis=1, tiled=True)
 
+    key_hm = to_heads(keys, KD)
+    query_hm = to_heads(queries, KD)
+    values, query_hm = lax.optimization_barrier((values, query_hm))
     value_hm = to_heads(values, VD)
-    key_hm = to_heads(keys, KD)
     heads_here, span_rows, _ = key_hm.shape
     block_rows = min(512, span_rows)
     block_count = span_rows // block_rows
@@ -163,8 +165,6 @@
             running = running + received
     if entering is None:
         entering = jnp.zeros_like(span_state)
-    queries, span_state = lax.optimization_barrier((queries, span_state))
-    query_hm = to_heads(queries, KD)
     query_hm, first_round = lax.optimization_barrier((query_hm, first_round))
     before = jnp.concatenate(
         [jnp.zeros_like(block_states[:, :1]), jnp.cumsum(block_states[:, :-1], axis=1)], axis=1

time: 156 us -> 164 us (1.051)
  starting transfers between devices: 24.2 us -> 26.9 us
  local copies, waits for them, and re-layouts: 25.7 us -> 28.2 us
  waiting for transfers between devices: 23.6 us -> 25.4 us
  other arithmetic: 7.54 us -> 9.2 us
    ppermute x3, starting transfers between devices: 11.5 us -> 14.8 us  [shifted(): return lax.ppermute(shard, axis, pairs)]
    optimization_barrier x1, local copies, waits for them, and re-layouts: 1.78 us -> 4.47 us  [per_device(): values, query_hm = lax.optimization_barrier((values, query_hm))]
    unnamed x20 -> x22, local copies, waits for them, and re-layouts: 5.88 us -> 3.63 us
    all_to_all x3, waiting for transfers between devices: 23.6 us -> 25.3 us  [to_heads(): return lax.all_to_all(tok, 'head', split_axis=0, concat_axis=1, tiled=True)]
  transfers between devices with their start and end apart: 6 -> 6, of which waited for: 3 -> 4; matrix products, arithmetic and copies ran while one was open for 18% -> 19% of each run, Pallas kernels for 13% -> 13%
where the time goes in v14:
time: 164 us; the launch traced here: 163 us
  Pallas kernels  29.3 us (18%)
  blocking collectives  29.3 us (18%)
  local copies, waits for them, and re-layouts  28.2 us (17%)
  starting transfers between devices  26.9 us (16%)
  waiting for transfers between devices  25.4 us (15%)
  matrix products  14.8 us (9%)
  other arithmetic  9.2 us (6%)
    all_to_all x1, blocking collectives, per_device(): lax.all_to_all(mixed, 'head', split_axis=0, concat_axis=1, tiled=True)  29.3 us
    all_to_all x3, waiting for transfers between devices, to_heads(): return lax.all_to_all(tok, 'head', split_axis=0, concat_axis=1, tiled=True)  25.3 us
    pallas_call x1, Pallas kernels, local_attention(): pl.pallas_call(body, grid_spec=pltpu.PrefetchScalarGridSpec(num_scalar_pr...  20.9 us
    ppermute x3, starting transfers between devices, shifted(): return lax.ppermute(shard, axis, pairs)  14.8 us
    all_to_all x3, starting transfers between devices, to_heads(): return lax.all_to_all(tok, 'head', split_axis=0, concat_axis=1, tiled=True)  12.1 us
    all_to_all x5, local copies, waits for them, and re-layouts, to_heads(): return lax.all_to_all(tok, 'head', split_axis=0, concat_axis=1, tiled=True)  9.4 us
    pallas_call x1, Pallas kernels, mix(): pl.pallas_call(mix_kernel, grid=(heads_here,), in_specs=[tile, pl.BlockSp...  8.42 us
    dot_general x2, matrix products, unique_features(): jnp.einsum('...d,df->...f', vector, pick_cols, preferred_element_type=jnp...  4.95 us
  transfers between devices with their start and end apart: 6, of which 4 were waited for; matrix products, arithmetic and copies ran while one was open for 19% of the time, Pallas kernels for 13%

profile of v14, /device:TPU:0, one launch (start us, length us, event | category | flops | bytes accessed | tf_op | source)
XLA Modules:
  0.0 163.3 jit_solution(1464162111571516180)
XLA Ops:
  0.0 1.8 %copy.82 = bf16[256,512]{0,1:T(8,128)(2,1)} copy(bf16[256,512]{1,0:T(8,128)(2,1)} %param.9) | data formatting | bytes 524288 | tf_op args[0]
  1.8 4.2 %all-to-all-start = ((bf16[32,256,16]{1,2,0:T(8,128)(2,1)}), bf16[32,256,16]{1,2,0:T(8,128)(2,1)S(1)}, u32[]{:S(2)}, u32[]{:S(2)}) async-start(bf16[32,256,16]{1,2,0:T(8,128)(2,1)} %bitcast.2), calls=%async_computation | async-start | bytes 524288 | tf_op jit(solution)/shard_map/all_to_all | solution.py:130
  6.0 1.8 %copy.84 = bf16[256,512]{0,1:T(8,128)(2,1)} copy(bf16[256,512]{1,0:T(8,128)(2,1)} %param.10) | data formatting | bytes 524288 | tf_op args[1]
  7.8 4.2 %all-to-all-done = bf16[32,256,16]{1,2,0:T(8,128)(2,1)S(1)} async-done(((bf16[32,256,16]{1,2,0:T(8,128)(2,1)}), bf16[32,256,16]{1,2,0:T(8,128)(2,1)S(1)}, u32[]{:S(2)}, u32[]{:S(2)}) %all-to-all-start) | async-done | bytes 262176 | tf_op jit(solution)/shard_map/all_to_all | solution.py:130
  12.0 3.4 %all-to-all-start.1 = ((bf16[32,256,16]{1,2,0:T(8,128)(2,1)}), bf16[32,256,16]{1,2,0:T(8,128)(2,1)S(1)}, u32[]{:S(2)}, u32[]{:S(2)}) async-start(bf16[32,256,16]{1,2,0:T(8,128)(2,1)} %bitcast.7), calls=%async_computation.1 | async-start | bytes 524288 | tf_op jit(solution)/shard_map/all_to_all | solution.py:130
  16.5 4.5 %copy.89 = bf16[256,4096]{0,1:T(8,128)(2,1)} copy(bf16[256,4096]{1,0:T(8,128)(2,1)} %param.11) | data formatting | bytes 4194304 | tf_op jit(solution)/shard_map/optimization_barrier | solution.py:134
  21.5 4.5 %all-to-all-start.2 = ((bf16[32,256,128]{1,2,0:T(8,128)(2,1)}), bf16[32,256,128]{1,2,0:T(8,128)(2,1)}, u32[]{:S(2)}, u32[]{:S(2)}) async-start(bf16[32,256,128]{1,2,0:T(8,128)(2,1)} %bitcast.61), calls=%async_computation.2 | async-start | bytes 4194304 | tf_op jit(solution)/shard_map/all_to_all | solution.py:130
  26.2 1.7 %copy.93 = bf16[8,4,256,16]{3,2,1,0:T(8,128)(2,1)} copy(bf16[8,4,256,16]{2,3,0,1:T(8,128)(2,1)S(1)} %bitcast.65) | data formatting | bytes 524288 | tf_op jit(solution)/shard_map/all_to_all | solution.py:130
  28.9 2.1 %fusion.11 = bf16[8,2,512,136]{2,3,1,0:T(8,128)(2,1)} fusion(f32[136,8,2,512]{3,0,2,1:T(8,128)S(1)} %fusion.16, bf16[16,136,1,1]{1,0,3,2:T(8,128)(2,1)S(1)} %copy-done.6, bf16[8,2,512,16]{2,1,3,0:T(2,128)(2,1)S(1)} %reshape.40), kind=kOutput, calls=%fused_computation.14 | convolution fusion | flops 38993920 | bytes 6951168 | tf_op jit(solution)/shard_map/...d,df->...f/dot_general | solution.py:32
  31.1 20.6 %all-to-all-done.2 = bf16[32,256,128]{1,2,0:T(8,128)(2,1)} async-done(((bf16[32,256,128]{1,2,0:T(8,128)(2,1)}), bf16[32,256,128]{1,2,0:T(8,128)(2,1)}, u32[]{:S(2)}, u32[]{:S(2)}) %all-to-all-start.2) | async-done | bytes 2097184 | tf_op jit(solution)/shard_map/all_to_all | solution.py:130
  51.7 3.9 %copy.91 = bf16[8,4,256,128]{3,2,1,0:T(8,128)(2,1)} copy(bf16[8,4,256,128]{2,3,0,1:T(8,128)(2,1)} %bitcast.19) | data formatting | bytes 4194304 | tf_op jit(solution)/shard_map/all_to_all | solution.py:130
  55.6 2.0 %pad_maximum_fusion.1 = bf16[8,64,144]{2,1,0:T(8,128)(2,1)} fusion(bf16[8,1024,128]{2,1,0:T(8,128)(2,1)} %bitcast.57, bf16[8,1024,16]{2,1,0:T(8,128)(2,1)} %bitcast.55), kind=kLoop, calls=%fused_computation.21 | loop fusion | flops 294912 | bytes 2506752 | tf_op jit(solution)/shard_map/concatenate | solution.py:142
  57.6 4.8 %collective-permute-start.1 = (bf16[8,64,144]{2,1,0:T(8,128)(2,1)}, bf16[8,64,144]{2,1,0:T(8,128)(2,1)}, u32[]{:S(2)}, u32[]{:S(2)}) collective-permute-start(bf16[8,64,144]{2,1,0:T(8,128)(2,1)} %pad_maximum_fusion.1), channel_id=1, source_target_pairs={{0,4},{4,8},{8,12},{1,5},{5,9},{9,13},{2,6},{6,10},{10,14},{3,7},{... | collective-permute-start | bytes 442376 | tf_op jit(solution)/shard_map/ppermute | solution.py:24
  62.4 2.4 %fusion.21 = (f32[8,153,128]{2,1,0:T(8,128)S(1)}, f32[8,2,153,128]{3,2,1,0:T(8,128)}) fusion(bf16[8,2,512,128]{3,2,1,0:T(8,128)(2,1)S(1)} %bitcast.59, bf16[8,2,512,136]{2,3,1,0:T(8,128)(2,1)S(1)} %copy-done.3, bf16[8,2,512,16]{2,3,1,0:T(8,128)(2,1)S(1)} %multiply_convert_fusion.3, bf16[153]{0:T(256)(128)(2,1)S(1)} %pad.9.clone), kind=kOutput, calls=%fused_computation.28 | convolution fusion | flops 328541184 | bytes 6467890 | tf_op jit(solution)/shard_map/hnrf,hnrv->hnfv/dot_general | solution.py:146
  64.7 1.2 copy.92
  65.9 3.7 %collective-permute-start = (f32[8,153,128]{2,0,1:T(8,128)}, f32[8,153,128]{2,0,1:T(8,128)}, u32[]{:S(2)}, u32[]{:S(2)}) collective-permute-start(f32[8,153,128]{2,0,1:T(8,128)} %copy.92), channel_id=1, source_target_pairs={{0,4},{4,8},{8,12},{1,5},{5,9},{9,13},{2,6},{6,10},{10,14},{3,7},{... | collective-permute-start | bytes 1880072 | tf_op jit(solution)/shard_map/ppermute | solution.py:24
  70.2 2.5 %copy.96 = bf16[8,1024,16]{1,2,0:T(8,128)(2,1)} copy(bf16[8,1024,16]{2,1,0:T(8,128)(2,1)} %bitcast.56) | data formatting | bytes 524288 | tf_op jit(solution)/shard_map/all_to_all | solution.py:130
  72.7 1.1 slice.26
  75.5 1.8 %concatenate.20 = bf16[8,1152,16]{1,2,0:T(8,128)(2,1)} concatenate(bf16[8,64,16]{1,2,0:T(8,128)(2,1)S(1)} %slice.18, bf16[8,64,16]{1,2,0:T(8,128)(2,1)} %copy.95, bf16[8,1024,16]{1,2,0:T(8,128)(2,1)} %copy.96), dimensions={1} | concatenate | bytes 589824 | tf_op jit(solution)/shard_map/concatenate | solution.py:183
  77.3 1.1 slice.25
  78.3 3.5 %pad_maximum_fusion.refs_3_ = bf16[8,1152,128]{2,1,0:T(8,128)(2,1)} fusion(bf16[8,1024,128]{2,1,0:T(8,128)(2,1)} %bitcast.58, bf16[8,64,128]{2,1,0:T(8,128)(2,1)S(1)} %slice.25, bf16[1152]{0:T(1024)(128)(2,1)} %pad.4.clone), kind=kLoop, calls=%fused_computation.12 | loop fusion | flops 7077888 | bytes 4589824 | tf_op jit(solution)/shard_map/concatenate | solution.py:184
  82.0 1.4 copy.97
  83.4 2.8 %fusion.22 = f32[8,2,512,136]{2,3,1,0:T(8,128)} fusion(bf16[8,2,512,16]{3,2,1,0:T(8,128)(2,1)S(1)} %bitcast.52, bf16[16,136,1,1]{1,0,3,2:T(8,128)(2,1)S(1)} %copy-done.6), kind=kOutput, calls=%fused_computation.29 | convolution fusion | flops 35651584 | bytes 4722944 | tf_op jit(solution)/shard_map/...d,df->...f/dot_general | solution.py:32
  86.2 2.3 %copy_add_fusion = f32[8,153,128]{2,0,1:T(8,128)} fusion(f32[8,153,128]{2,0,1:T(8,128)} %collective-permute-done, f32[8,153,128]{2,1,0:T(8,128)S(1)} %get-tuple-element.15), kind=kLoop, calls=%fused_computation.30 | loop fusion | flops 156672 | bytes 1880064 | tf_op jit(solution)/shard_map/add | solution.py:165
  88.5 6.4 %collective-permute-start.2 = (f32[8,153,128]{2,0,1:T(8,128)}, f32[8,153,128]{2,0,1:T(8,128)}, u32[]{:S(2)}, u32[]{:S(2)}) collective-permute-start(f32[8,153,128]{2,0,1:T(8,128)} %copy_add_fusion), channel_id=1, source_target_pairs={{0,8},{4,12},{1,9},{5,13},{2,10},{6,14},{3,11},{7,15},{16,24},{20,... | collective-permute-start | bytes 1880072 | tf_op jit(solution)/shard_map/ppermute | solution.py:24
  94.8 20.9 %shard_map.91 = (f32[1024,1024]{1,0:T(8,128)}, f32[1024,1024]{1,0:T(8,128)}) custom-call(s32[1]{0:T(128)} %bitcast.refs_0_, bf16[8,1024,16]{2,1,0:T(8,128)(2,1)} %bitcast.53, bf16[8,16,1152]{2,1,0:T(8,128)(2,1)} %bitcast.66, bf16[8,1152,128]{2,1,0:T(8,128)(2,1)} %pad_maximum_fusion.refs_3_), custom_call_target="tpu_custom_call" | custom-call | tf_op jit(solution)/shard_map/pallas_call | solution.py:83
  115.8 3.1 %fusion.10 = bf16[8,2,512,136]{2,3,1,0:T(8,128)(2,1)S(1)} fusion(f32[8,2,512,136]{2,3,1,0:T(8,128)} %fusion.22, bf16[8,2,512,16]{3,2,1,0:T(8,128)(2,1)S(1)} %bitcast.54, bf16[16,136,1,1]{1,0,3,2:T(8,128)(2,1)S(1)} %copy-done.5, bf16[136]{0:T(256)(128)(2,1)S(1)} %copy-done.7), kind=kOutput, calls=%fused_computation.13 | convolution fusion | flops 40108032 | bytes 6951440 | tf_op jit(solution)/shard_map/...d,df->...f/dot_general | solution.py:31
  118.9 1.3 add.18
  120.4 3.7 %fusion.5 = f32[8,2,512,128]{3,2,1,0:T(8,128)} fusion(bf16[8,2,512,136]{2,3,1,0:T(8,128)(2,1)S(1)} %fusion.10, bf16[8,2,512,16]{2,3,1,0:T(8,128)(2,1)S(1)} %multiply_convert_fusion.2, bf16[153]{0:T(256)(128)(2,1)S(1)} %copy-done.9, f32[8,1,153,128]{3,2,1,0:T(8,128)S(1)} %slice.26, f32[8,153,128]{2,1,0:T(8,128)S(1)} %copy.101), kind=kOutput, calls=%fused_computation.7 | convolution fusion | flops 329011200 | bytes 7938354 | tf_op jit(solution)/shard_map/hnrf,hnfv->hnrv/dot_general | solution.py:175
  124.0 8.4 %shard_map.92 = bf16[1024,1024]{1,0:T(8,128)(2,1)} custom-call(f32[1024,1024]{1,0:T(8,128)} %get-tuple-element.13.intra_ref, f32[8,1024,128]{2,1,0:T(8,128)} %bitcast.60, f32[1024,1024]{1,0:T(8,128)} %get-tuple-element.14.win_ref, f32[1,1024]{1,0:T(1,128)} %bitcast.68), custom_call_target="tpu_custom_call" | custom-call | tf_op jit(solution)/shard_map/pallas_call | solution.py:111
  132.5 29.3 %all_to_all.73 = bf16[4,256,1024]{2,1,0:T(8,128)(2,1)S(1)} all-to-all(bf16[4,256,1024]{2,1,0:T(8,128)(2,1)} %bitcast.63), channel_id=1, replica_groups=mesh['groups'=2,'ctx'=4,'head'=4] {'head'}, dimensions={0} | all-to-all | bytes 4194304 | tf_op jit(solution)/shard_map/all_to_all | solution.py:190
  161.7 1.6 copy.109
  (37 shorter events, 5.2 us)
Async XLA Ops:
  1.8 10.2 %all-to-all-start = ((bf16[32,256,16]{1,2,0:T(8,128)(2,1)}), bf16[32,256,16]{1,2,0:T(8,128)(2,1)S(1)}, u32[]{:S(2)}, u32[]{:S(2)}) async-start(bf16[32,256,16]{1,2,0:T(8,128)(2,1)} %bitcast.2), calls=%async_computation | async-start | bytes 524288 | tf_op jit(solution)/shard_map/all_to_all | solution.py:130
  12.0 9.4 %all-to-all-start.1 = ((bf16[32,256,16]{1,2,0:T(8,128)(2,1)}), bf16[32,256,16]{1,2,0:T(8,128)(2,1)S(1)}, u32[]{:S(2)}, u32[]{:S(2)}) async-start(bf16[32,256,16]{1,2,0:T(8,128)(2,1)} %bitcast.7), calls=%async_computation.1 | async-start | bytes 524288 | tf_op jit(solution)/shard_map/all_to_all | solution.py:130
  16.5 66.9 %copy-start = (bf16[8,4,256,16]{3,2,1,0:T(8,128)(2,1)}, bf16[8,4,256,16]{3,2,1,0:T(8,128)(2,1)S(1)}, u32[]{:S(2)}) copy-start(bf16[8,4,256,16]{3,2,1,0:T(8,128)(2,1)S(1)} %copy.83) | copy-start | bytes 786436
  21.5 30.2 %all-to-all-start.2 = ((bf16[32,256,128]{1,2,0:T(8,128)(2,1)}), bf16[32,256,128]{1,2,0:T(8,128)(2,1)}, u32[]{:S(2)}, u32[]{:S(2)}) async-start(bf16[32,256,128]{1,2,0:T(8,128)(2,1)} %bitcast.61), calls=%async_computation.2 | async-start | bytes 4194304 | tf_op jit(solution)/shard_map/all_to_all | solution.py:130
  25.9 2.2 %copy-start.5 = (bf16[16,136,1,1]{1,0,3,2:T(8,128)(2,1)S(1)}, bf16[16,136,1,1]{1,0,3,2:T(8,128)(2,1)}, u32[]{:S(2)}) copy-start(bf16[16,136,1,1]{1,0,3,2:T(8,128)(2,1)} %constant.33) | copy-start | bytes 13060
  25.9 36.4 %copy-start.8 = (bf16[153]{0:T(256)(128)(2,1)}, bf16[153]{0:T(256)(128)(2,1)S(1)}, u32[]{:S(2)}) copy-start(bf16[153]{0:T(256)(128)(2,1)S(1)} %pad.9.clone) | copy-start | bytes 922
  28.1 0.8 copy-start.6
  55.6 6.8 %copy-start.2 = (bf16[8,4,256,128]{3,2,1,0:T(8,128)(2,1)S(1)}, bf16[8,4,256,128]{3,2,1,0:T(8,128)(2,1)}, u32[]{:S(2)}) copy-start(bf16[8,4,256,128]{3,2,1,0:T(8,128)(2,1)} %copy.91) | copy-start | bytes 6291460
  55.6 6.8 %copy-start.3 = (bf16[8,2,512,136]{2,3,1,0:T(8,128)(2,1)S(1)}, bf16[8,2,512,136]{2,3,1,0:T(8,128)(2,1)}, u32[]{:S(2)}) copy-start(bf16[8,2,512,136]{2,3,1,0:T(8,128)(2,1)} %fusion.11) | copy-start | bytes 6684676
  57.6 16.3 %collective-permute-start.1 = (bf16[8,64,144]{2,1,0:T(8,128)(2,1)}, bf16[8,64,144]{2,1,0:T(8,128)(2,1)}, u32[]{:S(2)}, u32[]{:S(2)}) collective-permute-start(bf16[8,64,144]{2,1,0:T(8,128)(2,1)} %pad_maximum_fusion.1), channel_id=1, source_target_pairs={{0,4},{4,8},{8,12},{1,5},{5,9},{9,13},{2,6},{6,10},{10,14},{3,7},{... | collective-permute-start | bytes 442376 | tf_op jit(solution)/shard_map/ppermute | solution.py:24
  65.9 16.0 %collective-permute-start = (f32[8,153,128]{2,0,1:T(8,128)}, f32[8,153,128]{2,0,1:T(8,128)}, u32[]{:S(2)}, u32[]{:S(2)}) collective-permute-start(f32[8,153,128]{2,0,1:T(8,128)} %copy.92), channel_id=1, source_target_pairs={{0,4},{4,8},{8,12},{1,5},{5,9},{9,13},{2,6},{6,10},{10,14},{3,7},{... | collective-permute-start | bytes 1880072 | tf_op jit(solution)/shard_map/ppermute | solution.py:24
  88.5 27.3 %copy-start.4 = (bf16[8,2,512,16]{2,3,1,0:T(8,128)(2,1)S(1)}, bf16[8,2,512,16]{2,3,1,0:T(8,128)(2,1)}, u32[]{:S(2)}) copy-start(bf16[8,2,512,16]{2,3,1,0:T(8,128)(2,1)} %copy.97) | copy-start | bytes 786436
  88.5 30.4 %collective-permute-start.2 = (f32[8,153,128]{2,0,1:T(8,128)}, f32[8,153,128]{2,0,1:T(8,128)}, u32[]{:S(2)}, u32[]{:S(2)}) collective-permute-start(f32[8,153,128]{2,0,1:T(8,128)} %copy_add_fusion), channel_id=1, source_target_pairs={{0,8},{4,12},{1,9},{5,13},{2,10},{6,14},{3,11},{7,15},{16,24},{20,... | collective-permute-start | bytes 1880072 | tf_op jit(solution)/shard_map/ppermute | solution.py:24
  94.8 21.0 %copy-start.1 = (bf16[8,4,256,16]{3,2,1,0:T(8,128)(2,1)S(1)}, bf16[8,4,256,16]{3,2,1,0:T(8,128)(2,1)}, u32[]{:S(2)}) copy-start(bf16[8,4,256,16]{3,2,1,0:T(8,128)(2,1)} %copy-done) | copy-start | bytes 786436
  94.8 21.0 %copy-start.7 = (bf16[136]{0:T(256)(128)(2,1)S(1)}, bf16[136]{0:T(256)(128)(2,1)}, u32[]{:S(2)}) copy-start(bf16[136]{0:T(256)(128)(2,1)} %constant.30.clone) | copy-start | bytes 820
  118.9 1.5 copy-start.9

commit v15 on v13

--- a/solution.py
+++ b/solution.py
@@ -43,15 +43,17 @@
 LEAD = 128
 
 
-def local_attention_kernel(flag_ref, q_ref, kt_ref, vx_ref, intra_ref, win_ref, *, span_rows, block_rows):
+def local_attention_kernel(
+    flag_ref, q_ref, kt_ref, ktail_ref, v_ref, vtail_ref, intra_ref, win_ref, *, span_rows, block_rows
+):
     first_span = flag_ref[0] == 1
     for i in range(span_rows // CHUNK):
         r0 = i * CHUNK
         q_c = q_ref[0, r0 : r0 + CHUNK, :]
         bs = (r0 // block_rows) * block_rows
         width = r0 + CHUNK - bs
-        k_i = kt_ref[0, :, LEAD + bs : LEAD + r0 + CHUNK]
-        v_i = vx_ref[0, LEAD + bs : LEAD + r0 + CHUNK, :]
+        k_i = kt_ref[0, :, bs : r0 + CHUNK]
+        v_i = v_ref[0, bs : r0 + CHUNK, :]
         scores = jnp.dot(q_c, k_i, preferred_element_type=jnp.float32) * 0.25
         row = lax.broadcasted_iota(jnp.int32, (CHUNK, width), 0)
         col = lax.broadcasted_iota(jnp.int32, (CHUNK, width), 1)
@@ -60,8 +62,12 @@
         ).astype(jnp.bfloat16)
         intra_ref[r0 : r0 + CHUNK, :] = jnp.dot(kernel, v_i, preferred_element_type=jnp.float32)
 
-        k_w = kt_ref[0, :, r0 : r0 + CHUNK + LEAD]
-        v_w = vx_ref[0, r0 : r0 + CHUNK + LEAD, :]
+        if i == 0:
+            k_w = jnp.concatenate([ktail_ref[0], kt_ref[0, :, 0:CHUNK]], axis=1)
+            v_w = jnp.concatenate([vtail_ref[0], v_ref[0, 0:CHUNK, :]], axis=0)
+        else:
+            k_w = kt_ref[0, :, r0 - LEAD : r0 + CHUNK]
+            v_w = v_ref[0, r0 - LEAD : r0 + CHUNK, :]
         ws = jnp.dot(q_c, k_w, preferred_element_type=jnp.float32) * 0.25
         wrow = lax.broadcasted_iota(jnp.int32, (CHUNK, CHUNK + LEAD), 0)
         wcol = lax.broadcasted_iota(jnp.int32, (CHUNK, CHUNK + LEAD), 1)
@@ -75,9 +81,8 @@
         win_ref[r0 : r0 + CHUNK, :] = jnp.dot(weights, v_w, preferred_element_type=jnp.float32)
 
 
-def local_attention(flag, q_hm, kt_hm, vx, block_rows):
+def local_attention(flag, q_hm, kt_hm, ktail, v_hm, vtail, block_rows):
     heads_here, span_rows, _ = q_hm.shape
-    ext = kt_hm.shape[2]
     body = lambda *refs: local_attention_kernel(*refs, span_rows=span_rows, block_rows=block_rows)
     out = jax.ShapeDtypeStruct((span_rows, heads_here * VD), jnp.float32)
     return pl.pallas_call(
@@ -87,8 +92,10 @@
             grid=(heads_here,),
             in_specs=[
                 pl.BlockSpec((1, span_rows, KD), lambda h, f: (h, 0, 0)),
-                pl.BlockSpec((1, KD, ext), lambda h, f: (h, 0, 0)),
-                pl.BlockSpec((1, ext, VD), lambda h, f: (h, 0, 0)),
+                pl.BlockSpec((1, KD, span_rows), lambda h, f: (h, 0, 0)),
+                pl.BlockSpec((1, KD, LEAD), lambda h, f: (h, 0, 0)),
+                pl.BlockSpec((1, span_rows, VD), lambda h, f: (h, 0, 0)),
+                pl.BlockSpec((1, LEAD, VD), lambda h, f: (h, 0, 0)),
             ],
             out_specs=[
                 pl.BlockSpec((span_rows, VD), lambda h, f: (0, h)),
@@ -96,7 +103,7 @@
             ],
         ),
         out_shape=(out, out),
-    )(flag, q_hm, kt_hm, vx)
+    )(flag, q_hm, kt_hm, ktail, v_hm, vtail)
 
 
 def mix_kernel(intra_ref, inter_ref, win_ref, gain_ref, out_ref):
@@ -180,11 +187,17 @@
     ).reshape(heads_here, span_rows, VD)
 
     lead = jnp.zeros((heads_here, LEAD - WINDOW, KD + VD), jnp.bfloat16)
-    key_ext = jnp.concatenate([lead[:, :, :KD], tails[:, :, :KD], key_hm], axis=1)
-    value_ext = jnp.concatenate([lead[:, :, KD:], tails[:, :, KD:], value_hm], axis=1)
+    key_tail = jnp.concatenate([lead[:, :, :KD], tails[:, :, :KD]], axis=1)
+    value_tail = jnp.concatenate([lead[:, :, KD:], tails[:, :, KD:]], axis=1)
     flag = first_span.astype(jnp.int32).reshape(1)
     intra, window = local_attention(
-        flag, query_hm, jnp.transpose(key_ext, (0, 2, 1)), value_ext, block_rows
+        flag,
+        query_hm,
+        jnp.transpose(key_hm, (0, 2, 1)),
+        jnp.transpose(key_tail, (0, 2, 1)),
+        value_hm,
+        value_tail,
+        block_rows,
     )
     mixed = mix(intra, inter, window, gain)
     tokens_back = lax.all_to_all(mixed, "head", split_axis=0, concat_axis=1, tiled=True)

time: 156 us -> 162 us (1.038)
  waiting for transfers between devices: 23.6 us -> 29.9 us
  other arithmetic: 7.54 us -> 4.81 us
  matrix products: 14.8 us -> 17.1 us
    ppermute x3, waiting for transfers between devices: 0.01 us -> 5.69 us  [shifted(): return lax.ppermute(shard, axis, pairs)]
    transpose x0 -> x3, local copies, waits for them, and re-layouts: none -> 3.29 us  [the longest x1 2.51 us: per_device(): jnp.transpose(key_hm, (0, 2, 1))]
    ppermute x3, starting transfers between devices: 11.5 us -> 14.1 us  [shifted(): return lax.ppermute(shard, axis, pairs)]
    dot_general x1, matrix products: 2.35 us -> 4.65 us  [per_device(): jnp.einsum('hnrf,hnrv->hnfv', key_feat, value_hm.reshape(heads_here, bloc...]
    unnamed x20 -> x28, local copies, waits for them, and re-layouts: 5.88 us -> 7.92 us
    slice x5 -> x2, local copies, waits for them, and re-layouts: 2.08 us -> 0.13 us  [the longest x1 0.1 us: per_device(): value_tail = jnp.concatenate([lead[:, :, KD:], tails[:, :, KD:]], axis=1)]
    concatenate x1 -> x0, other arithmetic: 1.93 us -> none  [per_device(): jnp.concatenate([lead[:, :, KD:], tails[:, :, KD:], value_hm], axis=1)]
    all_to_all x5 -> x4, local copies, waits for them, and re-layouts: 8.49 us -> 6.84 us  [to_heads(): return lax.all_to_all(tok, 'head', split_axis=0, concat_axis=1, tiled=True)]
  transfers between devices with their start and end apart: 6 -> 6, of which waited for: 3 -> 3; matrix products, arithmetic and copies ran while one was open for 18% -> 13% of each run, Pallas kernels for 13% -> 13%
where the time goes in v15:
time: 162 us; the launch traced here: 160 us
  waiting for transfers between devices  29.9 us (18%)
  Pallas kernels  29.4 us (18%)
  blocking collectives  29.3 us (18%)
  starting transfers between devices  25.5 us (16%)
  local copies, waits for them, and re-layouts  24.2 us (15%)
  matrix products  17.1 us (11%)
  other arithmetic  4.81 us (3%)
    all_to_all x1, blocking collectives, per_device(): lax.all_to_all(mixed, 'head', split_axis=0, concat_axis=1, tiled=True)  29.3 us
    all_to_all x3, waiting for transfers between devices, to_heads(): return lax.all_to_all(tok, 'head', split_axis=0, concat_axis=1, tiled=True)  24.2 us
    pallas_call x1, Pallas kernels, local_attention(): pl.pallas_call(body, grid_spec=pltpu.PrefetchScalarGridSpec(num_scalar_pr...  21 us
    ppermute x3, starting transfers between devices, shifted(): return lax.ppermute(shard, axis, pairs)  14.1 us
    all_to_all x3, starting transfers between devices, to_heads(): return lax.all_to_all(tok, 'head', split_axis=0, concat_axis=1, tiled=True)  11.4 us
    pallas_call x1, Pallas kernels, mix(): pl.pallas_call(mix_kernel, grid=(heads_here,), in_specs=[tile, pl.BlockSp...  8.42 us
    unnamed x28, local copies, waits for them, and re-layouts  7.92 us
    all_to_all x4, local copies, waits for them, and re-layouts, to_heads(): return lax.all_to_all(tok, 'head', split_axis=0, concat_axis=1, tiled=True)  6.84 us
  transfers between devices with their start and end apart: 6, of which 3 were waited for; matrix products, arithmetic and copies ran while one was open for 13% of the time, Pallas kernels for 13%

profile of v15, /device:TPU:0, one launch (start us, length us, event | category | flops | bytes accessed | tf_op | source)
XLA Modules:
  0.0 160.4 jit_solution(8737212429262580561)
XLA Ops:
  0.0 1.8 %copy.85 = bf16[256,512]{0,1:T(8,128)(2,1)} copy(bf16[256,512]{1,0:T(8,128)(2,1)} %param.10) | data formatting | bytes 524288 | tf_op args[1]
  1.8 4.2 %all-to-all-start = ((bf16[32,256,16]{1,2,0:T(8,128)(2,1)}), bf16[32,256,16]{1,2,0:T(8,128)(2,1)S(1)}, u32[]{:S(2)}, u32[]{:S(2)}) async-start(bf16[32,256,16]{1,2,0:T(8,128)(2,1)} %bitcast.2), calls=%async_computation | async-start | bytes 524288 | tf_op jit(solution)/shard_map/all_to_all | solution.py:137
  6.0 4.1 %copy.90 = bf16[256,4096]{0,1:T(8,128)(2,1)} copy(bf16[256,4096]{1,0:T(8,128)(2,1)} %param.11) | data formatting | bytes 4194304 | tf_op args[2]
  10.1 2.0 %all-to-all-done = bf16[32,256,16]{1,2,0:T(8,128)(2,1)S(1)} async-done(((bf16[32,256,16]{1,2,0:T(8,128)(2,1)}), bf16[32,256,16]{1,2,0:T(8,128)(2,1)S(1)}, u32[]{:S(2)}, u32[]{:S(2)}) %all-to-all-start) | async-done | bytes 262176 | tf_op jit(solution)/shard_map/all_to_all | solution.py:137
  12.0 3.7 %all-to-all-start.1 = ((bf16[32,256,128]{1,2,0:T(8,128)(2,1)}), bf16[32,256,128]{1,2,0:T(8,128)(2,1)S(1)}, u32[]{:S(2)}, u32[]{:S(2)}) async-start(bf16[32,256,128]{1,2,0:T(8,128)(2,1)} %bitcast.11), calls=%async_computation.1 | async-start | bytes 4194304 | tf_op jit(solution)/shard_map/all_to_all | solution.py:137
  16.3 0.8 fusion.16
  17.0 2.1 %fusion.11 = bf16[8,2,512,136]{2,3,1,0:T(8,128)(2,1)} fusion(f32[136,8,2,512]{3,0,2,1:T(8,128)S(1)} %fusion.16, bf16[16,136,1,1]{1,0,3,2:T(8,128)(2,1)S(1)} %copy-done.9, bf16[8,2,512,16]{2,1,3,0:T(2,128)(2,1)S(1)} %reshape.39), kind=kOutput, calls=%fused_computation.13 | convolution fusion | flops 38993920 | bytes 6951168 | tf_op jit(solution)/shard_map/...d,df->...f/dot_general | solution.py:32
  19.2 22.3 %all-to-all-done.1 = bf16[32,256,128]{1,2,0:T(8,128)(2,1)S(1)} async-done(((bf16[32,256,128]{1,2,0:T(8,128)(2,1)}), bf16[32,256,128]{1,2,0:T(8,128)(2,1)S(1)}, u32[]{:S(2)}, u32[]{:S(2)}) %all-to-all-start.1) | async-done | bytes 2097184 | tf_op jit(solution)/shard_map/all_to_all | solution.py:137
  41.4 1.3 copy-done.3
  42.8 3.0 %copy.92 = bf16[8,4,256,128]{3,2,1,0:T(8,128)(2,1)S(1)} copy(bf16[8,4,256,128]{2,3,0,1:T(8,128)(2,1)} %bitcast.64) | data formatting | bytes 4194304 | tf_op jit(solution)/shard_map/all_to_all | solution.py:137
  45.8 4.7 %fusion.21 = (f32[8,153,128]{2,1,0:T(8,128)S(1)}, f32[8,2,153,128]{3,2,1,0:T(8,128)}) fusion(bf16[8,2,512,128]{3,2,1,0:T(8,128)(2,1)S(1)} %bitcast.58, bf16[8,2,512,136]{2,3,1,0:T(8,128)(2,1)} %fusion.11, bf16[8,2,512,16]{2,3,1,0:T(8,128)(2,1)S(1)} %multiply_convert_fusion.3, bf16[153]{0:T(256)(128)(2,1)S(1)} %pad.8.clone), kind=kOutput, calls=%fused_computation.28 | convolution fusion | flops 328541184 | bytes 6467890 | tf_op jit(solution)/shard_map/hnrf,hnrv->hnfv/dot_general | solution.py:151
  50.5 1.2 copy.95
  51.7 4.9 %collective-permute-start = (f32[8,153,128]{2,0,1:T(8,128)}, f32[8,153,128]{2,0,1:T(8,128)}, u32[]{:S(2)}, u32[]{:S(2)}) collective-permute-start(f32[8,153,128]{2,0,1:T(8,128)} %copy.95), channel_id=1, source_target_pairs={{0,4},{4,8},{8,12},{1,5},{5,9},{9,13},{2,6},{6,10},{10,14},{3,7},{... | collective-permute-start | bytes 1880072 | tf_op jit(solution)/shard_map/ppermute | solution.py:24
  56.6 1.7 %copy.96 = bf16[8,4,256,16]{3,2,1,0:T(8,128)(2,1)} copy(bf16[8,4,256,16]{2,3,0,1:T(8,128)(2,1)S(1)} %bitcast.68) | data formatting | bytes 524288 | tf_op jit(solution)/shard_map/all_to_all | solution.py:137
  58.3 1.1 pad_maximum_fusion
  59.4 2.8 %collective-permute-start.1 = (bf16[8,64,144]{2,1,0:T(8,128)(2,1)S(1)}, bf16[8,64,144]{2,1,0:T(8,128)(2,1)S(1)}, u32[]{:S(2)}, u32[]{:S(2)}) collective-permute-start(bf16[8,64,144]{2,1,0:T(8,128)(2,1)S(1)} %pad_maximum_fusion), channel_id=1, source_target_pairs={{0,4},{4,8},{8,12},{1,5},{5,9},{9,13},{2,6},{6,10},{10,14},{3,7},{... | collective-permute-start | bytes 442376 | tf_op jit(solution)/shard_map/ppermute | solution.py:24
  62.3 0.8 copy.93
  63.1 3.4 %all-to-all-start.2 = ((bf16[32,256,16]{1,2,0:T(8,128)(2,1)}), bf16[32,256,16]{1,2,0:T(8,128)(2,1)S(1)}, u32[]{:S(2)}, u32[]{:S(2)}) async-start(bf16[32,256,16]{1,2,0:T(8,128)(2,1)} %bitcast.17), calls=%async_computation.2 | async-start | bytes 524288 | tf_op jit(solution)/shard_map/all_to_all | solution.py:137
  66.5 2.5 %copy.98.refs_2_ = bf16[8,16,1024]{2,1,0:T(8,128)(2,1)} copy(bf16[8,16,1024]{1,2,0:T(8,128)(2,1)} %bitcast.62) | data formatting | bytes 524288 | tf_op jit(solution)/shard_map/transpose | solution.py:196
  69.1 5.7 %collective-permute-done.1 = bf16[8,64,144]{2,1,0:T(8,128)(2,1)S(1)} collective-permute-done((bf16[8,64,144]{2,1,0:T(8,128)(2,1)S(1)}, bf16[8,64,144]{2,1,0:T(8,128)(2,1)S(1)}, u32[]{:S(2)}, u32[]{:S(2)}) %collective-permute-start.1) | collective-permute-done | bytes 147488 | tf_op jit(solution)/shard_map/ppermute | solution.py:24
  77.1 1.9 %copy.94 = bf16[8,4,256,16]{3,2,1,0:T(8,128)(2,1)S(1)} copy(bf16[8,4,256,16]{2,3,0,1:T(8,128)(2,1)} %bitcast.69) | data formatting | bytes 524288 | tf_op jit(solution)/shard_map/all_to_all | solution.py:137
  79.0 1.4 copy.100
  80.5 2.8 %fusion.22 = f32[8,2,512,136]{2,3,1,0:T(8,128)} fusion(bf16[8,2,512,16]{3,2,1,0:T(8,128)(2,1)S(1)} %bitcast.55, bf16[16,136,1,1]{1,0,3,2:T(8,128)(2,1)S(1)} %copy-done.9), kind=kOutput, calls=%fused_computation.29 | convolution fusion | flops 35651584 | bytes 4722944 | tf_op jit(solution)/shard_map/...d,df->...f/dot_general | solution.py:32
  83.3 2.3 %copy_add_fusion = f32[8,153,128]{2,0,1:T(8,128)} fusion(f32[8,153,128]{2,0,1:T(8,128)} %collective-permute-done, f32[8,153,128]{2,1,0:T(8,128)S(1)} %get-tuple-element.13), kind=kLoop, calls=%fused_computation.30 | loop fusion | flops 156672 | bytes 1880064 | tf_op jit(solution)/shard_map/add | solution.py:170
  85.6 6.4 %collective-permute-start.2 = (f32[8,153,128]{2,0,1:T(8,128)}, f32[8,153,128]{2,0,1:T(8,128)}, u32[]{:S(2)}, u32[]{:S(2)}) collective-permute-start(f32[8,153,128]{2,0,1:T(8,128)} %copy_add_fusion), channel_id=1, source_target_pairs={{0,8},{4,12},{1,9},{5,13},{2,10},{6,14},{3,11},{7,15},{16,24},{20,... | collective-permute-start | bytes 1880072 | tf_op jit(solution)/shard_map/ppermute | solution.py:24
  92.0 21.0 %shard_map.91 = (f32[1024,1024]{1,0:T(8,128)}, f32[1024,1024]{1,0:T(8,128)}) custom-call(s32[1]{0:T(128)} %bitcast.refs_0_, bf16[8,1024,16]{2,1,0:T(8,128)(2,1)} %bitcast.56, bf16[8,16,1024]{2,1,0:T(8,128)(2,1)} %copy.98.refs_2_, bf16[8,16,128]{2,1,0:T(8,128)(2,1)} %copy.99.refs_3_, bf16[8,1024,128]{2,1,0:T(8,128)(2,1)} %bitcast.60, ...), custom_call_target="tpu_custom_call" | custom-call | tf_op jit(solution)/shard_map/pallas_call | solution.py:88
  113.0 3.1 %fusion.10 = bf16[8,2,512,136]{2,3,1,0:T(8,128)(2,1)S(1)} fusion(f32[8,2,512,136]{2,3,1,0:T(8,128)} %fusion.22, bf16[8,2,512,16]{3,2,1,0:T(8,128)(2,1)S(1)} %bitcast.57, bf16[16,136,1,1]{1,0,3,2:T(8,128)(2,1)S(1)} %copy-done.8, bf16[136]{0:T(256)(128)(2,1)S(1)} %copy-done.10), kind=kOutput, calls=%fused_computation.12 | convolution fusion | flops 40108032 | bytes 6951440 | tf_op jit(solution)/shard_map/...d,df->...f/dot_general | solution.py:31
  116.1 1.3 add.22
  117.6 3.6 %fusion.5 = f32[8,2,512,128]{3,2,1,0:T(8,128)} fusion(bf16[8,2,512,136]{2,3,1,0:T(8,128)(2,1)S(1)} %fusion.10, bf16[8,2,512,16]{2,3,1,0:T(8,128)(2,1)S(1)} %multiply_convert_fusion.2, bf16[153]{0:T(256)(128)(2,1)S(1)} %copy-done.12, f32[8,1,153,128]{3,2,1,0:T(8,128)S(1)} %slice.20, f32[8,153,128]{2,1,0:T(8,128)S(1)} %copy.104), kind=kOutput, calls=%fused_computation.7 | convolution fusion | flops 329011200 | bytes 7938354 | tf_op jit(solution)/shard_map/hnrf,hnfv->hnrv/dot_general | solution.py:182
  121.3 8.4 %shard_map.92 = bf16[1024,1024]{1,0:T(8,128)(2,1)} custom-call(f32[1024,1024]{1,0:T(8,128)} %get-tuple-element.11.intra_ref, f32[8,1024,128]{2,1,0:T(8,128)} %bitcast.63, f32[1024,1024]{1,0:T(8,128)} %get-tuple-element.12.win_ref, f32[1,1024]{1,0:T(1,128)} %bitcast.70), custom_call_target="tpu_custom_call" | custom-call | tf_op jit(solution)/shard_map/pallas_call | solution.py:118
  129.7 29.3 %all_to_all.73 = bf16[4,256,1024]{2,1,0:T(8,128)(2,1)S(1)} all-to-all(bf16[4,256,1024]{2,1,0:T(8,128)(2,1)} %bitcast.66), channel_id=1, replica_groups=mesh['groups'=2,'ctx'=4,'head'=4] {'head'}, dimensions={0} | all-to-all | bytes 4194304 | tf_op jit(solution)/shard_map/all_to_all | solution.py:203
  159.0 1.5 copy.112
  (40 shorter events, 3.0 us)
Async XLA Ops:
  1.8 10.2 %all-to-all-start = ((bf16[32,256,16]{1,2,0:T(8,128)(2,1)}), bf16[32,256,16]{1,2,0:T(8,128)(2,1)S(1)}, u32[]{:S(2)}, u32[]{:S(2)}) async-start(bf16[32,256,16]{1,2,0:T(8,128)(2,1)} %bitcast.2), calls=%async_computation | async-start | bytes 524288 | tf_op jit(solution)/shard_map/all_to_all | solution.py:137
  12.0 4.2 %copy-start.8 = (bf16[16,136,1,1]{1,0,3,2:T(8,128)(2,1)S(1)}, bf16[16,136,1,1]{1,0,3,2:T(8,128)(2,1)}, u32[]{:S(2)}) copy-start(bf16[16,136,1,1]{1,0,3,2:T(8,128)(2,1)} %constant.37) | copy-start | bytes 13060
  12.0 29.4 %all-to-all-start.1 = ((bf16[32,256,128]{1,2,0:T(8,128)(2,1)}), bf16[32,256,128]{1,2,0:T(8,128)(2,1)S(1)}, u32[]{:S(2)}, u32[]{:S(2)}) async-start(bf16[32,256,128]{1,2,0:T(8,128)(2,1)} %bitcast.11), calls=%async_computation.1 | async-start | bytes 4194304 | tf_op jit(solution)/shard_map/all_to_all | solution.py:137
  15.8 30.0 %copy-start.11 = (bf16[153]{0:T(256)(128)(2,1)}, bf16[153]{0:T(256)(128)(2,1)S(1)}, u32[]{:S(2)}) copy-start(bf16[153]{0:T(256)(128)(2,1)S(1)} %pad.8.clone) | copy-start | bytes 922
  16.2 0.8 copy-start.9
  41.4 1.3 copy-start.3
  45.8 12.5 %copy-start.2 = (bf16[8,4,256,128]{3,2,1,0:T(8,128)(2,1)}, bf16[8,4,256,128]{3,2,1,0:T(8,128)(2,1)S(1)}, u32[]{:S(2)}) copy-start(bf16[8,4,256,128]{3,2,1,0:T(8,128)(2,1)S(1)} %copy.92) | copy-start | bytes 6291460
  51.7 27.3 %collective-permute-start = (f32[8,153,128]{2,0,1:T(8,128)}, f32[8,153,128]{2,0,1:T(8,128)}, u32[]{:S(2)}, u32[]{:S(2)}) collective-permute-start(f32[8,153,128]{2,0,1:T(8,128)} %copy.95), channel_id=1, source_target_pairs={{0,4},{4,8},{8,12},{1,5},{5,9},{9,13},{2,6},{6,10},{10,14},{3,7},{... | collective-permute-start | bytes 1880072 | tf_op jit(solution)/shard_map/ppermute | solution.py:24
  58.3 3.9 %copy-start.7 = (bf16[256,512]{1,0:T(8,128)(2,1)S(1)}, bf16[256,512]{1,0:T(8,128)(2,1)}, u32[]{:S(2)}) copy-start(bf16[256,512]{1,0:T(8,128)(2,1)} %param.9) | copy-start | bytes 786436
  59.4 9.6 %copy-start.6 = (f32[8,2,153,128]{3,2,1,0:T(8,128)S(1)}, f32[8,2,153,128]{3,2,1,0:T(8,128)}, u32[]{:S(2)}) copy-start(f32[8,2,153,128]{3,2,1,0:T(8,128)} %get-tuple-element.14) | copy-start | bytes 3760132
  59.4 15.3 %collective-permute-start.1 = (bf16[8,64,144]{2,1,0:T(8,128)(2,1)S(1)}, bf16[8,64,144]{2,1,0:T(8,128)(2,1)S(1)}, u32[]{:S(2)}, u32[]{:S(2)}) collective-permute-start(bf16[8,64,144]{2,1,0:T(8,128)(2,1)S(1)} %pad_maximum_fusion), channel_id=1, source_target_pairs={{0,4},{4,8},{8,12},{1,5},{5,9},{9,13},{2,6},{6,10},{10,14},{3,7},{... | collective-permute-start | bytes 442376 | tf_op jit(solution)/shard_map/ppermute | solution.py:24
  63.1 13.3 %all-to-all-start.2 = ((bf16[32,256,16]{1,2,0:T(8,128)(2,1)}), bf16[32,256,16]{1,2,0:T(8,128)(2,1)S(1)}, u32[]{:S(2)}, u32[]{:S(2)}) async-start(bf16[32,256,16]{1,2,0:T(8,128)(2,1)} %bitcast.17), calls=%async_computation.2 | async-start | bytes 524288 | tf_op jit(solution)/shard_map/all_to_all | solution.py:137
  76.4 0.7 copy-start.4
  79.0 4.3 %copy-start = (bf16[8,4,256,16]{3,2,1,0:T(8,128)(2,1)}, bf16[8,4,256,16]{3,2,1,0:T(8,128)(2,1)S(1)}, u32[]{:S(2)}) copy-start(bf16[8,4,256,16]{3,2,1,0:T(8,128)(2,1)S(1)} %copy.94) | copy-start | bytes 786436
  85.6 27.4 %copy-start.5 = (bf16[8,2,512,16]{2,3,1,0:T(8,128)(2,1)S(1)}, bf16[8,2,512,16]{2,3,1,0:T(8,128)(2,1)}, u32[]{:S(2)}) copy-start(bf16[8,2,512,16]{2,3,1,0:T(8,128)(2,1)} %copy.100) | copy-start | bytes 786436
  85.6 30.5 %collective-permute-start.2 = (f32[8,153,128]{2,0,1:T(8,128)}, f32[8,153,128]{2,0,1:T(8,128)}, u32[]{:S(2)}, u32[]{:S(2)}) collective-permute-start(f32[8,153,128]{2,0,1:T(8,128)} %copy_add_fusion), channel_id=1, source_target_pairs={{0,8},{4,12},{1,9},{5,13},{2,10},{6,14},{3,11},{7,15},{16,24},{20,... | collective-permute-start | bytes 1880072 | tf_op jit(solution)/shard_map/ppermute | solution.py:24
  92.0 21.0 %copy-start.1 = (bf16[8,4,256,16]{3,2,1,0:T(8,128)(2,1)S(1)}, bf16[8,4,256,16]{3,2,1,0:T(8,128)(2,1)}, u32[]{:S(2)}) copy-start(bf16[8,4,256,16]{3,2,1,0:T(8,128)(2,1)} %copy-done) | copy-start | bytes 786436
  92.0 21.0 %copy-start.10 = (bf16[136]{0:T(256)(128)(2,1)S(1)}, bf16[136]{0:T(256)(128)(2,1)}, u32[]{:S(2)}) copy-start(bf16[136]{0:T(256)(128)(2,1)} %constant.30.clone) | copy-start | bytes 820
  116.1 1.5 copy-start.12

commit v16 on v13

--- a/solution.py
+++ b/solution.py
@@ -136,9 +136,6 @@
     block_count = span_rows // block_rows
     first_span = lax.axis_index("ctx") == 0
 
-    tails = shifted(
-        jnp.concatenate([key_hm, value_hm], axis=2)[:, span_rows - WINDOW :], "ctx", 1
-    )
 
     key_feat = unique_features(key_hm.reshape(heads_here, block_count, block_rows, KD), False)
     block_states = jnp.einsum(
@@ -153,8 +150,19 @@
     entering = None
     first_round = span_state
     shift = 1
+    tail = jnp.concatenate([key_hm, value_hm], axis=2)[:, span_rows - WINDOW :]
+    tail_rows = WINDOW * (KD + VD) // VD
     while shift < peers:
-        received = shifted(running, "ctx", shift)
+        if shift == 1:
+            packed = jnp.concatenate(
+                [running, tail.astype(jnp.float32).reshape(heads_here, tail_rows, VD)], axis=1
+            )
+            got = shifted(packed, "ctx", shift)
+            received = got[:, : running.shape[1]]
+            tails = got[:, running.shape[1] :].reshape(heads_here, WINDOW, KD + VD)
+            tails = tails.astype(jnp.bfloat16)
+        else:
+            received = shifted(running, "ctx", shift)
         entering = received if entering is None else entering + received
         if shift == 1:
             first_round = received
@@ -163,6 +171,7 @@
             running = running + received
     if entering is None:
         entering = jnp.zeros_like(span_state)
+        tails = jnp.zeros_like(tail)
     queries, span_state = lax.optimization_barrier((queries, span_state))
     query_hm = to_heads(queries, KD)
     query_hm, first_round = lax.optimization_barrier((query_hm, first_round))

time: 156 us -> 169 us (1.083)
  waiting for transfers between devices: 23.6 us -> 34.2 us
  local copies, waits for them, and re-layouts: 25.7 us -> 29 us
    ppermute x3 -> x2, waiting for transfers between devices: 0.01 us -> 11.6 us  [shifted(): return lax.ppermute(shard, axis, pairs)]
    dot_general x1, matrix products: 2.35 us -> 4.65 us  [per_device(): jnp.einsum('hnrf,hnrv->hnfv', key_feat, value_hm.reshape(heads_here, bloc...]
    dot_general x2, matrix products: 3.8 us -> 1.53 us  [unique_features(): jnp.einsum('...d,df->...f', vector, pick_rows, preferred_element_type=jnp...]
    add x1, other arithmetic: 2.28 us -> 0.14 us  [per_device(): running = running + received]
    slice x0 -> x3, local copies, waits for them, and re-layouts: none -> 2.12 us  [the longest x1 1.12 us: per_device(): received = got[:, :running.shape[1]]]
    concatenate x1, other arithmetic: 1.9 us -> 0.07 us  [per_device(): jnp.concatenate([running, tail.astype(jnp.float32).reshape(heads_here, ta...]
    ppermute x3 -> x2, starting transfers between devices: 11.5 us -> 11.2 us  [shifted(): return lax.ppermute(shard, axis, pairs)]
    unnamed x20 -> x22, local copies, waits for them, and re-layouts: 5.88 us -> 5.89 us
  transfers between devices with their start and end apart: 6 -> 5, of which waited for: 3 -> 3; matrix products, arithmetic and copies ran while one was open for 18% -> 17% of each run, Pallas kernels for 13% -> 12%
where the time goes in v16:
time: 169 us; the launch traced here: 168 us
  waiting for transfers between devices  34.2 us (20%)
  Pallas kernels  29.3 us (17%)
  blocking collectives  29.3 us (17%)
  local copies, waits for them, and re-layouts  29 us (17%)
  starting transfers between devices  23.3 us (14%)
  matrix products  15.2 us (9%)
  other arithmetic  7 us (4%)
    all_to_all x1, blocking collectives, per_device(): lax.all_to_all(mixed, 'head', split_axis=0, concat_axis=1, tiled=True)  29.3 us
    all_to_all x3, waiting for transfers between devices, to_heads(): return lax.all_to_all(tok, 'head', split_axis=0, concat_axis=1, tiled=True)  22.6 us
    pallas_call x1, Pallas kernels, local_attention(): pl.pallas_call(body, grid_spec=pltpu.PrefetchScalarGridSpec(num_scalar_pr...  20.9 us
    all_to_all x3, starting transfers between devices, to_heads(): return lax.all_to_all(tok, 'head', split_axis=0, concat_axis=1, tiled=True)  12.1 us
    ppermute x2, waiting for transfers between devices, shifted(): return lax.ppermute(shard, axis, pairs)  11.6 us
    ppermute x2, starting transfers between devices, shifted(): return lax.ppermute(shard, axis, pairs)  11.2 us
    pallas_call x1, Pallas kernels, mix(): pl.pallas_call(mix_kernel, grid=(heads_here,), in_specs=[tile, pl.BlockSp...  8.42 us
    all_to_all x5, local copies, waits for them, and re-layouts, to_heads(): return lax.all_to_all(tok, 'head', split_axis=0, concat_axis=1, tiled=True)  7.61 us
  transfers between devices with their start and end apart: 5, of which 3 were waited for; matrix products, arithmetic and copies ran while one was open for 17% of the time, Pallas kernels for 12%

profile of v16, /device:TPU:0, one launch (start us, length us, event | category | flops | bytes accessed | tf_op | source)
XLA Modules:
  0.0 167.6 jit_solution(16505497963562879540)
XLA Ops:
  0.0 1.8 %copy.62 = bf16[256,512]{0,1:T(8,128)(2,1)} copy(bf16[256,512]{1,0:T(8,128)(2,1)} %param.10) | data formatting | bytes 524288 | tf_op args[1]
  1.8 4.2 %all-to-all-start = ((bf16[32,256,16]{1,2,0:T(8,128)(2,1)}), bf16[32,256,16]{1,2,0:T(8,128)(2,1)S(1)}, u32[]{:S(2)}, u32[]{:S(2)}) async-start(bf16[32,256,16]{1,2,0:T(8,128)(2,1)} %bitcast.2), calls=%async_computation | async-start | bytes 524288 | tf_op jit(solution)/shard_map/all_to_all | solution.py:130
  6.0 4.1 %copy.67 = bf16[256,4096]{0,1:T(8,128)(2,1)} copy(bf16[256,4096]{1,0:T(8,128)(2,1)} %param.11) | data formatting | bytes 4194304 | tf_op args[2]
  10.1 2.0 %all-to-all-done = bf16[32,256,16]{1,2,0:T(8,128)(2,1)S(1)} async-done(((bf16[32,256,16]{1,2,0:T(8,128)(2,1)}), bf16[32,256,16]{1,2,0:T(8,128)(2,1)S(1)}, u32[]{:S(2)}, u32[]{:S(2)}) %all-to-all-start) | async-done | bytes 262176 | tf_op jit(solution)/shard_map/all_to_all | solution.py:130
  12.0 4.5 %all-to-all-start.1 = ((bf16[32,256,128]{1,2,0:T(8,128)(2,1)}), bf16[32,256,128]{1,2,0:T(8,128)(2,1)}, u32[]{:S(2)}, u32[]{:S(2)}) async-start(bf16[32,256,128]{1,2,0:T(8,128)(2,1)} %bitcast.11), calls=%async_computation.1 | async-start | bytes 4194304 | tf_op jit(solution)/shard_map/all_to_all | solution.py:130
  16.7 1.0 copy.72
  19.5 2.1 %fusion.11 = bf16[8,2,512,136]{2,3,1,0:T(8,128)(2,1)} fusion(f32[136,8,2,512]{3,0,2,1:T(8,128)S(1)} %fusion.17, bf16[16,136,1,1]{1,0,3,2:T(8,128)(2,1)S(1)} %copy-done.7, bf16[8,2,512,16]{2,1,3,0:T(2,128)(2,1)S(1)} %reshape.47), kind=kOutput, calls=%fused_computation.14 | convolution fusion | flops 38993920 | bytes 6951168 | tf_op jit(solution)/shard_map/...d,df->...f/dot_general | solution.py:32
  21.6 20.6 %all-to-all-done.1 = bf16[32,256,128]{1,2,0:T(8,128)(2,1)} async-done(((bf16[32,256,128]{1,2,0:T(8,128)(2,1)}), bf16[32,256,128]{1,2,0:T(8,128)(2,1)}, u32[]{:S(2)}, u32[]{:S(2)}) %all-to-all-start.1) | async-done | bytes 2097184 | tf_op jit(solution)/shard_map/all_to_all | solution.py:130
  42.2 3.9 %copy.69 = bf16[8,4,256,128]{3,2,1,0:T(8,128)(2,1)} copy(bf16[8,4,256,128]{2,3,0,1:T(8,128)(2,1)} %bitcast.14) | data formatting | bytes 4194304 | tf_op jit(solution)/shard_map/all_to_all | solution.py:130
  46.2 1.0 fusion.15
  47.6 4.7 %fusion.22 = (f32[8,153,128]{2,1,0:T(8,128)S(1)}, f32[8,2,153,128]{3,2,1,0:T(8,128)}) fusion(bf16[8,2,512,128]{3,2,1,0:T(8,128)(2,1)} %bitcast.58, bf16[8,2,512,136]{2,3,1,0:T(8,128)(2,1)} %fusion.11, bf16[8,2,512,16]{2,3,1,0:T(8,128)(2,1)} %multiply_convert_fusion.3, bf16[153]{0:T(256)(128)(2,1)S(1)} %pad.11.clone), kind=kOutput, calls=%fused_computation.33 | convolution fusion | flops 328541184 | bytes 6467890 | tf_op jit(solution)/shard_map/hnrf,hnrv->hnfv/dot_general | solution.py:141
  53.2 3.4 %all-to-all-start.2 = ((bf16[32,256,16]{1,2,0:T(8,128)(2,1)}), bf16[32,256,16]{1,2,0:T(8,128)(2,1)S(1)}, u32[]{:S(2)}, u32[]{:S(2)}) async-start(bf16[32,256,16]{1,2,0:T(8,128)(2,1)} %bitcast.67), calls=%async_computation.2 | async-start | bytes 524288 | tf_op jit(solution)/shard_map/all_to_all | solution.py:130
  56.7 1.2 copy.74
  57.8 5.0 %collective-permute-start = (f32[8,225,128]{2,0,1:T(8,128)}, f32[8,225,128]{2,0,1:T(8,128)}, u32[]{:S(2)}, u32[]{:S(2)}) collective-permute-start(f32[8,225,128]{2,0,1:T(8,128)} %copy.74), channel_id=1, source_target_pairs={{0,4},{4,8},{8,12},{1,5},{5,9},{9,13},{2,6},{6,10},{10,14},{3,7},{... | collective-permute-start | bytes 2764808 | tf_op jit(solution)/shard_map/ppermute | solution.py:24
  62.8 1.4 copy.78
  64.3 1.1 slice.37
  66.5 1.4 copy.79
  68.7 2.2 %fusion.10 = bf16[8,2,512,136]{2,3,1,0:T(8,128)(2,1)} fusion(f32[8,2,512,136]{2,3,1,0:T(8,128)S(1)} %fusion.23, bf16[8,2,512,16]{3,2,1,0:T(8,128)(2,1)S(1)} %bitcast.53, bf16[16,136,1,1]{1,0,3,2:T(8,128)(2,1)S(1)} %copy-done.7, bf16[136]{0:T(256)(128)(2,1)S(1)} %copy-done.9), kind=kOutput, calls=%fused_computation.13 | convolution fusion | flops 40108032 | bytes 6951440 | tf_op jit(solution)/shard_map/...d,df->...f/dot_general | solution.py:32
  70.9 11.6 %collective-permute-done = f32[8,225,128]{2,0,1:T(8,128)} collective-permute-done((f32[8,225,128]{2,0,1:T(8,128)}, f32[8,225,128]{2,0,1:T(8,128)}, u32[]{:S(2)}, u32[]{:S(2)}) %collective-permute-start) | collective-permute-done | bytes 921632 | tf_op jit(solution)/shard_map/ppermute | solution.py:24
  82.5 1.1 slice.33
  83.8 1.2 copy.82
  85.0 6.2 %collective-permute-start.1 = (f32[8,153,128]{2,0,1:T(8,128)}, f32[8,153,128]{2,0,1:T(8,128)}, u32[]{:S(2)}, u32[]{:S(2)}) collective-permute-start(f32[8,153,128]{2,0,1:T(8,128)} %copy.82), channel_id=1, source_target_pairs={{0,8},{4,12},{1,9},{5,13},{2,10},{6,14},{3,11},{7,15},{16,24},{20,... | collective-permute-start | bytes 1880072 | tf_op jit(solution)/shard_map/ppermute | solution.py:24
  93.0 1.0 convert_element_type.30
  94.1 1.7 %slice.36 = bf16[8,64,128]{2,1,0:T(8,128)(2,1)} slice(bf16[8,64,144]{2,1,0:T(8,128)(2,1)} %convert_element_type.30), slice={[0:8], [0:64], [16:144]} | slice | bytes 262144 | tf_op jit(solution)/shard_map/slice | solution.py:193
  96.8 1.7 %concatenate.24 = bf16[8,1152,16]{1,2,0:T(8,128)(2,1)} concatenate(bf16[8,64,16]{1,2,0:T(8,128)(2,1)S(1)} %slice.27, bf16[8,64,16]{1,2,0:T(8,128)(2,1)S(1)} %copy.77, bf16[8,1024,16]{1,2,0:T(8,128)(2,1)} %copy.78), dimensions={1} | concatenate | bytes 589824 | tf_op jit(solution)/shard_map/concatenate | solution.py:192
  98.6 2.9 %pad_maximum_fusion.refs_3_ = bf16[8,1152,128]{2,1,0:T(8,128)(2,1)} fusion(bf16[8,1024,128]{2,1,0:T(8,128)(2,1)S(1)} %bitcast.59, bf16[8,64,128]{2,1,0:T(8,128)(2,1)} %slice.36, bf16[1152]{0:T(1024)(128)(2,1)S(1)} %pad.4.clone), kind=kLoop, calls=%fused_computation.12 | loop fusion | flops 7077888 | bytes 4589824 | tf_op jit(solution)/shard_map/concatenate | solution.py:193
  101.5 20.9 %shard_map.91 = (f32[1024,1024]{1,0:T(8,128)}, f32[1024,1024]{1,0:T(8,128)}) custom-call(s32[1]{0:T(128)} %bitcast.refs_0_, bf16[8,1024,16]{2,1,0:T(8,128)(2,1)} %bitcast.54, bf16[8,16,1152]{2,1,0:T(8,128)(2,1)} %bitcast.65, bf16[8,1152,128]{2,1,0:T(8,128)(2,1)} %pad_maximum_fusion.refs_3_), custom_call_target="tpu_custom_call" | custom-call | tf_op jit(solution)/shard_map/pallas_call | solution.py:83
  122.4 1.3 copy_add_fusion
  123.7 4.7 %fusion.5 = f32[8,2,512,128]{3,2,1,0:T(8,128)} fusion(bf16[8,2,512,136]{2,3,1,0:T(8,128)(2,1)S(1)} %copy-done.2, bf16[8,2,512,16]{2,3,1,0:T(8,128)(2,1)} %multiply_convert_fusion.2, bf16[153]{0:T(256)(128)(2,1)S(1)} %pad.11.clone, f32[8,1,153,128]{3,2,1,0:T(8,128)S(1)} %slice.37, f32[8,153,128]{2,1,0:T(8,128)S(1)} %copy_add_fusion), kind=kOutput, calls=%fused_computation.7 | convolution fusion | flops 329011200 | bytes 7938354 | tf_op jit(solution)/shard_map/hnrf,hnfv->hnrv/dot_general | solution.py:184
  128.4 8.4 %shard_map.92 = bf16[1024,1024]{1,0:T(8,128)(2,1)} custom-call(f32[1024,1024]{1,0:T(8,128)} %get-tuple-element.11.intra_ref, f32[8,1024,128]{2,1,0:T(8,128)} %bitcast.60, f32[1024,1024]{1,0:T(8,128)} %get-tuple-element.12.win_ref, f32[1,1024]{1,0:T(1,128)} %bitcast.68), custom_call_target="tpu_custom_call" | custom-call | tf_op jit(solution)/shard_map/pallas_call | solution.py:111
  136.8 29.3 %all_to_all.73 = bf16[4,256,1024]{2,1,0:T(8,128)(2,1)S(1)} all-to-all(bf16[4,256,1024]{2,1,0:T(8,128)(2,1)} %bitcast.62), channel_id=1, replica_groups=mesh['groups'=2,'ctx'=4,'head'=4] {'head'}, dimensions={0} | all-to-all | bytes 4194304 | tf_op jit(solution)/shard_map/all_to_all | solution.py:199
  166.1 1.5 copy.92
  (41 shorter events, 8.0 us)
Async XLA Ops:
  1.8 10.2 %all-to-all-start = ((bf16[32,256,16]{1,2,0:T(8,128)(2,1)}), bf16[32,256,16]{1,2,0:T(8,128)(2,1)S(1)}, u32[]{:S(2)}, u32[]{:S(2)}) async-start(bf16[32,256,16]{1,2,0:T(8,128)(2,1)} %bitcast.2), calls=%async_computation | async-start | bytes 524288 | tf_op jit(solution)/shard_map/all_to_all | solution.py:130
  12.0 30.2 %all-to-all-start.1 = ((bf16[32,256,128]{1,2,0:T(8,128)(2,1)}), bf16[32,256,128]{1,2,0:T(8,128)(2,1)}, u32[]{:S(2)}, u32[]{:S(2)}) async-start(bf16[32,256,128]{1,2,0:T(8,128)(2,1)} %bitcast.11), calls=%async_computation.1 | async-start | bytes 4194304 | tf_op jit(solution)/shard_map/all_to_all | solution.py:130
  16.5 2.2 %copy-start.8 = (bf16[16,136,1,1]{1,0,3,2:T(8,128)(2,1)S(1)}, bf16[16,136,1,1]{1,0,3,2:T(8,128)(2,1)}, u32[]{:S(2)}) copy-start(bf16[16,136,1,1]{1,0,3,2:T(8,128)(2,1)} %constant.33) | copy-start | bytes 13060
  17.9 1.5 copy-start.7
  47.6 4.7 %copy-start.6 = (bf16[256,512]{1,0:T(8,128)(2,1)S(1)}, bf16[256,512]{1,0:T(8,128)(2,1)}, u32[]{:S(2)}) copy-start(bf16[256,512]{1,0:T(8,128)(2,1)} %param.9) | copy-start | bytes 786436
  52.2 12.0 %copy-start.3 = (f32[8,153,128]{2,1,0:T(8,128)}, f32[8,153,128]{2,1,0:T(8,128)S(1)}, u32[]{:S(2)}) copy-start(f32[8,153,128]{2,1,0:T(8,128)S(1)} %get-tuple-element.13) | copy-start | bytes 1880068
  53.2 12.2 %all-to-all-start.2 = ((bf16[32,256,16]{1,2,0:T(8,128)(2,1)}), bf16[32,256,16]{1,2,0:T(8,128)(2,1)S(1)}, u32[]{:S(2)}, u32[]{:S(2)}) async-start(bf16[32,256,16]{1,2,0:T(8,128)(2,1)} %bitcast.67), calls=%async_computation.2 | async-start | bytes 524288 | tf_op jit(solution)/shard_map/all_to_all | solution.py:130
  57.8 24.7 %collective-permute-start = (f32[8,225,128]{2,0,1:T(8,128)}, f32[8,225,128]{2,0,1:T(8,128)}, u32[]{:S(2)}, u32[]{:S(2)}) collective-permute-start(f32[8,225,128]{2,0,1:T(8,128)} %copy.74), channel_id=1, source_target_pairs={{0,4},{4,8},{8,12},{1,5},{5,9},{9,13},{2,6},{6,10},{10,14},{3,7},{... | collective-permute-start | bytes 2764808 | tf_op jit(solution)/shard_map/ppermute | solution.py:24
  66.5 2.2 %copy-start = (bf16[8,4,256,16]{3,2,1,0:T(8,128)(2,1)}, bf16[8,4,256,16]{3,2,1,0:T(8,128)(2,1)S(1)}, u32[]{:S(2)}) copy-start(bf16[8,4,256,16]{3,2,1,0:T(8,128)(2,1)S(1)} %copy.71) | copy-start | bytes 786436
  67.9 0.8 copy-start.9
  68.7 14.9 %copy-start.4 = (f32[8,153,128]{2,1,0:T(8,128)S(1)}, f32[8,153,128]{2,1,0:T(8,128)}, u32[]{:S(2)}) copy-start(f32[8,153,128]{2,1,0:T(8,128)} %copy-done.3) | copy-start | bytes 1880068
  70.9 20.3 %copy-start.5 = (bf16[8,2,512,16]{2,3,1,0:T(8,128)(2,1)S(1)}, bf16[8,2,512,16]{2,3,1,0:T(8,128)(2,1)}, u32[]{:S(2)}) copy-start(bf16[8,2,512,16]{2,3,1,0:T(8,128)(2,1)} %copy.79) | copy-start | bytes 786436
  83.7 14.9 %copy-start.1 = (bf16[8,4,256,128]{3,2,1,0:T(8,128)(2,1)S(1)}, bf16[8,4,256,128]{3,2,1,0:T(8,128)(2,1)}, u32[]{:S(2)}) copy-start(bf16[8,4,256,128]{3,2,1,0:T(8,128)(2,1)} %copy.69) | copy-start | bytes 6291460
  85.0 37.4 %collective-permute-start.1 = (f32[8,153,128]{2,0,1:T(8,128)}, f32[8,153,128]{2,0,1:T(8,128)}, u32[]{:S(2)}, u32[]{:S(2)}) collective-permute-start(f32[8,153,128]{2,0,1:T(8,128)} %copy.82), channel_id=1, source_target_pairs={{0,8},{4,12},{1,9},{5,13},{2,10},{6,14},{3,11},{7,15},{16,24},{20,... | collective-permute-start | bytes 1880072 | tf_op jit(solution)/shard_map/ppermute | solution.py:24
  101.5 22.2 %copy-start.2 = (bf16[8,2,512,136]{2,3,1,0:T(8,128)(2,1)S(1)}, bf16[8,2,512,136]{2,3,1,0:T(8,128)(2,1)}, u32[]{:S(2)}) copy-start(bf16[8,2,512,136]{2,3,1,0:T(8,128)(2,1)} %fusion.10) | copy-start | bytes 6684676

commit v17 on v13

--- a/solution.py
+++ b/solution.py
@@ -100,22 +100,27 @@
 
 
 def mix_kernel(intra_ref, inter_ref, win_ref, gain_ref, out_ref):
-    linear = intra_ref[...] + inter_ref[0]
-    scale = lax.rsqrt(jnp.mean(linear * linear, axis=1, keepdims=True) + epsilon)
-    out_ref[...] = (linear * scale * gain_ref[...] + win_ref[...]).astype(jnp.bfloat16)
+    for j in range(inter_ref.shape[0]):
+        cols = slice(j * VD, (j + 1) * VD)
+        linear = intra_ref[:, cols] + inter_ref[j]
+        scale = lax.rsqrt(jnp.mean(linear * linear, axis=1, keepdims=True) + epsilon)
+        out_ref[:, cols] = (linear * scale * gain_ref[:, cols] + win_ref[:, cols]).astype(
+            jnp.bfloat16
+        )
 
 
 def mix(intra, inter_hm, window, gain):
     heads_here, span_rows, _ = inter_hm.shape
-    tile = pl.BlockSpec((span_rows, VD), lambda h: (0, h))
+    step = 2 if heads_here % 2 == 0 else 1
+    tile = pl.BlockSpec((span_rows, step * VD), lambda h: (0, h))
     return pl.pallas_call(
         mix_kernel,
-        grid=(heads_here,),
+        grid=(heads_here // step,),
         in_specs=[
             tile,
-            pl.BlockSpec((1, span_rows, VD), lambda h: (h, 0, 0)),
+            pl.BlockSpec((step, span_rows, VD), lambda h: (h, 0, 0)),
             tile,
-            pl.BlockSpec((1, VD), lambda h: (0, h)),
+            pl.BlockSpec((1, step * VD), lambda h: (0, h)),
         ],
         out_specs=tile,
         out_shape=jax.ShapeDtypeStruct((span_rows, heads_here * VD), jnp.bfloat16),

time: 156 us -> 154 us (0.987)
  Pallas kernels: 29.3 us -> 27.7 us
    pallas_call x1, Pallas kernels: 8.42 us -> 6.79 us  [mix(): pl.pallas_call(mix_kernel, grid=(heads_here // step,), in_specs=[tile, pl...]
  transfers between devices with their start and end apart: 6 -> 6, of which waited for: 3 -> 3; matrix products, arithmetic and copies ran while one was open for 18% -> 18% of each run, Pallas kernels for 13% -> 14%
where the time goes in v17:
time: 154 us; the launch traced here: 153 us
  blocking collectives  29.3 us (19%)
  Pallas kernels  27.7 us (18%)
  local copies, waits for them, and re-layouts  25.7 us (17%)
  starting transfers between devices  24.2 us (16%)
  waiting for transfers between devices  23.6 us (15%)
  matrix products  14.8 us (10%)
  other arithmetic  7.54 us (5%)
    all_to_all x1, blocking collectives, per_device(): lax.all_to_all(mixed, 'head', split_axis=0, concat_axis=1, tiled=True)  29.3 us
    all_to_all x3, waiting for transfers between devices, to_heads(): return lax.all_to_all(tok, 'head', split_axis=0, concat_axis=1, tiled=True)  23.6 us
    pallas_call x1, Pallas kernels, local_attention(): pl.pallas_call(body, grid_spec=pltpu.PrefetchScalarGridSpec(num_scalar_pr...  20.9 us
    all_to_all x3, starting transfers between devices, to_heads(): return lax.all_to_all(tok, 'head', split_axis=0, concat_axis=1, tiled=True)  12.7 us
    ppermute x3, starting transfers between devices, shifted(): return lax.ppermute(shard, axis, pairs)  11.5 us
    all_to_all x5, local copies, waits for them, and re-layouts, to_heads(): return lax.all_to_all(tok, 'head', split_axis=0, concat_axis=1, tiled=True)  8.49 us
    pallas_call x1, Pallas kernels, mix(): pl.pallas_call(mix_kernel, grid=(heads_here // step,), in_specs=[tile, pl...  6.79 us
    unnamed x20, local copies, waits for them, and re-layouts  5.88 us
  transfers between devices with their start and end apart: 6, of which 3 were waited for; matrix products, arithmetic and copies ran while one was open for 18% of the time, Pallas kernels for 14%

profile of v17, /device:TPU:0, one launch (start us, length us, event | category | flops | bytes accessed | tf_op | source)
XLA Modules:
  0.0 153.0 jit_solution(8373964623738341299)
XLA Ops:
  0.0 1.8 %copy.82 = bf16[256,512]{0,1:T(8,128)(2,1)} copy(bf16[256,512]{1,0:T(8,128)(2,1)} %param.10) | data formatting | bytes 524288 | tf_op args[1]
  1.8 4.2 %all-to-all-start = ((bf16[32,256,16]{1,2,0:T(8,128)(2,1)}), bf16[32,256,16]{1,2,0:T(8,128)(2,1)S(1)}, u32[]{:S(2)}, u32[]{:S(2)}) async-start(bf16[32,256,16]{1,2,0:T(8,128)(2,1)} %bitcast.2), calls=%async_computation | async-start | bytes 524288 | tf_op jit(solution)/shard_map/all_to_all | solution.py:135
  6.0 4.1 %copy.87 = bf16[256,4096]{0,1:T(8,128)(2,1)} copy(bf16[256,4096]{1,0:T(8,128)(2,1)} %param.11) | data formatting | bytes 4194304 | tf_op args[2]
  10.1 2.0 %all-to-all-done = bf16[32,256,16]{1,2,0:T(8,128)(2,1)S(1)} async-done(((bf16[32,256,16]{1,2,0:T(8,128)(2,1)}), bf16[32,256,16]{1,2,0:T(8,128)(2,1)S(1)}, u32[]{:S(2)}, u32[]{:S(2)}) %all-to-all-start) | async-done | bytes 262176 | tf_op jit(solution)/shard_map/all_to_all | solution.py:135
  12.0 4.4 %all-to-all-start.1 = ((bf16[32,256,128]{1,2,0:T(8,128)(2,1)}), bf16[32,256,128]{1,2,0:T(8,128)(2,1)}, u32[]{:S(2)}, u32[]{:S(2)}) async-start(bf16[32,256,128]{1,2,0:T(8,128)(2,1)} %bitcast.11), calls=%async_computation.1 | async-start | bytes 4194304 | tf_op jit(solution)/shard_map/all_to_all | solution.py:135
  18.8 2.1 %fusion.11 = bf16[8,2,512,136]{2,3,1,0:T(8,128)(2,1)} fusion(f32[136,8,2,512]{3,0,2,1:T(8,128)S(1)} %fusion.16, bf16[16,136,1,1]{1,0,3,2:T(8,128)(2,1)S(1)} %copy-done.7, bf16[8,2,512,16]{2,1,3,0:T(2,128)(2,1)S(1)} %reshape.39), kind=kOutput, calls=%fused_computation.14 | convolution fusion | flops 38993920 | bytes 6951168 | tf_op jit(solution)/shard_map/...d,df->...f/dot_general | solution.py:32
  20.9 21.3 %all-to-all-done.1 = bf16[32,256,128]{1,2,0:T(8,128)(2,1)} async-done(((bf16[32,256,128]{1,2,0:T(8,128)(2,1)}), bf16[32,256,128]{1,2,0:T(8,128)(2,1)}, u32[]{:S(2)}, u32[]{:S(2)}) %all-to-all-start.1) | async-done | bytes 2097184 | tf_op jit(solution)/shard_map/all_to_all | solution.py:135
  42.2 3.9 %copy.89 = bf16[8,4,256,128]{3,2,1,0:T(8,128)(2,1)} copy(bf16[8,4,256,128]{2,3,0,1:T(8,128)(2,1)} %bitcast.14) | data formatting | bytes 4194304 | tf_op jit(solution)/shard_map/all_to_all | solution.py:135
  46.2 1.9 %pad_maximum_fusion.1 = bf16[8,64,144]{2,1,0:T(8,128)(2,1)} fusion(bf16[8,1024,128]{2,1,0:T(8,128)(2,1)} %bitcast.57, bf16[8,1024,16]{2,1,0:T(8,128)(2,1)S(1)} %bitcast.55), kind=kLoop, calls=%fused_computation.21 | loop fusion | flops 294912 | bytes 2506752 | tf_op jit(solution)/shard_map/concatenate | solution.py:145
  48.1 4.8 %collective-permute-start.1 = (bf16[8,64,144]{2,1,0:T(8,128)(2,1)}, bf16[8,64,144]{2,1,0:T(8,128)(2,1)}, u32[]{:S(2)}, u32[]{:S(2)}) collective-permute-start(bf16[8,64,144]{2,1,0:T(8,128)(2,1)} %pad_maximum_fusion.1), channel_id=1, source_target_pairs={{0,4},{4,8},{8,12},{1,5},{5,9},{9,13},{2,6},{6,10},{10,14},{3,7},{... | collective-permute-start | bytes 442376 | tf_op jit(solution)/shard_map/ppermute | solution.py:24
  52.9 2.4 %fusion.21 = (f32[8,153,128]{2,1,0:T(8,128)S(1)}, f32[8,2,153,128]{3,2,1,0:T(8,128)}) fusion(bf16[8,2,512,128]{3,2,1,0:T(8,128)(2,1)S(1)} %bitcast.58, bf16[8,2,512,136]{2,3,1,0:T(8,128)(2,1)S(1)} %copy-done.4, bf16[8,2,512,16]{2,3,1,0:T(8,128)(2,1)S(1)} %multiply_convert_fusion.3, bf16[153]{0:T(256)(128)(2,1)S(1)} %pad.9.clone), kind=kOutput, calls=%fused_computation.28 | convolution fusion | flops 328541184 | bytes 6467890 | tf_op jit(solution)/shard_map/hnrf,hnrv->hnfv/dot_general | solution.py:149
  55.2 1.2 copy.92
  56.4 3.6 %collective-permute-start = (f32[8,153,128]{2,0,1:T(8,128)}, f32[8,153,128]{2,0,1:T(8,128)}, u32[]{:S(2)}, u32[]{:S(2)}) collective-permute-start(f32[8,153,128]{2,0,1:T(8,128)} %copy.92), channel_id=1, source_target_pairs={{0,4},{4,8},{8,12},{1,5},{5,9},{9,13},{2,6},{6,10},{10,14},{3,7},{... | collective-permute-start | bytes 1880072 | tf_op jit(solution)/shard_map/ppermute | solution.py:24
  60.1 1.4 copy.96
  61.5 1.3 slice.26
  62.8 1.8 %copy.90 = bf16[256,512]{0,1:T(8,128)(2,1)} copy(bf16[256,512]{1,0:T(8,128)(2,1)} %param.9) | data formatting | bytes 524288 | tf_op jit(solution)/shard_map/optimization_barrier | solution.py:171
  64.6 4.0 %all-to-all-start.2 = ((bf16[32,256,16]{1,2,0:T(8,128)(2,1)}), bf16[32,256,16]{1,2,0:T(8,128)(2,1)}, u32[]{:S(2)}, u32[]{:S(2)}) async-start(bf16[32,256,16]{1,2,0:T(8,128)(2,1)} %bitcast.66), calls=%async_computation.2 | async-start | bytes 524288 | tf_op jit(solution)/shard_map/all_to_all | solution.py:135
  68.7 1.1 slice.25
  69.7 1.9 %pad_maximum_fusion.refs_3_ = bf16[8,1152,128]{2,1,0:T(8,128)(2,1)} fusion(bf16[8,1024,128]{2,1,0:T(8,128)(2,1)S(1)} %bitcast.59, bf16[8,64,128]{2,1,0:T(8,128)(2,1)S(1)} %slice.25, bf16[1152]{0:T(1024)(128)(2,1)S(1)} %pad.4.clone), kind=kLoop, calls=%fused_computation.12 | loop fusion | flops 7077888 | bytes 4589824 | tf_op jit(solution)/shard_map/concatenate | solution.py:189
  72.7 1.8 %concatenate.20 = bf16[8,1152,16]{1,2,0:T(8,128)(2,1)} concatenate(bf16[8,64,16]{1,2,0:T(8,128)(2,1)S(1)} %slice.18, bf16[8,64,16]{1,2,0:T(8,128)(2,1)S(1)} %copy.95, bf16[8,1024,16]{1,2,0:T(8,128)(2,1)} %copy.96), dimensions={1} | concatenate | bytes 589824 | tf_op jit(solution)/shard_map/concatenate | solution.py:188
  74.7 1.9 %copy.91 = bf16[8,4,256,16]{3,2,1,0:T(8,128)(2,1)S(1)} copy(bf16[8,4,256,16]{2,3,0,1:T(8,128)(2,1)} %bitcast.19) | data formatting | bytes 524288 | tf_op jit(solution)/shard_map/all_to_all | solution.py:135
  76.7 1.4 copy.97
  78.1 2.8 %fusion.22 = f32[8,2,512,136]{2,3,1,0:T(8,128)} fusion(bf16[8,2,512,16]{3,2,1,0:T(8,128)(2,1)S(1)} %bitcast.52, bf16[16,136,1,1]{1,0,3,2:T(8,128)(2,1)S(1)} %copy-done.7), kind=kOutput, calls=%fused_computation.29 | convolution fusion | flops 35651584 | bytes 4722944 | tf_op jit(solution)/shard_map/...d,df->...f/dot_general | solution.py:32
  80.9 2.3 %copy_add_fusion = f32[8,153,128]{2,0,1:T(8,128)} fusion(f32[8,153,128]{2,0,1:T(8,128)} %collective-permute-done, f32[8,153,128]{2,1,0:T(8,128)S(1)} %get-tuple-element.13), kind=kLoop, calls=%fused_computation.30 | loop fusion | flops 156672 | bytes 1880064 | tf_op jit(solution)/shard_map/add | solution.py:168
  83.2 3.1 %collective-permute-start.2 = (f32[8,153,128]{2,0,1:T(8,128)}, f32[8,153,128]{2,0,1:T(8,128)}, u32[]{:S(2)}, u32[]{:S(2)}) collective-permute-start(f32[8,153,128]{2,0,1:T(8,128)} %copy_add_fusion), channel_id=1, source_target_pairs={{0,8},{4,12},{1,9},{5,13},{2,10},{6,14},{3,11},{7,15},{16,24},{20,... | collective-permute-start | bytes 1880072 | tf_op jit(solution)/shard_map/ppermute | solution.py:24
  86.3 20.9 %shard_map.91 = (f32[1024,1024]{1,0:T(8,128)}, f32[1024,1024]{1,0:T(8,128)}) custom-call(s32[1]{0:T(128)} %bitcast.refs_0_, bf16[8,1024,16]{2,1,0:T(8,128)(2,1)} %bitcast.53, bf16[8,16,1152]{2,1,0:T(8,128)(2,1)} %bitcast.65, bf16[8,1152,128]{2,1,0:T(8,128)(2,1)} %pad_maximum_fusion.refs_3_), custom_call_target="tpu_custom_call" | custom-call | tf_op jit(solution)/shard_map/pallas_call | solution.py:83
  107.3 3.0 %fusion.10 = bf16[8,2,512,136]{2,3,1,0:T(8,128)(2,1)S(1)} fusion(f32[8,2,512,136]{2,3,1,0:T(8,128)} %fusion.22, bf16[8,2,512,16]{3,2,1,0:T(8,128)(2,1)S(1)} %bitcast.54, bf16[16,136,1,1]{1,0,3,2:T(8,128)(2,1)S(1)} %copy-done.6, bf16[136]{0:T(256)(128)(2,1)S(1)} %copy-done.8), kind=kOutput, calls=%fused_computation.13 | convolution fusion | flops 40108032 | bytes 6951440 | tf_op jit(solution)/shard_map/...d,df->...f/dot_general | solution.py:31
  110.3 1.3 add.18
  111.8 3.7 %fusion.5 = f32[8,2,512,128]{3,2,1,0:T(8,128)} fusion(bf16[8,2,512,136]{2,3,1,0:T(8,128)(2,1)S(1)} %fusion.10, bf16[8,2,512,16]{2,3,1,0:T(8,128)(2,1)S(1)} %multiply_convert_fusion.2, bf16[153]{0:T(256)(128)(2,1)S(1)} %pad.9.clone, f32[8,1,153,128]{3,2,1,0:T(8,128)S(1)} %slice.26, f32[8,153,128]{2,1,0:T(8,128)S(1)} %copy.101), kind=kOutput, calls=%fused_computation.7 | convolution fusion | flops 329011200 | bytes 7938354 | tf_op jit(solution)/shard_map/hnrf,hnfv->hnrv/dot_general | solution.py:180
  115.5 6.8 %shard_map.92 = bf16[1024,1024]{1,0:T(8,128)(2,1)} custom-call(f32[1024,1024]{1,0:T(8,128)} %get-tuple-element.11.intra_ref, f32[8,1024,128]{2,1,0:T(8,128)} %bitcast.60, f32[1024,1024]{1,0:T(8,128)} %get-tuple-element.12.win_ref, f32[1,1024]{1,0:T(1,128)} %bitcast.67), custom_call_target="tpu_custom_call" | custom-call | tf_op jit(solution)/shard_map/pallas_call | solution.py:116
  122.3 29.3 %all_to_all.73 = bf16[4,256,1024]{2,1,0:T(8,128)(2,1)S(1)} all-to-all(bf16[4,256,1024]{2,1,0:T(8,128)(2,1)} %bitcast.62), channel_id=1, replica_groups=mesh['groups'=2,'ctx'=4,'head'=4] {'head'}, dimensions={0} | all-to-all | bytes 4194304 | tf_op jit(solution)/shard_map/all_to_all | solution.py:195
  151.5 1.5 copy.109
  (35 shorter events, 3.7 us)
Async XLA Ops:
  1.8 10.2 %all-to-all-start = ((bf16[32,256,16]{1,2,0:T(8,128)(2,1)}), bf16[32,256,16]{1,2,0:T(8,128)(2,1)S(1)}, u32[]{:S(2)}, u32[]{:S(2)}) async-start(bf16[32,256,16]{1,2,0:T(8,128)(2,1)} %bitcast.2), calls=%async_computation | async-start | bytes 524288 | tf_op jit(solution)/shard_map/all_to_all | solution.py:135
  12.0 30.2 %all-to-all-start.1 = ((bf16[32,256,128]{1,2,0:T(8,128)(2,1)}), bf16[32,256,128]{1,2,0:T(8,128)(2,1)}, u32[]{:S(2)}, u32[]{:S(2)}) async-start(bf16[32,256,128]{1,2,0:T(8,128)(2,1)} %bitcast.11), calls=%async_computation.1 | async-start | bytes 4194304 | tf_op jit(solution)/shard_map/all_to_all | solution.py:135
  16.5 1.5 copy-start.6
  17.9 0.8 copy-start.7
  46.2 6.7 %copy-start.2 = (bf16[8,4,256,128]{3,2,1,0:T(8,128)(2,1)S(1)}, bf16[8,4,256,128]{3,2,1,0:T(8,128)(2,1)}, u32[]{:S(2)}) copy-start(bf16[8,4,256,128]{3,2,1,0:T(8,128)(2,1)} %copy.89) | copy-start | bytes 6291460
  46.2 6.7 %copy-start.4 = (bf16[8,2,512,136]{2,3,1,0:T(8,128)(2,1)S(1)}, bf16[8,2,512,136]{2,3,1,0:T(8,128)(2,1)}, u32[]{:S(2)}) copy-start(bf16[8,2,512,136]{2,3,1,0:T(8,128)(2,1)} %fusion.11) | copy-start | bytes 6684676
  48.1 20.6 %collective-permute-start.1 = (bf16[8,64,144]{2,1,0:T(8,128)(2,1)}, bf16[8,64,144]{2,1,0:T(8,128)(2,1)}, u32[]{:S(2)}, u32[]{:S(2)}) collective-permute-start(bf16[8,64,144]{2,1,0:T(8,128)(2,1)} %pad_maximum_fusion.1), channel_id=1, source_target_pairs={{0,4},{4,8},{8,12},{1,5},{5,9},{9,13},{2,6},{6,10},{10,14},{3,7},{... | collective-permute-start | bytes 442376 | tf_op jit(solution)/shard_map/ppermute | solution.py:24
  56.4 20.2 %collective-permute-start = (f32[8,153,128]{2,0,1:T(8,128)}, f32[8,153,128]{2,0,1:T(8,128)}, u32[]{:S(2)}, u32[]{:S(2)}) collective-permute-start(f32[8,153,128]{2,0,1:T(8,128)} %copy.92), channel_id=1, source_target_pairs={{0,4},{4,8},{8,12},{1,5},{5,9},{9,13},{2,6},{6,10},{10,14},{3,7},{... | collective-permute-start | bytes 1880072 | tf_op jit(solution)/shard_map/ppermute | solution.py:24
  61.5 8.2 %copy-start.3 = (bf16[8,4,256,128]{3,2,1,0:T(8,128)(2,1)S(1)}, bf16[8,4,256,128]{3,2,1,0:T(8,128)(2,1)}, u32[]{:S(2)}) copy-start(bf16[8,4,256,128]{3,2,1,0:T(8,128)(2,1)} %copy.89) | copy-start | bytes 6291460
  64.6 10.1 %all-to-all-start.2 = ((bf16[32,256,16]{1,2,0:T(8,128)(2,1)}), bf16[32,256,16]{1,2,0:T(8,128)(2,1)}, u32[]{:S(2)}, u32[]{:S(2)}) async-start(bf16[32,256,16]{1,2,0:T(8,128)(2,1)} %bitcast.66), calls=%async_computation.2 | async-start | bytes 524288 | tf_op jit(solution)/shard_map/all_to_all | solution.py:135
  76.6 4.3 %copy-start = (bf16[8,4,256,16]{3,2,1,0:T(8,128)(2,1)}, bf16[8,4,256,16]{3,2,1,0:T(8,128)(2,1)S(1)}, u32[]{:S(2)}) copy-start(bf16[8,4,256,16]{3,2,1,0:T(8,128)(2,1)S(1)} %copy.91) | copy-start | bytes 786436
  83.2 24.0 %copy-start.5 = (bf16[8,2,512,16]{2,3,1,0:T(8,128)(2,1)S(1)}, bf16[8,2,512,16]{2,3,1,0:T(8,128)(2,1)}, u32[]{:S(2)}) copy-start(bf16[8,2,512,16]{2,3,1,0:T(8,128)(2,1)} %copy.97) | copy-start | bytes 786436
  83.2 27.1 %collective-permute-start.2 = (f32[8,153,128]{2,0,1:T(8,128)}, f32[8,153,128]{2,0,1:T(8,128)}, u32[]{:S(2)}, u32[]{:S(2)}) collective-permute-start(f32[8,153,128]{2,0,1:T(8,128)} %copy_add_fusion), channel_id=1, source_target_pairs={{0,8},{4,12},{1,9},{5,13},{2,10},{6,14},{3,11},{7,15},{16,24},{20,... | collective-permute-start | bytes 1880072 | tf_op jit(solution)/shard_map/ppermute | solution.py:24
  86.3 20.9 %copy-start.1 = (bf16[8,4,256,16]{3,2,1,0:T(8,128)(2,1)S(1)}, bf16[8,4,256,16]{3,2,1,0:T(8,128)(2,1)}, u32[]{:S(2)}) copy-start(bf16[8,4,256,16]{3,2,1,0:T(8,128)(2,1)} %copy-done) | copy-start | bytes 786436
  86.3 20.9 %copy-start.8 = (bf16[136]{0:T(256)(128)(2,1)S(1)}, bf16[136]{0:T(256)(128)(2,1)}, u32[]{:S(2)}) copy-start(bf16[136]{0:T(256)(128)(2,1)} %constant.30.clone) | copy-start | bytes 820

commit v18 on v17

--- a/solution.py
+++ b/solution.py
@@ -111,7 +111,7 @@
 
 def mix(intra, inter_hm, window, gain):
     heads_here, span_rows, _ = inter_hm.shape
-    step = 2 if heads_here % 2 == 0 else 1
+    step = 4 if heads_here % 4 == 0 else (2 if heads_here % 2 == 0 else 1)
     tile = pl.BlockSpec((span_rows, step * VD), lambda h: (0, h))
     return pl.pallas_call(
         mix_kernel,

time: 154 us -> 154 us (level)
  no operation moved by 1% of the time
where the time goes in v18:
time: 154 us; the launch traced here: 153 us
  blocking collectives  29.3 us (19%)
  Pallas kernels  27.5 us (18%)
  local copies, waits for them, and re-layouts  25.7 us (17%)
  starting transfers between devices  24.2 us (16%)
  waiting for transfers between devices  23.6 us (15%)
  matrix products  14.8 us (10%)
  other arithmetic  7.54 us (5%)
    all_to_all x1, blocking collectives, per_device(): lax.all_to_all(mixed, 'head', split_axis=0, concat_axis=1, tiled=True)  29.3 us
    all_to_all x3, waiting for transfers between devices, to_heads(): return lax.all_to_all(tok, 'head', split_axis=0, concat_axis=1, tiled=True)  23.6 us
    pallas_call x1, Pallas kernels, local_attention(): pl.pallas_call(body, grid_spec=pltpu.PrefetchScalarGridSpec(num_scalar_pr...  20.9 us
    all_to_all x3, starting transfers between devices, to_heads(): return lax.all_to_all(tok, 'head', split_axis=0, concat_axis=1, tiled=True)  12.7 us
    ppermute x3, starting transfers between devices, shifted(): return lax.ppermute(shard, axis, pairs)  11.5 us
    all_to_all x5, local copies, waits for them, and re-layouts, to_heads(): return lax.all_to_all(tok, 'head', split_axis=0, concat_axis=1, tiled=True)  8.49 us
    pallas_call x1, Pallas kernels, mix(): pl.pallas_call(mix_kernel, grid=(heads_here // step,), in_specs=[tile, pl...  6.58 us
    unnamed x20, local copies, waits for them, and re-layouts  5.88 us
  transfers between devices with their start and end apart: 6, of which 3 were waited for; matrix products, arithmetic and copies ran while one was open for 18% of the time, Pallas kernels for 14%

profile of v18, /device:TPU:0, one launch (start us, length us, event | category | flops | bytes accessed | tf_op | source)
XLA Modules:
  0.0 152.8 jit_solution(14829256943917229536)
XLA Ops:
  0.0 1.8 %copy.82 = bf16[256,512]{0,1:T(8,128)(2,1)} copy(bf16[256,512]{1,0:T(8,128)(2,1)} %param.10) | data formatting | bytes 524288 | tf_op args[1]
  1.8 4.2 %all-to-all-start = ((bf16[32,256,16]{1,2,0:T(8,128)(2,1)}), bf16[32,256,16]{1,2,0:T(8,128)(2,1)S(1)}, u32[]{:S(2)}, u32[]{:S(2)}) async-start(bf16[32,256,16]{1,2,0:T(8,128)(2,1)} %bitcast.2), calls=%async_computation | async-start | bytes 524288 | tf_op jit(solution)/shard_map/all_to_all | solution.py:135
  6.0 4.1 %copy.87 = bf16[256,4096]{0,1:T(8,128)(2,1)} copy(bf16[256,4096]{1,0:T(8,128)(2,1)} %param.11) | data formatting | bytes 4194304 | tf_op args[2]
  10.1 2.0 %all-to-all-done = bf16[32,256,16]{1,2,0:T(8,128)(2,1)S(1)} async-done(((bf16[32,256,16]{1,2,0:T(8,128)(2,1)}), bf16[32,256,16]{1,2,0:T(8,128)(2,1)S(1)}, u32[]{:S(2)}, u32[]{:S(2)}) %all-to-all-start) | async-done | bytes 262176 | tf_op jit(solution)/shard_map/all_to_all | solution.py:135
  12.0 4.4 %all-to-all-start.1 = ((bf16[32,256,128]{1,2,0:T(8,128)(2,1)}), bf16[32,256,128]{1,2,0:T(8,128)(2,1)}, u32[]{:S(2)}, u32[]{:S(2)}) async-start(bf16[32,256,128]{1,2,0:T(8,128)(2,1)} %bitcast.11), calls=%async_computation.1 | async-start | bytes 4194304 | tf_op jit(solution)/shard_map/all_to_all | solution.py:135
  18.8 2.1 %fusion.11 = bf16[8,2,512,136]{2,3,1,0:T(8,128)(2,1)} fusion(f32[136,8,2,512]{3,0,2,1:T(8,128)S(1)} %fusion.16, bf16[16,136,1,1]{1,0,3,2:T(8,128)(2,1)S(1)} %copy-done.7, bf16[8,2,512,16]{2,1,3,0:T(2,128)(2,1)S(1)} %reshape.39), kind=kOutput, calls=%fused_computation.14 | convolution fusion | flops 38993920 | bytes 6951168 | tf_op jit(solution)/shard_map/...d,df->...f/dot_general | solution.py:32
  20.9 21.3 %all-to-all-done.1 = bf16[32,256,128]{1,2,0:T(8,128)(2,1)} async-done(((bf16[32,256,128]{1,2,0:T(8,128)(2,1)}), bf16[32,256,128]{1,2,0:T(8,128)(2,1)}, u32[]{:S(2)}, u32[]{:S(2)}) %all-to-all-start.1) | async-done | bytes 2097184 | tf_op jit(solution)/shard_map/all_to_all | solution.py:135
  42.2 3.9 %copy.89 = bf16[8,4,256,128]{3,2,1,0:T(8,128)(2,1)} copy(bf16[8,4,256,128]{2,3,0,1:T(8,128)(2,1)} %bitcast.14) | data formatting | bytes 4194304 | tf_op jit(solution)/shard_map/all_to_all | solution.py:135
  46.2 1.9 %pad_maximum_fusion.1 = bf16[8,64,144]{2,1,0:T(8,128)(2,1)} fusion(bf16[8,1024,128]{2,1,0:T(8,128)(2,1)} %bitcast.57, bf16[8,1024,16]{2,1,0:T(8,128)(2,1)S(1)} %bitcast.55), kind=kLoop, calls=%fused_computation.21 | loop fusion | flops 294912 | bytes 2506752 | tf_op jit(solution)/shard_map/concatenate | solution.py:145
  48.1 4.8 %collective-permute-start.1 = (bf16[8,64,144]{2,1,0:T(8,128)(2,1)}, bf16[8,64,144]{2,1,0:T(8,128)(2,1)}, u32[]{:S(2)}, u32[]{:S(2)}) collective-permute-start(bf16[8,64,144]{2,1,0:T(8,128)(2,1)} %pad_maximum_fusion.1), channel_id=1, source_target_pairs={{0,4},{4,8},{8,12},{1,5},{5,9},{9,13},{2,6},{6,10},{10,14},{3,7},{... | collective-permute-start | bytes 442376 | tf_op jit(solution)/shard_map/ppermute | solution.py:24
  52.9 2.4 %fusion.21 = (f32[8,153,128]{2,1,0:T(8,128)S(1)}, f32[8,2,153,128]{3,2,1,0:T(8,128)}) fusion(bf16[8,2,512,128]{3,2,1,0:T(8,128)(2,1)S(1)} %bitcast.58, bf16[8,2,512,136]{2,3,1,0:T(8,128)(2,1)S(1)} %copy-done.4, bf16[8,2,512,16]{2,3,1,0:T(8,128)(2,1)S(1)} %multiply_convert_fusion.3, bf16[153]{0:T(256)(128)(2,1)S(1)} %pad.9.clone), kind=kOutput, calls=%fused_computation.28 | convolution fusion | flops 328541184 | bytes 6467890 | tf_op jit(solution)/shard_map/hnrf,hnrv->hnfv/dot_general | solution.py:149
  55.2 1.2 copy.92
  56.4 3.6 %collective-permute-start = (f32[8,153,128]{2,0,1:T(8,128)}, f32[8,153,128]{2,0,1:T(8,128)}, u32[]{:S(2)}, u32[]{:S(2)}) collective-permute-start(f32[8,153,128]{2,0,1:T(8,128)} %copy.92), channel_id=1, source_target_pairs={{0,4},{4,8},{8,12},{1,5},{5,9},{9,13},{2,6},{6,10},{10,14},{3,7},{... | collective-permute-start | bytes 1880072 | tf_op jit(solution)/shard_map/ppermute | solution.py:24
  60.1 1.4 copy.96
  61.5 1.3 slice.26
  62.8 1.8 %copy.90 = bf16[256,512]{0,1:T(8,128)(2,1)} copy(bf16[256,512]{1,0:T(8,128)(2,1)} %param.9) | data formatting | bytes 524288 | tf_op jit(solution)/shard_map/optimization_barrier | solution.py:171
  64.6 4.0 %all-to-all-start.2 = ((bf16[32,256,16]{1,2,0:T(8,128)(2,1)}), bf16[32,256,16]{1,2,0:T(8,128)(2,1)}, u32[]{:S(2)}, u32[]{:S(2)}) async-start(bf16[32,256,16]{1,2,0:T(8,128)(2,1)} %bitcast.66), calls=%async_computation.2 | async-start | bytes 524288 | tf_op jit(solution)/shard_map/all_to_all | solution.py:135
  68.7 1.1 slice.25
  69.7 1.9 %pad_maximum_fusion.refs_3_ = bf16[8,1152,128]{2,1,0:T(8,128)(2,1)} fusion(bf16[8,1024,128]{2,1,0:T(8,128)(2,1)S(1)} %bitcast.59, bf16[8,64,128]{2,1,0:T(8,128)(2,1)S(1)} %slice.25, bf16[1152]{0:T(1024)(128)(2,1)S(1)} %pad.4.clone), kind=kLoop, calls=%fused_computation.12 | loop fusion | flops 7077888 | bytes 4589824 | tf_op jit(solution)/shard_map/concatenate | solution.py:189
  72.7 1.8 %concatenate.20 = bf16[8,1152,16]{1,2,0:T(8,128)(2,1)} concatenate(bf16[8,64,16]{1,2,0:T(8,128)(2,1)S(1)} %slice.18, bf16[8,64,16]{1,2,0:T(8,128)(2,1)S(1)} %copy.95, bf16[8,1024,16]{1,2,0:T(8,128)(2,1)} %copy.96), dimensions={1} | concatenate | bytes 589824 | tf_op jit(solution)/shard_map/concatenate | solution.py:188
  74.7 1.9 %copy.91 = bf16[8,4,256,16]{3,2,1,0:T(8,128)(2,1)S(1)} copy(bf16[8,4,256,16]{2,3,0,1:T(8,128)(2,1)} %bitcast.19) | data formatting | bytes 524288 | tf_op jit(solution)/shard_map/all_to_all | solution.py:135
  76.7 1.4 copy.97
  78.1 2.8 %fusion.22 = f32[8,2,512,136]{2,3,1,0:T(8,128)} fusion(bf16[8,2,512,16]{3,2,1,0:T(8,128)(2,1)S(1)} %bitcast.52, bf16[16,136,1,1]{1,0,3,2:T(8,128)(2,1)S(1)} %copy-done.7), kind=kOutput, calls=%fused_computation.29 | convolution fusion | flops 35651584 | bytes 4722944 | tf_op jit(solution)/shard_map/...d,df->...f/dot_general | solution.py:32
  80.9 2.3 %copy_add_fusion = f32[8,153,128]{2,0,1:T(8,128)} fusion(f32[8,153,128]{2,0,1:T(8,128)} %collective-permute-done, f32[8,153,128]{2,1,0:T(8,128)S(1)} %get-tuple-element.13), kind=kLoop, calls=%fused_computation.30 | loop fusion | flops 156672 | bytes 1880064 | tf_op jit(solution)/shard_map/add | solution.py:168
  83.2 3.1 %collective-permute-start.2 = (f32[8,153,128]{2,0,1:T(8,128)}, f32[8,153,128]{2,0,1:T(8,128)}, u32[]{:S(2)}, u32[]{:S(2)}) collective-permute-start(f32[8,153,128]{2,0,1:T(8,128)} %copy_add_fusion), channel_id=1, source_target_pairs={{0,8},{4,12},{1,9},{5,13},{2,10},{6,14},{3,11},{7,15},{16,24},{20,... | collective-permute-start | bytes 1880072 | tf_op jit(solution)/shard_map/ppermute | solution.py:24
  86.3 20.9 %shard_map.91 = (f32[1024,1024]{1,0:T(8,128)}, f32[1024,1024]{1,0:T(8,128)}) custom-call(s32[1]{0:T(128)} %bitcast.refs_0_, bf16[8,1024,16]{2,1,0:T(8,128)(2,1)} %bitcast.53, bf16[8,16,1152]{2,1,0:T(8,128)(2,1)} %bitcast.65, bf16[8,1152,128]{2,1,0:T(8,128)(2,1)} %pad_maximum_fusion.refs_3_), custom_call_target="tpu_custom_call" | custom-call | tf_op jit(solution)/shard_map/pallas_call | solution.py:83
  107.3 3.0 %fusion.10 = bf16[8,2,512,136]{2,3,1,0:T(8,128)(2,1)S(1)} fusion(f32[8,2,512,136]{2,3,1,0:T(8,128)} %fusion.22, bf16[8,2,512,16]{3,2,1,0:T(8,128)(2,1)S(1)} %bitcast.54, bf16[16,136,1,1]{1,0,3,2:T(8,128)(2,1)S(1)} %copy-done.6, bf16[136]{0:T(256)(128)(2,1)S(1)} %copy-done.8), kind=kOutput, calls=%fused_computation.13 | convolution fusion | flops 40108032 | bytes 6951440 | tf_op jit(solution)/shard_map/...d,df->...f/dot_general | solution.py:31
  110.3 1.3 add.18
  111.8 3.7 %fusion.5 = f32[8,2,512,128]{3,2,1,0:T(8,128)} fusion(bf16[8,2,512,136]{2,3,1,0:T(8,128)(2,1)S(1)} %fusion.10, bf16[8,2,512,16]{2,3,1,0:T(8,128)(2,1)S(1)} %multiply_convert_fusion.2, bf16[153]{0:T(256)(128)(2,1)S(1)} %pad.9.clone, f32[8,1,153,128]{3,2,1,0:T(8,128)S(1)} %slice.26, f32[8,153,128]{2,1,0:T(8,128)S(1)} %copy.101), kind=kOutput, calls=%fused_computation.7 | convolution fusion | flops 329011200 | bytes 7938354 | tf_op jit(solution)/shard_map/hnrf,hnfv->hnrv/dot_general | solution.py:180
  115.5 6.6 %shard_map.92 = bf16[1024,1024]{1,0:T(8,128)(2,1)} custom-call(f32[1024,1024]{1,0:T(8,128)} %get-tuple-element.11.intra_ref, f32[8,1024,128]{2,1,0:T(8,128)} %bitcast.60, f32[1024,1024]{1,0:T(8,128)} %get-tuple-element.12.win_ref, f32[1,1024]{1,0:T(1,128)} %bitcast.67), custom_call_target="tpu_custom_call" | custom-call | tf_op jit(solution)/shard_map/pallas_call | solution.py:116
  122.0 29.3 %all_to_all.73 = bf16[4,256,1024]{2,1,0:T(8,128)(2,1)S(1)} all-to-all(bf16[4,256,1024]{2,1,0:T(8,128)(2,1)} %bitcast.62), channel_id=1, replica_groups=mesh['groups'=2,'ctx'=4,'head'=4] {'head'}, dimensions={0} | all-to-all | bytes 4194304 | tf_op jit(solution)/shard_map/all_to_all | solution.py:195
  151.3 1.5 copy.109
  (35 shorter events, 3.7 us)
Async XLA Ops:
  1.8 10.2 %all-to-all-start = ((bf16[32,256,16]{1,2,0:T(8,128)(2,1)}), bf16[32,256,16]{1,2,0:T(8,128)(2,1)S(1)}, u32[]{:S(2)}, u32[]{:S(2)}) async-start(bf16[32,256,16]{1,2,0:T(8,128)(2,1)} %bitcast.2), calls=%async_computation | async-start | bytes 524288 | tf_op jit(solution)/shard_map/all_to_all | solution.py:135
  12.0 30.2 %all-to-all-start.1 = ((bf16[32,256,128]{1,2,0:T(8,128)(2,1)}), bf16[32,256,128]{1,2,0:T(8,128)(2,1)}, u32[]{:S(2)}, u32[]{:S(2)}) async-start(bf16[32,256,128]{1,2,0:T(8,128)(2,1)} %bitcast.11), calls=%async_computation.1 | async-start | bytes 4194304 | tf_op jit(solution)/shard_map/all_to_all | solution.py:135
  16.5 1.5 copy-start.6
  17.9 0.8 copy-start.7
  46.2 6.7 %copy-start.2 = (bf16[8,4,256,128]{3,2,1,0:T(8,128)(2,1)S(1)}, bf16[8,4,256,128]{3,2,1,0:T(8,128)(2,1)}, u32[]{:S(2)}) copy-start(bf16[8,4,256,128]{3,2,1,0:T(8,128)(2,1)} %copy.89) | copy-start | bytes 6291460
  46.2 6.7 %copy-start.4 = (bf16[8,2,512,136]{2,3,1,0:T(8,128)(2,1)S(1)}, bf16[8,2,512,136]{2,3,1,0:T(8,128)(2,1)}, u32[]{:S(2)}) copy-start(bf16[8,2,512,136]{2,3,1,0:T(8,128)(2,1)} %fusion.11) | copy-start | bytes 6684676
  48.1 20.6 %collective-permute-start.1 = (bf16[8,64,144]{2,1,0:T(8,128)(2,1)}, bf16[8,64,144]{2,1,0:T(8,128)(2,1)}, u32[]{:S(2)}, u32[]{:S(2)}) collective-permute-start(bf16[8,64,144]{2,1,0:T(8,128)(2,1)} %pad_maximum_fusion.1), channel_id=1, source_target_pairs={{0,4},{4,8},{8,12},{1,5},{5,9},{9,13},{2,6},{6,10},{10,14},{3,7},{... | collective-permute-start | bytes 442376 | tf_op jit(solution)/shard_map/ppermute | solution.py:24
  56.4 20.2 %collective-permute-start = (f32[8,153,128]{2,0,1:T(8,128)}, f32[8,153,128]{2,0,1:T(8,128)}, u32[]{:S(2)}, u32[]{:S(2)}) collective-permute-start(f32[8,153,128]{2,0,1:T(8,128)} %copy.92), channel_id=1, source_target_pairs={{0,4},{4,8},{8,12},{1,5},{5,9},{9,13},{2,6},{6,10},{10,14},{3,7},{... | collective-permute-start | bytes 1880072 | tf_op jit(solution)/shard_map/ppermute | solution.py:24
  61.5 8.2 %copy-start.3 = (bf16[8,4,256,128]{3,2,1,0:T(8,128)(2,1)S(1)}, bf16[8,4,256,128]{3,2,1,0:T(8,128)(2,1)}, u32[]{:S(2)}) copy-start(bf16[8,4,256,128]{3,2,1,0:T(8,128)(2,1)} %copy.89) | copy-start | bytes 6291460
  64.6 10.1 %all-to-all-start.2 = ((bf16[32,256,16]{1,2,0:T(8,128)(2,1)}), bf16[32,256,16]{1,2,0:T(8,128)(2,1)}, u32[]{:S(2)}, u32[]{:S(2)}) async-start(bf16[32,256,16]{1,2,0:T(8,128)(2,1)} %bitcast.66), calls=%async_computation.2 | async-start | bytes 524288 | tf_op jit(solution)/shard_map/all_to_all | solution.py:135
  76.6 4.3 %copy-start = (bf16[8,4,256,16]{3,2,1,0:T(8,128)(2,1)}, bf16[8,4,256,16]{3,2,1,0:T(8,128)(2,1)S(1)}, u32[]{:S(2)}) copy-start(bf16[8,4,256,16]{3,2,1,0:T(8,128)(2,1)S(1)} %copy.91) | copy-start | bytes 786436
  83.2 24.0 %copy-start.5 = (bf16[8,2,512,16]{2,3,1,0:T(8,128)(2,1)S(1)}, bf16[8,2,512,16]{2,3,1,0:T(8,128)(2,1)}, u32[]{:S(2)}) copy-start(bf16[8,2,512,16]{2,3,1,0:T(8,128)(2,1)} %copy.97) | copy-start | bytes 786436
  83.2 27.1 %collective-permute-start.2 = (f32[8,153,128]{2,0,1:T(8,128)}, f32[8,153,128]{2,0,1:T(8,128)}, u32[]{:S(2)}, u32[]{:S(2)}) collective-permute-start(f32[8,153,128]{2,0,1:T(8,128)} %copy_add_fusion), channel_id=1, source_target_pairs={{0,8},{4,12},{1,9},{5,13},{2,10},{6,14},{3,11},{7,15},{16,24},{20,... | collective-permute-start | bytes 1880072 | tf_op jit(solution)/shard_map/ppermute | solution.py:24
  86.3 20.9 %copy-start.1 = (bf16[8,4,256,16]{3,2,1,0:T(8,128)(2,1)S(1)}, bf16[8,4,256,16]{3,2,1,0:T(8,128)(2,1)}, u32[]{:S(2)}) copy-start(bf16[8,4,256,16]{3,2,1,0:T(8,128)(2,1)} %copy-done) | copy-start | bytes 786436
  86.3 20.9 %copy-start.8 = (bf16[136]{0:T(256)(128)(2,1)S(1)}, bf16[136]{0:T(256)(128)(2,1)}, u32[]{:S(2)}) copy-start(bf16[136]{0:T(256)(128)(2,1)} %constant.30.clone) | copy-start | bytes 820

commit v19 on v18

--- a/solution.py
+++ b/solution.py
@@ -45,23 +45,29 @@
 
 def local_attention_kernel(flag_ref, q_ref, kt_ref, vx_ref, intra_ref, win_ref, *, span_rows, block_rows):
     first_span = flag_ref[0] == 1
+    for j in range(q_ref.shape[0]):
+        one_head(j, first_span, q_ref, kt_ref, vx_ref, intra_ref, win_ref, span_rows, block_rows)
+
+
+def one_head(j, first_span, q_ref, kt_ref, vx_ref, intra_ref, win_ref, span_rows, block_rows):
+    cols = slice(j * VD, (j + 1) * VD)
     for i in range(span_rows // CHUNK):
         r0 = i * CHUNK
-        q_c = q_ref[0, r0 : r0 + CHUNK, :]
+        q_c = q_ref[j, r0 : r0 + CHUNK, :]
         bs = (r0 // block_rows) * block_rows
         width = r0 + CHUNK - bs
-        k_i = kt_ref[0, :, LEAD + bs : LEAD + r0 + CHUNK]
-        v_i = vx_ref[0, LEAD + bs : LEAD + r0 + CHUNK, :]
+        k_i = kt_ref[j, :, LEAD + bs : LEAD + r0 + CHUNK]
+        v_i = vx_ref[j, LEAD + bs : LEAD + r0 + CHUNK, :]
         scores = jnp.dot(q_c, k_i, preferred_element_type=jnp.float32) * 0.25
         row = lax.broadcasted_iota(jnp.int32, (CHUNK, width), 0)
         col = lax.broadcasted_iota(jnp.int32, (CHUNK, width), 1)
         kernel = jnp.where(
             col <= row + (r0 - bs), 1.0 + scores + 0.5 * scores * scores, 0.0
         ).astype(jnp.bfloat16)
-        intra_ref[r0 : r0 + CHUNK, :] = jnp.dot(kernel, v_i, preferred_element_type=jnp.float32)
-
-        k_w = kt_ref[0, :, r0 : r0 + CHUNK + LEAD]
-        v_w = vx_ref[0, r0 : r0 + CHUNK + LEAD, :]
+        intra_ref[r0 : r0 + CHUNK, cols] = jnp.dot(kernel, v_i, preferred_element_type=jnp.float32)
+
+        k_w = kt_ref[j, :, r0 : r0 + CHUNK + LEAD]
+        v_w = vx_ref[j, r0 : r0 + CHUNK + LEAD, :]
         ws = jnp.dot(q_c, k_w, preferred_element_type=jnp.float32) * 0.25
         wrow = lax.broadcasted_iota(jnp.int32, (CHUNK, CHUNK + LEAD), 0)
         wcol = lax.broadcasted_iota(jnp.int32, (CHUNK, CHUNK + LEAD), 1)
@@ -72,27 +78,28 @@
         highest = jnp.max(masked, axis=1, keepdims=True)
         expo = jnp.where(valid, jnp.exp(ws - highest), 0.0)
         weights = (expo / jnp.sum(expo, axis=1, keepdims=True)).astype(jnp.bfloat16)
-        win_ref[r0 : r0 + CHUNK, :] = jnp.dot(weights, v_w, preferred_element_type=jnp.float32)
+        win_ref[r0 : r0 + CHUNK, cols] = jnp.dot(weights, v_w, preferred_element_type=jnp.float32)
 
 
 def local_attention(flag, q_hm, kt_hm, vx, block_rows):
     heads_here, span_rows, _ = q_hm.shape
     ext = kt_hm.shape[2]
+    step = 2 if heads_here % 2 == 0 else 1
     body = lambda *refs: local_attention_kernel(*refs, span_rows=span_rows, block_rows=block_rows)
     out = jax.ShapeDtypeStruct((span_rows, heads_here * VD), jnp.float32)
     return pl.pallas_call(
         body,
         grid_spec=pltpu.PrefetchScalarGridSpec(
             num_scalar_prefetch=1,
-            grid=(heads_here,),
+            grid=(heads_here // step,),
             in_specs=[
-                pl.BlockSpec((1, span_rows, KD), lambda h, f: (h, 0, 0)),
-                pl.BlockSpec((1, KD, ext), lambda h, f: (h, 0, 0)),
-                pl.BlockSpec((1, ext, VD), lambda h, f: (h, 0, 0)),
+                pl.BlockSpec((step, span_rows, KD), lambda h, f: (h, 0, 0)),
+                pl.BlockSpec((step, KD, ext), lambda h, f: (h, 0, 0)),
+                pl.BlockSpec((step, ext, VD), lambda h, f: (h, 0, 0)),
             ],
             out_specs=[
-                pl.BlockSpec((span_rows, VD), lambda h, f: (0, h)),
-                pl.BlockSpec((span_rows, VD), lambda h, f: (0, h)),
+                pl.BlockSpec((span_rows, step * VD), lambda h, f: (0, h)),
+                pl.BlockSpec((span_rows, step * VD), lambda h, f: (0, h)),
             ],
         ),
         out_shape=(out, out),

time: 154 us -> 154 us (level)
  the two profiles are of different devices: /device:TPU:0 before, /device:TPU:28 now
where the time goes in v19:
time: 154 us; the launch traced here: 153 us
  waiting for transfers between devices  34.1 us (22%)
  blocking collectives  29.3 us (19%)
  local copies, waits for them, and re-layouts  25.7 us (17%)
  Pallas kernels  25.6 us (17%)
  starting transfers between devices  16 us (10%)
  matrix products  14.8 us (10%)
  other arithmetic  7.54 us (5%)
    all_to_all x1, blocking collectives, per_device(): lax.all_to_all(mixed, 'head', split_axis=0, concat_axis=1, tiled=True)  29.3 us
    all_to_all x3, waiting for transfers between devices, to_heads(): return lax.all_to_all(tok, 'head', split_axis=0, concat_axis=1, tiled=True)  23.5 us
    pallas_call x1, Pallas kernels, local_attention(): pl.pallas_call(body, grid_spec=pltpu.PrefetchScalarGridSpec(num_scalar_pr...  19 us
    all_to_all x3, starting transfers between devices, to_heads(): return lax.all_to_all(tok, 'head', split_axis=0, concat_axis=1, tiled=True)  11.9 us
    ppermute x3, waiting for transfers between devices, shifted(): return lax.ppermute(shard, axis, pairs)  10.6 us
    all_to_all x5, local copies, waits for them, and re-layouts, to_heads(): return lax.all_to_all(tok, 'head', split_axis=0, concat_axis=1, tiled=True)  8.5 us
    pallas_call x1, Pallas kernels, mix(): pl.pallas_call(mix_kernel, grid=(heads_here // step,), in_specs=[tile, pl...  6.58 us
    unnamed x20, local copies, waits for them, and re-layouts  5.9 us
  transfers between devices with their start and end apart: 6, of which 5 were waited for; matrix products, arithmetic and copies ran while one was open for 18% of the time, Pallas kernels for 12%

profile of v19, /device:TPU:28, one launch (start us, length us, event | category | flops | bytes accessed | tf_op | source)
XLA Modules:
  0.0 153.4 jit_solution(9588666167827074340)
XLA Ops:
  0.0 1.8 %copy.82 = bf16[256,512]{0,1:T(8,128)(2,1)} copy(bf16[256,512]{1,0:T(8,128)(2,1)} %param.10) | data formatting | bytes 524288 | tf_op args[1]
  1.8 3.4 %all-to-all-start = ((bf16[32,256,16]{1,2,0:T(8,128)(2,1)}), bf16[32,256,16]{1,2,0:T(8,128)(2,1)S(1)}, u32[]{:S(2)}, u32[]{:S(2)}) async-start(bf16[32,256,16]{1,2,0:T(8,128)(2,1)} %bitcast.2), calls=%async_computation | async-start | bytes 524288 | tf_op jit(solution)/shard_map/all_to_all | solution.py:142
  5.2 4.1 %copy.87 = bf16[256,4096]{0,1:T(8,128)(2,1)} copy(bf16[256,4096]{1,0:T(8,128)(2,1)} %param.11) | data formatting | bytes 4194304 | tf_op args[2]
  9.3 1.9 %all-to-all-done = bf16[32,256,16]{1,2,0:T(8,128)(2,1)S(1)} async-done(((bf16[32,256,16]{1,2,0:T(8,128)(2,1)}), bf16[32,256,16]{1,2,0:T(8,128)(2,1)S(1)}, u32[]{:S(2)}, u32[]{:S(2)}) %all-to-all-start) | async-done | bytes 262176 | tf_op jit(solution)/shard_map/all_to_all | solution.py:142
  11.2 4.4 %all-to-all-start.1 = ((bf16[32,256,128]{1,2,0:T(8,128)(2,1)}), bf16[32,256,128]{1,2,0:T(8,128)(2,1)}, u32[]{:S(2)}, u32[]{:S(2)}) async-start(bf16[32,256,128]{1,2,0:T(8,128)(2,1)} %bitcast.11), calls=%async_computation.1 | async-start | bytes 4194304 | tf_op jit(solution)/shard_map/all_to_all | solution.py:142
  17.9 2.1 %fusion.11 = bf16[8,2,512,136]{2,3,1,0:T(8,128)(2,1)} fusion(f32[136,8,2,512]{3,0,2,1:T(8,128)S(1)} %fusion.16, bf16[16,136,1,1]{1,0,3,2:T(8,128)(2,1)S(1)} %copy-done.7, bf16[8,2,512,16]{2,1,3,0:T(2,128)(2,1)S(1)} %reshape.39), kind=kOutput, calls=%fused_computation.14 | convolution fusion | flops 38993920 | bytes 6951168 | tf_op jit(solution)/shard_map/...d,df->...f/dot_general | solution.py:32
  20.1 21.3 %all-to-all-done.1 = bf16[32,256,128]{1,2,0:T(8,128)(2,1)} async-done(((bf16[32,256,128]{1,2,0:T(8,128)(2,1)}), bf16[32,256,128]{1,2,0:T(8,128)(2,1)}, u32[]{:S(2)}, u32[]{:S(2)}) %all-to-all-start.1) | async-done | bytes 2097184 | tf_op jit(solution)/shard_map/all_to_all | solution.py:142
  41.4 3.9 %copy.89 = bf16[8,4,256,128]{3,2,1,0:T(8,128)(2,1)} copy(bf16[8,4,256,128]{2,3,0,1:T(8,128)(2,1)} %bitcast.14) | data formatting | bytes 4194304 | tf_op jit(solution)/shard_map/all_to_all | solution.py:142
  45.3 1.9 %pad_maximum_fusion.1 = bf16[8,64,144]{2,1,0:T(8,128)(2,1)} fusion(bf16[8,1024,128]{2,1,0:T(8,128)(2,1)} %bitcast.57, bf16[8,1024,16]{2,1,0:T(8,128)(2,1)S(1)} %bitcast.55), kind=kLoop, calls=%fused_computation.21 | loop fusion | flops 294912 | bytes 2506752 | tf_op jit(solution)/shard_map/concatenate | solution.py:152
  47.2 1.3 collective-permute-start.1
  48.6 2.4 %fusion.21 = (f32[8,153,128]{2,1,0:T(8,128)S(1)}, f32[8,2,153,128]{3,2,1,0:T(8,128)}) fusion(bf16[8,2,512,128]{3,2,1,0:T(8,128)(2,1)S(1)} %bitcast.58, bf16[8,2,512,136]{2,3,1,0:T(8,128)(2,1)S(1)} %copy-done.4, bf16[8,2,512,16]{2,3,1,0:T(8,128)(2,1)S(1)} %multiply_convert_fusion.3, bf16[153]{0:T(256)(128)(2,1)S(1)} %pad.9.clone), kind=kOutput, calls=%fused_computation.28 | convolution fusion | flops 328541184 | bytes 6467890 | tf_op jit(solution)/shard_map/hnrf,hnrv->hnfv/dot_general | solution.py:156
  50.9 1.2 copy.92
  52.1 1.3 collective-permute-start
  53.4 1.4 copy.96
  54.9 1.3 slice.26
  56.2 1.8 %copy.90 = bf16[256,512]{0,1:T(8,128)(2,1)} copy(bf16[256,512]{1,0:T(8,128)(2,1)} %param.9) | data formatting | bytes 524288 | tf_op jit(solution)/shard_map/optimization_barrier | solution.py:178
  57.9 4.0 %all-to-all-start.2 = ((bf16[32,256,16]{1,2,0:T(8,128)(2,1)}), bf16[32,256,16]{1,2,0:T(8,128)(2,1)}, u32[]{:S(2)}, u32[]{:S(2)}) async-start(bf16[32,256,16]{1,2,0:T(8,128)(2,1)} %bitcast.66), calls=%async_computation.2 | async-start | bytes 524288 | tf_op jit(solution)/shard_map/all_to_all | solution.py:142
  63.1 1.9 %pad_maximum_fusion.refs_3_ = bf16[8,1152,128]{2,1,0:T(8,128)(2,1)} fusion(bf16[8,1024,128]{2,1,0:T(8,128)(2,1)S(1)} %bitcast.59, bf16[8,64,128]{2,1,0:T(8,128)(2,1)S(1)} %slice.25, bf16[1152]{0:T(1024)(128)(2,1)S(1)} %pad.4.clone), kind=kLoop, calls=%fused_computation.12 | loop fusion | flops 7077888 | bytes 4589824 | tf_op jit(solution)/shard_map/concatenate | solution.py:196
  66.0 1.8 %concatenate.20 = bf16[8,1152,16]{1,2,0:T(8,128)(2,1)} concatenate(bf16[8,64,16]{1,2,0:T(8,128)(2,1)S(1)} %slice.18, bf16[8,64,16]{1,2,0:T(8,128)(2,1)S(1)} %copy.95, bf16[8,1024,16]{1,2,0:T(8,128)(2,1)} %copy.96), dimensions={1} | concatenate | bytes 589824 | tf_op jit(solution)/shard_map/concatenate | solution.py:195
  68.1 1.9 %copy.91 = bf16[8,4,256,16]{3,2,1,0:T(8,128)(2,1)S(1)} copy(bf16[8,4,256,16]{2,3,0,1:T(8,128)(2,1)} %bitcast.19) | data formatting | bytes 524288 | tf_op jit(solution)/shard_map/all_to_all | solution.py:142
  70.7 1.4 copy.97
  72.2 2.8 %fusion.22 = f32[8,2,512,136]{2,3,1,0:T(8,128)} fusion(bf16[8,2,512,16]{3,2,1,0:T(8,128)(2,1)S(1)} %bitcast.52, bf16[16,136,1,1]{1,0,3,2:T(8,128)(2,1)S(1)} %copy-done.7), kind=kOutput, calls=%fused_computation.29 | convolution fusion | flops 35651584 | bytes 4722944 | tf_op jit(solution)/shard_map/...d,df->...f/dot_general | solution.py:32
  75.0 2.3 %copy_add_fusion = f32[8,153,128]{2,0,1:T(8,128)} fusion(f32[8,153,128]{2,0,1:T(8,128)} %collective-permute-done, f32[8,153,128]{2,1,0:T(8,128)S(1)} %get-tuple-element.13), kind=kLoop, calls=%fused_computation.30 | loop fusion | flops 156672 | bytes 1880064 | tf_op jit(solution)/shard_map/add | solution.py:175
  77.3 1.6 %collective-permute-start.2 = (f32[8,153,128]{2,0,1:T(8,128)}, f32[8,153,128]{2,0,1:T(8,128)}, u32[]{:S(2)}, u32[]{:S(2)}) collective-permute-start(f32[8,153,128]{2,0,1:T(8,128)} %copy_add_fusion), channel_id=1, source_target_pairs={{0,8},{4,12},{1,9},{5,13},{2,10},{6,14},{3,11},{7,15},{16,24},{20,... | collective-permute-start | bytes 1880072 | tf_op jit(solution)/shard_map/ppermute | solution.py:24
  78.9 19.0 %shard_map.91 = (f32[1024,1024]{1,0:T(8,128)}, f32[1024,1024]{1,0:T(8,128)}) custom-call(s32[1]{0:T(128)} %bitcast.refs_0_, bf16[8,1024,16]{2,1,0:T(8,128)(2,1)} %bitcast.53, bf16[8,16,1152]{2,1,0:T(8,128)(2,1)} %bitcast.65, bf16[8,1152,128]{2,1,0:T(8,128)(2,1)} %pad_maximum_fusion.refs_3_), custom_call_target="tpu_custom_call" | custom-call | tf_op jit(solution)/shard_map/pallas_call | solution.py:90
  98.0 3.0 %fusion.10 = bf16[8,2,512,136]{2,3,1,0:T(8,128)(2,1)S(1)} fusion(f32[8,2,512,136]{2,3,1,0:T(8,128)} %fusion.22, bf16[8,2,512,16]{3,2,1,0:T(8,128)(2,1)S(1)} %bitcast.54, bf16[16,136,1,1]{1,0,3,2:T(8,128)(2,1)S(1)} %copy-done.6, bf16[136]{0:T(256)(128)(2,1)S(1)} %copy-done.8), kind=kOutput, calls=%fused_computation.13 | convolution fusion | flops 40108032 | bytes 6951440 | tf_op jit(solution)/shard_map/...d,df->...f/dot_general | solution.py:31
  101.0 9.9 %collective-permute-done.2 = f32[8,153,128]{2,0,1:T(8,128)} collective-permute-done((f32[8,153,128]{2,0,1:T(8,128)}, f32[8,153,128]{2,0,1:T(8,128)}, u32[]{:S(2)}, u32[]{:S(2)}) %collective-permute-start.2) | collective-permute-done | bytes 626720 | tf_op jit(solution)/shard_map/ppermute | solution.py:24
  110.9 1.3 add.18
  112.3 3.7 %fusion.5 = f32[8,2,512,128]{3,2,1,0:T(8,128)} fusion(bf16[8,2,512,136]{2,3,1,0:T(8,128)(2,1)S(1)} %fusion.10, bf16[8,2,512,16]{2,3,1,0:T(8,128)(2,1)S(1)} %multiply_convert_fusion.2, bf16[153]{0:T(256)(128)(2,1)S(1)} %pad.9.clone, f32[8,1,153,128]{3,2,1,0:T(8,128)S(1)} %slice.26, f32[8,153,128]{2,1,0:T(8,128)S(1)} %copy.101), kind=kOutput, calls=%fused_computation.7 | convolution fusion | flops 329011200 | bytes 7938354 | tf_op jit(solution)/shard_map/hnrf,hnfv->hnrv/dot_general | solution.py:187
  116.0 6.6 %shard_map.92 = bf16[1024,1024]{1,0:T(8,128)(2,1)} custom-call(f32[1024,1024]{1,0:T(8,128)} %get-tuple-element.11.intra_ref, f32[8,1024,128]{2,1,0:T(8,128)} %bitcast.60, f32[1024,1024]{1,0:T(8,128)} %get-tuple-element.12.win_ref, f32[1,1024]{1,0:T(1,128)} %bitcast.67), custom_call_target="tpu_custom_call" | custom-call | tf_op jit(solution)/shard_map/pallas_call | solution.py:123
  122.6 29.3 %all_to_all.73 = bf16[4,256,1024]{2,1,0:T(8,128)(2,1)S(1)} all-to-all(bf16[4,256,1024]{2,1,0:T(8,128)(2,1)} %bitcast.62), channel_id=1, replica_groups=mesh['groups'=2,'ctx'=4,'head'=4] {'head'}, dimensions={0} | all-to-all | bytes 4194304 | tf_op jit(solution)/shard_map/all_to_all | solution.py:202
  151.9 1.5 copy.109
  (35 shorter events, 5.5 us)
Async XLA Ops:
  1.8 9.4 %all-to-all-start = ((bf16[32,256,16]{1,2,0:T(8,128)(2,1)}), bf16[32,256,16]{1,2,0:T(8,128)(2,1)S(1)}, u32[]{:S(2)}, u32[]{:S(2)}) async-start(bf16[32,256,16]{1,2,0:T(8,128)(2,1)} %bitcast.2), calls=%async_computation | async-start | bytes 524288 | tf_op jit(solution)/shard_map/all_to_all | solution.py:142
  11.2 30.2 %all-to-all-start.1 = ((bf16[32,256,128]{1,2,0:T(8,128)(2,1)}), bf16[32,256,128]{1,2,0:T(8,128)(2,1)}, u32[]{:S(2)}, u32[]{:S(2)}) async-start(bf16[32,256,128]{1,2,0:T(8,128)(2,1)} %bitcast.11), calls=%async_computation.1 | async-start | bytes 4194304 | tf_op jit(solution)/shard_map/all_to_all | solution.py:142
  15.6 1.5 copy-start.6
  17.1 0.8 copy-start.7
  45.3 3.2 %copy-start.2 = (bf16[8,4,256,128]{3,2,1,0:T(8,128)(2,1)S(1)}, bf16[8,4,256,128]{3,2,1,0:T(8,128)(2,1)}, u32[]{:S(2)}) copy-start(bf16[8,4,256,128]{3,2,1,0:T(8,128)(2,1)} %copy.89) | copy-start | bytes 6291460
  45.3 3.2 %copy-start.4 = (bf16[8,2,512,136]{2,3,1,0:T(8,128)(2,1)S(1)}, bf16[8,2,512,136]{2,3,1,0:T(8,128)(2,1)}, u32[]{:S(2)}) copy-start(bf16[8,2,512,136]{2,3,1,0:T(8,128)(2,1)} %fusion.11) | copy-start | bytes 6684676
  47.2 14.7 %collective-permute-start.1 = (bf16[8,64,144]{2,1,0:T(8,128)(2,1)}, bf16[8,64,144]{2,1,0:T(8,128)(2,1)}, u32[]{:S(2)}, u32[]{:S(2)}) collective-permute-start(bf16[8,64,144]{2,1,0:T(8,128)(2,1)} %pad_maximum_fusion.1), channel_id=1, source_target_pairs={{0,4},{4,8},{8,12},{1,5},{5,9},{9,13},{2,6},{6,10},{10,14},{3,7},{... | collective-permute-start | bytes 442376 | tf_op jit(solution)/shard_map/ppermute | solution.py:24
  52.1 18.6 %collective-permute-start = (f32[8,153,128]{2,0,1:T(8,128)}, f32[8,153,128]{2,0,1:T(8,128)}, u32[]{:S(2)}, u32[]{:S(2)}) collective-permute-start(f32[8,153,128]{2,0,1:T(8,128)} %copy.92), channel_id=1, source_target_pairs={{0,4},{4,8},{8,12},{1,5},{5,9},{9,13},{2,6},{6,10},{10,14},{3,7},{... | collective-permute-start | bytes 1880072 | tf_op jit(solution)/shard_map/ppermute | solution.py:24
  54.9 8.2 %copy-start.3 = (bf16[8,4,256,128]{3,2,1,0:T(8,128)(2,1)S(1)}, bf16[8,4,256,128]{3,2,1,0:T(8,128)(2,1)}, u32[]{:S(2)}) copy-start(bf16[8,4,256,128]{3,2,1,0:T(8,128)(2,1)} %copy.89) | copy-start | bytes 6291460
  57.9 10.1 %all-to-all-start.2 = ((bf16[32,256,16]{1,2,0:T(8,128)(2,1)}), bf16[32,256,16]{1,2,0:T(8,128)(2,1)}, u32[]{:S(2)}, u32[]{:S(2)}) async-start(bf16[32,256,16]{1,2,0:T(8,128)(2,1)} %bitcast.66), calls=%async_computation.2 | async-start | bytes 524288 | tf_op jit(solution)/shard_map/all_to_all | solution.py:142
  70.0 5.0 %copy-start = (bf16[8,4,256,16]{3,2,1,0:T(8,128)(2,1)}, bf16[8,4,256,16]{3,2,1,0:T(8,128)(2,1)S(1)}, u32[]{:S(2)}) copy-start(bf16[8,4,256,16]{3,2,1,0:T(8,128)(2,1)S(1)} %copy.91) | copy-start | bytes 786436
  77.3 20.6 %copy-start.5 = (bf16[8,2,512,16]{2,3,1,0:T(8,128)(2,1)S(1)}, bf16[8,2,512,16]{2,3,1,0:T(8,128)(2,1)}, u32[]{:S(2)}) copy-start(bf16[8,2,512,16]{2,3,1,0:T(8,128)(2,1)} %copy.97) | copy-start | bytes 786436
  77.3 33.6 %collective-permute-start.2 = (f32[8,153,128]{2,0,1:T(8,128)}, f32[8,153,128]{2,0,1:T(8,128)}, u32[]{:S(2)}, u32[]{:S(2)}) collective-permute-start(f32[8,153,128]{2,0,1:T(8,128)} %copy_add_fusion), channel_id=1, source_target_pairs={{0,8},{4,12},{1,9},{5,13},{2,10},{6,14},{3,11},{7,15},{16,24},{20,... | collective-permute-start | bytes 1880072 | tf_op jit(solution)/shard_map/ppermute | solution.py:24
  78.9 19.1 %copy-start.1 = (bf16[8,4,256,16]{3,2,1,0:T(8,128)(2,1)S(1)}, bf16[8,4,256,16]{3,2,1,0:T(8,128)(2,1)}, u32[]{:S(2)}) copy-start(bf16[8,4,256,16]{3,2,1,0:T(8,128)(2,1)} %copy-done) | copy-start | bytes 786436
  78.9 19.1 %copy-start.8 = (bf16[136]{0:T(256)(128)(2,1)S(1)}, bf16[136]{0:T(256)(128)(2,1)}, u32[]{:S(2)}) copy-start(bf16[136]{0:T(256)(128)(2,1)} %constant.30.clone) | copy-start | bytes 820

commit v20 on v19

--- a/solution.py
+++ b/solution.py
@@ -84,7 +84,7 @@
 def local_attention(flag, q_hm, kt_hm, vx, block_rows):
     heads_here, span_rows, _ = q_hm.shape
     ext = kt_hm.shape[2]
-    step = 2 if heads_here % 2 == 0 else 1
+    step = 4 if heads_here % 4 == 0 else (2 if heads_here % 2 == 0 else 1)
     body = lambda *refs: local_attention_kernel(*refs, span_rows=span_rows, block_rows=block_rows)
     out = jax.ShapeDtypeStruct((span_rows, heads_here * VD), jnp.float32)
     return pl.pallas_call(

time: 154 us -> 154 us (level)
  no operation moved by 1% of the time
where the time goes in v20:
time: 154 us; the launch traced here: 153 us
  waiting for transfers between devices  34.3 us (22%)
  blocking collectives  29.3 us (19%)
  local copies, waits for them, and re-layouts  25.7 us (17%)
  Pallas kernels  25.4 us (16%)
  starting transfers between devices  16 us (10%)
  matrix products  14.8 us (10%)
  other arithmetic  7.54 us (5%)
    all_to_all x1, blocking collectives, per_device(): lax.all_to_all(mixed, 'head', split_axis=0, concat_axis=1, tiled=True)  29.3 us
    all_to_all x3, waiting for transfers between devices, to_heads(): return lax.all_to_all(tok, 'head', split_axis=0, concat_axis=1, tiled=True)  23.5 us
    pallas_call x1, Pallas kernels, local_attention(): pl.pallas_call(body, grid_spec=pltpu.PrefetchScalarGridSpec(num_scalar_pr...  18.8 us
    all_to_all x3, starting transfers between devices, to_heads(): return lax.all_to_all(tok, 'head', split_axis=0, concat_axis=1, tiled=True)  11.9 us
    ppermute x3, waiting for transfers between devices, shifted(): return lax.ppermute(shard, axis, pairs)  10.8 us
    all_to_all x5, local copies, waits for them, and re-layouts, to_heads(): return lax.all_to_all(tok, 'head', split_axis=0, concat_axis=1, tiled=True)  8.5 us
    pallas_call x1, Pallas kernels, mix(): pl.pallas_call(mix_kernel, grid=(heads_here // step,), in_specs=[tile, pl...  6.58 us
    unnamed x20, local copies, waits for them, and re-layouts  5.9 us
  transfers between devices with their start and end apart: 6, of which 5 were waited for; matrix products, arithmetic and copies ran while one was open for 18% of the time, Pallas kernels for 12%

profile of v20, /device:TPU:28, one launch (start us, length us, event | category | flops | bytes accessed | tf_op | source)
XLA Modules:
  0.0 153.4 jit_solution(4603314631815216698)
XLA Ops:
  0.0 1.8 %copy.82 = bf16[256,512]{0,1:T(8,128)(2,1)} copy(bf16[256,512]{1,0:T(8,128)(2,1)} %param.10) | data formatting | bytes 524288 | tf_op args[1]
  1.8 3.4 %all-to-all-start = ((bf16[32,256,16]{1,2,0:T(8,128)(2,1)}), bf16[32,256,16]{1,2,0:T(8,128)(2,1)S(1)}, u32[]{:S(2)}, u32[]{:S(2)}) async-start(bf16[32,256,16]{1,2,0:T(8,128)(2,1)} %bitcast.2), calls=%async_computation | async-start | bytes 524288 | tf_op jit(solution)/shard_map/all_to_all | solution.py:142
  5.2 4.1 %copy.87 = bf16[256,4096]{0,1:T(8,128)(2,1)} copy(bf16[256,4096]{1,0:T(8,128)(2,1)} %param.11) | data formatting | bytes 4194304 | tf_op args[2]
  9.3 1.9 %all-to-all-done = bf16[32,256,16]{1,2,0:T(8,128)(2,1)S(1)} async-done(((bf16[32,256,16]{1,2,0:T(8,128)(2,1)}), bf16[32,256,16]{1,2,0:T(8,128)(2,1)S(1)}, u32[]{:S(2)}, u32[]{:S(2)}) %all-to-all-start) | async-done | bytes 262176 | tf_op jit(solution)/shard_map/all_to_all | solution.py:142
  11.2 4.4 %all-to-all-start.1 = ((bf16[32,256,128]{1,2,0:T(8,128)(2,1)}), bf16[32,256,128]{1,2,0:T(8,128)(2,1)}, u32[]{:S(2)}, u32[]{:S(2)}) async-start(bf16[32,256,128]{1,2,0:T(8,128)(2,1)} %bitcast.11), calls=%async_computation.1 | async-start | bytes 4194304 | tf_op jit(solution)/shard_map/all_to_all | solution.py:142
  17.9 2.1 %fusion.11 = bf16[8,2,512,136]{2,3,1,0:T(8,128)(2,1)} fusion(f32[136,8,2,512]{3,0,2,1:T(8,128)S(1)} %fusion.16, bf16[16,136,1,1]{1,0,3,2:T(8,128)(2,1)S(1)} %copy-done.7, bf16[8,2,512,16]{2,1,3,0:T(2,128)(2,1)S(1)} %reshape.39), kind=kOutput, calls=%fused_computation.14 | convolution fusion | flops 38993920 | bytes 6951168 | tf_op jit(solution)/shard_map/...d,df->...f/dot_general | solution.py:32
  20.1 21.3 %all-to-all-done.1 = bf16[32,256,128]{1,2,0:T(8,128)(2,1)} async-done(((bf16[32,256,128]{1,2,0:T(8,128)(2,1)}), bf16[32,256,128]{1,2,0:T(8,128)(2,1)}, u32[]{:S(2)}, u32[]{:S(2)}) %all-to-all-start.1) | async-done | bytes 2097184 | tf_op jit(solution)/shard_map/all_to_all | solution.py:142
  41.4 3.9 %copy.89 = bf16[8,4,256,128]{3,2,1,0:T(8,128)(2,1)} copy(bf16[8,4,256,128]{2,3,0,1:T(8,128)(2,1)} %bitcast.14) | data formatting | bytes 4194304 | tf_op jit(solution)/shard_map/all_to_all | solution.py:142
  45.3 1.9 %pad_maximum_fusion.1 = bf16[8,64,144]{2,1,0:T(8,128)(2,1)} fusion(bf16[8,1024,128]{2,1,0:T(8,128)(2,1)} %bitcast.57, bf16[8,1024,16]{2,1,0:T(8,128)(2,1)S(1)} %bitcast.55), kind=kLoop, calls=%fused_computation.21 | loop fusion | flops 294912 | bytes 2506752 | tf_op jit(solution)/shard_map/concatenate | solution.py:152
  47.2 1.3 collective-permute-start.1
  48.6 2.4 %fusion.21 = (f32[8,153,128]{2,1,0:T(8,128)S(1)}, f32[8,2,153,128]{3,2,1,0:T(8,128)}) fusion(bf16[8,2,512,128]{3,2,1,0:T(8,128)(2,1)S(1)} %bitcast.58, bf16[8,2,512,136]{2,3,1,0:T(8,128)(2,1)S(1)} %copy-done.4, bf16[8,2,512,16]{2,3,1,0:T(8,128)(2,1)S(1)} %multiply_convert_fusion.3, bf16[153]{0:T(256)(128)(2,1)S(1)} %pad.9.clone), kind=kOutput, calls=%fused_computation.28 | convolution fusion | flops 328541184 | bytes 6467890 | tf_op jit(solution)/shard_map/hnrf,hnrv->hnfv/dot_general | solution.py:156
  50.9 1.2 copy.92
  52.1 1.3 collective-permute-start
  53.4 1.4 copy.96
  54.9 1.3 slice.26
  56.2 1.8 %copy.90 = bf16[256,512]{0,1:T(8,128)(2,1)} copy(bf16[256,512]{1,0:T(8,128)(2,1)} %param.9) | data formatting | bytes 524288 | tf_op jit(solution)/shard_map/optimization_barrier | solution.py:178
  57.9 4.0 %all-to-all-start.2 = ((bf16[32,256,16]{1,2,0:T(8,128)(2,1)}), bf16[32,256,16]{1,2,0:T(8,128)(2,1)}, u32[]{:S(2)}, u32[]{:S(2)}) async-start(bf16[32,256,16]{1,2,0:T(8,128)(2,1)} %bitcast.66), calls=%async_computation.2 | async-start | bytes 524288 | tf_op jit(solution)/shard_map/all_to_all | solution.py:142
  63.1 1.9 %pad_maximum_fusion.refs_3_ = bf16[8,1152,128]{2,1,0:T(8,128)(2,1)} fusion(bf16[8,1024,128]{2,1,0:T(8,128)(2,1)S(1)} %bitcast.59, bf16[8,64,128]{2,1,0:T(8,128)(2,1)S(1)} %slice.25, bf16[1152]{0:T(1024)(128)(2,1)S(1)} %pad.4.clone), kind=kLoop, calls=%fused_computation.12 | loop fusion | flops 7077888 | bytes 4589824 | tf_op jit(solution)/shard_map/concatenate | solution.py:196
  66.0 1.8 %concatenate.20 = bf16[8,1152,16]{1,2,0:T(8,128)(2,1)} concatenate(bf16[8,64,16]{1,2,0:T(8,128)(2,1)S(1)} %slice.18, bf16[8,64,16]{1,2,0:T(8,128)(2,1)S(1)} %copy.95, bf16[8,1024,16]{1,2,0:T(8,128)(2,1)} %copy.96), dimensions={1} | concatenate | bytes 589824 | tf_op jit(solution)/shard_map/concatenate | solution.py:195
  68.1 1.9 %copy.91 = bf16[8,4,256,16]{3,2,1,0:T(8,128)(2,1)S(1)} copy(bf16[8,4,256,16]{2,3,0,1:T(8,128)(2,1)} %bitcast.19) | data formatting | bytes 524288 | tf_op jit(solution)/shard_map/all_to_all | solution.py:142
  70.7 1.4 copy.97
  72.2 2.8 %fusion.22 = f32[8,2,512,136]{2,3,1,0:T(8,128)} fusion(bf16[8,2,512,16]{3,2,1,0:T(8,128)(2,1)S(1)} %bitcast.52, bf16[16,136,1,1]{1,0,3,2:T(8,128)(2,1)S(1)} %copy-done.7), kind=kOutput, calls=%fused_computation.29 | convolution fusion | flops 35651584 | bytes 4722944 | tf_op jit(solution)/shard_map/...d,df->...f/dot_general | solution.py:32
  75.0 2.3 %copy_add_fusion = f32[8,153,128]{2,0,1:T(8,128)} fusion(f32[8,153,128]{2,0,1:T(8,128)} %collective-permute-done, f32[8,153,128]{2,1,0:T(8,128)S(1)} %get-tuple-element.13), kind=kLoop, calls=%fused_computation.30 | loop fusion | flops 156672 | bytes 1880064 | tf_op jit(solution)/shard_map/add | solution.py:175
  77.3 1.6 %collective-permute-start.2 = (f32[8,153,128]{2,0,1:T(8,128)}, f32[8,153,128]{2,0,1:T(8,128)}, u32[]{:S(2)}, u32[]{:S(2)}) collective-permute-start(f32[8,153,128]{2,0,1:T(8,128)} %copy_add_fusion), channel_id=1, source_target_pairs={{0,8},{4,12},{1,9},{5,13},{2,10},{6,14},{3,11},{7,15},{16,24},{20,... | collective-permute-start | bytes 1880072 | tf_op jit(solution)/shard_map/ppermute | solution.py:24
  78.9 18.8 %shard_map.91 = (f32[1024,1024]{1,0:T(8,128)}, f32[1024,1024]{1,0:T(8,128)}) custom-call(s32[1]{0:T(128)} %bitcast.refs_0_, bf16[8,1024,16]{2,1,0:T(8,128)(2,1)} %bitcast.53, bf16[8,16,1152]{2,1,0:T(8,128)(2,1)} %bitcast.65, bf16[8,1152,128]{2,1,0:T(8,128)(2,1)} %pad_maximum_fusion.refs_3_), custom_call_target="tpu_custom_call" | custom-call | tf_op jit(solution)/shard_map/pallas_call | solution.py:90
  97.8 3.1 %fusion.10 = bf16[8,2,512,136]{2,3,1,0:T(8,128)(2,1)S(1)} fusion(f32[8,2,512,136]{2,3,1,0:T(8,128)} %fusion.22, bf16[8,2,512,16]{3,2,1,0:T(8,128)(2,1)S(1)} %bitcast.54, bf16[16,136,1,1]{1,0,3,2:T(8,128)(2,1)S(1)} %copy-done.6, bf16[136]{0:T(256)(128)(2,1)S(1)} %copy-done.8), kind=kOutput, calls=%fused_computation.13 | convolution fusion | flops 40108032 | bytes 6951440 | tf_op jit(solution)/shard_map/...d,df->...f/dot_general | solution.py:31
  100.8 10.1 %collective-permute-done.2 = f32[8,153,128]{2,0,1:T(8,128)} collective-permute-done((f32[8,153,128]{2,0,1:T(8,128)}, f32[8,153,128]{2,0,1:T(8,128)}, u32[]{:S(2)}, u32[]{:S(2)}) %collective-permute-start.2) | collective-permute-done | bytes 626720 | tf_op jit(solution)/shard_map/ppermute | solution.py:24
  110.9 1.3 add.18
  112.3 3.7 %fusion.5 = f32[8,2,512,128]{3,2,1,0:T(8,128)} fusion(bf16[8,2,512,136]{2,3,1,0:T(8,128)(2,1)S(1)} %fusion.10, bf16[8,2,512,16]{2,3,1,0:T(8,128)(2,1)S(1)} %multiply_convert_fusion.2, bf16[153]{0:T(256)(128)(2,1)S(1)} %pad.9.clone, f32[8,1,153,128]{3,2,1,0:T(8,128)S(1)} %slice.26, f32[8,153,128]{2,1,0:T(8,128)S(1)} %copy.101), kind=kOutput, calls=%fused_computation.7 | convolution fusion | flops 329011200 | bytes 7938354 | tf_op jit(solution)/shard_map/hnrf,hnfv->hnrv/dot_general | solution.py:187
  116.0 6.6 %shard_map.92 = bf16[1024,1024]{1,0:T(8,128)(2,1)} custom-call(f32[1024,1024]{1,0:T(8,128)} %get-tuple-element.11.intra_ref, f32[8,1024,128]{2,1,0:T(8,128)} %bitcast.60, f32[1024,1024]{1,0:T(8,128)} %get-tuple-element.12.win_ref, f32[1,1024]{1,0:T(1,128)} %bitcast.67), custom_call_target="tpu_custom_call" | custom-call | tf_op jit(solution)/shard_map/pallas_call | solution.py:123
  122.6 29.3 %all_to_all.73 = bf16[4,256,1024]{2,1,0:T(8,128)(2,1)S(1)} all-to-all(bf16[4,256,1024]{2,1,0:T(8,128)(2,1)} %bitcast.62), channel_id=1, replica_groups=mesh['groups'=2,'ctx'=4,'head'=4] {'head'}, dimensions={0} | all-to-all | bytes 4194304 | tf_op jit(solution)/shard_map/all_to_all | solution.py:202
  151.9 1.5 copy.109
  (35 shorter events, 5.5 us)
Async XLA Ops:
  1.8 9.4 %all-to-all-start = ((bf16[32,256,16]{1,2,0:T(8,128)(2,1)}), bf16[32,256,16]{1,2,0:T(8,128)(2,1)S(1)}, u32[]{:S(2)}, u32[]{:S(2)}) async-start(bf16[32,256,16]{1,2,0:T(8,128)(2,1)} %bitcast.2), calls=%async_computation | async-start | bytes 524288 | tf_op jit(solution)/shard_map/all_to_all | solution.py:142
  11.2 30.2 %all-to-all-start.1 = ((bf16[32,256,128]{1,2,0:T(8,128)(2,1)}), bf16[32,256,128]{1,2,0:T(8,128)(2,1)}, u32[]{:S(2)}, u32[]{:S(2)}) async-start(bf16[32,256,128]{1,2,0:T(8,128)(2,1)} %bitcast.11), calls=%async_computation.1 | async-start | bytes 4194304 | tf_op jit(solution)/shard_map/all_to_all | solution.py:142
  15.6 1.5 copy-start.6
  17.1 0.8 copy-start.7
  45.3 3.2 %copy-start.2 = (bf16[8,4,256,128]{3,2,1,0:T(8,128)(2,1)S(1)}, bf16[8,4,256,128]{3,2,1,0:T(8,128)(2,1)}, u32[]{:S(2)}) copy-start(bf16[8,4,256,128]{3,2,1,0:T(8,128)(2,1)} %copy.89) | copy-start | bytes 6291460
  45.3 3.2 %copy-start.4 = (bf16[8,2,512,136]{2,3,1,0:T(8,128)(2,1)S(1)}, bf16[8,2,512,136]{2,3,1,0:T(8,128)(2,1)}, u32[]{:S(2)}) copy-start(bf16[8,2,512,136]{2,3,1,0:T(8,128)(2,1)} %fusion.11) | copy-start | bytes 6684676
  47.2 14.7 %collective-permute-start.1 = (bf16[8,64,144]{2,1,0:T(8,128)(2,1)}, bf16[8,64,144]{2,1,0:T(8,128)(2,1)}, u32[]{:S(2)}, u32[]{:S(2)}) collective-permute-start(bf16[8,64,144]{2,1,0:T(8,128)(2,1)} %pad_maximum_fusion.1), channel_id=1, source_target_pairs={{0,4},{4,8},{8,12},{1,5},{5,9},{9,13},{2,6},{6,10},{10,14},{3,7},{... | collective-permute-start | bytes 442376 | tf_op jit(solution)/shard_map/ppermute | solution.py:24
  52.1 18.6 %collective-permute-start = (f32[8,153,128]{2,0,1:T(8,128)}, f32[8,153,128]{2,0,1:T(8,128)}, u32[]{:S(2)}, u32[]{:S(2)}) collective-permute-start(f32[8,153,128]{2,0,1:T(8,128)} %copy.92), channel_id=1, source_target_pairs={{0,4},{4,8},{8,12},{1,5},{5,9},{9,13},{2,6},{6,10},{10,14},{3,7},{... | collective-permute-start | bytes 1880072 | tf_op jit(solution)/shard_map/ppermute | solution.py:24
  54.9 8.2 %copy-start.3 = (bf16[8,4,256,128]{3,2,1,0:T(8,128)(2,1)S(1)}, bf16[8,4,256,128]{3,2,1,0:T(8,128)(2,1)}, u32[]{:S(2)}) copy-start(bf16[8,4,256,128]{3,2,1,0:T(8,128)(2,1)} %copy.89) | copy-start | bytes 6291460
  57.9 10.1 %all-to-all-start.2 = ((bf16[32,256,16]{1,2,0:T(8,128)(2,1)}), bf16[32,256,16]{1,2,0:T(8,128)(2,1)}, u32[]{:S(2)}, u32[]{:S(2)}) async-start(bf16[32,256,16]{1,2,0:T(8,128)(2,1)} %bitcast.66), calls=%async_computation.2 | async-start | bytes 524288 | tf_op jit(solution)/shard_map/all_to_all | solution.py:142
  70.0 5.0 %copy-start = (bf16[8,4,256,16]{3,2,1,0:T(8,128)(2,1)}, bf16[8,4,256,16]{3,2,1,0:T(8,128)(2,1)S(1)}, u32[]{:S(2)}) copy-start(bf16[8,4,256,16]{3,2,1,0:T(8,128)(2,1)S(1)} %copy.91) | copy-start | bytes 786436
  77.3 20.4 %copy-start.5 = (bf16[8,2,512,16]{2,3,1,0:T(8,128)(2,1)S(1)}, bf16[8,2,512,16]{2,3,1,0:T(8,128)(2,1)}, u32[]{:S(2)}) copy-start(bf16[8,2,512,16]{2,3,1,0:T(8,128)(2,1)} %copy.97) | copy-start | bytes 786436
  77.3 33.6 %collective-permute-start.2 = (f32[8,153,128]{2,0,1:T(8,128)}, f32[8,153,128]{2,0,1:T(8,128)}, u32[]{:S(2)}, u32[]{:S(2)}) collective-permute-start(f32[8,153,128]{2,0,1:T(8,128)} %copy_add_fusion), channel_id=1, source_target_pairs={{0,8},{4,12},{1,9},{5,13},{2,10},{6,14},{3,11},{7,15},{16,24},{20,... | collective-permute-start | bytes 1880072 | tf_op jit(solution)/shard_map/ppermute | solution.py:24
  78.9 18.9 %copy-start.1 = (bf16[8,4,256,16]{3,2,1,0:T(8,128)(2,1)S(1)}, bf16[8,4,256,16]{3,2,1,0:T(8,128)(2,1)}, u32[]{:S(2)}) copy-start(bf16[8,4,256,16]{3,2,1,0:T(8,128)(2,1)} %copy-done) | copy-start | bytes 786436
  78.9 18.9 %copy-start.8 = (bf16[136]{0:T(256)(128)(2,1)S(1)}, bf16[136]{0:T(256)(128)(2,1)}, u32[]{:S(2)}) copy-start(bf16[136]{0:T(256)(128)(2,1)} %constant.30.clone) | copy-start | bytes 820

commit v21 on v20

--- a/solution.py
+++ b/solution.py
@@ -163,11 +163,13 @@
     peers = lax.axis_size("ctx")
     running = span_state
     entering = None
+    arrivals = []
     first_round = span_state
     shift = 1
     while shift < peers:
         received = shifted(running, "ctx", shift)
         entering = received if entering is None else entering + received
+        arrivals.append(received)
         if shift == 1:
             first_round = received
         shift *= 2
@@ -181,7 +183,9 @@
     before = jnp.concatenate(
         [jnp.zeros_like(block_states[:, :1]), jnp.cumsum(block_states[:, :-1], axis=1)], axis=1
     )
-    states = (before + entering[:, None]).astype(jnp.bfloat16)
+    for received in arrivals:
+        before = before + received[:, None]
+    states = before.astype(jnp.bfloat16)
 
     query_feat = unique_features(query_hm.reshape(heads_here, block_count, block_rows, KD), True)
     inter = jnp.einsum(

time: 154 us -> 154 us (level)
  the two profiles are of different devices: /device:TPU:28 before, /device:TPU:0 now
where the time goes in v21:
time: 154 us; the launch traced here: 152 us
  blocking collectives  29.3 us (19%)
  local copies, waits for them, and re-layouts  28 us (18%)
  Pallas kernels  25.4 us (16%)
  starting transfers between devices  24.1 us (16%)
  waiting for transfers between devices  23.6 us (15%)
  matrix products  14.9 us (10%)
  other arithmetic  6.23 us (4%)
    all_to_all x1, blocking collectives, per_device(): lax.all_to_all(mixed, 'head', split_axis=0, concat_axis=1, tiled=True)  29.3 us
    all_to_all x3, waiting for transfers between devices, to_heads(): return lax.all_to_all(tok, 'head', split_axis=0, concat_axis=1, tiled=True)  23.6 us
    pallas_call x1, Pallas kernels, local_attention(): pl.pallas_call(body, grid_spec=pltpu.PrefetchScalarGridSpec(num_scalar_pr...  18.8 us
    all_to_all x3, starting transfers between devices, to_heads(): return lax.all_to_all(tok, 'head', split_axis=0, concat_axis=1, tiled=True)  12.7 us
    ppermute x3, starting transfers between devices, shifted(): return lax.ppermute(shard, axis, pairs)  11.4 us
    all_to_all x5, local copies, waits for them, and re-layouts, to_heads(): return lax.all_to_all(tok, 'head', split_axis=0, concat_axis=1, tiled=True)  8.49 us
    pallas_call x1, Pallas kernels, mix(): pl.pallas_call(mix_kernel, grid=(heads_here // step,), in_specs=[tile, pl...  6.58 us
    unnamed x20, local copies, waits for them, and re-layouts  5.88 us
  transfers between devices with their start and end apart: 6, of which 3 were waited for; matrix products, arithmetic and copies ran while one was open for 19% of the time, Pallas kernels for 12%

profile of v21, /device:TPU:0, one launch (start us, length us, event | category | flops | bytes accessed | tf_op | source)
XLA Modules:
  0.0 151.6 jit_solution(7093713202659680263)
XLA Ops:
  0.0 1.8 %copy.84 = bf16[256,512]{0,1:T(8,128)(2,1)} copy(bf16[256,512]{1,0:T(8,128)(2,1)} %param.10) | data formatting | bytes 524288 | tf_op args[1]
  1.8 4.2 %all-to-all-start = ((bf16[32,256,16]{1,2,0:T(8,128)(2,1)}), bf16[32,256,16]{1,2,0:T(8,128)(2,1)S(1)}, u32[]{:S(2)}, u32[]{:S(2)}) async-start(bf16[32,256,16]{1,2,0:T(8,128)(2,1)} %bitcast.2), calls=%async_computation | async-start | bytes 524288 | tf_op jit(solution)/shard_map/all_to_all | solution.py:142
  6.0 4.1 %copy.89 = bf16[256,4096]{0,1:T(8,128)(2,1)} copy(bf16[256,4096]{1,0:T(8,128)(2,1)} %param.11) | data formatting | bytes 4194304 | tf_op args[2]
  10.1 2.0 %all-to-all-done = bf16[32,256,16]{1,2,0:T(8,128)(2,1)S(1)} async-done(((bf16[32,256,16]{1,2,0:T(8,128)(2,1)}), bf16[32,256,16]{1,2,0:T(8,128)(2,1)S(1)}, u32[]{:S(2)}, u32[]{:S(2)}) %all-to-all-start) | async-done | bytes 262176 | tf_op jit(solution)/shard_map/all_to_all | solution.py:142
  12.0 4.4 %all-to-all-start.1 = ((bf16[32,256,128]{1,2,0:T(8,128)(2,1)}), bf16[32,256,128]{1,2,0:T(8,128)(2,1)}, u32[]{:S(2)}, u32[]{:S(2)}) async-start(bf16[32,256,128]{1,2,0:T(8,128)(2,1)} %bitcast.11), calls=%async_computation.1 | async-start | bytes 4194304 | tf_op jit(solution)/shard_map/all_to_all | solution.py:142
  18.8 2.1 %fusion.11 = bf16[8,2,512,136]{2,3,1,0:T(8,128)(2,1)} fusion(f32[136,8,2,512]{3,0,2,1:T(8,128)S(1)} %fusion.17, bf16[16,136,1,1]{1,0,3,2:T(8,128)(2,1)S(1)} %copy-done.7, bf16[8,2,512,16]{2,1,3,0:T(2,128)(2,1)S(1)} %reshape.40), kind=kOutput, calls=%fused_computation.14 | convolution fusion | flops 38993920 | bytes 6951168 | tf_op jit(solution)/shard_map/...d,df->...f/dot_general | solution.py:32
  20.9 21.3 %all-to-all-done.1 = bf16[32,256,128]{1,2,0:T(8,128)(2,1)} async-done(((bf16[32,256,128]{1,2,0:T(8,128)(2,1)}), bf16[32,256,128]{1,2,0:T(8,128)(2,1)}, u32[]{:S(2)}, u32[]{:S(2)}) %all-to-all-start.1) | async-done | bytes 2097184 | tf_op jit(solution)/shard_map/all_to_all | solution.py:142
  42.2 3.9 %copy.91 = bf16[8,4,256,128]{3,2,1,0:T(8,128)(2,1)} copy(bf16[8,4,256,128]{2,3,0,1:T(8,128)(2,1)} %bitcast.14) | data formatting | bytes 4194304 | tf_op jit(solution)/shard_map/all_to_all | solution.py:142
  46.2 1.9 %pad_maximum_fusion.1 = bf16[8,64,144]{2,1,0:T(8,128)(2,1)} fusion(bf16[8,1024,128]{2,1,0:T(8,128)(2,1)} %bitcast.57, bf16[8,1024,16]{2,1,0:T(8,128)(2,1)S(1)} %bitcast.55), kind=kLoop, calls=%fused_computation.22 | loop fusion | flops 294912 | bytes 2506752 | tf_op jit(solution)/shard_map/concatenate | solution.py:152
  48.1 4.8 %collective-permute-start.1 = (bf16[8,64,144]{2,1,0:T(8,128)(2,1)}, bf16[8,64,144]{2,1,0:T(8,128)(2,1)}, u32[]{:S(2)}, u32[]{:S(2)}) collective-permute-start(bf16[8,64,144]{2,1,0:T(8,128)(2,1)} %pad_maximum_fusion.1), channel_id=1, source_target_pairs={{0,4},{4,8},{8,12},{1,5},{5,9},{9,13},{2,6},{6,10},{10,14},{3,7},{... | collective-permute-start | bytes 442376 | tf_op jit(solution)/shard_map/ppermute | solution.py:24
  52.9 2.4 %fusion.22 = (f32[8,153,128]{2,1,0:T(8,128)S(1)}, f32[8,2,153,128]{3,2,1,0:T(8,128)}) fusion(bf16[8,2,512,128]{3,2,1,0:T(8,128)(2,1)S(1)} %bitcast.58, bf16[8,2,512,136]{2,3,1,0:T(8,128)(2,1)S(1)} %copy-done.4, bf16[8,2,512,16]{2,3,1,0:T(8,128)(2,1)S(1)} %multiply_convert_fusion.3, bf16[153]{0:T(256)(128)(2,1)S(1)} %pad.9.clone), kind=kOutput, calls=%fused_computation.29 | convolution fusion | flops 328541184 | bytes 6467890 | tf_op jit(solution)/shard_map/hnrf,hnrv->hnfv/dot_general | solution.py:156
  55.2 1.2 copy.94
  56.4 3.6 %collective-permute-start = (f32[8,153,128]{2,0,1:T(8,128)}, f32[8,153,128]{2,0,1:T(8,128)}, u32[]{:S(2)}, u32[]{:S(2)}) collective-permute-start(f32[8,153,128]{2,0,1:T(8,128)} %copy.94), channel_id=1, source_target_pairs={{0,4},{4,8},{8,12},{1,5},{5,9},{9,13},{2,6},{6,10},{10,14},{3,7},{... | collective-permute-start | bytes 1880072 | tf_op jit(solution)/shard_map/ppermute | solution.py:24
  60.1 1.4 copy.98
  61.5 1.3 slice.26
  62.8 1.8 %copy.92 = bf16[256,512]{0,1:T(8,128)(2,1)} copy(bf16[256,512]{1,0:T(8,128)(2,1)} %param.9) | data formatting | bytes 524288 | tf_op jit(solution)/shard_map/optimization_barrier | solution.py:180
  64.6 4.0 %all-to-all-start.2 = ((bf16[32,256,16]{1,2,0:T(8,128)(2,1)}), bf16[32,256,16]{1,2,0:T(8,128)(2,1)}, u32[]{:S(2)}, u32[]{:S(2)}) async-start(bf16[32,256,16]{1,2,0:T(8,128)(2,1)} %bitcast.66), calls=%async_computation.2 | async-start | bytes 524288 | tf_op jit(solution)/shard_map/all_to_all | solution.py:142
  69.7 1.9 %pad_maximum_fusion.refs_3_ = bf16[8,1152,128]{2,1,0:T(8,128)(2,1)} fusion(bf16[8,1024,128]{2,1,0:T(8,128)(2,1)S(1)} %bitcast.59, bf16[8,64,128]{2,1,0:T(8,128)(2,1)S(1)} %slice.25, bf16[1152]{0:T(1024)(128)(2,1)S(1)} %pad.4.clone), kind=kLoop, calls=%fused_computation.12 | loop fusion | flops 7077888 | bytes 4589824 | tf_op jit(solution)/shard_map/concatenate | solution.py:200
  72.7 1.8 %concatenate.20 = bf16[8,1152,16]{1,2,0:T(8,128)(2,1)} concatenate(bf16[8,64,16]{1,2,0:T(8,128)(2,1)S(1)} %slice.18, bf16[8,64,16]{1,2,0:T(8,128)(2,1)S(1)} %copy.97, bf16[8,1024,16]{1,2,0:T(8,128)(2,1)} %copy.98), dimensions={1} | concatenate | bytes 589824 | tf_op jit(solution)/shard_map/concatenate | solution.py:199
  74.7 1.9 %copy.93 = bf16[8,4,256,16]{3,2,1,0:T(8,128)(2,1)S(1)} copy(bf16[8,4,256,16]{2,3,0,1:T(8,128)(2,1)} %bitcast.19) | data formatting | bytes 524288 | tf_op jit(solution)/shard_map/all_to_all | solution.py:142
  76.7 1.4 copy.99
  78.1 2.8 %fusion.23 = f32[8,2,512,136]{2,3,1,0:T(8,128)} fusion(bf16[8,2,512,16]{3,2,1,0:T(8,128)(2,1)S(1)} %bitcast.52, bf16[16,136,1,1]{1,0,3,2:T(8,128)(2,1)S(1)} %copy-done.7), kind=kOutput, calls=%fused_computation.30 | convolution fusion | flops 35651584 | bytes 4722944 | tf_op jit(solution)/shard_map/...d,df->...f/dot_general | solution.py:32
  80.9 2.3 %copy_add_fusion = f32[8,153,128]{2,0,1:T(8,128)} fusion(f32[8,153,128]{2,0,1:T(8,128)} %collective-permute-done, f32[8,153,128]{2,1,0:T(8,128)S(1)} %get-tuple-element.13), kind=kLoop, calls=%fused_computation.31 | loop fusion | flops 156672 | bytes 1880064 | tf_op jit(solution)/shard_map/add | solution.py:177
  83.2 2.9 %collective-permute-start.2 = (f32[8,153,128]{2,0,1:T(8,128)}, f32[8,153,128]{2,0,1:T(8,128)}, u32[]{:S(2)}, u32[]{:S(2)}) collective-permute-start(f32[8,153,128]{2,0,1:T(8,128)} %copy_add_fusion), channel_id=1, source_target_pairs={{0,8},{4,12},{1,9},{5,13},{2,10},{6,14},{3,11},{7,15},{16,24},{20,... | collective-permute-start | bytes 1880072 | tf_op jit(solution)/shard_map/ppermute | solution.py:24
  86.2 18.8 %shard_map.91 = (f32[1024,1024]{1,0:T(8,128)}, f32[1024,1024]{1,0:T(8,128)}) custom-call(s32[1]{0:T(128)} %bitcast.refs_0_, bf16[8,1024,16]{2,1,0:T(8,128)(2,1)} %bitcast.53, bf16[8,16,1152]{2,1,0:T(8,128)(2,1)} %bitcast.65, bf16[8,1152,128]{2,1,0:T(8,128)(2,1)} %pad_maximum_fusion.refs_3_), custom_call_target="tpu_custom_call" | custom-call | tf_op jit(solution)/shard_map/pallas_call | solution.py:90
  105.0 1.2 copy.102
  106.3 3.1 %fusion.10 = bf16[8,2,512,136]{2,3,1,0:T(8,128)(2,1)S(1)} fusion(f32[8,2,512,136]{2,3,1,0:T(8,128)} %fusion.23, bf16[8,2,512,16]{3,2,1,0:T(8,128)(2,1)S(1)} %bitcast.54, bf16[16,136,1,1]{1,0,3,2:T(8,128)(2,1)S(1)} %copy-done.6, bf16[136]{0:T(256)(128)(2,1)S(1)} %copy-done.8), kind=kOutput, calls=%fused_computation.13 | convolution fusion | flops 40108032 | bytes 6951440 | tf_op jit(solution)/shard_map/...d,df->...f/dot_general | solution.py:31
  109.3 1.2 copy.104
  110.5 3.8 %fusion.5 = f32[8,2,512,128]{3,2,1,0:T(8,128)} fusion(bf16[8,2,512,136]{2,3,1,0:T(8,128)(2,1)S(1)} %fusion.10, bf16[8,2,512,16]{2,3,1,0:T(8,128)(2,1)S(1)} %multiply_convert_fusion.2, bf16[153]{0:T(256)(128)(2,1)S(1)} %pad.9.clone, f32[8,1,153,128]{3,2,1,0:T(8,128)S(1)} %slice.26, f32[8,153,128]{2,1,0:T(8,128)S(1)} %copy.104, f32[8,153,128]{2,1,0:T(8,128)S(1)} %copy.102), kind=kOutput, calls=%fused_computation.7 | convolution fusion | flops 329324544 | bytes 8565042 | tf_op jit(solution)/shard_map/hnrf,hnfv->hnrv/dot_general | solution.py:191
  114.3 6.6 %shard_map.92 = bf16[1024,1024]{1,0:T(8,128)(2,1)} custom-call(f32[1024,1024]{1,0:T(8,128)} %get-tuple-element.11.intra_ref, f32[8,1024,128]{2,1,0:T(8,128)} %bitcast.60, f32[1024,1024]{1,0:T(8,128)} %get-tuple-element.12.win_ref, f32[1,1024]{1,0:T(1,128)} %bitcast.67), custom_call_target="tpu_custom_call" | custom-call | tf_op jit(solution)/shard_map/pallas_call | solution.py:123
  120.9 29.3 %all_to_all.73 = bf16[4,256,1024]{2,1,0:T(8,128)(2,1)S(1)} all-to-all(bf16[4,256,1024]{2,1,0:T(8,128)(2,1)} %bitcast.62), channel_id=1, replica_groups=mesh['groups'=2,'ctx'=4,'head'=4] {'head'}, dimensions={0} | all-to-all | bytes 4194304 | tf_op jit(solution)/shard_map/all_to_all | solution.py:206
  150.2 1.5 copy.112
  (35 shorter events, 4.7 us)
Async XLA Ops:
  1.8 10.2 %all-to-all-start = ((bf16[32,256,16]{1,2,0:T(8,128)(2,1)}), bf16[32,256,16]{1,2,0:T(8,128)(2,1)S(1)}, u32[]{:S(2)}, u32[]{:S(2)}) async-start(bf16[32,256,16]{1,2,0:T(8,128)(2,1)} %bitcast.2), calls=%async_computation | async-start | bytes 524288 | tf_op jit(solution)/shard_map/all_to_all | solution.py:142
  12.0 30.2 %all-to-all-start.1 = ((bf16[32,256,128]{1,2,0:T(8,128)(2,1)}), bf16[32,256,128]{1,2,0:T(8,128)(2,1)}, u32[]{:S(2)}, u32[]{:S(2)}) async-start(bf16[32,256,128]{1,2,0:T(8,128)(2,1)} %bitcast.11), calls=%async_computation.1 | async-start | bytes 4194304 | tf_op jit(solution)/shard_map/all_to_all | solution.py:142
  16.5 1.5 %copy-start.6 = (bf16[16,136,1,1]{1,0,3,2:T(8,128)(2,1)S(1)}, bf16[16,136,1,1]{1,0,3,2:T(8,128)(2,1)}, u32[]{:S(2)}) copy-start(bf16[16,136,1,1]{1,0,3,2:T(8,128)(2,1)} %constant.33) | copy-start | bytes 13060
  17.9 0.8 copy-start.7
  46.2 6.7 %copy-start.2 = (bf16[8,4,256,128]{3,2,1,0:T(8,128)(2,1)S(1)}, bf16[8,4,256,128]{3,2,1,0:T(8,128)(2,1)}, u32[]{:S(2)}) copy-start(bf16[8,4,256,128]{3,2,1,0:T(8,128)(2,1)} %copy.91) | copy-start | bytes 6291460
  46.2 6.7 %copy-start.4 = (bf16[8,2,512,136]{2,3,1,0:T(8,128)(2,1)S(1)}, bf16[8,2,512,136]{2,3,1,0:T(8,128)(2,1)}, u32[]{:S(2)}) copy-start(bf16[8,2,512,136]{2,3,1,0:T(8,128)(2,1)} %fusion.11) | copy-start | bytes 6684676
  48.1 20.6 %collective-permute-start.1 = (bf16[8,64,144]{2,1,0:T(8,128)(2,1)}, bf16[8,64,144]{2,1,0:T(8,128)(2,1)}, u32[]{:S(2)}, u32[]{:S(2)}) collective-permute-start(bf16[8,64,144]{2,1,0:T(8,128)(2,1)} %pad_maximum_fusion.1), channel_id=1, source_target_pairs={{0,4},{4,8},{8,12},{1,5},{5,9},{9,13},{2,6},{6,10},{10,14},{3,7},{... | collective-permute-start | bytes 442376 | tf_op jit(solution)/shard_map/ppermute | solution.py:24
  56.4 20.2 %collective-permute-start = (f32[8,153,128]{2,0,1:T(8,128)}, f32[8,153,128]{2,0,1:T(8,128)}, u32[]{:S(2)}, u32[]{:S(2)}) collective-permute-start(f32[8,153,128]{2,0,1:T(8,128)} %copy.94), channel_id=1, source_target_pairs={{0,4},{4,8},{8,12},{1,5},{5,9},{9,13},{2,6},{6,10},{10,14},{3,7},{... | collective-permute-start | bytes 1880072 | tf_op jit(solution)/shard_map/ppermute | solution.py:24
  61.5 8.2 %copy-start.3 = (bf16[8,4,256,128]{3,2,1,0:T(8,128)(2,1)S(1)}, bf16[8,4,256,128]{3,2,1,0:T(8,128)(2,1)}, u32[]{:S(2)}) copy-start(bf16[8,4,256,128]{3,2,1,0:T(8,128)(2,1)} %copy.91) | copy-start | bytes 6291460
  64.6 10.1 %all-to-all-start.2 = ((bf16[32,256,16]{1,2,0:T(8,128)(2,1)}), bf16[32,256,16]{1,2,0:T(8,128)(2,1)}, u32[]{:S(2)}, u32[]{:S(2)}) async-start(bf16[32,256,16]{1,2,0:T(8,128)(2,1)} %bitcast.66), calls=%async_computation.2 | async-start | bytes 524288 | tf_op jit(solution)/shard_map/all_to_all | solution.py:142
  76.6 4.3 %copy-start = (bf16[8,4,256,16]{3,2,1,0:T(8,128)(2,1)}, bf16[8,4,256,16]{3,2,1,0:T(8,128)(2,1)S(1)}, u32[]{:S(2)}) copy-start(bf16[8,4,256,16]{3,2,1,0:T(8,128)(2,1)S(1)} %copy.93) | copy-start | bytes 786436
  83.2 26.1 %collective-permute-start.2 = (f32[8,153,128]{2,0,1:T(8,128)}, f32[8,153,128]{2,0,1:T(8,128)}, u32[]{:S(2)}, u32[]{:S(2)}) collective-permute-start(f32[8,153,128]{2,0,1:T(8,128)} %copy_add_fusion), channel_id=1, source_target_pairs={{0,8},{4,12},{1,9},{5,13},{2,10},{6,14},{3,11},{7,15},{16,24},{20,... | collective-permute-start | bytes 1880072 | tf_op jit(solution)/shard_map/ppermute | solution.py:24
  86.2 20.0 %copy-start.5 = (bf16[8,2,512,16]{2,3,1,0:T(8,128)(2,1)S(1)}, bf16[8,2,512,16]{2,3,1,0:T(8,128)(2,1)}, u32[]{:S(2)}) copy-start(bf16[8,2,512,16]{2,3,1,0:T(8,128)(2,1)} %copy.99) | copy-start | bytes 786436
  86.2 20.1 %copy-start.1 = (bf16[8,4,256,16]{3,2,1,0:T(8,128)(2,1)S(1)}, bf16[8,4,256,16]{3,2,1,0:T(8,128)(2,1)}, u32[]{:S(2)}) copy-start(bf16[8,4,256,16]{3,2,1,0:T(8,128)(2,1)} %copy-done) | copy-start | bytes 786436
  86.2 20.1 %copy-start.8 = (bf16[136]{0:T(256)(128)(2,1)S(1)}, bf16[136]{0:T(256)(128)(2,1)}, u32[]{:S(2)}) copy-start(bf16[136]{0:T(256)(128)(2,1)} %constant.30.clone) | copy-start | bytes 820

commit v22 on v20

--- a/solution.py
+++ b/solution.py
@@ -66,9 +66,12 @@
         ).astype(jnp.bfloat16)
         intra_ref[r0 : r0 + CHUNK, cols] = jnp.dot(kernel, v_i, preferred_element_type=jnp.float32)
 
-        k_w = kt_ref[j, :, r0 : r0 + CHUNK + LEAD]
         v_w = vx_ref[j, r0 : r0 + CHUNK + LEAD, :]
-        ws = jnp.dot(q_c, k_w, preferred_element_type=jnp.float32) * 0.25
+        if r0 - bs >= LEAD:
+            ws = scores[:, r0 - bs - LEAD : r0 - bs + CHUNK]
+        else:
+            k_w = kt_ref[j, :, r0 : r0 + CHUNK + LEAD]
+            ws = jnp.dot(q_c, k_w, preferred_element_type=jnp.float32) * 0.25
         wrow = lax.broadcasted_iota(jnp.int32, (CHUNK, CHUNK + LEAD), 0)
         wcol = lax.broadcasted_iota(jnp.int32, (CHUNK, CHUNK + LEAD), 1)
         valid = (wcol > wrow + LEAD - WINDOW) & (wcol <= wrow + LEAD)

time: 154 us -> 154 us (level)
  transfers between devices with their start and end apart: 6 -> 6, of which waited for: 5 -> 5; matrix products, arithmetic and copies ran while one was open for 18% -> 18% of each run, Pallas kernels for 12% -> 13%
where the time goes in v22:
time: 154 us; the launch traced here: 153 us
  waiting for transfers between devices  33.9 us (22%)
  blocking collectives  29.3 us (19%)
  Pallas kernels  25.8 us (17%)
  local copies, waits for them, and re-layouts  25.7 us (17%)
  starting transfers between devices  16 us (10%)
  matrix products  14.8 us (10%)
  other arithmetic  7.54 us (5%)
    all_to_all x1, blocking collectives, per_device(): lax.all_to_all(mixed, 'head', split_axis=0, concat_axis=1, tiled=True)  29.3 us
    all_to_all x3, waiting for transfers between devices, to_heads(): return lax.all_to_all(tok, 'head', split_axis=0, concat_axis=1, tiled=True)  23.5 us
    pallas_call x1, Pallas kernels, local_attention(): pl.pallas_call(body, grid_spec=pltpu.PrefetchScalarGridSpec(num_scalar_pr...  19.2 us
    all_to_all x3, starting transfers between devices, to_heads(): return lax.all_to_all(tok, 'head', split_axis=0, concat_axis=1, tiled=True)  11.9 us
    ppermute x3, waiting for transfers between devices, shifted(): return lax.ppermute(shard, axis, pairs)  10.3 us
    all_to_all x5, local copies, waits for them, and re-layouts, to_heads(): return lax.all_to_all(tok, 'head', split_axis=0, concat_axis=1, tiled=True)  8.5 us
    pallas_call x1, Pallas kernels, mix(): pl.pallas_call(mix_kernel, grid=(heads_here // step,), in_specs=[tile, pl...  6.58 us
    unnamed x20, local copies, waits for them, and re-layouts  5.9 us
  transfers between devices with their start and end apart: 6, of which 5 were waited for; matrix products, arithmetic and copies ran while one was open for 18% of the time, Pallas kernels for 13%

profile of v22, /device:TPU:28, one launch (start us, length us, event | category | flops | bytes accessed | tf_op | source)
XLA Modules:
  0.0 153.4 jit_solution(13799815974085858473)
XLA Ops:
  0.0 1.8 %copy.82 = bf16[256,512]{0,1:T(8,128)(2,1)} copy(bf16[256,512]{1,0:T(8,128)(2,1)} %param.10) | data formatting | bytes 524288 | tf_op args[1]
  1.8 3.4 %all-to-all-start = ((bf16[32,256,16]{1,2,0:T(8,128)(2,1)}), bf16[32,256,16]{1,2,0:T(8,128)(2,1)S(1)}, u32[]{:S(2)}, u32[]{:S(2)}) async-start(bf16[32,256,16]{1,2,0:T(8,128)(2,1)} %bitcast.2), calls=%async_computation | async-start | bytes 524288 | tf_op jit(solution)/shard_map/all_to_all | solution.py:145
  5.2 4.1 %copy.87 = bf16[256,4096]{0,1:T(8,128)(2,1)} copy(bf16[256,4096]{1,0:T(8,128)(2,1)} %param.11) | data formatting | bytes 4194304 | tf_op args[2]
  9.3 1.9 %all-to-all-done = bf16[32,256,16]{1,2,0:T(8,128)(2,1)S(1)} async-done(((bf16[32,256,16]{1,2,0:T(8,128)(2,1)}), bf16[32,256,16]{1,2,0:T(8,128)(2,1)S(1)}, u32[]{:S(2)}, u32[]{:S(2)}) %all-to-all-start) | async-done | bytes 262176 | tf_op jit(solution)/shard_map/all_to_all | solution.py:145
  11.2 4.4 %all-to-all-start.1 = ((bf16[32,256,128]{1,2,0:T(8,128)(2,1)}), bf16[32,256,128]{1,2,0:T(8,128)(2,1)}, u32[]{:S(2)}, u32[]{:S(2)}) async-start(bf16[32,256,128]{1,2,0:T(8,128)(2,1)} %bitcast.11), calls=%async_computation.1 | async-start | bytes 4194304 | tf_op jit(solution)/shard_map/all_to_all | solution.py:145
  17.9 2.1 %fusion.11 = bf16[8,2,512,136]{2,3,1,0:T(8,128)(2,1)} fusion(f32[136,8,2,512]{3,0,2,1:T(8,128)S(1)} %fusion.16, bf16[16,136,1,1]{1,0,3,2:T(8,128)(2,1)S(1)} %copy-done.7, bf16[8,2,512,16]{2,1,3,0:T(2,128)(2,1)S(1)} %reshape.39), kind=kOutput, calls=%fused_computation.14 | convolution fusion | flops 38993920 | bytes 6951168 | tf_op jit(solution)/shard_map/...d,df->...f/dot_general | solution.py:32
  20.1 21.3 %all-to-all-done.1 = bf16[32,256,128]{1,2,0:T(8,128)(2,1)} async-done(((bf16[32,256,128]{1,2,0:T(8,128)(2,1)}), bf16[32,256,128]{1,2,0:T(8,128)(2,1)}, u32[]{:S(2)}, u32[]{:S(2)}) %all-to-all-start.1) | async-done | bytes 2097184 | tf_op jit(solution)/shard_map/all_to_all | solution.py:145
  41.4 3.9 %copy.89 = bf16[8,4,256,128]{3,2,1,0:T(8,128)(2,1)} copy(bf16[8,4,256,128]{2,3,0,1:T(8,128)(2,1)} %bitcast.14) | data formatting | bytes 4194304 | tf_op jit(solution)/shard_map/all_to_all | solution.py:145
  45.3 1.9 %pad_maximum_fusion.1 = bf16[8,64,144]{2,1,0:T(8,128)(2,1)} fusion(bf16[8,1024,128]{2,1,0:T(8,128)(2,1)} %bitcast.57, bf16[8,1024,16]{2,1,0:T(8,128)(2,1)S(1)} %bitcast.55), kind=kLoop, calls=%fused_computation.21 | loop fusion | flops 294912 | bytes 2506752 | tf_op jit(solution)/shard_map/concatenate | solution.py:155
  47.2 1.3 collective-permute-start.1
  48.6 2.4 %fusion.21 = (f32[8,153,128]{2,1,0:T(8,128)S(1)}, f32[8,2,153,128]{3,2,1,0:T(8,128)}) fusion(bf16[8,2,512,128]{3,2,1,0:T(8,128)(2,1)S(1)} %bitcast.58, bf16[8,2,512,136]{2,3,1,0:T(8,128)(2,1)S(1)} %copy-done.4, bf16[8,2,512,16]{2,3,1,0:T(8,128)(2,1)S(1)} %multiply_convert_fusion.3, bf16[153]{0:T(256)(128)(2,1)S(1)} %pad.9.clone), kind=kOutput, calls=%fused_computation.28 | convolution fusion | flops 328541184 | bytes 6467890 | tf_op jit(solution)/shard_map/hnrf,hnrv->hnfv/dot_general | solution.py:159
  50.9 1.2 copy.92
  52.1 1.3 collective-permute-start
  53.4 1.4 copy.96
  54.9 1.3 slice.26
  56.2 1.8 %copy.90 = bf16[256,512]{0,1:T(8,128)(2,1)} copy(bf16[256,512]{1,0:T(8,128)(2,1)} %param.9) | data formatting | bytes 524288 | tf_op jit(solution)/shard_map/optimization_barrier | solution.py:181
  57.9 4.0 %all-to-all-start.2 = ((bf16[32,256,16]{1,2,0:T(8,128)(2,1)}), bf16[32,256,16]{1,2,0:T(8,128)(2,1)}, u32[]{:S(2)}, u32[]{:S(2)}) async-start(bf16[32,256,16]{1,2,0:T(8,128)(2,1)} %bitcast.66), calls=%async_computation.2 | async-start | bytes 524288 | tf_op jit(solution)/shard_map/all_to_all | solution.py:145
  63.1 1.9 %pad_maximum_fusion.refs_3_ = bf16[8,1152,128]{2,1,0:T(8,128)(2,1)} fusion(bf16[8,1024,128]{2,1,0:T(8,128)(2,1)S(1)} %bitcast.59, bf16[8,64,128]{2,1,0:T(8,128)(2,1)S(1)} %slice.25, bf16[1152]{0:T(1024)(128)(2,1)S(1)} %pad.4.clone), kind=kLoop, calls=%fused_computation.12 | loop fusion | flops 7077888 | bytes 4589824 | tf_op jit(solution)/shard_map/concatenate | solution.py:199
  66.0 1.8 %concatenate.20 = bf16[8,1152,16]{1,2,0:T(8,128)(2,1)} concatenate(bf16[8,64,16]{1,2,0:T(8,128)(2,1)S(1)} %slice.18, bf16[8,64,16]{1,2,0:T(8,128)(2,1)S(1)} %copy.95, bf16[8,1024,16]{1,2,0:T(8,128)(2,1)} %copy.96), dimensions={1} | concatenate | bytes 589824 | tf_op jit(solution)/shard_map/concatenate | solution.py:198
  68.1 1.9 %copy.91 = bf16[8,4,256,16]{3,2,1,0:T(8,128)(2,1)S(1)} copy(bf16[8,4,256,16]{2,3,0,1:T(8,128)(2,1)} %bitcast.19) | data formatting | bytes 524288 | tf_op jit(solution)/shard_map/all_to_all | solution.py:145
  70.7 1.4 copy.97
  72.2 2.8 %fusion.22 = f32[8,2,512,136]{2,3,1,0:T(8,128)} fusion(bf16[8,2,512,16]{3,2,1,0:T(8,128)(2,1)S(1)} %bitcast.52, bf16[16,136,1,1]{1,0,3,2:T(8,128)(2,1)S(1)} %copy-done.7), kind=kOutput, calls=%fused_computation.29 | convolution fusion | flops 35651584 | bytes 4722944 | tf_op jit(solution)/shard_map/...d,df->...f/dot_general | solution.py:32
  75.0 2.3 %copy_add_fusion = f32[8,153,128]{2,0,1:T(8,128)} fusion(f32[8,153,128]{2,0,1:T(8,128)} %collective-permute-done, f32[8,153,128]{2,1,0:T(8,128)S(1)} %get-tuple-element.13), kind=kLoop, calls=%fused_computation.30 | loop fusion | flops 156672 | bytes 1880064 | tf_op jit(solution)/shard_map/add | solution.py:178
  77.3 1.6 %collective-permute-start.2 = (f32[8,153,128]{2,0,1:T(8,128)}, f32[8,153,128]{2,0,1:T(8,128)}, u32[]{:S(2)}, u32[]{:S(2)}) collective-permute-start(f32[8,153,128]{2,0,1:T(8,128)} %copy_add_fusion), channel_id=1, source_target_pairs={{0,8},{4,12},{1,9},{5,13},{2,10},{6,14},{3,11},{7,15},{16,24},{20,... | collective-permute-start | bytes 1880072 | tf_op jit(solution)/shard_map/ppermute | solution.py:24
  78.9 19.2 %shard_map.91 = (f32[1024,1024]{1,0:T(8,128)}, f32[1024,1024]{1,0:T(8,128)}) custom-call(s32[1]{0:T(128)} %bitcast.refs_0_, bf16[8,1024,16]{2,1,0:T(8,128)(2,1)} %bitcast.53, bf16[8,16,1152]{2,1,0:T(8,128)(2,1)} %bitcast.65, bf16[8,1152,128]{2,1,0:T(8,128)(2,1)} %pad_maximum_fusion.refs_3_), custom_call_target="tpu_custom_call" | custom-call | tf_op jit(solution)/shard_map/pallas_call | solution.py:93
  98.2 3.1 %fusion.10 = bf16[8,2,512,136]{2,3,1,0:T(8,128)(2,1)S(1)} fusion(f32[8,2,512,136]{2,3,1,0:T(8,128)} %fusion.22, bf16[8,2,512,16]{3,2,1,0:T(8,128)(2,1)S(1)} %bitcast.54, bf16[16,136,1,1]{1,0,3,2:T(8,128)(2,1)S(1)} %copy-done.6, bf16[136]{0:T(256)(128)(2,1)S(1)} %copy-done.8), kind=kOutput, calls=%fused_computation.13 | convolution fusion | flops 40108032 | bytes 6951440 | tf_op jit(solution)/shard_map/...d,df->...f/dot_general | solution.py:31
  101.3 9.6 %collective-permute-done.2 = f32[8,153,128]{2,0,1:T(8,128)} collective-permute-done((f32[8,153,128]{2,0,1:T(8,128)}, f32[8,153,128]{2,0,1:T(8,128)}, u32[]{:S(2)}, u32[]{:S(2)}) %collective-permute-start.2) | collective-permute-done | bytes 626720 | tf_op jit(solution)/shard_map/ppermute | solution.py:24
  110.9 1.3 add.18
  112.3 3.7 %fusion.5 = f32[8,2,512,128]{3,2,1,0:T(8,128)} fusion(bf16[8,2,512,136]{2,3,1,0:T(8,128)(2,1)S(1)} %fusion.10, bf16[8,2,512,16]{2,3,1,0:T(8,128)(2,1)S(1)} %multiply_convert_fusion.2, bf16[153]{0:T(256)(128)(2,1)S(1)} %pad.9.clone, f32[8,1,153,128]{3,2,1,0:T(8,128)S(1)} %slice.26, f32[8,153,128]{2,1,0:T(8,128)S(1)} %copy.101), kind=kOutput, calls=%fused_computation.7 | convolution fusion | flops 329011200 | bytes 7938354 | tf_op jit(solution)/shard_map/hnrf,hnfv->hnrv/dot_general | solution.py:190
  116.0 6.6 %shard_map.92 = bf16[1024,1024]{1,0:T(8,128)(2,1)} custom-call(f32[1024,1024]{1,0:T(8,128)} %get-tuple-element.11.intra_ref, f32[8,1024,128]{2,1,0:T(8,128)} %bitcast.60, f32[1024,1024]{1,0:T(8,128)} %get-tuple-element.12.win_ref, f32[1,1024]{1,0:T(1,128)} %bitcast.67), custom_call_target="tpu_custom_call" | custom-call | tf_op jit(solution)/shard_map/pallas_call | solution.py:126
  122.6 29.3 %all_to_all.73 = bf16[4,256,1024]{2,1,0:T(8,128)(2,1)S(1)} all-to-all(bf16[4,256,1024]{2,1,0:T(8,128)(2,1)} %bitcast.62), channel_id=1, replica_groups=mesh['groups'=2,'ctx'=4,'head'=4] {'head'}, dimensions={0} | all-to-all | bytes 4194304 | tf_op jit(solution)/shard_map/all_to_all | solution.py:205
  151.9 1.5 copy.109
  (35 shorter events, 5.5 us)
Async XLA Ops:
  1.8 9.4 %all-to-all-start = ((bf16[32,256,16]{1,2,0:T(8,128)(2,1)}), bf16[32,256,16]{1,2,0:T(8,128)(2,1)S(1)}, u32[]{:S(2)}, u32[]{:S(2)}) async-start(bf16[32,256,16]{1,2,0:T(8,128)(2,1)} %bitcast.2), calls=%async_computation | async-start | bytes 524288 | tf_op jit(solution)/shard_map/all_to_all | solution.py:145
  11.2 30.2 %all-to-all-start.1 = ((bf16[32,256,128]{1,2,0:T(8,128)(2,1)}), bf16[32,256,128]{1,2,0:T(8,128)(2,1)}, u32[]{:S(2)}, u32[]{:S(2)}) async-start(bf16[32,256,128]{1,2,0:T(8,128)(2,1)} %bitcast.11), calls=%async_computation.1 | async-start | bytes 4194304 | tf_op jit(solution)/shard_map/all_to_all | solution.py:145
  15.6 1.5 copy-start.6
  17.1 0.8 copy-start.7
  45.3 3.2 %copy-start.2 = (bf16[8,4,256,128]{3,2,1,0:T(8,128)(2,1)S(1)}, bf16[8,4,256,128]{3,2,1,0:T(8,128)(2,1)}, u32[]{:S(2)}) copy-start(bf16[8,4,256,128]{3,2,1,0:T(8,128)(2,1)} %copy.89) | copy-start | bytes 6291460
  45.3 3.2 %copy-start.4 = (bf16[8,2,512,136]{2,3,1,0:T(8,128)(2,1)S(1)}, bf16[8,2,512,136]{2,3,1,0:T(8,128)(2,1)}, u32[]{:S(2)}) copy-start(bf16[8,2,512,136]{2,3,1,0:T(8,128)(2,1)} %fusion.11) | copy-start | bytes 6684676
  47.2 14.7 %collective-permute-start.1 = (bf16[8,64,144]{2,1,0:T(8,128)(2,1)}, bf16[8,64,144]{2,1,0:T(8,128)(2,1)}, u32[]{:S(2)}, u32[]{:S(2)}) collective-permute-start(bf16[8,64,144]{2,1,0:T(8,128)(2,1)} %pad_maximum_fusion.1), channel_id=1, source_target_pairs={{0,4},{4,8},{8,12},{1,5},{5,9},{9,13},{2,6},{6,10},{10,14},{3,7},{... | collective-permute-start | bytes 442376 | tf_op jit(solution)/shard_map/ppermute | solution.py:24
  52.1 18.6 %collective-permute-start = (f32[8,153,128]{2,0,1:T(8,128)}, f32[8,153,128]{2,0,1:T(8,128)}, u32[]{:S(2)}, u32[]{:S(2)}) collective-permute-start(f32[8,153,128]{2,0,1:T(8,128)} %copy.92), channel_id=1, source_target_pairs={{0,4},{4,8},{8,12},{1,5},{5,9},{9,13},{2,6},{6,10},{10,14},{3,7},{... | collective-permute-start | bytes 1880072 | tf_op jit(solution)/shard_map/ppermute | solution.py:24
  54.9 8.2 %copy-start.3 = (bf16[8,4,256,128]{3,2,1,0:T(8,128)(2,1)S(1)}, bf16[8,4,256,128]{3,2,1,0:T(8,128)(2,1)}, u32[]{:S(2)}) copy-start(bf16[8,4,256,128]{3,2,1,0:T(8,128)(2,1)} %copy.89) | copy-start | bytes 6291460
  57.9 10.1 %all-to-all-start.2 = ((bf16[32,256,16]{1,2,0:T(8,128)(2,1)}), bf16[32,256,16]{1,2,0:T(8,128)(2,1)}, u32[]{:S(2)}, u32[]{:S(2)}) async-start(bf16[32,256,16]{1,2,0:T(8,128)(2,1)} %bitcast.66), calls=%async_computation.2 | async-start | bytes 524288 | tf_op jit(solution)/shard_map/all_to_all | solution.py:145
  70.0 5.0 %copy-start = (bf16[8,4,256,16]{3,2,1,0:T(8,128)(2,1)}, bf16[8,4,256,16]{3,2,1,0:T(8,128)(2,1)S(1)}, u32[]{:S(2)}) copy-start(bf16[8,4,256,16]{3,2,1,0:T(8,128)(2,1)S(1)} %copy.91) | copy-start | bytes 786436
  77.3 20.9 %copy-start.5 = (bf16[8,2,512,16]{2,3,1,0:T(8,128)(2,1)S(1)}, bf16[8,2,512,16]{2,3,1,0:T(8,128)(2,1)}, u32[]{:S(2)}) copy-start(bf16[8,2,512,16]{2,3,1,0:T(8,128)(2,1)} %copy.97) | copy-start | bytes 786436
  77.3 33.6 %collective-permute-start.2 = (f32[8,153,128]{2,0,1:T(8,128)}, f32[8,153,128]{2,0,1:T(8,128)}, u32[]{:S(2)}, u32[]{:S(2)}) collective-permute-start(f32[8,153,128]{2,0,1:T(8,128)} %copy_add_fusion), channel_id=1, source_target_pairs={{0,8},{4,12},{1,9},{5,13},{2,10},{6,14},{3,11},{7,15},{16,24},{20,... | collective-permute-start | bytes 1880072 | tf_op jit(solution)/shard_map/ppermute | solution.py:24
  78.9 19.3 %copy-start.1 = (bf16[8,4,256,16]{3,2,1,0:T(8,128)(2,1)S(1)}, bf16[8,4,256,16]{3,2,1,0:T(8,128)(2,1)}, u32[]{:S(2)}) copy-start(bf16[8,4,256,16]{3,2,1,0:T(8,128)(2,1)} %copy-done) | copy-start | bytes 786436
  78.9 19.3 %copy-start.8 = (bf16[136]{0:T(256)(128)(2,1)S(1)}, bf16[136]{0:T(256)(128)(2,1)}, u32[]{:S(2)}) copy-start(bf16[136]{0:T(256)(128)(2,1)} %constant.30.clone) | copy-start | bytes 820

commit v23 on v20

--- a/solution.py
+++ b/solution.py
@@ -118,7 +118,7 @@
 
 def mix(intra, inter_hm, window, gain):
     heads_here, span_rows, _ = inter_hm.shape
-    step = 4 if heads_here % 4 == 0 else (2 if heads_here % 2 == 0 else 1)
+    step = heads_here
     tile = pl.BlockSpec((span_rows, step * VD), lambda h: (0, h))
     return pl.pallas_call(
         mix_kernel,

time: 154 us -> 155 us (level)
  no operation moved by 1% of the time
where the time goes in v23:
time: 155 us; the launch traced here: 154 us
  waiting for transfers between devices  34.3 us (22%)
  blocking collectives  29.3 us (19%)
  Pallas kernels  26.1 us (17%)
  local copies, waits for them, and re-layouts  25.7 us (17%)
  starting transfers between devices  16 us (10%)
  matrix products  14.8 us (10%)
  other arithmetic  7.54 us (5%)
    all_to_all x1, blocking collectives, per_device(): lax.all_to_all(mixed, 'head', split_axis=0, concat_axis=1, tiled=True)  29.3 us
    all_to_all x3, waiting for transfers between devices, to_heads(): return lax.all_to_all(tok, 'head', split_axis=0, concat_axis=1, tiled=True)  23.5 us
    pallas_call x1, Pallas kernels, local_attention(): pl.pallas_call(body, grid_spec=pltpu.PrefetchScalarGridSpec(num_scalar_pr...  18.8 us
    all_to_all x3, starting transfers between devices, to_heads(): return lax.all_to_all(tok, 'head', split_axis=0, concat_axis=1, tiled=True)  11.9 us
    ppermute x3, waiting for transfers between devices, shifted(): return lax.ppermute(shard, axis, pairs)  10.8 us
    all_to_all x5, local copies, waits for them, and re-layouts, to_heads(): return lax.all_to_all(tok, 'head', split_axis=0, concat_axis=1, tiled=True)  8.5 us
    pallas_call x1, Pallas kernels, mix(): pl.pallas_call(mix_kernel, grid=(heads_here // step,), in_specs=[tile, pl...  7.3 us
    unnamed x20, local copies, waits for them, and re-layouts  5.9 us
  transfers between devices with their start and end apart: 6, of which 5 were waited for; matrix products, arithmetic and copies ran while one was open for 18% of the time, Pallas kernels for 12%

profile of v23, /device:TPU:28, one launch (start us, length us, event | category | flops | bytes accessed | tf_op | source)
XLA Modules:
  0.0 154.1 jit_solution(9411415242755917829)
XLA Ops:
  0.0 1.8 %copy.82 = bf16[256,512]{0,1:T(8,128)(2,1)} copy(bf16[256,512]{1,0:T(8,128)(2,1)} %param.10) | data formatting | bytes 524288 | tf_op args[1]
  1.8 3.4 %all-to-all-start = ((bf16[32,256,16]{1,2,0:T(8,128)(2,1)}), bf16[32,256,16]{1,2,0:T(8,128)(2,1)S(1)}, u32[]{:S(2)}, u32[]{:S(2)}) async-start(bf16[32,256,16]{1,2,0:T(8,128)(2,1)} %bitcast.2), calls=%async_computation | async-start | bytes 524288 | tf_op jit(solution)/shard_map/all_to_all | solution.py:142
  5.2 4.1 %copy.87 = bf16[256,4096]{0,1:T(8,128)(2,1)} copy(bf16[256,4096]{1,0:T(8,128)(2,1)} %param.11) | data formatting | bytes 4194304 | tf_op args[2]
  9.3 1.9 %all-to-all-done = bf16[32,256,16]{1,2,0:T(8,128)(2,1)S(1)} async-done(((bf16[32,256,16]{1,2,0:T(8,128)(2,1)}), bf16[32,256,16]{1,2,0:T(8,128)(2,1)S(1)}, u32[]{:S(2)}, u32[]{:S(2)}) %all-to-all-start) | async-done | bytes 262176 | tf_op jit(solution)/shard_map/all_to_all | solution.py:142
  11.2 4.4 %all-to-all-start.1 = ((bf16[32,256,128]{1,2,0:T(8,128)(2,1)}), bf16[32,256,128]{1,2,0:T(8,128)(2,1)}, u32[]{:S(2)}, u32[]{:S(2)}) async-start(bf16[32,256,128]{1,2,0:T(8,128)(2,1)} %bitcast.11), calls=%async_computation.1 | async-start | bytes 4194304 | tf_op jit(solution)/shard_map/all_to_all | solution.py:142
  17.9 2.1 %fusion.11 = bf16[8,2,512,136]{2,3,1,0:T(8,128)(2,1)} fusion(f32[136,8,2,512]{3,0,2,1:T(8,128)S(1)} %fusion.16, bf16[16,136,1,1]{1,0,3,2:T(8,128)(2,1)S(1)} %copy-done.7, bf16[8,2,512,16]{2,1,3,0:T(2,128)(2,1)S(1)} %reshape.39), kind=kOutput, calls=%fused_computation.14 | convolution fusion | flops 38993920 | bytes 6951168 | tf_op jit(solution)/shard_map/...d,df->...f/dot_general | solution.py:32
  20.1 21.3 %all-to-all-done.1 = bf16[32,256,128]{1,2,0:T(8,128)(2,1)} async-done(((bf16[32,256,128]{1,2,0:T(8,128)(2,1)}), bf16[32,256,128]{1,2,0:T(8,128)(2,1)}, u32[]{:S(2)}, u32[]{:S(2)}) %all-to-all-start.1) | async-done | bytes 2097184 | tf_op jit(solution)/shard_map/all_to_all | solution.py:142
  41.4 3.9 %copy.89 = bf16[8,4,256,128]{3,2,1,0:T(8,128)(2,1)} copy(bf16[8,4,256,128]{2,3,0,1:T(8,128)(2,1)} %bitcast.14) | data formatting | bytes 4194304 | tf_op jit(solution)/shard_map/all_to_all | solution.py:142
  45.3 1.9 %pad_maximum_fusion.1 = bf16[8,64,144]{2,1,0:T(8,128)(2,1)} fusion(bf16[8,1024,128]{2,1,0:T(8,128)(2,1)} %bitcast.57, bf16[8,1024,16]{2,1,0:T(8,128)(2,1)S(1)} %bitcast.55), kind=kLoop, calls=%fused_computation.21 | loop fusion | flops 294912 | bytes 2506752 | tf_op jit(solution)/shard_map/concatenate | solution.py:152
  47.2 1.3 collective-permute-start.1
  48.6 2.4 %fusion.21 = (f32[8,153,128]{2,1,0:T(8,128)S(1)}, f32[8,2,153,128]{3,2,1,0:T(8,128)}) fusion(bf16[8,2,512,128]{3,2,1,0:T(8,128)(2,1)S(1)} %bitcast.58, bf16[8,2,512,136]{2,3,1,0:T(8,128)(2,1)S(1)} %copy-done.4, bf16[8,2,512,16]{2,3,1,0:T(8,128)(2,1)S(1)} %multiply_convert_fusion.3, bf16[153]{0:T(256)(128)(2,1)S(1)} %pad.9.clone), kind=kOutput, calls=%fused_computation.28 | convolution fusion | flops 328541184 | bytes 6467890 | tf_op jit(solution)/shard_map/hnrf,hnrv->hnfv/dot_general | solution.py:156
  50.9 1.2 copy.92
  52.1 1.3 collective-permute-start
  53.4 1.4 copy.96
  54.9 1.3 slice.26
  56.2 1.8 %copy.90 = bf16[256,512]{0,1:T(8,128)(2,1)} copy(bf16[256,512]{1,0:T(8,128)(2,1)} %param.9) | data formatting | bytes 524288 | tf_op jit(solution)/shard_map/optimization_barrier | solution.py:178
  57.9 4.0 %all-to-all-start.2 = ((bf16[32,256,16]{1,2,0:T(8,128)(2,1)}), bf16[32,256,16]{1,2,0:T(8,128)(2,1)}, u32[]{:S(2)}, u32[]{:S(2)}) async-start(bf16[32,256,16]{1,2,0:T(8,128)(2,1)} %bitcast.66), calls=%async_computation.2 | async-start | bytes 524288 | tf_op jit(solution)/shard_map/all_to_all | solution.py:142
  63.1 1.9 %pad_maximum_fusion.refs_3_ = bf16[8,1152,128]{2,1,0:T(8,128)(2,1)} fusion(bf16[8,1024,128]{2,1,0:T(8,128)(2,1)S(1)} %bitcast.59, bf16[8,64,128]{2,1,0:T(8,128)(2,1)S(1)} %slice.25, bf16[1152]{0:T(1024)(128)(2,1)S(1)} %pad.4.clone), kind=kLoop, calls=%fused_computation.12 | loop fusion | flops 7077888 | bytes 4589824 | tf_op jit(solution)/shard_map/concatenate | solution.py:196
  66.0 1.8 %concatenate.20 = bf16[8,1152,16]{1,2,0:T(8,128)(2,1)} concatenate(bf16[8,64,16]{1,2,0:T(8,128)(2,1)S(1)} %slice.18, bf16[8,64,16]{1,2,0:T(8,128)(2,1)S(1)} %copy.95, bf16[8,1024,16]{1,2,0:T(8,128)(2,1)} %copy.96), dimensions={1} | concatenate | bytes 589824 | tf_op jit(solution)/shard_map/concatenate | solution.py:195
  68.1 1.9 %copy.91 = bf16[8,4,256,16]{3,2,1,0:T(8,128)(2,1)S(1)} copy(bf16[8,4,256,16]{2,3,0,1:T(8,128)(2,1)} %bitcast.19) | data formatting | bytes 524288 | tf_op jit(solution)/shard_map/all_to_all | solution.py:142
  70.7 1.4 copy.97
  72.2 2.8 %fusion.22 = f32[8,2,512,136]{2,3,1,0:T(8,128)} fusion(bf16[8,2,512,16]{3,2,1,0:T(8,128)(2,1)S(1)} %bitcast.52, bf16[16,136,1,1]{1,0,3,2:T(8,128)(2,1)S(1)} %copy-done.7), kind=kOutput, calls=%fused_computation.29 | convolution fusion | flops 35651584 | bytes 4722944 | tf_op jit(solution)/shard_map/...d,df->...f/dot_general | solution.py:32
  75.0 2.3 %copy_add_fusion = f32[8,153,128]{2,0,1:T(8,128)} fusion(f32[8,153,128]{2,0,1:T(8,128)} %collective-permute-done, f32[8,153,128]{2,1,0:T(8,128)S(1)} %get-tuple-element.13), kind=kLoop, calls=%fused_computation.30 | loop fusion | flops 156672 | bytes 1880064 | tf_op jit(solution)/shard_map/add | solution.py:175
  77.3 1.6 %collective-permute-start.2 = (f32[8,153,128]{2,0,1:T(8,128)}, f32[8,153,128]{2,0,1:T(8,128)}, u32[]{:S(2)}, u32[]{:S(2)}) collective-permute-start(f32[8,153,128]{2,0,1:T(8,128)} %copy_add_fusion), channel_id=1, source_target_pairs={{0,8},{4,12},{1,9},{5,13},{2,10},{6,14},{3,11},{7,15},{16,24},{20,... | collective-permute-start | bytes 1880072 | tf_op jit(solution)/shard_map/ppermute | solution.py:24
  78.9 18.8 %shard_map.91 = (f32[1024,1024]{1,0:T(8,128)}, f32[1024,1024]{1,0:T(8,128)}) custom-call(s32[1]{0:T(128)} %bitcast.refs_0_, bf16[8,1024,16]{2,1,0:T(8,128)(2,1)} %bitcast.53, bf16[8,16,1152]{2,1,0:T(8,128)(2,1)} %bitcast.65, bf16[8,1152,128]{2,1,0:T(8,128)(2,1)} %pad_maximum_fusion.refs_3_), custom_call_target="tpu_custom_call" | custom-call | tf_op jit(solution)/shard_map/pallas_call | solution.py:90
  97.8 3.1 %fusion.10 = bf16[8,2,512,136]{2,3,1,0:T(8,128)(2,1)S(1)} fusion(f32[8,2,512,136]{2,3,1,0:T(8,128)} %fusion.22, bf16[8,2,512,16]{3,2,1,0:T(8,128)(2,1)S(1)} %bitcast.54, bf16[16,136,1,1]{1,0,3,2:T(8,128)(2,1)S(1)} %copy-done.6, bf16[136]{0:T(256)(128)(2,1)S(1)} %copy-done.8), kind=kOutput, calls=%fused_computation.13 | convolution fusion | flops 40108032 | bytes 6951440 | tf_op jit(solution)/shard_map/...d,df->...f/dot_general | solution.py:31
  100.8 10.1 %collective-permute-done.2 = f32[8,153,128]{2,0,1:T(8,128)} collective-permute-done((f32[8,153,128]{2,0,1:T(8,128)}, f32[8,153,128]{2,0,1:T(8,128)}, u32[]{:S(2)}, u32[]{:S(2)}) %collective-permute-start.2) | collective-permute-done | bytes 626720 | tf_op jit(solution)/shard_map/ppermute | solution.py:24
  110.9 1.3 add.18
  112.3 3.7 %fusion.5 = f32[8,2,512,128]{3,2,1,0:T(8,128)} fusion(bf16[8,2,512,136]{2,3,1,0:T(8,128)(2,1)S(1)} %fusion.10, bf16[8,2,512,16]{2,3,1,0:T(8,128)(2,1)S(1)} %multiply_convert_fusion.2, bf16[153]{0:T(256)(128)(2,1)S(1)} %pad.9.clone, f32[8,1,153,128]{3,2,1,0:T(8,128)S(1)} %slice.26, f32[8,153,128]{2,1,0:T(8,128)S(1)} %copy.101), kind=kOutput, calls=%fused_computation.7 | convolution fusion | flops 329011200 | bytes 7938354 | tf_op jit(solution)/shard_map/hnrf,hnfv->hnrv/dot_general | solution.py:187
  116.0 7.3 %shard_map.92 = bf16[1024,1024]{1,0:T(8,128)(2,1)} custom-call(f32[1024,1024]{1,0:T(8,128)} %get-tuple-element.11.intra_ref, f32[8,1024,128]{2,1,0:T(8,128)} %bitcast.60, f32[1024,1024]{1,0:T(8,128)} %get-tuple-element.12.win_ref, f32[1,1024]{1,0:T(1,128)} %bitcast.67), custom_call_target="tpu_custom_call" | custom-call | tf_op jit(solution)/shard_map/pallas_call | solution.py:123
  123.3 29.3 %all_to_all.73 = bf16[4,256,1024]{2,1,0:T(8,128)(2,1)S(1)} all-to-all(bf16[4,256,1024]{2,1,0:T(8,128)(2,1)} %bitcast.62), channel_id=1, replica_groups=mesh['groups'=2,'ctx'=4,'head'=4] {'head'}, dimensions={0} | all-to-all | bytes 4194304 | tf_op jit(solution)/shard_map/all_to_all | solution.py:202
  152.6 1.5 copy.109
  (35 shorter events, 5.5 us)
Async XLA Ops:
  1.8 9.4 %all-to-all-start = ((bf16[32,256,16]{1,2,0:T(8,128)(2,1)}), bf16[32,256,16]{1,2,0:T(8,128)(2,1)S(1)}, u32[]{:S(2)}, u32[]{:S(2)}) async-start(bf16[32,256,16]{1,2,0:T(8,128)(2,1)} %bitcast.2), calls=%async_computation | async-start | bytes 524288 | tf_op jit(solution)/shard_map/all_to_all | solution.py:142
  11.2 30.2 %all-to-all-start.1 = ((bf16[32,256,128]{1,2,0:T(8,128)(2,1)}), bf16[32,256,128]{1,2,0:T(8,128)(2,1)}, u32[]{:S(2)}, u32[]{:S(2)}) async-start(bf16[32,256,128]{1,2,0:T(8,128)(2,1)} %bitcast.11), calls=%async_computation.1 | async-start | bytes 4194304 | tf_op jit(solution)/shard_map/all_to_all | solution.py:142
  15.6 1.5 copy-start.6
  17.1 0.8 copy-start.7
  45.3 3.2 %copy-start.2 = (bf16[8,4,256,128]{3,2,1,0:T(8,128)(2,1)S(1)}, bf16[8,4,256,128]{3,2,1,0:T(8,128)(2,1)}, u32[]{:S(2)}) copy-start(bf16[8,4,256,128]{3,2,1,0:T(8,128)(2,1)} %copy.89) | copy-start | bytes 6291460
  45.3 3.2 %copy-start.4 = (bf16[8,2,512,136]{2,3,1,0:T(8,128)(2,1)S(1)}, bf16[8,2,512,136]{2,3,1,0:T(8,128)(2,1)}, u32[]{:S(2)}) copy-start(bf16[8,2,512,136]{2,3,1,0:T(8,128)(2,1)} %fusion.11) | copy-start | bytes 6684676
  47.2 14.7 %collective-permute-start.1 = (bf16[8,64,144]{2,1,0:T(8,128)(2,1)}, bf16[8,64,144]{2,1,0:T(8,128)(2,1)}, u32[]{:S(2)}, u32[]{:S(2)}) collective-permute-start(bf16[8,64,144]{2,1,0:T(8,128)(2,1)} %pad_maximum_fusion.1), channel_id=1, source_target_pairs={{0,4},{4,8},{8,12},{1,5},{5,9},{9,13},{2,6},{6,10},{10,14},{3,7},{... | collective-permute-start | bytes 442376 | tf_op jit(solution)/shard_map/ppermute | solution.py:24
  52.1 18.6 %collective-permute-start = (f32[8,153,128]{2,0,1:T(8,128)}, f32[8,153,128]{2,0,1:T(8,128)}, u32[]{:S(2)}, u32[]{:S(2)}) collective-permute-start(f32[8,153,128]{2,0,1:T(8,128)} %copy.92), channel_id=1, source_target_pairs={{0,4},{4,8},{8,12},{1,5},{5,9},{9,13},{2,6},{6,10},{10,14},{3,7},{... | collective-permute-start | bytes 1880072 | tf_op jit(solution)/shard_map/ppermute | solution.py:24
  54.9 8.2 %copy-start.3 = (bf16[8,4,256,128]{3,2,1,0:T(8,128)(2,1)S(1)}, bf16[8,4,256,128]{3,2,1,0:T(8,128)(2,1)}, u32[]{:S(2)}) copy-start(bf16[8,4,256,128]{3,2,1,0:T(8,128)(2,1)} %copy.89) | copy-start | bytes 6291460
  57.9 10.1 %all-to-all-start.2 = ((bf16[32,256,16]{1,2,0:T(8,128)(2,1)}), bf16[32,256,16]{1,2,0:T(8,128)(2,1)}, u32[]{:S(2)}, u32[]{:S(2)}) async-start(bf16[32,256,16]{1,2,0:T(8,128)(2,1)} %bitcast.66), calls=%async_computation.2 | async-start | bytes 524288 | tf_op jit(solution)/shard_map/all_to_all | solution.py:142
  70.0 5.0 %copy-start = (bf16[8,4,256,16]{3,2,1,0:T(8,128)(2,1)}, bf16[8,4,256,16]{3,2,1,0:T(8,128)(2,1)S(1)}, u32[]{:S(2)}) copy-start(bf16[8,4,256,16]{3,2,1,0:T(8,128)(2,1)S(1)} %copy.91) | copy-start | bytes 786436
  77.3 20.4 %copy-start.5 = (bf16[8,2,512,16]{2,3,1,0:T(8,128)(2,1)S(1)}, bf16[8,2,512,16]{2,3,1,0:T(8,128)(2,1)}, u32[]{:S(2)}) copy-start(bf16[8,2,512,16]{2,3,1,0:T(8,128)(2,1)} %copy.97) | copy-start | bytes 786436
  77.3 33.6 %collective-permute-start.2 = (f32[8,153,128]{2,0,1:T(8,128)}, f32[8,153,128]{2,0,1:T(8,128)}, u32[]{:S(2)}, u32[]{:S(2)}) collective-permute-start(f32[8,153,128]{2,0,1:T(8,128)} %copy_add_fusion), channel_id=1, source_target_pairs={{0,8},{4,12},{1,9},{5,13},{2,10},{6,14},{3,11},{7,15},{16,24},{20,... | collective-permute-start | bytes 1880072 | tf_op jit(solution)/shard_map/ppermute | solution.py:24
  78.9 18.9 %copy-start.1 = (bf16[8,4,256,16]{3,2,1,0:T(8,128)(2,1)S(1)}, bf16[8,4,256,16]{3,2,1,0:T(8,128)(2,1)}, u32[]{:S(2)}) copy-start(bf16[8,4,256,16]{3,2,1,0:T(8,128)(2,1)} %copy-done) | copy-start | bytes 786436
  78.9 18.9 %copy-start.8 = (bf16[136]{0:T(256)(128)(2,1)S(1)}, bf16[136]{0:T(256)(128)(2,1)}, u32[]{:S(2)}) copy-start(bf16[136]{0:T(256)(128)(2,1)} %constant.30.clone) | copy-start | bytes 820
